TPU v7x, 128 devices: a whole 4x4x4 slice. The times are simulated.
128 devices in a mesh: section: 8 (over x, core), dp: 16 (over z, y).
Axes of the slice: x: 4, y: 4, z: 4, core: 2. Of those that a mesh axis runs over, the one named last changes fastest.
Arguments:
- micro_inputs: bfloat16 [4, 1024, 4096], P(None, 'dp'), may hold values from -6 to 6
- out_cotangent: bfloat16 [4, 1024, 4096], P(None, 'dp'), may hold values from -0.25 to 0.25
- weight_a: bfloat16 [2, 8, 4096, 512], P(None, 'section'), may hold values from -0.09375 to 0.09375
- weight_b: bfloat16 [2, 8, 512, 4096], P(None, 'section'), may hold values from -0.25 to 0.25
- mask_a: int32 [2, 8, 64, 8], P(None, 'section'), may hold values from 0 to 1, as said below
- mask_b: int32 [2, 8, 8, 64], P(None, 'section'), may hold values from 0 to 1, as said below
Outputs:
- grad_a: float32 [2, 8, 4096, 512], P(None, 'section', 'dp')
- grad_b: float32 [2, 8, 512, 4096], P(None, 'section', None, 'dp')
Inputs may be any that keep to these rules, and one draw needn't show every extreme that they name: Each block of a layer is kept with a probability drawn for that layer from 30 to 50 percent; mask_a and mask_b of one layer share it. `mask_b`: drawn with the same per-layer probabilities as mask_a.
All inputs are finite; a program needn't handle non-finite values.
Results may differ from a plain program's by a relative error of at most 0.033.
Values may be sent and summed in bfloat16 or wider, within the bound.
No kernel may reach another device: no remote copies, remote signals or barrier semaphores. Data moves between devices by JAX's collectives and lax.ppermute only.
A program may use at most 192 MiB of HBM per device.

v0:
```python
import jax
import jax.numpy as jnp
from jax import lax
from jax.sharding import PartitionSpec as P

BLK = 64


EPS = 1e-05


def shortened(shard):
    return jax.tree.map(lambda a: a.astype(jnp.bfloat16) if a.dtype == jnp.float32 else a, shard)


def shifted(block, axis, distance):
    devices = range(lax.axis_size(axis))
    route = [((i - distance) % len(devices), i) for i in devices]
    return lax.ppermute(block, axis, route)


def expand_blocks(mask):
    return jnp.repeat(jnp.repeat(mask, BLK, axis=-2), BLK, axis=-1)


def normalize(values):
    wide = values.astype(jnp.float32)
    inverse = lax.rsqrt(jnp.mean(wide * wide, axis=-1, keepdims=True) + EPS)
    return (wide * inverse, inverse)


def forward_layer(values, eff_a, eff_b):
    scaled, inverse = normalize(values)
    preact = jnp.dot(scaled.astype(jnp.bfloat16), eff_a, preferred_element_type=jnp.float32)
    hidden = (preact * jax.nn.sigmoid(preact)).astype(jnp.bfloat16)
    mixed = values.astype(jnp.float32) + jnp.dot(hidden, eff_b, preferred_element_type=jnp.float32)
    return mixed.astype(jnp.bfloat16)


def backward_layer(values, upstream, eff_a, eff_b):
    scaled, inverse = normalize(values)
    normed = scaled.astype(jnp.bfloat16)
    preact = jnp.dot(normed, eff_a, preferred_element_type=jnp.float32)
    sigma = jax.nn.sigmoid(preact)
    hidden = (preact * sigma).astype(jnp.bfloat16)
    back_hidden = lax.dot_general(
        upstream, eff_b, (((1,), (1,)), ((), ())), preferred_element_type=jnp.float32
    )
    back_pre = (back_hidden * sigma * (1.0 + preact * (1.0 - sigma))).astype(jnp.bfloat16)
    back_norm = lax.dot_general(
        back_pre, eff_a, (((1,), (1,)), ((), ())), preferred_element_type=jnp.float32
    )
    center = jnp.mean(back_norm * scaled, axis=-1, keepdims=True)
    downstream = (upstream.astype(jnp.float32) + inverse * (back_norm - scaled * center)).astype(
        jnp.bfloat16
    )
    return (downstream, normed, hidden, back_pre)


def place_item(buffer, lap_now, micro, value):
    anchor = jnp.int32(0)
    return lax.dynamic_update_slice(buffer, value[None, None], (lap_now, micro, anchor, anchor))


def settle(lap_idx, stores, mask_a, mask_b):
    normed_all, upstream_all, hidden_all, back_all = [
        buffer[lap_idx].reshape(-1, buffer.shape[-1]) for buffer in stores
    ]
    groups = lax.axis_size("dp")
    owner = lax.axis_index("dp")
    span = normed_all.shape[1] // groups
    part_a = lax.dot_general(
        normed_all, back_all, (((0,), (0,)), ((), ())), preferred_element_type=jnp.float32
    )
    part_b = lax.dot_general(
        upstream_all, hidden_all, (((0,), (0,)), ((), ())), preferred_element_type=jnp.float32
    )
    sum_a, sum_b = (
        lax.psum_scatter(part_a.astype(jnp.bfloat16), "dp", scatter_dimension=0, tiled=True).astype(
            jnp.float32
        ),
        lax.psum_scatter(part_b.astype(jnp.bfloat16), "dp", scatter_dimension=0, tiled=True).astype(
            jnp.float32
        ),
    )
    full_a = expand_blocks(mask_a[lap_idx, 0]).astype(jnp.float32)
    full_b = expand_blocks(mask_b[lap_idx, 0]).astype(jnp.float32)
    owned_a = lax.dynamic_slice_in_dim(full_a, owner * span, span, 0)
    owned_b = lax.dynamic_slice_in_dim(full_b, owner * span, span, 1)
    return (sum_a * owned_a, jnp.transpose(sum_b) * owned_b)


def on_device(micro_inputs, out_cotangent, weight_a, weight_b, mask_a, mask_b):
    sections = lax.axis_size("section")
    here = lax.axis_index("section")
    batches, tokens, width = micro_inputs.shape
    inner = weight_a.shape[3]
    eff_a = weight_a[:, 0] * expand_blocks(mask_a[:, 0]).astype(jnp.bfloat16)
    eff_b = weight_b[:, 0] * expand_blocks(mask_b[:, 0]).astype(jnp.bfloat16)

    def spare_forward(values):
        return jnp.zeros_like(values)

    def forward_zero(values):
        return forward_layer(values, eff_a[0], eff_b[0])

    def forward_one(values):
        return forward_layer(values, eff_a[1], eff_b[1])

    def forward_step(step, carry):
        incoming, saved = carry
        first_micro = step - here
        second_micro = first_micro - sections
        first_on = (first_micro >= 0) & (first_micro < batches)
        second_on = (second_micro >= 0) & (second_micro < batches)
        lap_now = second_on.astype(jnp.int32)
        micro = jnp.clip(jnp.where(second_on, second_micro, first_micro), 0, batches - 1)
        values = jnp.where((here == 0) & (lap_now == 0), micro_inputs[micro], incoming)
        branch = first_on.astype(jnp.int32) + 2 * second_on.astype(jnp.int32)
        result = lax.switch(branch, [spare_forward, forward_zero, forward_one], values)
        keep = jnp.where(first_on | second_on, values, saved[lap_now, micro])
        saved = place_item(saved, lap_now, micro, keep)
        incoming = jax.tree.map(
            lambda part, own: part.astype(own.dtype),
            shifted(shortened(result), "section", 1),
            result,
        )
        return (incoming, saved)

    start_rows = jnp.zeros((tokens, width), jnp.bfloat16)
    saved_rows = jnp.zeros((2, batches, tokens, width), jnp.bfloat16)
    incoming, saved_rows = lax.fori_loop(
        0, batches + 2 * sections - 1, forward_step, (start_rows, saved_rows)
    )

    def spare_backward(values, upstream):
        wide_zero = jnp.zeros((tokens, width), jnp.bfloat16)
        narrow_zero = jnp.zeros((tokens, inner), jnp.bfloat16)
        return (wide_zero, wide_zero, narrow_zero, narrow_zero)

    def backward_zero(values, upstream):
        return backward_layer(values, upstream, eff_a[0], eff_b[0])

    def backward_one(values, upstream):
        return backward_layer(values, upstream, eff_a[1], eff_b[1])

    def backward_step(step, carry):
        incoming, stores = carry
        second_micro = step - (sections - 1 - here)
        first_micro = second_micro - sections
        first_on = (first_micro >= 0) & (first_micro < batches)
        second_on = (second_micro >= 0) & (second_micro < batches)
        lap_now = jnp.where(first_on, 0, 1).astype(jnp.int32)
        micro = jnp.clip(jnp.where(first_on, first_micro, second_micro), 0, batches - 1)
        upstream = jnp.where(
            (here == sections - 1) & (lap_now == 1), out_cotangent[micro], incoming
        )
        values = saved_rows[lap_now, micro]
        branch = first_on.astype(jnp.int32) + 2 * second_on.astype(jnp.int32)
        downstream, normed, hidden, back_pre = lax.switch(
            branch, [spare_backward, backward_zero, backward_one], values, upstream
        )
        active = first_on | second_on
        fresh = (normed, upstream, hidden, back_pre)
        stores = tuple(
            (
                place_item(buffer, lap_now, micro, jnp.where(active, item, buffer[lap_now, micro]))
                for buffer, item in zip(stores, fresh)
            )
        )
        incoming = jax.tree.map(
            lambda part, own: part.astype(own.dtype),
            shifted(shortened(downstream), "section", -1),
            downstream,
        )
        return (incoming, stores)

    stores = (
        jnp.zeros((2, batches, tokens, width), jnp.bfloat16),
        jnp.zeros((2, batches, tokens, width), jnp.bfloat16),
        jnp.zeros((2, batches, tokens, inner), jnp.bfloat16),
        jnp.zeros((2, batches, tokens, inner), jnp.bfloat16),
    )
    middle = batches + sections - 1
    finish = batches + 2 * sections - 1
    carry = lax.fori_loop(0, middle, backward_step, (start_rows, stores))
    carry = lax.fori_loop(middle, finish, backward_step, carry)
    later_one = settle(1, carry[1], mask_a, mask_b)
    later_zero = settle(0, carry[1], mask_a, mask_b)
    grad_a = jnp.stack([later_zero[0], later_one[0]])[:, None]
    grad_b = jnp.stack([later_zero[1], later_one[1]])[:, None]
    return (grad_a, grad_b)


def solution(mesh):
    placed = (
        P(None, "dp", None),
        P(None, "dp", None),
        P(None, "section", None, None),
        P(None, "section", None, None),
        P(None, "section", None, None),
        P(None, "section", None, None),
    )
    return jax.shard_map(
        on_device,
        mesh=mesh,
        in_specs=placed,
        out_specs=(P(None, "section", "dp", None), P(None, "section", None, "dp")),
        check_vma=False,
    )
```

profile of v0, /device:TPU:0, one launch (start us, length us, event | category | flops | bytes accessed | tf_op | source)
XLA Modules:
  0.0 1129.2 jit_solution(7353159801726661730)
XLA Ops:
  7.2 12.0 %copy.16 = bf16[2,1,512,4096]{2,3,0,1:T(8,128)(2,1)} copy(bf16[2,1,512,4096]{3,2,1,0:T(8,128)(2,1)} %param.24) | data formatting | bytes 16777216 | tf_op args[3]
  26.9 11.3 copy.19
  38.2 11.2 copy.15
  57.2 12.0 %copy.18 = bf16[2,4096,512]{2,1,0:T(8,128)(2,1)} copy(bf16[2,4096,512]{1,2,0:T(8,128)(2,1)} %bitcast_multiply_fusion.1) | data formatting | bytes 16777216 | tf_op jit(solution)/shard_map/while | solution.py:132
  71.6 298.9 %while.63 = (s32[]{:T(128)}, bf16[64,4096]{1,0:T(8,128)(2,1)S(1)}, bf16[2,4,64,4096]{3,2,1,0:T(8,128)(2,1)}, s32[]{:T(128)}, pred[]{:T(512)}, /*index=5*/bf16[4,...) while((s32[]{:T(128)}, bf16[64,4096]{1,0:T(8,128)(2,1)S(1)}, ...), condition=%wide.region_6.7_spmd, body=%wide.region_0.6_spmd.sunk | while | flops 539918400 | bytes 16254634 | solution.py:132
  80.3 9.8 collective-permute-done
  98.7 9.8 collective-permute-done
  117.1 9.8 collective-permute-done
  187.6 11.5 %collective-permute-done = bf16[64,4096]{1,0:T(8,128)(2,1)S(1)} collective-permute-done((bf16[64,4096]{1,0:T(8,128)(2,1)S(1)}, bf16[64,4096]{1,0:T(8,128)(2,1)S(1)}, u32[]{:S(2)}, u32[]{:S(2)}) %collective-permute-start) | collective-permute-done | bytes 524320 | tf_op jit(solution)/shard_map/while/body/eval_jaxpr/ppermute | solution.py:19
  314.9 11.5 %collective-permute-done = bf16[64,4096]{1,0:T(8,128)(2,1)S(1)} collective-permute-done((bf16[64,4096]{1,0:T(8,128)(2,1)S(1)}, bf16[64,4096]{1,0:T(8,128)(2,1)S(1)}, u32[]{:S(2)}, u32[]{:S(2)}) %collective-permute-start) | collective-permute-done | bytes 524320 | tf_op jit(solution)/shard_map/while/body/eval_jaxpr/ppermute | solution.py:19
  329.6 11.5 %collective-permute-done = bf16[64,4096]{1,0:T(8,128)(2,1)S(1)} collective-permute-done((bf16[64,4096]{1,0:T(8,128)(2,1)S(1)}, bf16[64,4096]{1,0:T(8,128)(2,1)S(1)}, u32[]{:S(2)}, u32[]{:S(2)}) %collective-permute-start) | collective-permute-done | bytes 524320 | tf_op jit(solution)/shard_map/while/body/eval_jaxpr/ppermute | solution.py:19
  344.3 11.5 %collective-permute-done = bf16[64,4096]{1,0:T(8,128)(2,1)S(1)} collective-permute-done((bf16[64,4096]{1,0:T(8,128)(2,1)S(1)}, bf16[64,4096]{1,0:T(8,128)(2,1)S(1)}, u32[]{:S(2)}, u32[]{:S(2)}) %collective-permute-start) | collective-permute-done | bytes 524320 | tf_op jit(solution)/shard_map/while/body/eval_jaxpr/ppermute | solution.py:19
  359.0 11.5 %collective-permute-done = bf16[64,4096]{1,0:T(8,128)(2,1)S(1)} collective-permute-done((bf16[64,4096]{1,0:T(8,128)(2,1)S(1)}, bf16[64,4096]{1,0:T(8,128)(2,1)S(1)}, u32[]{:S(2)}, u32[]{:S(2)}) %collective-permute-start) | collective-permute-done | bytes 524320 | tf_op jit(solution)/shard_map/while/body/eval_jaxpr/ppermute | solution.py:19
  375.6 245.6 %while.64 = (s32[]{:T(128)}, bf16[64,4096]{1,0:T(8,128)(2,1)S(1)}, bf16[2,4,64,4096]{3,2,1,0:T(8,128)(2,1)}, bf16[2,4,64,4096]{3,2,1,0:T(8,128)(2,1)}, bf16[2,4,...) while((s32[]{:T(128)}, bf16[64,4096]{1,0:T(8,128)(2,1)S(1)}, ...), condition=%wide.region_15.16_spmd, body=%wide.region_7.15_spmd.sunk | while | flops 811597888 | bytes 61937964 | solution.py:186
  379.7 11.9 %collective-permute-start.1 = (bf16[64,4096]{1,0:T(8,128)(2,1)S(1)}, bf16[64,4096]{1,0:T(8,128)(2,1)S(1)}, u32[]{:S(2)}, u32[]{:S(2)}) collective-permute-start(bf16[64,4096]{1,0:T(8,128)(2,1)S(1)} %get-tuple-element.1254), channel_id=1, source_target_pairs={{16,0},{32,16},{48,32},{64,48},{80,64},{96,80},{112,96},{0,112},{1... | collective-permute-start | bytes 1572872 | tf_op jit(solution)/shard_map/while/body/eval_jaxpr/ppermute | solution.py:19
  402.1 15.7 %collective-permute-start.1 = (bf16[64,4096]{1,0:T(8,128)(2,1)S(1)}, bf16[64,4096]{1,0:T(8,128)(2,1)S(1)}, u32[]{:S(2)}, u32[]{:S(2)}) collective-permute-start(bf16[64,4096]{1,0:T(8,128)(2,1)S(1)} %get-tuple-element.1254), channel_id=1, source_target_pairs={{16,0},{32,16},{48,32},{64,48},{80,64},{96,80},{112,96},{0,112},{1... | collective-permute-start | bytes 1572872 | tf_op jit(solution)/shard_map/while/body/eval_jaxpr/ppermute | solution.py:19
  428.4 15.7 %collective-permute-start.1 = (bf16[64,4096]{1,0:T(8,128)(2,1)S(1)}, bf16[64,4096]{1,0:T(8,128)(2,1)S(1)}, u32[]{:S(2)}, u32[]{:S(2)}) collective-permute-start(bf16[64,4096]{1,0:T(8,128)(2,1)S(1)} %get-tuple-element.1254), channel_id=1, source_target_pairs={{16,0},{32,16},{48,32},{64,48},{80,64},{96,80},{112,96},{0,112},{1... | collective-permute-start | bytes 1572872 | tf_op jit(solution)/shard_map/while/body/eval_jaxpr/ppermute | solution.py:19
  454.7 15.7 %collective-permute-start.1 = (bf16[64,4096]{1,0:T(8,128)(2,1)S(1)}, bf16[64,4096]{1,0:T(8,128)(2,1)S(1)}, u32[]{:S(2)}, u32[]{:S(2)}) collective-permute-start(bf16[64,4096]{1,0:T(8,128)(2,1)S(1)} %get-tuple-element.1254), channel_id=1, source_target_pairs={{16,0},{32,16},{48,32},{64,48},{80,64},{96,80},{112,96},{0,112},{1... | collective-permute-start | bytes 1572872 | tf_op jit(solution)/shard_map/while/body/eval_jaxpr/ppermute | solution.py:19
  521.9 13.3 %conditional.7 = (bf16[64,4096]{1,0:T(8,128)(2,1)S(1)}, bf16[64,4096]{1,0:T(8,128)(2,1)S(1)}, bf16[64,512]{1,0:T(8,128)(2,1)S(1)}, bf16[64,512]{1,0:T(8,128)(2,1)}) conditional(s32[]{:T(128)} %clamp.34, () %tuple.182, (bf16[64,4096]{1,0:T(8,128)(2,1)S(1)}, bf16[2,4,64,4096]{3,2,1,0:T(8,128)(2,1)}, s32[]{:T(128)}, s32[]{:T(128)}, ...), branch_computations={%region_8.8_spmd, %region_9.11_spmd, %region_12.14_spmd} | conditional | flops 810745920 | bytes 52891476 | solution.py:160
  548.1 13.3 %conditional.7 = (bf16[64,4096]{1,0:T(8,128)(2,1)S(1)}, bf16[64,4096]{1,0:T(8,128)(2,1)S(1)}, bf16[64,512]{1,0:T(8,128)(2,1)S(1)}, bf16[64,512]{1,0:T(8,128)(2,1)}) conditional(s32[]{:T(128)} %clamp.34, () %tuple.182, (bf16[64,4096]{1,0:T(8,128)(2,1)S(1)}, bf16[2,4,64,4096]{3,2,1,0:T(8,128)(2,1)}, s32[]{:T(128)}, s32[]{:T(128)}, ...), branch_computations={%region_8.8_spmd, %region_9.11_spmd, %region_12.14_spmd} | conditional | flops 810745920 | bytes 52891476 | solution.py:160
  574.3 13.3 %conditional.7 = (bf16[64,4096]{1,0:T(8,128)(2,1)S(1)}, bf16[64,4096]{1,0:T(8,128)(2,1)S(1)}, bf16[64,512]{1,0:T(8,128)(2,1)S(1)}, bf16[64,512]{1,0:T(8,128)(2,1)}) conditional(s32[]{:T(128)} %clamp.34, () %tuple.182, (bf16[64,4096]{1,0:T(8,128)(2,1)S(1)}, bf16[2,4,64,4096]{3,2,1,0:T(8,128)(2,1)}, s32[]{:T(128)}, s32[]{:T(128)}, ...), branch_computations={%region_8.8_spmd, %region_9.11_spmd, %region_12.14_spmd} | conditional | flops 810745920 | bytes 52891476 | solution.py:160
  601.1 13.3 %conditional.7 = (bf16[64,4096]{1,0:T(8,128)(2,1)S(1)}, bf16[64,4096]{1,0:T(8,128)(2,1)S(1)}, bf16[64,512]{1,0:T(8,128)(2,1)S(1)}, bf16[64,512]{1,0:T(8,128)(2,1)}) conditional(s32[]{:T(128)} %clamp.34, () %tuple.182, (bf16[64,4096]{1,0:T(8,128)(2,1)S(1)}, bf16[2,4,64,4096]{3,2,1,0:T(8,128)(2,1)}, s32[]{:T(128)}, s32[]{:T(128)}, ...), branch_computations={%region_8.8_spmd, %region_9.11_spmd, %region_12.14_spmd} | conditional | flops 810745920 | bytes 52891476 | solution.py:160
  621.2 169.9 %while.65 = (s32[]{:T(128)}, bf16[64,4096]{1,0:T(8,128)(2,1)S(1)}, bf16[2,4,64,4096]{3,2,1,0:T(8,128)(2,1)}, bf16[2,4,64,4096]{3,2,1,0:T(8,128)(2,1)}, bf16[2,4,...) while((s32[]{:T(128)}, bf16[64,4096]{1,0:T(8,128)(2,1)S(1)}, ...), condition=%wide.region_24.25_spmd, body=%wide.region_16.24_spmd.sunk | while | flops 811597888 | bytes 61937984 | solution.py:187
  625.1 15.6 %collective-permute-start.2 = (bf16[64,4096]{1,0:T(8,128)(2,1)S(1)}, bf16[64,4096]{1,0:T(8,128)(2,1)S(1)}, u32[]{:S(2)}, u32[]{:S(2)}) collective-permute-start(bf16[64,4096]{1,0:T(8,128)(2,1)S(1)} %get-tuple-element.1274), channel_id=1, source_target_pairs={{16,0},{32,16},{48,32},{64,48},{80,64},{96,80},{112,96},{0,112},{1... | collective-permute-start | bytes 1572872 | tf_op jit(solution)/shard_map/while/body/eval_jaxpr/ppermute | solution.py:19
  691.9 13.3 %conditional.8 = (bf16[64,4096]{1,0:T(8,128)(2,1)S(1)}, bf16[64,4096]{1,0:T(8,128)(2,1)S(1)}, bf16[64,512]{1,0:T(8,128)(2,1)S(1)}, bf16[64,512]{1,0:T(8,128)(2,1)}) conditional(s32[]{:T(128)} %clamp.35, () %tuple.187, (bf16[64,4096]{1,0:T(8,128)(2,1)S(1)}, bf16[2,4,64,4096]{3,2,1,0:T(8,128)(2,1)}, s32[]{:T(128)}, s32[]{:T(128)}, ...), branch_computations={%region_17.17_spmd, %region_18.20_spmd, %region_21.23_spmd} | conditional | flops 810745920 | bytes 52891476 | solution.py:160
  718.2 13.3 %conditional.8 = (bf16[64,4096]{1,0:T(8,128)(2,1)S(1)}, bf16[64,4096]{1,0:T(8,128)(2,1)S(1)}, bf16[64,512]{1,0:T(8,128)(2,1)S(1)}, bf16[64,512]{1,0:T(8,128)(2,1)}) conditional(s32[]{:T(128)} %clamp.35, () %tuple.187, (bf16[64,4096]{1,0:T(8,128)(2,1)S(1)}, bf16[2,4,64,4096]{3,2,1,0:T(8,128)(2,1)}, s32[]{:T(128)}, s32[]{:T(128)}, ...), branch_computations={%region_17.17_spmd, %region_18.20_spmd, %region_21.23_spmd} | conditional | flops 810745920 | bytes 52891476 | solution.py:160
  744.7 13.3 %conditional.8 = (bf16[64,4096]{1,0:T(8,128)(2,1)S(1)}, bf16[64,4096]{1,0:T(8,128)(2,1)S(1)}, bf16[64,512]{1,0:T(8,128)(2,1)S(1)}, bf16[64,512]{1,0:T(8,128)(2,1)}) conditional(s32[]{:T(128)} %clamp.35, () %tuple.187, (bf16[64,4096]{1,0:T(8,128)(2,1)S(1)}, bf16[2,4,64,4096]{3,2,1,0:T(8,128)(2,1)}, s32[]{:T(128)}, s32[]{:T(128)}, ...), branch_computations={%region_17.17_spmd, %region_18.20_spmd, %region_21.23_spmd} | conditional | flops 810745920 | bytes 52891476 | solution.py:160
  771.0 13.3 %conditional.8 = (bf16[64,4096]{1,0:T(8,128)(2,1)S(1)}, bf16[64,4096]{1,0:T(8,128)(2,1)S(1)}, bf16[64,512]{1,0:T(8,128)(2,1)S(1)}, bf16[64,512]{1,0:T(8,128)(2,1)}) conditional(s32[]{:T(128)} %clamp.35, () %tuple.187, (bf16[64,4096]{1,0:T(8,128)(2,1)S(1)}, bf16[2,4,64,4096]{3,2,1,0:T(8,128)(2,1)}, s32[]{:T(128)}, s32[]{:T(128)}, ...), branch_computations={%region_17.17_spmd, %region_18.20_spmd, %region_21.23_spmd} | conditional | flops 810745920 | bytes 52891476 | solution.py:160
  815.3 62.1 %reduce-scatter.9.cloned.1.call-done = bf16[256,512]{1,0:T(8,128)(2,1)} async-done(((bf16[4096,512]{1,0:T(8,128)(2,1)}), bf16[256,512]{1,0:T(8,128)(2,1)}) %reduce-scatter.9.cloned.1.call-update) | async-done | bytes 262160 | tf_op jit(solution)/shard_map/reduce_scatter | solution.py:82
  878.6 80.0 %reduce-scatter.11.cloned.1.call-done = bf16[256,512]{1,0:T(8,128)(2,1)} async-done(((bf16[4096,512]{1,0:T(8,128)(2,1)}), bf16[256,512]{1,0:T(8,128)(2,1)}) %reduce-scatter.11.cloned.1.call-update) | async-done | bytes 262160 | tf_op jit(solution)/shard_map/reduce_scatter | solution.py:82
  961.1 78.6 %reduce-scatter.5.cloned.1.call-done = bf16[256,512]{1,0:T(8,128)(2,1)} async-done(((bf16[4096,512]{1,0:T(8,128)(2,1)}), bf16[256,512]{1,0:T(8,128)(2,1)}) %reduce-scatter.5.cloned.1.call-update) | async-done | bytes 262160 | tf_op jit(solution)/shard_map/reduce_scatter | solution.py:79
  1040.7 79.9 %reduce-scatter.7.cloned.1.call-done = bf16[256,512]{1,0:T(8,128)(2,1)} async-done(((bf16[4096,512]{1,0:T(8,128)(2,1)}), bf16[256,512]{1,0:T(8,128)(2,1)}) %reduce-scatter.7.cloned.1.call-update) | async-done | bytes 262160 | tf_op jit(solution)/shard_map/reduce_scatter | solution.py:79
  (482 shorter events, 656.7 us)
Async XLA Ops:
  7.2 870.3 %reduce-scatter.9.cloned.1.call-start = ((), (), s32[]{:S(2)}) async-start(), calls=%async_computation.6 | async-start | bytes 4456448 | tf_op jit(solution)/shard_map/reduce_scatter | solution.py:82
  80.3 9.8 collective-permute-start
  98.7 9.8 collective-permute-start
  117.1 9.8 collective-permute-start
  135.5 9.8 collective-permute-start
  148.5 9.8 collective-permute-start
  161.5 9.8 collective-permute-start
  174.6 9.8 collective-permute-start
  187.6 11.5 %collective-permute-start = (bf16[64,4096]{1,0:T(8,128)(2,1)S(1)}, bf16[64,4096]{1,0:T(8,128)(2,1)S(1)}, u32[]{:S(2)}, u32[]{:S(2)}) collective-permute-start(bf16[64,4096]{1,0:T(8,128)(2,1)S(1)} %get-tuple-element.1458), channel_id=1, source_target_pairs={{112,0},{0,16},{16,32},{32,48},{48,64},{64,80},{80,96},{96,112},{1... | collective-permute-start | bytes 1572872 | tf_op jit(solution)/shard_map/while/body/eval_jaxpr/ppermute | solution.py:19
  207.7 9.8 collective-permute-start
  275.8 9.8 collective-permute-start
  288.9 9.8 collective-permute-start
  301.9 9.8 collective-permute-start
  314.9 11.5 %collective-permute-start = (bf16[64,4096]{1,0:T(8,128)(2,1)S(1)}, bf16[64,4096]{1,0:T(8,128)(2,1)S(1)}, u32[]{:S(2)}, u32[]{:S(2)}) collective-permute-start(bf16[64,4096]{1,0:T(8,128)(2,1)S(1)} %get-tuple-element.1458), channel_id=1, source_target_pairs={{112,0},{0,16},{16,32},{32,48},{48,64},{64,80},{80,96},{96,112},{1... | collective-permute-start | bytes 1572872 | tf_op jit(solution)/shard_map/while/body/eval_jaxpr/ppermute | solution.py:19
  329.6 11.5 %collective-permute-start = (bf16[64,4096]{1,0:T(8,128)(2,1)S(1)}, bf16[64,4096]{1,0:T(8,128)(2,1)S(1)}, u32[]{:S(2)}, u32[]{:S(2)}) collective-permute-start(bf16[64,4096]{1,0:T(8,128)(2,1)S(1)} %get-tuple-element.1458), channel_id=1, source_target_pairs={{112,0},{0,16},{16,32},{32,48},{48,64},{64,80},{80,96},{96,112},{1... | collective-permute-start | bytes 1572872 | tf_op jit(solution)/shard_map/while/body/eval_jaxpr/ppermute | solution.py:19
  344.3 11.5 %collective-permute-start = (bf16[64,4096]{1,0:T(8,128)(2,1)S(1)}, bf16[64,4096]{1,0:T(8,128)(2,1)S(1)}, u32[]{:S(2)}, u32[]{:S(2)}) collective-permute-start(bf16[64,4096]{1,0:T(8,128)(2,1)S(1)} %get-tuple-element.1458), channel_id=1, source_target_pairs={{112,0},{0,16},{16,32},{32,48},{48,64},{64,80},{80,96},{96,112},{1... | collective-permute-start | bytes 1572872 | tf_op jit(solution)/shard_map/while/body/eval_jaxpr/ppermute | solution.py:19
  359.0 11.5 %collective-permute-start = (bf16[64,4096]{1,0:T(8,128)(2,1)S(1)}, bf16[64,4096]{1,0:T(8,128)(2,1)S(1)}, u32[]{:S(2)}, u32[]{:S(2)}) collective-permute-start(bf16[64,4096]{1,0:T(8,128)(2,1)S(1)} %get-tuple-element.1458), channel_id=1, source_target_pairs={{112,0},{0,16},{16,32},{32,48},{48,64},{64,80},{80,96},{96,112},{1... | collective-permute-start | bytes 1572872 | tf_op jit(solution)/shard_map/while/body/eval_jaxpr/ppermute | solution.py:19
  379.7 18.6 %collective-permute-start.1 = (bf16[64,4096]{1,0:T(8,128)(2,1)S(1)}, bf16[64,4096]{1,0:T(8,128)(2,1)S(1)}, u32[]{:S(2)}, u32[]{:S(2)}) collective-permute-start(bf16[64,4096]{1,0:T(8,128)(2,1)S(1)} %get-tuple-element.1254), channel_id=1, source_target_pairs={{16,0},{32,16},{48,32},{64,48},{80,64},{96,80},{112,96},{0,112},{1... | collective-permute-start | bytes 1572872 | tf_op jit(solution)/shard_map/while/body/eval_jaxpr/ppermute | solution.py:19
  402.1 22.4 %collective-permute-start.1 = (bf16[64,4096]{1,0:T(8,128)(2,1)S(1)}, bf16[64,4096]{1,0:T(8,128)(2,1)S(1)}, u32[]{:S(2)}, u32[]{:S(2)}) collective-permute-start(bf16[64,4096]{1,0:T(8,128)(2,1)S(1)} %get-tuple-element.1254), channel_id=1, source_target_pairs={{16,0},{32,16},{48,32},{64,48},{80,64},{96,80},{112,96},{0,112},{1... | collective-permute-start | bytes 1572872 | tf_op jit(solution)/shard_map/while/body/eval_jaxpr/ppermute | solution.py:19
  428.4 22.4 %collective-permute-start.1 = (bf16[64,4096]{1,0:T(8,128)(2,1)S(1)}, bf16[64,4096]{1,0:T(8,128)(2,1)S(1)}, u32[]{:S(2)}, u32[]{:S(2)}) collective-permute-start(bf16[64,4096]{1,0:T(8,128)(2,1)S(1)} %get-tuple-element.1254), channel_id=1, source_target_pairs={{16,0},{32,16},{48,32},{64,48},{80,64},{96,80},{112,96},{0,112},{1... | collective-permute-start | bytes 1572872 | tf_op jit(solution)/shard_map/while/body/eval_jaxpr/ppermute | solution.py:19
  454.7 22.4 %collective-permute-start.1 = (bf16[64,4096]{1,0:T(8,128)(2,1)S(1)}, bf16[64,4096]{1,0:T(8,128)(2,1)S(1)}, u32[]{:S(2)}, u32[]{:S(2)}) collective-permute-start(bf16[64,4096]{1,0:T(8,128)(2,1)S(1)} %get-tuple-element.1254), channel_id=1, source_target_pairs={{16,0},{32,16},{48,32},{64,48},{80,64},{96,80},{112,96},{0,112},{1... | collective-permute-start | bytes 1572872 | tf_op jit(solution)/shard_map/while/body/eval_jaxpr/ppermute | solution.py:19
  481.0 9.9 collective-permute-start.1
  494.8 9.9 collective-permute-start.1
  508.5 10.3 collective-permute-start.1
  587.6 10.3 collective-permute-start.1
  625.1 22.3 %collective-permute-start.2 = (bf16[64,4096]{1,0:T(8,128)(2,1)S(1)}, bf16[64,4096]{1,0:T(8,128)(2,1)S(1)}, u32[]{:S(2)}, u32[]{:S(2)}) collective-permute-start(bf16[64,4096]{1,0:T(8,128)(2,1)S(1)} %get-tuple-element.1274), channel_id=1, source_target_pairs={{16,0},{32,16},{48,32},{64,48},{80,64},{96,80},{112,96},{0,112},{1... | collective-permute-start | bytes 1572872 | tf_op jit(solution)/shard_map/while/body/eval_jaxpr/ppermute | solution.py:19
  678.9 9.9 collective-permute-start.2
  705.3 9.8 collective-permute-start.2
  731.6 10.0 collective-permute-start.2
  795.9 162.6 %reduce-scatter.11.cloned.1.call-start = ((), (), s32[]{:S(2)}) async-start(), calls=%async_computation.7 | async-start | bytes 4456448 | tf_op jit(solution)/shard_map/reduce_scatter | solution.py:82
  800.8 238.8 %reduce-scatter.5.cloned.1.call-start = ((), (), s32[]{:S(2)}) async-start(), calls=%async_computation.4 | async-start | bytes 4456448 | tf_op jit(solution)/shard_map/reduce_scatter | solution.py:79
  805.7 314.9 %reduce-scatter.7.cloned.1.call-start = ((), (), s32[]{:S(2)}) async-start(), calls=%async_computation.5 | async-start | bytes 4456448 | tf_op jit(solution)/shard_map/reduce_scatter | solution.py:79
  (24 other events, 183.7 us)
Sparse Core Ops, SparseCore 0:
  796.0 81.3 reduce-scatter.8
  880.8 77.7 reduce-scatter.10
  961.9 77.7 reduce-scatter.4
  1042.8 77.7 reduce-scatter.6
where the time goes:
time: 1140 us; the launch traced here: 1130 us
  waiting for transfers between devices  596 us (52%)
  matrix products  146 us (13%)
  other arithmetic  145 us (13%)
  local copies, waits for them, and re-layouts  133 us (12%)
  starting transfers between devices  94.6 us (8%)
  between operations  14 us (1%)
    ppermute x38, waiting for transfers between devices, shifted(): return lax.ppermute(block, axis, route)  295 us
    reduce_scatter x2, waiting for transfers between devices, settle(): lax.psum_scatter(part_a.astype(jnp.bfloat16), 'dp', scatter_dimension=0,...  159 us
    reduce_scatter x2, waiting for transfers between devices, settle(): lax.psum_scatter(part_b.astype(jnp.bfloat16), 'dp', scatter_dimension=0,...  142 us
    dynamic_update_slice x76, other arithmetic, place_item(): lax.dynamic_update_slice(buffer, value[None, None], (lap_now, micro, anch...  104 us
    ppermute x38, starting transfers between devices, shifted(): return lax.ppermute(block, axis, route)  94.2 us
    dot_general x8, matrix products, forward_layer(): jnp.dot(hidden, eff_b, preferred_element_type=jnp.float32)  41.5 us
    dynamic_slice x76, local copies, waits for them, and re-layouts, backward_step(): buffer[lap_now, micro]  41.1 us
    dot_general x8, matrix products, backward_layer(): lax.dot_general(upstream, eff_b, (((1,), (1,)), ((), ())), preferred_elem...  36.9 us
  transfers between devices with their start and end apart: 42, of which 42 were waited for; matrix products, arithmetic and copies ran while one was open for 6% of the time, Pallas kernels for 0%

commit v1 on v0

--- a/solution.py
+++ b/solution.py
@@ -75,14 +75,10 @@
     part_b = lax.dot_general(
         upstream_all, hidden_all, (((0,), (0,)), ((), ())), preferred_element_type=jnp.float32
     )
-    sum_a, sum_b = (
-        lax.psum_scatter(part_a.astype(jnp.bfloat16), "dp", scatter_dimension=0, tiled=True).astype(
-            jnp.float32
-        ),
-        lax.psum_scatter(part_b.astype(jnp.bfloat16), "dp", scatter_dimension=0, tiled=True).astype(
-            jnp.float32
-        ),
-    )
+    inner = part_a.shape[1]
+    joined = jnp.concatenate([part_a.astype(jnp.bfloat16), part_b.astype(jnp.bfloat16)], axis=1)
+    summed = lax.psum_scatter(joined, "dp", scatter_dimension=0, tiled=True).astype(jnp.float32)
+    sum_a, sum_b = summed[:, :inner], summed[:, inner:]
     full_a = expand_blocks(mask_a[lap_idx, 0]).astype(jnp.float32)
     full_b = expand_blocks(mask_b[lap_idx, 0]).astype(jnp.float32)
     owned_a = lax.dynamic_slice_in_dim(full_a, owner * span, span, 0)
@@ -184,8 +180,8 @@
     middle = batches + sections - 1
     finish = batches + 2 * sections - 1
     carry = lax.fori_loop(0, middle, backward_step, (start_rows, stores))
+    later_one = settle(1, carry[1], mask_a, mask_b)
     carry = lax.fori_loop(middle, finish, backward_step, carry)
-    later_one = settle(1, carry[1], mask_a, mask_b)
     later_zero = settle(0, carry[1], mask_a, mask_b)
     grad_a = jnp.stack([later_zero[0], later_one[0]])[:, None]
     grad_b = jnp.stack([later_zero[1], later_one[1]])[:, None]

time: 1140 us -> 936 us (0.82)
  waiting for transfers between devices: 596 us -> 376 us
  other arithmetic: 145 us -> 163 us
    reduce_scatter x4 -> x2, waiting for transfers between devices: 301 us -> 80.3 us  [settle(): lax.psum_scatter(joined, 'dp', scatter_dimension=0, tiled=True)]
    concatenate x0 -> x2, other arithmetic: none -> 15.6 us  [settle(): jnp.concatenate([part_a.astype(jnp.bfloat16), part_b.astype(jnp.bfloat16)...]
    unnamed x17 -> x19, local copies, waits for them, and re-layouts: 25.6 us -> 27.4 us
  transfers between devices with their start and end apart: 42 -> 40, of which waited for: 42 -> 39; matrix products, arithmetic and copies ran while one was open for 6% -> 16% of each run, Pallas kernels for 0% -> 0%
where the time goes in v1:
time: 936 us; the launch traced here: 928 us
  waiting for transfers between devices  376 us (40%)
  other arithmetic  163 us (17%)
  matrix products  143 us (15%)
  local copies, waits for them, and re-layouts  135 us (14%)
  starting transfers between devices  94.6 us (10%)
  between operations  14.3 us (2%)
    ppermute x38, waiting for transfers between devices, shifted(): return lax.ppermute(block, axis, route)  296 us
    dynamic_update_slice x76, other arithmetic, place_item(): lax.dynamic_update_slice(buffer, value[None, None], (lap_now, micro, anch...  104 us
    ppermute x38, starting transfers between devices, shifted(): return lax.ppermute(block, axis, route)  94.5 us
    reduce_scatter x2, waiting for transfers between devices, settle(): lax.psum_scatter(joined, 'dp', scatter_dimension=0, tiled=True)  80.3 us
    dot_general x8, matrix products, forward_layer(): jnp.dot(hidden, eff_b, preferred_element_type=jnp.float32)  41.5 us
    dynamic_slice x76, local copies, waits for them, and re-layouts, backward_step(): buffer[lap_now, micro]  41.2 us
    dot_general x8, matrix products, backward_layer(): lax.dot_general(upstream, eff_b, (((1,), (1,)), ((), ())), preferred_elem...  37 us
    unnamed x19, local copies, waits for them, and re-layouts  27.4 us
  transfers between devices with their start and end apart: 40, of which 39 were waited for; matrix products, arithmetic and copies ran while one was open for 16% of the time, Pallas kernels for 0%

profile of v1, /device:TPU:0, one launch (start us, length us, event | category | flops | bytes accessed | tf_op | source)
XLA Modules:
  0.0 928.3 jit_solution(3065684538378376607)
XLA Ops:
  7.2 11.4 %copy.11 = bf16[2,1,4096,512]{2,3,0,1:T(8,128)(2,1)} copy(bf16[2,1,4096,512]{3,2,1,0:T(8,128)(2,1)} %param.23) | data formatting | bytes 16777216 | tf_op args[2]
  26.4 12.0 %copy.14 = bf16[2,4096,512]{2,1,0:T(8,128)(2,1)} copy(bf16[2,4096,512]{1,2,0:T(8,128)(2,1)} %bitcast_multiply_fusion.1) | data formatting | bytes 16777216 | tf_op jit(solution)/shard_map/while | solution.py:128
  38.3 12.0 %copy.12 = bf16[2,1,512,4096]{2,3,0,1:T(8,128)(2,1)} copy(bf16[2,1,512,4096]{3,2,1,0:T(8,128)(2,1)} %param.24) | data formatting | bytes 16777216 | tf_op args[3]
  58.0 11.4 %copy.15 = bf16[2,512,4096]{2,1,0:T(8,128)(2,1)} copy(bf16[2,512,4096]{1,2,0:T(8,128)(2,1)} %bitcast_multiply_fusion) | data formatting | bytes 16777216 | tf_op jit(solution)/shard_map/while | solution.py:128
  72.0 298.8 %while.63 = (s32[]{:T(128)}, bf16[64,4096]{1,0:T(8,128)(2,1)S(1)}, bf16[2,4,64,4096]{3,2,1,0:T(8,128)(2,1)}, s32[]{:T(128)}, pred[]{:T(512)}, /*index=5*/bf16[4,...) while((s32[]{:T(128)}, bf16[64,4096]{1,0:T(8,128)(2,1)S(1)}, ...), condition=%wide.region_6.7_spmd, body=%wide.region_0.6_spmd.sunk | while | flops 539918400 | bytes 16254634 | solution.py:128
  117.5 9.8 %collective-permute-done = bf16[64,4096]{1,0:T(8,128)(2,1)S(1)} collective-permute-done((bf16[64,4096]{1,0:T(8,128)(2,1)S(1)}, bf16[64,4096]{1,0:T(8,128)(2,1)S(1)}, u32[]{:S(2)}, u32[]{:S(2)}) %collective-permute-start) | collective-permute-done | bytes 524320 | tf_op jit(solution)/shard_map/while/body/eval_jaxpr/ppermute | solution.py:19
  135.8 9.8 %collective-permute-done = bf16[64,4096]{1,0:T(8,128)(2,1)S(1)} collective-permute-done((bf16[64,4096]{1,0:T(8,128)(2,1)S(1)}, bf16[64,4096]{1,0:T(8,128)(2,1)S(1)}, u32[]{:S(2)}, u32[]{:S(2)}) %collective-permute-start) | collective-permute-done | bytes 524320 | tf_op jit(solution)/shard_map/while/body/eval_jaxpr/ppermute | solution.py:19
  148.9 9.8 %collective-permute-done = bf16[64,4096]{1,0:T(8,128)(2,1)S(1)} collective-permute-done((bf16[64,4096]{1,0:T(8,128)(2,1)S(1)}, bf16[64,4096]{1,0:T(8,128)(2,1)S(1)}, u32[]{:S(2)}, u32[]{:S(2)}) %collective-permute-start) | collective-permute-done | bytes 524320 | tf_op jit(solution)/shard_map/while/body/eval_jaxpr/ppermute | solution.py:19
  174.9 9.8 %collective-permute-done = bf16[64,4096]{1,0:T(8,128)(2,1)S(1)} collective-permute-done((bf16[64,4096]{1,0:T(8,128)(2,1)S(1)}, bf16[64,4096]{1,0:T(8,128)(2,1)S(1)}, u32[]{:S(2)}, u32[]{:S(2)}) %collective-permute-start) | collective-permute-done | bytes 524320 | tf_op jit(solution)/shard_map/while/body/eval_jaxpr/ppermute | solution.py:19
  187.9 11.5 %collective-permute-done = bf16[64,4096]{1,0:T(8,128)(2,1)S(1)} collective-permute-done((bf16[64,4096]{1,0:T(8,128)(2,1)S(1)}, bf16[64,4096]{1,0:T(8,128)(2,1)S(1)}, u32[]{:S(2)}, u32[]{:S(2)}) %collective-permute-start) | collective-permute-done | bytes 524320 | tf_op jit(solution)/shard_map/while/body/eval_jaxpr/ppermute | solution.py:19
  208.0 9.8 %collective-permute-done = bf16[64,4096]{1,0:T(8,128)(2,1)S(1)} collective-permute-done((bf16[64,4096]{1,0:T(8,128)(2,1)S(1)}, bf16[64,4096]{1,0:T(8,128)(2,1)S(1)}, u32[]{:S(2)}, u32[]{:S(2)}) %collective-permute-start) | collective-permute-done | bytes 524320 | tf_op jit(solution)/shard_map/while/body/eval_jaxpr/ppermute | solution.py:19
  244.8 9.8 %collective-permute-done = bf16[64,4096]{1,0:T(8,128)(2,1)S(1)} collective-permute-done((bf16[64,4096]{1,0:T(8,128)(2,1)S(1)}, bf16[64,4096]{1,0:T(8,128)(2,1)S(1)}, u32[]{:S(2)}, u32[]{:S(2)}) %collective-permute-start) | collective-permute-done | bytes 524320 | tf_op jit(solution)/shard_map/while/body/eval_jaxpr/ppermute | solution.py:19
  315.2 11.5 %collective-permute-done = bf16[64,4096]{1,0:T(8,128)(2,1)S(1)} collective-permute-done((bf16[64,4096]{1,0:T(8,128)(2,1)S(1)}, bf16[64,4096]{1,0:T(8,128)(2,1)S(1)}, u32[]{:S(2)}, u32[]{:S(2)}) %collective-permute-start) | collective-permute-done | bytes 524320 | tf_op jit(solution)/shard_map/while/body/eval_jaxpr/ppermute | solution.py:19
  329.9 11.5 %collective-permute-done = bf16[64,4096]{1,0:T(8,128)(2,1)S(1)} collective-permute-done((bf16[64,4096]{1,0:T(8,128)(2,1)S(1)}, bf16[64,4096]{1,0:T(8,128)(2,1)S(1)}, u32[]{:S(2)}, u32[]{:S(2)}) %collective-permute-start) | collective-permute-done | bytes 524320 | tf_op jit(solution)/shard_map/while/body/eval_jaxpr/ppermute | solution.py:19
  344.6 11.5 %collective-permute-done = bf16[64,4096]{1,0:T(8,128)(2,1)S(1)} collective-permute-done((bf16[64,4096]{1,0:T(8,128)(2,1)S(1)}, bf16[64,4096]{1,0:T(8,128)(2,1)S(1)}, u32[]{:S(2)}, u32[]{:S(2)}) %collective-permute-start) | collective-permute-done | bytes 524320 | tf_op jit(solution)/shard_map/while/body/eval_jaxpr/ppermute | solution.py:19
  359.3 11.5 %collective-permute-done = bf16[64,4096]{1,0:T(8,128)(2,1)S(1)} collective-permute-done((bf16[64,4096]{1,0:T(8,128)(2,1)S(1)}, bf16[64,4096]{1,0:T(8,128)(2,1)S(1)}, u32[]{:S(2)}, u32[]{:S(2)}) %collective-permute-start) | collective-permute-done | bytes 524320 | tf_op jit(solution)/shard_map/while/body/eval_jaxpr/ppermute | solution.py:19
  375.9 245.5 %while.64 = (s32[]{:T(128)}, bf16[64,4096]{1,0:T(8,128)(2,1)S(1)}, bf16[2,4,64,4096]{3,2,1,0:T(8,128)(2,1)}, bf16[2,4,64,4096]{3,2,1,0:T(8,128)(2,1)}, bf16[2,4,...) while((s32[]{:T(128)}, bf16[64,4096]{1,0:T(8,128)(2,1)S(1)}, ...), condition=%wide.region_15.16_spmd, body=%wide.region_7.15_spmd.sunk | while | flops 811597888 | bytes 61937964 | solution.py:182
  379.9 11.8 %collective-permute-start.1 = (bf16[64,4096]{1,0:T(8,128)(2,1)S(1)}, bf16[64,4096]{1,0:T(8,128)(2,1)S(1)}, u32[]{:S(2)}, u32[]{:S(2)}) collective-permute-start(bf16[64,4096]{1,0:T(8,128)(2,1)S(1)} %get-tuple-element.1254), channel_id=1, source_target_pairs={{16,0},{32,16},{48,32},{64,48},{80,64},{96,80},{112,96},{0,112},{1... | collective-permute-start | bytes 1572872 | tf_op jit(solution)/shard_map/while/body/eval_jaxpr/ppermute | solution.py:19
  402.4 15.7 %collective-permute-start.1 = (bf16[64,4096]{1,0:T(8,128)(2,1)S(1)}, bf16[64,4096]{1,0:T(8,128)(2,1)S(1)}, u32[]{:S(2)}, u32[]{:S(2)}) collective-permute-start(bf16[64,4096]{1,0:T(8,128)(2,1)S(1)} %get-tuple-element.1254), channel_id=1, source_target_pairs={{16,0},{32,16},{48,32},{64,48},{80,64},{96,80},{112,96},{0,112},{1... | collective-permute-start | bytes 1572872 | tf_op jit(solution)/shard_map/while/body/eval_jaxpr/ppermute | solution.py:19
  428.7 15.8 %collective-permute-start.1 = (bf16[64,4096]{1,0:T(8,128)(2,1)S(1)}, bf16[64,4096]{1,0:T(8,128)(2,1)S(1)}, u32[]{:S(2)}, u32[]{:S(2)}) collective-permute-start(bf16[64,4096]{1,0:T(8,128)(2,1)S(1)} %get-tuple-element.1254), channel_id=1, source_target_pairs={{16,0},{32,16},{48,32},{64,48},{80,64},{96,80},{112,96},{0,112},{1... | collective-permute-start | bytes 1572872 | tf_op jit(solution)/shard_map/while/body/eval_jaxpr/ppermute | solution.py:19
  455.0 15.7 %collective-permute-start.1 = (bf16[64,4096]{1,0:T(8,128)(2,1)S(1)}, bf16[64,4096]{1,0:T(8,128)(2,1)S(1)}, u32[]{:S(2)}, u32[]{:S(2)}) collective-permute-start(bf16[64,4096]{1,0:T(8,128)(2,1)S(1)} %get-tuple-element.1254), channel_id=1, source_target_pairs={{16,0},{32,16},{48,32},{64,48},{80,64},{96,80},{112,96},{0,112},{1... | collective-permute-start | bytes 1572872 | tf_op jit(solution)/shard_map/while/body/eval_jaxpr/ppermute | solution.py:19
  522.0 13.3 %conditional.7 = (bf16[64,4096]{1,0:T(8,128)(2,1)S(1)}, bf16[64,4096]{1,0:T(8,128)(2,1)S(1)}, bf16[64,512]{1,0:T(8,128)(2,1)S(1)}, bf16[64,512]{1,0:T(8,128)(2,1)}) conditional(s32[]{:T(128)} %clamp.34, () %tuple.182, (bf16[64,4096]{1,0:T(8,128)(2,1)S(1)}, bf16[2,4,64,4096]{3,2,1,0:T(8,128)(2,1)}, s32[]{:T(128)}, s32[]{:T(128)}, ...), branch_computations={%region_8.8_spmd, %region_9.11_spmd, %region_12.14_spmd} | conditional | flops 810745920 | bytes 52891476 | solution.py:156
  548.5 13.3 %conditional.7 = (bf16[64,4096]{1,0:T(8,128)(2,1)S(1)}, bf16[64,4096]{1,0:T(8,128)(2,1)S(1)}, bf16[64,512]{1,0:T(8,128)(2,1)S(1)}, bf16[64,512]{1,0:T(8,128)(2,1)}) conditional(s32[]{:T(128)} %clamp.34, () %tuple.182, (bf16[64,4096]{1,0:T(8,128)(2,1)S(1)}, bf16[2,4,64,4096]{3,2,1,0:T(8,128)(2,1)}, s32[]{:T(128)}, s32[]{:T(128)}, ...), branch_computations={%region_8.8_spmd, %region_9.11_spmd, %region_12.14_spmd} | conditional | flops 810745920 | bytes 52891476 | solution.py:156
  575.0 13.3 %conditional.7 = (bf16[64,4096]{1,0:T(8,128)(2,1)S(1)}, bf16[64,4096]{1,0:T(8,128)(2,1)S(1)}, bf16[64,512]{1,0:T(8,128)(2,1)S(1)}, bf16[64,512]{1,0:T(8,128)(2,1)}) conditional(s32[]{:T(128)} %clamp.34, () %tuple.182, (bf16[64,4096]{1,0:T(8,128)(2,1)S(1)}, bf16[2,4,64,4096]{3,2,1,0:T(8,128)(2,1)}, s32[]{:T(128)}, s32[]{:T(128)}, ...), branch_computations={%region_8.8_spmd, %region_9.11_spmd, %region_12.14_spmd} | conditional | flops 810745920 | bytes 52891476 | solution.py:156
  601.1 13.3 %conditional.7 = (bf16[64,4096]{1,0:T(8,128)(2,1)S(1)}, bf16[64,4096]{1,0:T(8,128)(2,1)S(1)}, bf16[64,512]{1,0:T(8,128)(2,1)S(1)}, bf16[64,512]{1,0:T(8,128)(2,1)}) conditional(s32[]{:T(128)} %clamp.34, () %tuple.182, (bf16[64,4096]{1,0:T(8,128)(2,1)S(1)}, bf16[2,4,64,4096]{3,2,1,0:T(8,128)(2,1)}, s32[]{:T(128)}, s32[]{:T(128)}, ...), branch_computations={%region_8.8_spmd, %region_9.11_spmd, %region_12.14_spmd} | conditional | flops 810745920 | bytes 52891476 | solution.py:156
  637.4 171.5 %while.65 = (s32[]{:T(128)}, bf16[64,4096]{1,0:T(8,128)(2,1)S(1)}, bf16[2,4,64,4096]{3,2,1,0:T(8,128)(2,1)}, bf16[2,4,64,4096]{3,2,1,0:T(8,128)(2,1)}, bf16[2,4,...) while((s32[]{:T(128)}, bf16[64,4096]{1,0:T(8,128)(2,1)S(1)}, ...), condition=%wide.region_24.25_spmd, body=%wide.region_16.24_spmd.sunk | while | flops 811597888 | bytes 61937984 | solution.py:184
  641.6 15.7 %collective-permute-start.2 = (bf16[64,4096]{1,0:T(8,128)(2,1)S(1)}, bf16[64,4096]{1,0:T(8,128)(2,1)S(1)}, u32[]{:S(2)}, u32[]{:S(2)}) collective-permute-start(bf16[64,4096]{1,0:T(8,128)(2,1)S(1)} %get-tuple-element.1274), channel_id=1, source_target_pairs={{16,0},{32,16},{48,32},{64,48},{80,64},{96,80},{112,96},{0,112},{1... | collective-permute-start | bytes 1572872 | tf_op jit(solution)/shard_map/while/body/eval_jaxpr/ppermute | solution.py:19
  710.0 13.4 %conditional.8 = (bf16[64,4096]{1,0:T(8,128)(2,1)S(1)}, bf16[64,4096]{1,0:T(8,128)(2,1)S(1)}, bf16[64,512]{1,0:T(8,128)(2,1)S(1)}, bf16[64,512]{1,0:T(8,128)(2,1)}) conditional(s32[]{:T(128)} %clamp.35, () %tuple.187, (bf16[64,4096]{1,0:T(8,128)(2,1)S(1)}, bf16[2,4,64,4096]{3,2,1,0:T(8,128)(2,1)}, s32[]{:T(128)}, s32[]{:T(128)}, ...), branch_computations={%region_17.17_spmd, %region_18.20_spmd, %region_21.23_spmd} | conditional | flops 810745920 | bytes 52891476 | solution.py:156
  737.3 13.3 %conditional.8 = (bf16[64,4096]{1,0:T(8,128)(2,1)S(1)}, bf16[64,4096]{1,0:T(8,128)(2,1)S(1)}, bf16[64,512]{1,0:T(8,128)(2,1)S(1)}, bf16[64,512]{1,0:T(8,128)(2,1)}) conditional(s32[]{:T(128)} %clamp.35, () %tuple.187, (bf16[64,4096]{1,0:T(8,128)(2,1)S(1)}, bf16[2,4,64,4096]{3,2,1,0:T(8,128)(2,1)}, s32[]{:T(128)}, s32[]{:T(128)}, ...), branch_computations={%region_17.17_spmd, %region_18.20_spmd, %region_21.23_spmd} | conditional | flops 810745920 | bytes 52891476 | solution.py:156
  763.7 13.3 %conditional.8 = (bf16[64,4096]{1,0:T(8,128)(2,1)S(1)}, bf16[64,4096]{1,0:T(8,128)(2,1)S(1)}, bf16[64,512]{1,0:T(8,128)(2,1)S(1)}, bf16[64,512]{1,0:T(8,128)(2,1)}) conditional(s32[]{:T(128)} %clamp.35, () %tuple.187, (bf16[64,4096]{1,0:T(8,128)(2,1)S(1)}, bf16[2,4,64,4096]{3,2,1,0:T(8,128)(2,1)}, s32[]{:T(128)}, s32[]{:T(128)}, ...), branch_computations={%region_17.17_spmd, %region_18.20_spmd, %region_21.23_spmd} | conditional | flops 810745920 | bytes 52891476 | solution.py:156
  789.0 13.3 %conditional.8 = (bf16[64,4096]{1,0:T(8,128)(2,1)S(1)}, bf16[64,4096]{1,0:T(8,128)(2,1)S(1)}, bf16[64,512]{1,0:T(8,128)(2,1)S(1)}, bf16[64,512]{1,0:T(8,128)(2,1)}) conditional(s32[]{:T(128)} %clamp.35, () %tuple.187, (bf16[64,4096]{1,0:T(8,128)(2,1)S(1)}, bf16[2,4,64,4096]{3,2,1,0:T(8,128)(2,1)}, s32[]{:T(128)}, s32[]{:T(128)}, ...), branch_computations={%region_17.17_spmd, %region_18.20_spmd, %region_21.23_spmd} | conditional | flops 810745920 | bytes 52891476 | solution.py:156
  834.2 80.3 %reduce-scatter.3.cloned.1.call-done = bf16[256,1024]{0,1:T(8,128)(2,1)} async-done(((bf16[4096,1024]{0,1:T(8,128)(2,1)}), bf16[256,1024]{0,1:T(8,128)(2,1)}) %reduce-scatter.3.cloned.1.call-update) | async-done | bytes 524304 | tf_op jit(solution)/shard_map/reduce_scatter | solution.py:80
  (482 shorter events, 645.6 us)
Async XLA Ops:
  7.2 824.0 %reduce-scatter.5.cloned.1.call-start = ((), (), s32[]{:S(2)}) async-start(), calls=%async_computation.3 | async-start | bytes 8912896 | tf_op jit(solution)/shard_map/reduce_scatter | solution.py:80
  80.6 9.8 %collective-permute-start = (bf16[64,4096]{1,0:T(8,128)(2,1)S(1)}, bf16[64,4096]{1,0:T(8,128)(2,1)S(1)}, u32[]{:S(2)}, u32[]{:S(2)}) collective-permute-start(bf16[64,4096]{1,0:T(8,128)(2,1)S(1)} %get-tuple-element.1458), channel_id=1, source_target_pairs={{112,0},{0,16},{16,32},{32,48},{48,64},{64,80},{80,96},{96,112},{1... | collective-permute-start | bytes 1572872 | tf_op jit(solution)/shard_map/while/body/eval_jaxpr/ppermute | solution.py:19
  99.0 9.8 %collective-permute-start = (bf16[64,4096]{1,0:T(8,128)(2,1)S(1)}, bf16[64,4096]{1,0:T(8,128)(2,1)S(1)}, u32[]{:S(2)}, u32[]{:S(2)}) collective-permute-start(bf16[64,4096]{1,0:T(8,128)(2,1)S(1)} %get-tuple-element.1458), channel_id=1, source_target_pairs={{112,0},{0,16},{16,32},{32,48},{48,64},{64,80},{80,96},{96,112},{1... | collective-permute-start | bytes 1572872 | tf_op jit(solution)/shard_map/while/body/eval_jaxpr/ppermute | solution.py:19
  117.4 9.8 %collective-permute-start = (bf16[64,4096]{1,0:T(8,128)(2,1)S(1)}, bf16[64,4096]{1,0:T(8,128)(2,1)S(1)}, u32[]{:S(2)}, u32[]{:S(2)}) collective-permute-start(bf16[64,4096]{1,0:T(8,128)(2,1)S(1)} %get-tuple-element.1458), channel_id=1, source_target_pairs={{112,0},{0,16},{16,32},{32,48},{48,64},{64,80},{80,96},{96,112},{1... | collective-permute-start | bytes 1572872 | tf_op jit(solution)/shard_map/while/body/eval_jaxpr/ppermute | solution.py:19
  135.8 9.8 %collective-permute-start = (bf16[64,4096]{1,0:T(8,128)(2,1)S(1)}, bf16[64,4096]{1,0:T(8,128)(2,1)S(1)}, u32[]{:S(2)}, u32[]{:S(2)}) collective-permute-start(bf16[64,4096]{1,0:T(8,128)(2,1)S(1)} %get-tuple-element.1458), channel_id=1, source_target_pairs={{112,0},{0,16},{16,32},{32,48},{48,64},{64,80},{80,96},{96,112},{1... | collective-permute-start | bytes 1572872 | tf_op jit(solution)/shard_map/while/body/eval_jaxpr/ppermute | solution.py:19
  148.8 9.8 %collective-permute-start = (bf16[64,4096]{1,0:T(8,128)(2,1)S(1)}, bf16[64,4096]{1,0:T(8,128)(2,1)S(1)}, u32[]{:S(2)}, u32[]{:S(2)}) collective-permute-start(bf16[64,4096]{1,0:T(8,128)(2,1)S(1)} %get-tuple-element.1458), channel_id=1, source_target_pairs={{112,0},{0,16},{16,32},{32,48},{48,64},{64,80},{80,96},{96,112},{1... | collective-permute-start | bytes 1572872 | tf_op jit(solution)/shard_map/while/body/eval_jaxpr/ppermute | solution.py:19
  161.8 9.8 %collective-permute-start = (bf16[64,4096]{1,0:T(8,128)(2,1)S(1)}, bf16[64,4096]{1,0:T(8,128)(2,1)S(1)}, u32[]{:S(2)}, u32[]{:S(2)}) collective-permute-start(bf16[64,4096]{1,0:T(8,128)(2,1)S(1)} %get-tuple-element.1458), channel_id=1, source_target_pairs={{112,0},{0,16},{16,32},{32,48},{48,64},{64,80},{80,96},{96,112},{1... | collective-permute-start | bytes 1572872 | tf_op jit(solution)/shard_map/while/body/eval_jaxpr/ppermute | solution.py:19
  174.8 9.8 %collective-permute-start = (bf16[64,4096]{1,0:T(8,128)(2,1)S(1)}, bf16[64,4096]{1,0:T(8,128)(2,1)S(1)}, u32[]{:S(2)}, u32[]{:S(2)}) collective-permute-start(bf16[64,4096]{1,0:T(8,128)(2,1)S(1)} %get-tuple-element.1458), channel_id=1, source_target_pairs={{112,0},{0,16},{16,32},{32,48},{48,64},{64,80},{80,96},{96,112},{1... | collective-permute-start | bytes 1572872 | tf_op jit(solution)/shard_map/while/body/eval_jaxpr/ppermute | solution.py:19
  187.9 11.5 %collective-permute-start = (bf16[64,4096]{1,0:T(8,128)(2,1)S(1)}, bf16[64,4096]{1,0:T(8,128)(2,1)S(1)}, u32[]{:S(2)}, u32[]{:S(2)}) collective-permute-start(bf16[64,4096]{1,0:T(8,128)(2,1)S(1)} %get-tuple-element.1458), channel_id=1, source_target_pairs={{112,0},{0,16},{16,32},{32,48},{48,64},{64,80},{80,96},{96,112},{1... | collective-permute-start | bytes 1572872 | tf_op jit(solution)/shard_map/while/body/eval_jaxpr/ppermute | solution.py:19
  208.0 9.8 %collective-permute-start = (bf16[64,4096]{1,0:T(8,128)(2,1)S(1)}, bf16[64,4096]{1,0:T(8,128)(2,1)S(1)}, u32[]{:S(2)}, u32[]{:S(2)}) collective-permute-start(bf16[64,4096]{1,0:T(8,128)(2,1)S(1)} %get-tuple-element.1458), channel_id=1, source_target_pairs={{112,0},{0,16},{16,32},{32,48},{48,64},{64,80},{80,96},{96,112},{1... | collective-permute-start | bytes 1572872 | tf_op jit(solution)/shard_map/while/body/eval_jaxpr/ppermute | solution.py:19
  244.8 9.8 %collective-permute-start = (bf16[64,4096]{1,0:T(8,128)(2,1)S(1)}, bf16[64,4096]{1,0:T(8,128)(2,1)S(1)}, u32[]{:S(2)}, u32[]{:S(2)}) collective-permute-start(bf16[64,4096]{1,0:T(8,128)(2,1)S(1)} %get-tuple-element.1458), channel_id=1, source_target_pairs={{112,0},{0,16},{16,32},{32,48},{48,64},{64,80},{80,96},{96,112},{1... | collective-permute-start | bytes 1572872 | tf_op jit(solution)/shard_map/while/body/eval_jaxpr/ppermute | solution.py:19
  276.1 9.8 %collective-permute-start = (bf16[64,4096]{1,0:T(8,128)(2,1)S(1)}, bf16[64,4096]{1,0:T(8,128)(2,1)S(1)}, u32[]{:S(2)}, u32[]{:S(2)}) collective-permute-start(bf16[64,4096]{1,0:T(8,128)(2,1)S(1)} %get-tuple-element.1458), channel_id=1, source_target_pairs={{112,0},{0,16},{16,32},{32,48},{48,64},{64,80},{80,96},{96,112},{1... | collective-permute-start | bytes 1572872 | tf_op jit(solution)/shard_map/while/body/eval_jaxpr/ppermute | solution.py:19
  289.2 9.8 %collective-permute-start = (bf16[64,4096]{1,0:T(8,128)(2,1)S(1)}, bf16[64,4096]{1,0:T(8,128)(2,1)S(1)}, u32[]{:S(2)}, u32[]{:S(2)}) collective-permute-start(bf16[64,4096]{1,0:T(8,128)(2,1)S(1)} %get-tuple-element.1458), channel_id=1, source_target_pairs={{112,0},{0,16},{16,32},{32,48},{48,64},{64,80},{80,96},{96,112},{1... | collective-permute-start | bytes 1572872 | tf_op jit(solution)/shard_map/while/body/eval_jaxpr/ppermute | solution.py:19
  302.2 9.8 %collective-permute-start = (bf16[64,4096]{1,0:T(8,128)(2,1)S(1)}, bf16[64,4096]{1,0:T(8,128)(2,1)S(1)}, u32[]{:S(2)}, u32[]{:S(2)}) collective-permute-start(bf16[64,4096]{1,0:T(8,128)(2,1)S(1)} %get-tuple-element.1458), channel_id=1, source_target_pairs={{112,0},{0,16},{16,32},{32,48},{48,64},{64,80},{80,96},{96,112},{1... | collective-permute-start | bytes 1572872 | tf_op jit(solution)/shard_map/while/body/eval_jaxpr/ppermute | solution.py:19
  315.2 11.5 %collective-permute-start = (bf16[64,4096]{1,0:T(8,128)(2,1)S(1)}, bf16[64,4096]{1,0:T(8,128)(2,1)S(1)}, u32[]{:S(2)}, u32[]{:S(2)}) collective-permute-start(bf16[64,4096]{1,0:T(8,128)(2,1)S(1)} %get-tuple-element.1458), channel_id=1, source_target_pairs={{112,0},{0,16},{16,32},{32,48},{48,64},{64,80},{80,96},{96,112},{1... | collective-permute-start | bytes 1572872 | tf_op jit(solution)/shard_map/while/body/eval_jaxpr/ppermute | solution.py:19
  329.9 11.5 %collective-permute-start = (bf16[64,4096]{1,0:T(8,128)(2,1)S(1)}, bf16[64,4096]{1,0:T(8,128)(2,1)S(1)}, u32[]{:S(2)}, u32[]{:S(2)}) collective-permute-start(bf16[64,4096]{1,0:T(8,128)(2,1)S(1)} %get-tuple-element.1458), channel_id=1, source_target_pairs={{112,0},{0,16},{16,32},{32,48},{48,64},{64,80},{80,96},{96,112},{1... | collective-permute-start | bytes 1572872 | tf_op jit(solution)/shard_map/while/body/eval_jaxpr/ppermute | solution.py:19
  344.6 11.6 %collective-permute-start = (bf16[64,4096]{1,0:T(8,128)(2,1)S(1)}, bf16[64,4096]{1,0:T(8,128)(2,1)S(1)}, u32[]{:S(2)}, u32[]{:S(2)}) collective-permute-start(bf16[64,4096]{1,0:T(8,128)(2,1)S(1)} %get-tuple-element.1458), channel_id=1, source_target_pairs={{112,0},{0,16},{16,32},{32,48},{48,64},{64,80},{80,96},{96,112},{1... | collective-permute-start | bytes 1572872 | tf_op jit(solution)/shard_map/while/body/eval_jaxpr/ppermute | solution.py:19
  359.3 11.5 %collective-permute-start = (bf16[64,4096]{1,0:T(8,128)(2,1)S(1)}, bf16[64,4096]{1,0:T(8,128)(2,1)S(1)}, u32[]{:S(2)}, u32[]{:S(2)}) collective-permute-start(bf16[64,4096]{1,0:T(8,128)(2,1)S(1)} %get-tuple-element.1458), channel_id=1, source_target_pairs={{112,0},{0,16},{16,32},{32,48},{48,64},{64,80},{80,96},{96,112},{1... | collective-permute-start | bytes 1572872 | tf_op jit(solution)/shard_map/while/body/eval_jaxpr/ppermute | solution.py:19
  379.9 18.5 %collective-permute-start.1 = (bf16[64,4096]{1,0:T(8,128)(2,1)S(1)}, bf16[64,4096]{1,0:T(8,128)(2,1)S(1)}, u32[]{:S(2)}, u32[]{:S(2)}) collective-permute-start(bf16[64,4096]{1,0:T(8,128)(2,1)S(1)} %get-tuple-element.1254), channel_id=1, source_target_pairs={{16,0},{32,16},{48,32},{64,48},{80,64},{96,80},{112,96},{0,112},{1... | collective-permute-start | bytes 1572872 | tf_op jit(solution)/shard_map/while/body/eval_jaxpr/ppermute | solution.py:19
  402.4 22.4 %collective-permute-start.1 = (bf16[64,4096]{1,0:T(8,128)(2,1)S(1)}, bf16[64,4096]{1,0:T(8,128)(2,1)S(1)}, u32[]{:S(2)}, u32[]{:S(2)}) collective-permute-start(bf16[64,4096]{1,0:T(8,128)(2,1)S(1)} %get-tuple-element.1254), channel_id=1, source_target_pairs={{16,0},{32,16},{48,32},{64,48},{80,64},{96,80},{112,96},{0,112},{1... | collective-permute-start | bytes 1572872 | tf_op jit(solution)/shard_map/while/body/eval_jaxpr/ppermute | solution.py:19
  428.7 22.5 %collective-permute-start.1 = (bf16[64,4096]{1,0:T(8,128)(2,1)S(1)}, bf16[64,4096]{1,0:T(8,128)(2,1)S(1)}, u32[]{:S(2)}, u32[]{:S(2)}) collective-permute-start(bf16[64,4096]{1,0:T(8,128)(2,1)S(1)} %get-tuple-element.1254), channel_id=1, source_target_pairs={{16,0},{32,16},{48,32},{64,48},{80,64},{96,80},{112,96},{0,112},{1... | collective-permute-start | bytes 1572872 | tf_op jit(solution)/shard_map/while/body/eval_jaxpr/ppermute | solution.py:19
  455.0 22.4 %collective-permute-start.1 = (bf16[64,4096]{1,0:T(8,128)(2,1)S(1)}, bf16[64,4096]{1,0:T(8,128)(2,1)S(1)}, u32[]{:S(2)}, u32[]{:S(2)}) collective-permute-start(bf16[64,4096]{1,0:T(8,128)(2,1)S(1)} %get-tuple-element.1254), channel_id=1, source_target_pairs={{16,0},{32,16},{48,32},{64,48},{80,64},{96,80},{112,96},{0,112},{1... | collective-permute-start | bytes 1572872 | tf_op jit(solution)/shard_map/while/body/eval_jaxpr/ppermute | solution.py:19
  481.3 9.8 %collective-permute-start.1 = (bf16[64,4096]{1,0:T(8,128)(2,1)S(1)}, bf16[64,4096]{1,0:T(8,128)(2,1)S(1)}, u32[]{:S(2)}, u32[]{:S(2)}) collective-permute-start(bf16[64,4096]{1,0:T(8,128)(2,1)S(1)} %get-tuple-element.1254), channel_id=1, source_target_pairs={{16,0},{32,16},{48,32},{64,48},{80,64},{96,80},{112,96},{0,112},{1... | collective-permute-start | bytes 1572872 | tf_op jit(solution)/shard_map/while/body/eval_jaxpr/ppermute | solution.py:19
  495.0 9.8 %collective-permute-start.1 = (bf16[64,4096]{1,0:T(8,128)(2,1)S(1)}, bf16[64,4096]{1,0:T(8,128)(2,1)S(1)}, u32[]{:S(2)}, u32[]{:S(2)}) collective-permute-start(bf16[64,4096]{1,0:T(8,128)(2,1)S(1)} %get-tuple-element.1254), channel_id=1, source_target_pairs={{16,0},{32,16},{48,32},{64,48},{80,64},{96,80},{112,96},{0,112},{1... | collective-permute-start | bytes 1572872 | tf_op jit(solution)/shard_map/while/body/eval_jaxpr/ppermute | solution.py:19
  508.7 10.2 %collective-permute-start.1 = (bf16[64,4096]{1,0:T(8,128)(2,1)S(1)}, bf16[64,4096]{1,0:T(8,128)(2,1)S(1)}, u32[]{:S(2)}, u32[]{:S(2)}) collective-permute-start(bf16[64,4096]{1,0:T(8,128)(2,1)S(1)} %get-tuple-element.1254), channel_id=1, source_target_pairs={{16,0},{32,16},{48,32},{64,48},{80,64},{96,80},{112,96},{0,112},{1... | collective-permute-start | bytes 1572872 | tf_op jit(solution)/shard_map/while/body/eval_jaxpr/ppermute | solution.py:19
  535.3 10.1 %collective-permute-start.1 = (bf16[64,4096]{1,0:T(8,128)(2,1)S(1)}, bf16[64,4096]{1,0:T(8,128)(2,1)S(1)}, u32[]{:S(2)}, u32[]{:S(2)}) collective-permute-start(bf16[64,4096]{1,0:T(8,128)(2,1)S(1)} %get-tuple-element.1254), channel_id=1, source_target_pairs={{16,0},{32,16},{48,32},{64,48},{80,64},{96,80},{112,96},{0,112},{1... | collective-permute-start | bytes 1572872 | tf_op jit(solution)/shard_map/while/body/eval_jaxpr/ppermute | solution.py:19
  561.9 10.0 %collective-permute-start.1 = (bf16[64,4096]{1,0:T(8,128)(2,1)S(1)}, bf16[64,4096]{1,0:T(8,128)(2,1)S(1)}, u32[]{:S(2)}, u32[]{:S(2)}) collective-permute-start(bf16[64,4096]{1,0:T(8,128)(2,1)S(1)} %get-tuple-element.1254), channel_id=1, source_target_pairs={{16,0},{32,16},{48,32},{64,48},{80,64},{96,80},{112,96},{0,112},{1... | collective-permute-start | bytes 1572872 | tf_op jit(solution)/shard_map/while/body/eval_jaxpr/ppermute | solution.py:19
  637.4 277.1 %reduce-scatter.3.cloned.1.call-start = ((), (), s32[]{:S(2)}) async-start(), calls=%async_computation.2 | async-start | bytes 8912896 | tf_op jit(solution)/shard_map/reduce_scatter | solution.py:80
  641.6 22.4 %collective-permute-start.2 = (bf16[64,4096]{1,0:T(8,128)(2,1)S(1)}, bf16[64,4096]{1,0:T(8,128)(2,1)S(1)}, u32[]{:S(2)}, u32[]{:S(2)}) collective-permute-start(bf16[64,4096]{1,0:T(8,128)(2,1)S(1)} %get-tuple-element.1274), channel_id=1, source_target_pairs={{16,0},{32,16},{48,32},{64,48},{80,64},{96,80},{112,96},{0,112},{1... | collective-permute-start | bytes 1572872 | tf_op jit(solution)/shard_map/while/body/eval_jaxpr/ppermute | solution.py:19
  695.4 11.4 %collective-permute-start.2 = (bf16[64,4096]{1,0:T(8,128)(2,1)S(1)}, bf16[64,4096]{1,0:T(8,128)(2,1)S(1)}, u32[]{:S(2)}, u32[]{:S(2)}) collective-permute-start(bf16[64,4096]{1,0:T(8,128)(2,1)S(1)} %get-tuple-element.1274), channel_id=1, source_target_pairs={{16,0},{32,16},{48,32},{64,48},{80,64},{96,80},{112,96},{0,112},{1... | collective-permute-start | bytes 1572872 | tf_op jit(solution)/shard_map/while/body/eval_jaxpr/ppermute | solution.py:19
  723.4 10.7 %collective-permute-start.2 = (bf16[64,4096]{1,0:T(8,128)(2,1)S(1)}, bf16[64,4096]{1,0:T(8,128)(2,1)S(1)}, u32[]{:S(2)}, u32[]{:S(2)}) collective-permute-start(bf16[64,4096]{1,0:T(8,128)(2,1)S(1)} %get-tuple-element.1274), channel_id=1, source_target_pairs={{16,0},{32,16},{48,32},{64,48},{80,64},{96,80},{112,96},{0,112},{1... | collective-permute-start | bytes 1572872 | tf_op jit(solution)/shard_map/while/body/eval_jaxpr/ppermute | solution.py:19
  750.6 10.0 %collective-permute-start.2 = (bf16[64,4096]{1,0:T(8,128)(2,1)S(1)}, bf16[64,4096]{1,0:T(8,128)(2,1)S(1)}, u32[]{:S(2)}, u32[]{:S(2)}) collective-permute-start(bf16[64,4096]{1,0:T(8,128)(2,1)S(1)} %get-tuple-element.1274), channel_id=1, source_target_pairs={{16,0},{32,16},{48,32},{64,48},{80,64},{96,80},{112,96},{0,112},{1... | collective-permute-start | bytes 1572872 | tf_op jit(solution)/shard_map/while/body/eval_jaxpr/ppermute | solution.py:19
  (23 other events, 172.2 us)
Sparse Core Ops, SparseCore 0:
  637.5 88.5 reduce-scatter.4
  825.1 89.3 reduce-scatter.2

commit v2 on v1

--- a/solution.py
+++ b/solution.py
@@ -4,6 +4,7 @@
 from jax.sharding import PartitionSpec as P
 
 BLK = 64
+SPLIT = 2
 
 
 EPS = 1e-05
@@ -69,16 +70,19 @@
     groups = lax.axis_size("dp")
     owner = lax.axis_index("dp")
     span = normed_all.shape[1] // groups
-    part_a = lax.dot_general(
-        normed_all, back_all, (((0,), (0,)), ((), ())), preferred_element_type=jnp.float32
-    )
-    part_b = lax.dot_general(
-        upstream_all, hidden_all, (((0,), (0,)), ((), ())), preferred_element_type=jnp.float32
-    )
-    inner = part_a.shape[1]
-    joined = jnp.concatenate([part_a.astype(jnp.bfloat16), part_b.astype(jnp.bfloat16)], axis=1)
+    rows = normed_all.shape[0]
+    part_a = jnp.einsum(
+        "rqd,rk->qdk", normed_all.reshape(rows, groups, span), back_all,
+        preferred_element_type=jnp.float32,
+    )
+    part_b = jnp.einsum(
+        "rqd,rk->qdk", upstream_all.reshape(rows, groups, span), hidden_all,
+        preferred_element_type=jnp.float32,
+    )
+    joined = jnp.stack([part_a.astype(jnp.bfloat16), part_b.astype(jnp.bfloat16)], axis=1)
+    joined = joined.reshape(-1, joined.shape[-1])
     summed = lax.psum_scatter(joined, "dp", scatter_dimension=0, tiled=True).astype(jnp.float32)
-    sum_a, sum_b = summed[:, :inner], summed[:, inner:]
+    sum_a, sum_b = summed[:span], summed[span:]
     full_a = expand_blocks(mask_a[lap_idx, 0]).astype(jnp.float32)
     full_b = expand_blocks(mask_b[lap_idx, 0]).astype(jnp.float32)
     owned_a = lax.dynamic_slice_in_dim(full_a, owner * span, span, 0)
@@ -90,6 +94,9 @@
     sections = lax.axis_size("section")
     here = lax.axis_index("section")
     batches, tokens, width = micro_inputs.shape
+    batches, tokens = batches * SPLIT, tokens // SPLIT
+    micro_inputs = micro_inputs.reshape(batches, tokens, width)
+    out_cotangent = out_cotangent.reshape(batches, tokens, width)
     inner = weight_a.shape[3]
     eff_a = weight_a[:, 0] * expand_blocks(mask_a[:, 0]).astype(jnp.bfloat16)
     eff_b = weight_b[:, 0] * expand_blocks(mask_b[:, 0]).astype(jnp.bfloat16)

time: 936 us -> 1060 us (1.13)
  matrix products: 143 us -> 260 us
  waiting for transfers between devices: 376 us -> 300 us
  starting transfers between devices: 94.6 us -> 130 us
  local copies, waits for them, and re-layouts: 135 us -> 157 us
  other arithmetic: 163 us -> 183 us
    ppermute x38 -> x46, waiting for transfers between devices: 296 us -> 219 us  [shifted(): return lax.ppermute(block, axis, route)]
    dot_general x8 -> x16, matrix products: 41.5 us -> 82.4 us  [forward_layer(): jnp.dot(hidden, eff_b, preferred_element_type=jnp.float32)]
    dot_general x8 -> x16, matrix products: 37 us -> 74 us  [backward_layer(): lax.dot_general(upstream, eff_b, (((1,), (1,)), ((), ())), preferred_elem...]
    ppermute x38 -> x46, starting transfers between devices: 94.5 us -> 130 us  [shifted(): return lax.ppermute(block, axis, route)]
    dot_general x8 -> x16, matrix products: 27.3 us -> 53.4 us  [backward_layer(): preact = jnp.dot(normed, eff_a, preferred_element_type=jnp.float32)]
    dot_general x8 -> x16, matrix products: 20.6 us -> 38.5 us  [backward_layer(): lax.dot_general(back_pre, eff_a, (((1,), (1,)), ((), ())), preferred_elem...]
    concatenate x2 -> x0, other arithmetic: 15.6 us -> none  [settle(): jnp.concatenate([part_a.astype(jnp.bfloat16), part_b.astype(jnp.bfloat16)...]
    another operation x0 -> x2, other arithmetic: none -> 13.6 us  [settle(): jnp.stack([part_a.astype(jnp.bfloat16), part_b.astype(jnp.bfloat16)], axi...]
  transfers between devices with their start and end apart: 40 -> 48, of which waited for: 39 -> 47; matrix products, arithmetic and copies ran while one was open for 16% -> 20% of each run, Pallas kernels for 0% -> 0%
where the time goes in v2:
time: 1060 us; the launch traced here: 1050 us
  waiting for transfers between devices  300 us (28%)
  matrix products  260 us (25%)
  other arithmetic  183 us (17%)
  local copies, waits for them, and re-layouts  157 us (15%)
  starting transfers between devices  130 us (12%)
  between operations  14.4 us (1%)
    ppermute x46, waiting for transfers between devices, shifted(): return lax.ppermute(block, axis, route)  219 us
    ppermute x46, starting transfers between devices, shifted(): return lax.ppermute(block, axis, route)  130 us
    dynamic_update_slice x92, other arithmetic, place_item(): lax.dynamic_update_slice(buffer, value[None, None], (lap_now, micro, anch...  112 us
    dot_general x16, matrix products, forward_layer(): jnp.dot(hidden, eff_b, preferred_element_type=jnp.float32)  82.4 us
    reduce_scatter x2, waiting for transfers between devices, settle(): lax.psum_scatter(joined, 'dp', scatter_dimension=0, tiled=True)  81 us
    dot_general x16, matrix products, backward_layer(): lax.dot_general(upstream, eff_b, (((1,), (1,)), ((), ())), preferred_elem...  74 us
    dot_general x16, matrix products, backward_layer(): preact = jnp.dot(normed, eff_a, preferred_element_type=jnp.float32)  53.4 us
    dynamic_slice x92, local copies, waits for them, and re-layouts, backward_step(): buffer[lap_now, micro]  45 us
  transfers between devices with their start and end apart: 48, of which 47 were waited for; matrix products, arithmetic and copies ran while one was open for 20% of the time, Pallas kernels for 0%

profile of v2, /device:TPU:0, one launch (start us, length us, event | category | flops | bytes accessed | tf_op | source)
XLA Modules:
  0.0 1048.1 jit_solution(18352401196701955384)
XLA Ops:
  7.2 11.4 %copy.34 = bf16[2,1,4096,512]{2,3,0,1:T(8,128)(2,1)} copy(bf16[2,1,4096,512]{3,2,1,0:T(8,128)(2,1)} %param.23) | data formatting | bytes 16777216 | tf_op args[2]
  26.4 12.0 %copy.37 = bf16[2,4096,512]{2,1,0:T(8,128)(2,1)} copy(bf16[2,4096,512]{1,2,0:T(8,128)(2,1)} %bitcast_multiply_fusion.1) | data formatting | bytes 16777216 | tf_op jit(solution)/shard_map/while | solution.py:135
  38.4 12.0 %copy.35 = bf16[2,1,512,4096]{2,3,0,1:T(8,128)(2,1)} copy(bf16[2,1,512,4096]{3,2,1,0:T(8,128)(2,1)} %param.24) | data formatting | bytes 16777216 | tf_op args[3]
  58.1 11.4 %copy.38 = bf16[2,512,4096]{2,1,0:T(8,128)(2,1)} copy(bf16[2,512,4096]{1,2,0:T(8,128)(2,1)} %bitcast_multiply_fusion) | data formatting | bytes 16777216 | tf_op jit(solution)/shard_map/while | solution.py:135
  72.1 327.6 %while.63 = (s32[]{:T(128)}, bf16[32,4096]{1,0:T(8,128)(2,1)S(1)}, bf16[2,8,32,4096]{3,2,1,0:T(8,128)(2,1)}, s32[]{:T(128)}, pred[]{:T(512)}, /*index=5*/bf16[8,...) while((s32[]{:T(128)}, bf16[32,4096]{1,0:T(8,128)(2,1)S(1)}, ...), condition=%wide.region_6.7_spmd, body=%wide.region_0.6_spmd.sunk | while | flops 269959232 | bytes 12322090 | solution.py:135
  388.6 11.1 %collective-permute-done = bf16[32,4096]{1,0:T(8,128)(2,1)S(1)} collective-permute-done((bf16[32,4096]{1,0:T(8,128)(2,1)S(1)}, bf16[32,4096]{1,0:T(8,128)(2,1)S(1)}, u32[]{:S(2)}, u32[]{:S(2)}) %collective-permute-start) | collective-permute-done | bytes 262176 | tf_op jit(solution)/shard_map/while/body/eval_jaxpr/ppermute | solution.py:20
  404.8 332.2 %while.64 = (s32[]{:T(128)}, bf16[32,4096]{1,0:T(8,128)(2,1)S(1)}, bf16[2,8,32,4096]{3,2,1,0:T(8,128)(2,1)}, bf16[2,8,32,4096]{3,2,1,0:T(8,128)(2,1)}, bf16[2,8,...) while((s32[]{:T(128)}, bf16[32,4096]{1,0:T(8,128)(2,1)S(1)}, ...), condition=%wide.region_15.16_spmd, body=%wide.region_7.15_spmd.sunk | while | flops 405798976 | bytes 54039724 | solution.py:189
  408.5 11.2 %collective-permute-start.1 = (bf16[32,4096]{1,0:T(8,128)(2,1)S(1)}, bf16[32,4096]{1,0:T(8,128)(2,1)S(1)}, u32[]{:S(2)}, u32[]{:S(2)}) collective-permute-start(bf16[32,4096]{1,0:T(8,128)(2,1)S(1)} %get-tuple-element.1286), channel_id=1, source_target_pairs={{16,0},{32,16},{48,32},{64,48},{80,64},{96,80},{112,96},{0,112},{1... | collective-permute-start | bytes 786440 | tf_op jit(solution)/shard_map/while/body/eval_jaxpr/ppermute | solution.py:20
  427.0 15.0 %collective-permute-start.1 = (bf16[32,4096]{1,0:T(8,128)(2,1)S(1)}, bf16[32,4096]{1,0:T(8,128)(2,1)S(1)}, u32[]{:S(2)}, u32[]{:S(2)}) collective-permute-start(bf16[32,4096]{1,0:T(8,128)(2,1)S(1)} %get-tuple-element.1286), channel_id=1, source_target_pairs={{16,0},{32,16},{48,32},{64,48},{80,64},{96,80},{112,96},{0,112},{1... | collective-permute-start | bytes 786440 | tf_op jit(solution)/shard_map/while/body/eval_jaxpr/ppermute | solution.py:20
  449.4 15.0 %collective-permute-start.1 = (bf16[32,4096]{1,0:T(8,128)(2,1)S(1)}, bf16[32,4096]{1,0:T(8,128)(2,1)S(1)}, u32[]{:S(2)}, u32[]{:S(2)}) collective-permute-start(bf16[32,4096]{1,0:T(8,128)(2,1)S(1)} %get-tuple-element.1286), channel_id=1, source_target_pairs={{16,0},{32,16},{48,32},{64,48},{80,64},{96,80},{112,96},{0,112},{1... | collective-permute-start | bytes 786440 | tf_op jit(solution)/shard_map/while/body/eval_jaxpr/ppermute | solution.py:20
  471.8 15.0 %collective-permute-start.1 = (bf16[32,4096]{1,0:T(8,128)(2,1)S(1)}, bf16[32,4096]{1,0:T(8,128)(2,1)S(1)}, u32[]{:S(2)}, u32[]{:S(2)}) collective-permute-start(bf16[32,4096]{1,0:T(8,128)(2,1)S(1)} %get-tuple-element.1286), channel_id=1, source_target_pairs={{16,0},{32,16},{48,32},{64,48},{80,64},{96,80},{112,96},{0,112},{1... | collective-permute-start | bytes 786440 | tf_op jit(solution)/shard_map/while/body/eval_jaxpr/ppermute | solution.py:20
  494.2 15.0 %collective-permute-start.1 = (bf16[32,4096]{1,0:T(8,128)(2,1)S(1)}, bf16[32,4096]{1,0:T(8,128)(2,1)S(1)}, u32[]{:S(2)}, u32[]{:S(2)}) collective-permute-start(bf16[32,4096]{1,0:T(8,128)(2,1)S(1)} %get-tuple-element.1286), channel_id=1, source_target_pairs={{16,0},{32,16},{48,32},{64,48},{80,64},{96,80},{112,96},{0,112},{1... | collective-permute-start | bytes 786440 | tf_op jit(solution)/shard_map/while/body/eval_jaxpr/ppermute | solution.py:20
  516.6 15.0 %collective-permute-start.1 = (bf16[32,4096]{1,0:T(8,128)(2,1)S(1)}, bf16[32,4096]{1,0:T(8,128)(2,1)S(1)}, u32[]{:S(2)}, u32[]{:S(2)}) collective-permute-start(bf16[32,4096]{1,0:T(8,128)(2,1)S(1)} %get-tuple-element.1286), channel_id=1, source_target_pairs={{16,0},{32,16},{48,32},{64,48},{80,64},{96,80},{112,96},{0,112},{1... | collective-permute-start | bytes 786440 | tf_op jit(solution)/shard_map/while/body/eval_jaxpr/ppermute | solution.py:20
  538.9 15.1 %collective-permute-start.1 = (bf16[32,4096]{1,0:T(8,128)(2,1)S(1)}, bf16[32,4096]{1,0:T(8,128)(2,1)S(1)}, u32[]{:S(2)}, u32[]{:S(2)}) collective-permute-start(bf16[32,4096]{1,0:T(8,128)(2,1)S(1)} %get-tuple-element.1286), channel_id=1, source_target_pairs={{16,0},{32,16},{48,32},{64,48},{80,64},{96,80},{112,96},{0,112},{1... | collective-permute-start | bytes 786440 | tf_op jit(solution)/shard_map/while/body/eval_jaxpr/ppermute | solution.py:20
  560.6 12.6 %conditional.7 = (bf16[32,4096]{1,0:T(8,128)(2,1)S(1)}, bf16[32,4096]{1,0:T(8,128)(2,1)S(1)}, bf16[32,512]{1,0:T(8,128)(2,1)S(1)}, bf16[32,512]{1,0:T(8,128)(2,1)}) conditional(s32[]{:T(128)} %clamp.34, () %tuple.185, (bf16[32,4096]{1,0:T(8,128)(2,1)S(1)}, bf16[2,8,32,4096]{3,2,1,0:T(8,128)(2,1)}, s32[]{:T(128)}, s32[]{:T(128)}, ...), branch_computations={%region_8.8_spmd, %region_9.11_spmd, %region_12.14_spmd} | conditional | flops 405372960 | bytes 49515220 | solution.py:163
  583.0 12.6 %conditional.7 = (bf16[32,4096]{1,0:T(8,128)(2,1)S(1)}, bf16[32,4096]{1,0:T(8,128)(2,1)S(1)}, bf16[32,512]{1,0:T(8,128)(2,1)S(1)}, bf16[32,512]{1,0:T(8,128)(2,1)}) conditional(s32[]{:T(128)} %clamp.34, () %tuple.185, (bf16[32,4096]{1,0:T(8,128)(2,1)S(1)}, bf16[2,8,32,4096]{3,2,1,0:T(8,128)(2,1)}, s32[]{:T(128)}, s32[]{:T(128)}, ...), branch_computations={%region_8.8_spmd, %region_9.11_spmd, %region_12.14_spmd} | conditional | flops 405372960 | bytes 49515220 | solution.py:163
  605.4 12.6 %conditional.7 = (bf16[32,4096]{1,0:T(8,128)(2,1)S(1)}, bf16[32,4096]{1,0:T(8,128)(2,1)S(1)}, bf16[32,512]{1,0:T(8,128)(2,1)S(1)}, bf16[32,512]{1,0:T(8,128)(2,1)}) conditional(s32[]{:T(128)} %clamp.34, () %tuple.185, (bf16[32,4096]{1,0:T(8,128)(2,1)S(1)}, bf16[2,8,32,4096]{3,2,1,0:T(8,128)(2,1)}, s32[]{:T(128)}, s32[]{:T(128)}, ...), branch_computations={%region_8.8_spmd, %region_9.11_spmd, %region_12.14_spmd} | conditional | flops 405372960 | bytes 49515220 | solution.py:163
  627.8 12.6 %conditional.7 = (bf16[32,4096]{1,0:T(8,128)(2,1)S(1)}, bf16[32,4096]{1,0:T(8,128)(2,1)S(1)}, bf16[32,512]{1,0:T(8,128)(2,1)S(1)}, bf16[32,512]{1,0:T(8,128)(2,1)}) conditional(s32[]{:T(128)} %clamp.34, () %tuple.185, (bf16[32,4096]{1,0:T(8,128)(2,1)S(1)}, bf16[2,8,32,4096]{3,2,1,0:T(8,128)(2,1)}, s32[]{:T(128)}, s32[]{:T(128)}, ...), branch_computations={%region_8.8_spmd, %region_9.11_spmd, %region_12.14_spmd} | conditional | flops 405372960 | bytes 49515220 | solution.py:163
  650.2 12.6 %conditional.7 = (bf16[32,4096]{1,0:T(8,128)(2,1)S(1)}, bf16[32,4096]{1,0:T(8,128)(2,1)S(1)}, bf16[32,512]{1,0:T(8,128)(2,1)S(1)}, bf16[32,512]{1,0:T(8,128)(2,1)}) conditional(s32[]{:T(128)} %clamp.34, () %tuple.185, (bf16[32,4096]{1,0:T(8,128)(2,1)S(1)}, bf16[2,8,32,4096]{3,2,1,0:T(8,128)(2,1)}, s32[]{:T(128)}, s32[]{:T(128)}, ...), branch_computations={%region_8.8_spmd, %region_9.11_spmd, %region_12.14_spmd} | conditional | flops 405372960 | bytes 49515220 | solution.py:163
  672.6 12.6 %conditional.7 = (bf16[32,4096]{1,0:T(8,128)(2,1)S(1)}, bf16[32,4096]{1,0:T(8,128)(2,1)S(1)}, bf16[32,512]{1,0:T(8,128)(2,1)S(1)}, bf16[32,512]{1,0:T(8,128)(2,1)}) conditional(s32[]{:T(128)} %clamp.34, () %tuple.185, (bf16[32,4096]{1,0:T(8,128)(2,1)S(1)}, bf16[2,8,32,4096]{3,2,1,0:T(8,128)(2,1)}, s32[]{:T(128)}, s32[]{:T(128)}, ...), branch_computations={%region_8.8_spmd, %region_9.11_spmd, %region_12.14_spmd} | conditional | flops 405372960 | bytes 49515220 | solution.py:163
  695.0 12.6 %conditional.7 = (bf16[32,4096]{1,0:T(8,128)(2,1)S(1)}, bf16[32,4096]{1,0:T(8,128)(2,1)S(1)}, bf16[32,512]{1,0:T(8,128)(2,1)S(1)}, bf16[32,512]{1,0:T(8,128)(2,1)}) conditional(s32[]{:T(128)} %clamp.34, () %tuple.185, (bf16[32,4096]{1,0:T(8,128)(2,1)S(1)}, bf16[2,8,32,4096]{3,2,1,0:T(8,128)(2,1)}, s32[]{:T(128)}, s32[]{:T(128)}, ...), branch_computations={%region_8.8_spmd, %region_9.11_spmd, %region_12.14_spmd} | conditional | flops 405372960 | bytes 49515220 | solution.py:163
  717.4 12.6 %conditional.7 = (bf16[32,4096]{1,0:T(8,128)(2,1)S(1)}, bf16[32,4096]{1,0:T(8,128)(2,1)S(1)}, bf16[32,512]{1,0:T(8,128)(2,1)S(1)}, bf16[32,512]{1,0:T(8,128)(2,1)}) conditional(s32[]{:T(128)} %clamp.34, () %tuple.185, (bf16[32,4096]{1,0:T(8,128)(2,1)S(1)}, bf16[2,8,32,4096]{3,2,1,0:T(8,128)(2,1)}, s32[]{:T(128)}, s32[]{:T(128)}, ...), branch_computations={%region_8.8_spmd, %region_9.11_spmd, %region_12.14_spmd} | conditional | flops 405372960 | bytes 49515220 | solution.py:163
  762.5 163.8 %while.65 = (s32[]{:T(128)}, bf16[32,4096]{1,0:T(8,128)(2,1)S(1)}, bf16[2,8,32,4096]{3,2,1,0:T(8,128)(2,1)}, bf16[2,8,32,4096]{3,2,1,0:T(8,128)(2,1)}, bf16[2,8,...) while((s32[]{:T(128)}, bf16[32,4096]{1,0:T(8,128)(2,1)S(1)}, ...), condition=%wide.region_24.25_spmd, body=%wide.region_16.24_spmd.sunk | while | flops 405798976 | bytes 54039744 | solution.py:191
  765.5 12.6 %conditional.8 = (bf16[32,4096]{1,0:T(8,128)(2,1)S(1)}, bf16[32,4096]{1,0:T(8,128)(2,1)S(1)}, bf16[32,512]{1,0:T(8,128)(2,1)S(1)}, bf16[32,512]{1,0:T(8,128)(2,1)}) conditional(s32[]{:T(128)} %clamp.35, () %tuple.190, (bf16[32,4096]{1,0:T(8,128)(2,1)S(1)}, bf16[2,8,32,4096]{3,2,1,0:T(8,128)(2,1)}, s32[]{:T(128)}, s32[]{:T(128)}, ...), branch_computations={%region_17.17_spmd, %region_18.20_spmd, %region_21.23_spmd} | conditional | flops 405372960 | bytes 49515220 | solution.py:163
  787.9 13.1 %conditional.8 = (bf16[32,4096]{1,0:T(8,128)(2,1)S(1)}, bf16[32,4096]{1,0:T(8,128)(2,1)S(1)}, bf16[32,512]{1,0:T(8,128)(2,1)S(1)}, bf16[32,512]{1,0:T(8,128)(2,1)}) conditional(s32[]{:T(128)} %clamp.35, () %tuple.190, (bf16[32,4096]{1,0:T(8,128)(2,1)S(1)}, bf16[2,8,32,4096]{3,2,1,0:T(8,128)(2,1)}, s32[]{:T(128)}, s32[]{:T(128)}, ...), branch_computations={%region_17.17_spmd, %region_18.20_spmd, %region_21.23_spmd} | conditional | flops 405372960 | bytes 49515220 | solution.py:163
  807.7 13.0 %conditional.8 = (bf16[32,4096]{1,0:T(8,128)(2,1)S(1)}, bf16[32,4096]{1,0:T(8,128)(2,1)S(1)}, bf16[32,512]{1,0:T(8,128)(2,1)S(1)}, bf16[32,512]{1,0:T(8,128)(2,1)}) conditional(s32[]{:T(128)} %clamp.35, () %tuple.190, (bf16[32,4096]{1,0:T(8,128)(2,1)S(1)}, bf16[2,8,32,4096]{3,2,1,0:T(8,128)(2,1)}, s32[]{:T(128)}, s32[]{:T(128)}, ...), branch_computations={%region_17.17_spmd, %region_18.20_spmd, %region_21.23_spmd} | conditional | flops 405372960 | bytes 49515220 | solution.py:163
  827.4 12.6 %conditional.8 = (bf16[32,4096]{1,0:T(8,128)(2,1)S(1)}, bf16[32,4096]{1,0:T(8,128)(2,1)S(1)}, bf16[32,512]{1,0:T(8,128)(2,1)S(1)}, bf16[32,512]{1,0:T(8,128)(2,1)}) conditional(s32[]{:T(128)} %clamp.35, () %tuple.190, (bf16[32,4096]{1,0:T(8,128)(2,1)S(1)}, bf16[2,8,32,4096]{3,2,1,0:T(8,128)(2,1)}, s32[]{:T(128)}, s32[]{:T(128)}, ...), branch_computations={%region_17.17_spmd, %region_18.20_spmd, %region_21.23_spmd} | conditional | flops 405372960 | bytes 49515220 | solution.py:163
  846.7 12.8 %conditional.8 = (bf16[32,4096]{1,0:T(8,128)(2,1)S(1)}, bf16[32,4096]{1,0:T(8,128)(2,1)S(1)}, bf16[32,512]{1,0:T(8,128)(2,1)S(1)}, bf16[32,512]{1,0:T(8,128)(2,1)}) conditional(s32[]{:T(128)} %clamp.35, () %tuple.190, (bf16[32,4096]{1,0:T(8,128)(2,1)S(1)}, bf16[2,8,32,4096]{3,2,1,0:T(8,128)(2,1)}, s32[]{:T(128)}, s32[]{:T(128)}, ...), branch_computations={%region_17.17_spmd, %region_18.20_spmd, %region_21.23_spmd} | conditional | flops 405372960 | bytes 49515220 | solution.py:163
  867.4 12.6 %conditional.8 = (bf16[32,4096]{1,0:T(8,128)(2,1)S(1)}, bf16[32,4096]{1,0:T(8,128)(2,1)S(1)}, bf16[32,512]{1,0:T(8,128)(2,1)S(1)}, bf16[32,512]{1,0:T(8,128)(2,1)}) conditional(s32[]{:T(128)} %clamp.35, () %tuple.190, (bf16[32,4096]{1,0:T(8,128)(2,1)S(1)}, bf16[2,8,32,4096]{3,2,1,0:T(8,128)(2,1)}, s32[]{:T(128)}, s32[]{:T(128)}, ...), branch_computations={%region_17.17_spmd, %region_18.20_spmd, %region_21.23_spmd} | conditional | flops 405372960 | bytes 49515220 | solution.py:163
  888.6 12.6 %conditional.8 = (bf16[32,4096]{1,0:T(8,128)(2,1)S(1)}, bf16[32,4096]{1,0:T(8,128)(2,1)S(1)}, bf16[32,512]{1,0:T(8,128)(2,1)S(1)}, bf16[32,512]{1,0:T(8,128)(2,1)}) conditional(s32[]{:T(128)} %clamp.35, () %tuple.190, (bf16[32,4096]{1,0:T(8,128)(2,1)S(1)}, bf16[2,8,32,4096]{3,2,1,0:T(8,128)(2,1)}, s32[]{:T(128)}, s32[]{:T(128)}, ...), branch_computations={%region_17.17_spmd, %region_18.20_spmd, %region_21.23_spmd} | conditional | flops 405372960 | bytes 49515220 | solution.py:163
  909.8 12.6 %conditional.8 = (bf16[32,4096]{1,0:T(8,128)(2,1)S(1)}, bf16[32,4096]{1,0:T(8,128)(2,1)S(1)}, bf16[32,512]{1,0:T(8,128)(2,1)S(1)}, bf16[32,512]{1,0:T(8,128)(2,1)}) conditional(s32[]{:T(128)} %clamp.35, () %tuple.190, (bf16[32,4096]{1,0:T(8,128)(2,1)S(1)}, bf16[2,8,32,4096]{3,2,1,0:T(8,128)(2,1)}, s32[]{:T(128)}, s32[]{:T(128)}, ...), branch_computations={%region_17.17_spmd, %region_18.20_spmd, %region_21.23_spmd} | conditional | flops 405372960 | bytes 49515220 | solution.py:163
  955.4 81.0 %reduce-scatter.3.cloned.1.call-done = bf16[512,512]{1,0:T(8,128)(2,1)} async-done(((bf16[8192,512]{1,0:T(8,128)(2,1)}), bf16[512,512]{1,0:T(8,128)(2,1)}) %reduce-scatter.3.cloned.1.call-update) | async-done | bytes 524304 | tf_op jit(solution)/shard_map/reduce_scatter | solution.py:84
  (630 shorter events, 881.0 us)
Async XLA Ops:
  7.2 945.8 %reduce-scatter.5.cloned.1.call-start = ((), (), s32[]{:S(2)}) async-start(), calls=%async_computation.3 | async-start | bytes 8912896 | tf_op jit(solution)/shard_map/reduce_scatter | solution.py:84
  80.1 7.0 collective-permute-start
  95.3 7.0 collective-permute-start
  110.4 7.0 collective-permute-start
  125.5 7.0 collective-permute-start
  140.6 7.0 collective-permute-start
  155.7 7.0 collective-permute-start
  170.8 7.0 collective-permute-start
  185.9 7.0 collective-permute-start
  201.1 7.0 collective-permute-start
  216.2 7.0 collective-permute-start
  306.8 7.0 collective-permute-start
  316.6 8.6 collective-permute-start
  328.0 8.7 collective-permute-start
  339.4 8.6 collective-permute-start
  350.8 8.6 collective-permute-start
  362.3 9.6 collective-permute-start
  374.7 11.1 %collective-permute-start = (bf16[32,4096]{1,0:T(8,128)(2,1)S(1)}, bf16[32,4096]{1,0:T(8,128)(2,1)S(1)}, u32[]{:S(2)}, u32[]{:S(2)}) collective-permute-start(bf16[32,4096]{1,0:T(8,128)(2,1)S(1)} %get-tuple-element.1490), channel_id=1, source_target_pairs={{112,0},{0,16},{16,32},{32,48},{48,64},{64,80},{80,96},{96,112},{1... | collective-permute-start | bytes 786440 | tf_op jit(solution)/shard_map/while/body/eval_jaxpr/ppermute | solution.py:20
  388.5 11.1 %collective-permute-start = (bf16[32,4096]{1,0:T(8,128)(2,1)S(1)}, bf16[32,4096]{1,0:T(8,128)(2,1)S(1)}, u32[]{:S(2)}, u32[]{:S(2)}) collective-permute-start(bf16[32,4096]{1,0:T(8,128)(2,1)S(1)} %get-tuple-element.1490), channel_id=1, source_target_pairs={{112,0},{0,16},{16,32},{32,48},{48,64},{64,80},{80,96},{96,112},{1... | collective-permute-start | bytes 786440 | tf_op jit(solution)/shard_map/while/body/eval_jaxpr/ppermute | solution.py:20
  408.5 15.1 %collective-permute-start.1 = (bf16[32,4096]{1,0:T(8,128)(2,1)S(1)}, bf16[32,4096]{1,0:T(8,128)(2,1)S(1)}, u32[]{:S(2)}, u32[]{:S(2)}) collective-permute-start(bf16[32,4096]{1,0:T(8,128)(2,1)S(1)} %get-tuple-element.1286), channel_id=1, source_target_pairs={{16,0},{32,16},{48,32},{64,48},{80,64},{96,80},{112,96},{0,112},{1... | collective-permute-start | bytes 786440 | tf_op jit(solution)/shard_map/while/body/eval_jaxpr/ppermute | solution.py:20
  427.0 18.9 %collective-permute-start.1 = (bf16[32,4096]{1,0:T(8,128)(2,1)S(1)}, bf16[32,4096]{1,0:T(8,128)(2,1)S(1)}, u32[]{:S(2)}, u32[]{:S(2)}) collective-permute-start(bf16[32,4096]{1,0:T(8,128)(2,1)S(1)} %get-tuple-element.1286), channel_id=1, source_target_pairs={{16,0},{32,16},{48,32},{64,48},{80,64},{96,80},{112,96},{0,112},{1... | collective-permute-start | bytes 786440 | tf_op jit(solution)/shard_map/while/body/eval_jaxpr/ppermute | solution.py:20
  449.4 18.9 %collective-permute-start.1 = (bf16[32,4096]{1,0:T(8,128)(2,1)S(1)}, bf16[32,4096]{1,0:T(8,128)(2,1)S(1)}, u32[]{:S(2)}, u32[]{:S(2)}) collective-permute-start(bf16[32,4096]{1,0:T(8,128)(2,1)S(1)} %get-tuple-element.1286), channel_id=1, source_target_pairs={{16,0},{32,16},{48,32},{64,48},{80,64},{96,80},{112,96},{0,112},{1... | collective-permute-start | bytes 786440 | tf_op jit(solution)/shard_map/while/body/eval_jaxpr/ppermute | solution.py:20
  471.8 18.9 %collective-permute-start.1 = (bf16[32,4096]{1,0:T(8,128)(2,1)S(1)}, bf16[32,4096]{1,0:T(8,128)(2,1)S(1)}, u32[]{:S(2)}, u32[]{:S(2)}) collective-permute-start(bf16[32,4096]{1,0:T(8,128)(2,1)S(1)} %get-tuple-element.1286), channel_id=1, source_target_pairs={{16,0},{32,16},{48,32},{64,48},{80,64},{96,80},{112,96},{0,112},{1... | collective-permute-start | bytes 786440 | tf_op jit(solution)/shard_map/while/body/eval_jaxpr/ppermute | solution.py:20
  494.2 18.9 %collective-permute-start.1 = (bf16[32,4096]{1,0:T(8,128)(2,1)S(1)}, bf16[32,4096]{1,0:T(8,128)(2,1)S(1)}, u32[]{:S(2)}, u32[]{:S(2)}) collective-permute-start(bf16[32,4096]{1,0:T(8,128)(2,1)S(1)} %get-tuple-element.1286), channel_id=1, source_target_pairs={{16,0},{32,16},{48,32},{64,48},{80,64},{96,80},{112,96},{0,112},{1... | collective-permute-start | bytes 786440 | tf_op jit(solution)/shard_map/while/body/eval_jaxpr/ppermute | solution.py:20
  516.6 18.9 %collective-permute-start.1 = (bf16[32,4096]{1,0:T(8,128)(2,1)S(1)}, bf16[32,4096]{1,0:T(8,128)(2,1)S(1)}, u32[]{:S(2)}, u32[]{:S(2)}) collective-permute-start(bf16[32,4096]{1,0:T(8,128)(2,1)S(1)} %get-tuple-element.1286), channel_id=1, source_target_pairs={{16,0},{32,16},{48,32},{64,48},{80,64},{96,80},{112,96},{0,112},{1... | collective-permute-start | bytes 786440 | tf_op jit(solution)/shard_map/while/body/eval_jaxpr/ppermute | solution.py:20
  538.9 18.9 %collective-permute-start.1 = (bf16[32,4096]{1,0:T(8,128)(2,1)S(1)}, bf16[32,4096]{1,0:T(8,128)(2,1)S(1)}, u32[]{:S(2)}, u32[]{:S(2)}) collective-permute-start(bf16[32,4096]{1,0:T(8,128)(2,1)S(1)} %get-tuple-element.1286), channel_id=1, source_target_pairs={{16,0},{32,16},{48,32},{64,48},{80,64},{96,80},{112,96},{0,112},{1... | collective-permute-start | bytes 786440 | tf_op jit(solution)/shard_map/while/body/eval_jaxpr/ppermute | solution.py:20
  595.6 7.0 collective-permute-start.1
  640.4 7.1 collective-permute-start.1
  662.8 7.0 collective-permute-start.1
  685.2 7.0 collective-permute-start.1
  707.6 7.0 collective-permute-start.1
  762.4 273.9 %reduce-scatter.3.cloned.1.call-start = ((), (), s32[]{:S(2)}) async-start(), calls=%async_computation.2 | async-start | bytes 8912896 | tf_op jit(solution)/shard_map/reduce_scatter | solution.py:84
  (38 other events, 254.3 us)
Sparse Core Ops, SparseCore 0:
  762.6 88.8 reduce-scatter.4
  948.6 87.6 reduce-scatter.2

commit v3 on v2

--- a/solution.py
+++ b/solution.py
@@ -1,13 +1,114 @@
 import jax
 import jax.numpy as jnp
 from jax import lax
+from jax.experimental import pallas as pl
+from jax.experimental.pallas import tpu as pltpu
 from jax.sharding import PartitionSpec as P
 
 BLK = 64
-SPLIT = 2
+SPLIT = 1
+TK = 128
 
 
 EPS = 1e-05
+
+
+def _fwd_kernel(lap_ref, x_ref, ea_ref, eb_ref, o_ref, n_scr, acc_scr):
+    k = pl.program_id(0)
+
+    @pl.when(k == 0)
+    def _():
+        wide = x_ref[...].astype(jnp.float32)
+        inv = lax.rsqrt(jnp.mean(wide * wide, axis=-1, keepdims=True) + EPS)
+        n_scr[...] = (wide * inv).astype(jnp.bfloat16)
+        acc_scr[...] = wide
+
+    p = jnp.dot(n_scr[...], ea_ref[...], preferred_element_type=jnp.float32)
+    h = (p * jax.nn.sigmoid(p)).astype(jnp.bfloat16)
+    acc_scr[...] += jnp.dot(h, eb_ref[...], preferred_element_type=jnp.float32)
+
+    @pl.when(k == pl.num_programs(0) - 1)
+    def _():
+        o_ref[...] = acc_scr[...].astype(o_ref.dtype)
+
+
+def fwd_call(lap, x, ea_all, eb_all):
+    rows, width = x.shape
+    inner = ea_all.shape[-1]
+    return pl.pallas_call(
+        _fwd_kernel,
+        grid_spec=pltpu.PrefetchScalarGridSpec(
+            num_scalar_prefetch=1,
+            grid=(inner // TK,),
+            in_specs=[
+                pl.BlockSpec((rows, width), lambda k, lp: (0, 0)),
+                pl.BlockSpec((None, width, TK), lambda k, lp: (lp[0], 0, k)),
+                pl.BlockSpec((None, TK, width), lambda k, lp: (lp[0], k, 0)),
+            ],
+            out_specs=pl.BlockSpec((rows, width), lambda k, lp: (0, 0)),
+            scratch_shapes=[pltpu.VMEM((rows, width), jnp.bfloat16), pltpu.VMEM((rows, width), jnp.float32)],
+        ),
+        out_shape=jax.ShapeDtypeStruct((rows, width), jnp.bfloat16),
+        compiler_params=pltpu.CompilerParams(dimension_semantics=("arbitrary",), vmem_limit_bytes=48 * 1024 * 1024)
+    )(jnp.reshape(lap, (1,)).astype(jnp.int32), x, ea_all, eb_all)
+
+
+def _bwd_kernel(lap_ref, x_ref, g_ref, ea_ref, eb_ref, down_ref, normed_ref, hidden_ref, bp_ref, gn_scr):
+    k = pl.program_id(0)
+
+    @pl.when(k == 0)
+    def _():
+        wide = x_ref[...].astype(jnp.float32)
+        inv = lax.rsqrt(jnp.mean(wide * wide, axis=-1, keepdims=True) + EPS)
+        normed_ref[...] = (wide * inv).astype(jnp.bfloat16)
+        gn_scr[...] = jnp.zeros_like(gn_scr)
+
+    ea = ea_ref[...]
+    p = jnp.dot(normed_ref[...], ea, preferred_element_type=jnp.float32)
+    sg = jax.nn.sigmoid(p)
+    hidden_ref[...] = (p * sg).astype(jnp.bfloat16)
+    gh = lax.dot_general(g_ref[...], eb_ref[...], (((1,), (1,)), ((), ())), preferred_element_type=jnp.float32)
+    gp = (gh * sg * (1.0 + p * (1.0 - sg))).astype(jnp.bfloat16)
+    bp_ref[...] = gp
+    gn_scr[...] += lax.dot_general(gp, ea, (((1,), (1,)), ((), ())), preferred_element_type=jnp.float32)
+
+    @pl.when(k == pl.num_programs(0) - 1)
+    def _():
+        wide = x_ref[...].astype(jnp.float32)
+        inv = lax.rsqrt(jnp.mean(wide * wide, axis=-1, keepdims=True) + EPS)
+        scaled = wide * inv
+        gn = gn_scr[...]
+        center = jnp.mean(gn * scaled, axis=-1, keepdims=True)
+        down_ref[...] = (g_ref[...].astype(jnp.float32) + inv * (gn - scaled * center)).astype(down_ref.dtype)
+
+
+def bwd_call(lap, x, g, ea_all, eb_all):
+    rows, width = x.shape
+    inner = ea_all.shape[-1]
+    full = pl.BlockSpec((rows, width), lambda k, lp: (0, 0))
+    part = pl.BlockSpec((rows, TK), lambda k, lp: (0, k))
+    return pl.pallas_call(
+        _bwd_kernel,
+        grid_spec=pltpu.PrefetchScalarGridSpec(
+            num_scalar_prefetch=1,
+            grid=(inner // TK,),
+            in_specs=[
+                full,
+                full,
+                pl.BlockSpec((None, width, TK), lambda k, lp: (lp[0], 0, k)),
+                pl.BlockSpec((None, TK, width), lambda k, lp: (lp[0], k, 0)),
+            ],
+            out_specs=[full, full, part, part],
+            scratch_shapes=[pltpu.VMEM((rows, width), jnp.float32)],
+        ),
+        out_shape=[
+            jax.ShapeDtypeStruct((rows, width), jnp.bfloat16),
+            jax.ShapeDtypeStruct((rows, width), jnp.bfloat16),
+            jax.ShapeDtypeStruct((rows, inner), jnp.bfloat16),
+            jax.ShapeDtypeStruct((rows, inner), jnp.bfloat16),
+        ],
+        compiler_params=pltpu.CompilerParams(dimension_semantics=("arbitrary",), vmem_limit_bytes=48 * 1024 * 1024)
+    )(jnp.reshape(lap, (1,)).astype(jnp.int32), x, g, ea_all, eb_all)
 
 
 def shortened(shard):
@@ -120,7 +221,7 @@
         micro = jnp.clip(jnp.where(second_on, second_micro, first_micro), 0, batches - 1)
         values = jnp.where((here == 0) & (lap_now == 0), micro_inputs[micro], incoming)
         branch = first_on.astype(jnp.int32) + 2 * second_on.astype(jnp.int32)
-        result = lax.switch(branch, [spare_forward, forward_zero, forward_one], values)
+        result = fwd_call(lap_now, values, eff_a, eff_b)
         keep = jnp.where(first_on | second_on, values, saved[lap_now, micro])
         saved = place_item(saved, lap_now, micro, keep)
         incoming = jax.tree.map(
@@ -160,9 +261,7 @@
         )
         values = saved_rows[lap_now, micro]
         branch = first_on.astype(jnp.int32) + 2 * second_on.astype(jnp.int32)
-        downstream, normed, hidden, back_pre = lax.switch(
-            branch, [spare_backward, backward_zero, backward_one], values, upstream
-        )
+        downstream, normed, hidden, back_pre = bwd_call(lap_now, values, upstream, eff_a, eff_b)
         active = first_on | second_on
         fresh = (normed, upstream, hidden, back_pre)
         stores = tuple(

time: 1060 us -> 1020 us (0.962)
  Pallas kernels: 0 us -> 269 us
  matrix products: 260 us -> 11.7 us
  starting transfers between devices: 130 us -> 57.3 us
  waiting for transfers between devices: 300 us -> 356 us
  other arithmetic: 183 us -> 130 us
  local copies, waits for them, and re-layouts: 157 us -> 170 us
    pallas_call x0 -> x38, Pallas kernels: none -> 269 us  [the longest x19 167 us: bwd_call(): pl.pallas_call(_bwd_kernel, grid_spec=pltpu.PrefetchScalarGridSpec(num_sc...]
    dot_general x64 -> x0, matrix products: 248 us -> none  [the longest x16 82.4 us: forward_layer(): jnp.dot(hidden, eff_b, preferred_element_type=jnp.float32)]
    ppermute x46 -> x38, starting transfers between devices: 130 us -> 57.2 us  [shifted(): return lax.ppermute(block, axis, route)]
    ppermute x46 -> x38, waiting for transfers between devices: 219 us -> 274 us  [shifted(): return lax.ppermute(block, axis, route)]
    squeeze x0 -> x19, local copies, waits for them, and re-layouts: none -> 20.5 us  [backward_step(): values = saved_rows[lap_now, micro]]
    reduce_sum x32 -> x0, other arithmetic: 20.4 us -> none  [normalize(): inverse = lax.rsqrt(jnp.mean(wide * wide, axis=-1, keepdims=True) + EPS)]
    convert_element_type x16 -> x0, other arithmetic: 18.8 us -> none  [backward_layer(): normed = scaled.astype(jnp.bfloat16)]
    dynamic_update_slice x92 -> x76, other arithmetic: 112 us -> 97.8 us  [place_item(): lax.dynamic_update_slice(buffer, value[None, None], (lap_now, micro, anch...]
  transfers between devices with their start and end apart: 48 -> 40, of which waited for: 47 -> 39; matrix products, arithmetic and copies ran while one was open for 20% -> 10% of each run, Pallas kernels for 0% -> 7%
where the time goes in v3:
time: 1020 us; the launch traced here: 1010 us
  waiting for transfers between devices  356 us (35%)
  Pallas kernels  269 us (26%)
  local copies, waits for them, and re-layouts  170 us (17%)
  other arithmetic  130 us (13%)
  starting transfers between devices  57.3 us (6%)
  between operations  14.4 us (1%)
  matrix products  11.7 us (1%)
    ppermute x38, waiting for transfers between devices, shifted(): return lax.ppermute(block, axis, route)  274 us
    pallas_call x19, Pallas kernels, bwd_call(): pl.pallas_call(_bwd_kernel, grid_spec=pltpu.PrefetchScalarGridSpec(num_sc...  167 us
    pallas_call x19, Pallas kernels, fwd_call(): pl.pallas_call(_fwd_kernel, grid_spec=pltpu.PrefetchScalarGridSpec(num_sc...  102 us
    dynamic_update_slice x76, other arithmetic, place_item(): lax.dynamic_update_slice(buffer, value[None, None], (lap_now, micro, anch...  97.8 us
    reduce_scatter x2, waiting for transfers between devices, settle(): lax.psum_scatter(joined, 'dp', scatter_dimension=0, tiled=True)  82 us
    ppermute x38, starting transfers between devices, shifted(): return lax.ppermute(block, axis, route)  57.2 us
    dynamic_slice x76, local copies, waits for them, and re-layouts, backward_step(): buffer[lap_now, micro]  41.3 us
    unnamed x17, local copies, waits for them, and re-layouts  28.5 us
  transfers between devices with their start and end apart: 40, of which 39 were waited for; matrix products, arithmetic and copies ran while one was open for 10% of the time, Pallas kernels for 7%

profile of v3, /device:TPU:0, one launch (start us, length us, event | category | flops | bytes accessed | tf_op | source)
XLA Modules:
  0.0 1009.8 jit_solution(14323513383494069014)
XLA Ops:
  7.2 11.5 %copy.34 = bf16[2,1,4096,512]{2,3,0,1:T(8,128)(2,1)} copy(bf16[2,1,4096,512]{3,2,1,0:T(8,128)(2,1)} %param.14) | data formatting | bytes 16777216 | tf_op args[2]
  26.5 12.0 %copy.37 = bf16[2,4096,512]{2,1,0:T(8,128)(2,1)} copy(bf16[2,4096,512]{1,2,0:T(8,128)(2,1)} %bitcast_multiply_fusion.1) | data formatting | bytes 16777216 | tf_op jit(solution)/shard_map/while | solution.py:236
  38.5 12.0 %copy.35 = bf16[2,1,512,4096]{2,3,0,1:T(8,128)(2,1)} copy(bf16[2,1,512,4096]{3,2,1,0:T(8,128)(2,1)} %param.15) | data formatting | bytes 16777216 | tf_op args[3]
  58.2 11.5 %copy.38 = bf16[2,512,4096]{2,1,0:T(8,128)(2,1)} copy(bf16[2,512,4096]{1,2,0:T(8,128)(2,1)} %bitcast_multiply_fusion) | data formatting | bytes 16777216 | tf_op jit(solution)/shard_map/while | solution.py:236
  72.2 349.2 %while.63 = (s32[]{:T(128)}, bf16[64,4096]{1,0:T(8,128)(2,1)S(1)}, bf16[2,4,64,4096]{3,2,1,0:T(8,128)(2,1)}, s32[]{:T(128)}, pred[]{:T(512)}, /*index=5*/bf16[4,...) while((s32[]{:T(128)}, bf16[64,4096]{1,0:T(8,128)(2,1)S(1)}, ...), condition=%wide.region_1.2_spmd, body=%wide.region_0.1_spmd.sunk | while | flops 524308 | bytes 5767516 | solution.py:236
  80.8 9.8 collective-permute-done
  99.2 9.8 collective-permute-done
  117.6 9.8 collective-permute-done
  135.9 9.8 collective-permute-done
  154.3 9.8 collective-permute-done
  172.7 9.8 collective-permute-done
  191.1 9.8 collective-permute-done
  209.5 9.8 collective-permute-done
  227.8 9.8 collective-permute-done
  246.2 9.8 collective-permute-done
  264.6 9.8 collective-permute-done
  282.9 9.8 collective-permute-done
  301.3 9.8 collective-permute-done
  319.7 9.8 collective-permute-done
  338.1 9.8 collective-permute-done
  356.5 9.8 collective-permute-done
  374.9 9.8 collective-permute-done
  393.2 9.8 collective-permute-done
  411.6 9.8 collective-permute-done
  426.6 248.5 %while.64 = (s32[]{:T(128)}, bf16[64,4096]{1,0:T(8,128)(2,1)S(1)}, bf16[2,4,64,4096]{3,2,1,0:T(8,128)(2,1)}, bf16[2,4,64,4096]{3,2,1,0:T(8,128)(2,1)}, bf16[2,4,...) while((s32[]{:T(128)}, bf16[64,4096]{1,0:T(8,128)(2,1)S(1)}, ...), condition=%wide.region_3.4_spmd, body=%wide.region_2.3_spmd.sunk | while | flops 851985 | bytes 10093956 | solution.py:288
  431.0 8.8 eval_jaxpr.25
  610.8 8.8 eval_jaxpr.25
  701.8 184.2 %while.65 = (s32[]{:T(128)}, bf16[64,4096]{1,0:T(8,128)(2,1)S(1)}, bf16[2,4,64,4096]{3,2,1,0:T(8,128)(2,1)}, bf16[2,4,64,4096]{3,2,1,0:T(8,128)(2,1)}, bf16[2,4,...) while((s32[]{:T(128)}, bf16[64,4096]{1,0:T(8,128)(2,1)S(1)}, ...), condition=%wide.region_5.6_spmd, body=%wide.region_4.5_spmd.sunk | while | flops 851986 | bytes 10093976 | solution.py:290
  729.0 9.0 eval_jaxpr.26
  752.4 8.8 eval_jaxpr.26
  775.8 8.8 eval_jaxpr.26
  916.2 82.0 %reduce-scatter.3.cloned.1.call-done = bf16[512,512]{1,0:T(8,128)(2,1)} async-done(((bf16[8192,512]{1,0:T(8,128)(2,1)}), bf16[512,512]{1,0:T(8,128)(2,1)}) %reduce-scatter.3.cloned.1.call-update) | async-done | bytes 524304 | tf_op jit(solution)/shard_map/reduce_scatter | solution.py:185
  (358 shorter events, 634.7 us)
Async XLA Ops:
  7.2 906.6 %reduce-scatter.5.cloned.1.call-start = ((), (), s32[]{:S(2)}) async-start(), calls=%async_computation.3 | async-start | bytes 8912896 | tf_op jit(solution)/shard_map/reduce_scatter | solution.py:185
  80.8 9.8 collective-permute-start
  99.1 9.8 collective-permute-start
  117.5 9.8 collective-permute-start
  135.9 9.8 collective-permute-start
  154.3 9.8 collective-permute-start
  172.7 9.8 collective-permute-start
  191.1 9.8 collective-permute-start
  209.4 9.8 collective-permute-start
  227.8 9.8 collective-permute-start
  246.2 9.8 collective-permute-start
  264.5 9.8 collective-permute-start
  282.9 9.8 collective-permute-start
  301.3 9.8 collective-permute-start
  319.7 9.8 collective-permute-start
  338.1 9.8 collective-permute-start
  356.4 9.8 collective-permute-start
  374.8 9.8 collective-permute-start
  393.2 9.8 collective-permute-start
  411.6 9.8 collective-permute-start
  505.2 9.8 collective-permute-start.1
  528.1 9.8 collective-permute-start.1
  619.6 9.8 collective-permute-start.1
  642.4 9.9 collective-permute-start.1
  701.7 296.4 %reduce-scatter.3.cloned.1.call-start = ((), (), s32[]{:S(2)}) async-start(), calls=%async_computation.2 | async-start | bytes 8912896 | tf_op jit(solution)/shard_map/reduce_scatter | solution.py:185
  738.0 10.1 collective-permute-start.2
  761.2 10.2 %collective-permute-start.2 = (bf16[64,4096]{1,0:T(8,128)(2,1)S(1)}, bf16[64,4096]{1,0:T(8,128)(2,1)S(1)}, u32[]{:S(2)}, u32[]{:S(2)}) collective-permute-start(bf16[64,4096]{1,0:T(8,128)(2,1)S(1)} %get-tuple-element.1109), channel_id=1, source_target_pairs={{16,0},{32,16},{48,32},{64,48},{80,64},{96,80},{112,96},{0,112},{1... | collective-permute-start | bytes 1572872 | tf_op jit(solution)/shard_map/while/body/eval_jaxpr/ppermute | solution.py:121
  784.5 9.9 collective-permute-start.2
  807.4 9.9 collective-permute-start.2
  830.4 9.8 collective-permute-start.2
  853.2 9.9 collective-permute-start.2
  876.1 9.9 collective-permute-start.2
  (12 other events, 100.8 us)
Sparse Core Ops, SparseCore 0:
  701.9 88.6 reduce-scatter.4
  909.4 88.6 reduce-scatter.2

commit v4 on v3

--- a/solution.py
+++ b/solution.py
@@ -221,7 +221,12 @@
         micro = jnp.clip(jnp.where(second_on, second_micro, first_micro), 0, batches - 1)
         values = jnp.where((here == 0) & (lap_now == 0), micro_inputs[micro], incoming)
         branch = first_on.astype(jnp.int32) + 2 * second_on.astype(jnp.int32)
-        result = fwd_call(lap_now, values, eff_a, eff_b)
+        result = lax.cond(
+            first_on | second_on,
+            lambda v: fwd_call(lap_now, v, eff_a, eff_b),
+            spare_forward,
+            values,
+        )
         keep = jnp.where(first_on | second_on, values, saved[lap_now, micro])
         saved = place_item(saved, lap_now, micro, keep)
         incoming = jax.tree.map(
@@ -261,7 +266,13 @@
         )
         values = saved_rows[lap_now, micro]
         branch = first_on.astype(jnp.int32) + 2 * second_on.astype(jnp.int32)
-        downstream, normed, hidden, back_pre = bwd_call(lap_now, values, upstream, eff_a, eff_b)
+        downstream, normed, hidden, back_pre = lax.cond(
+            first_on | second_on,
+            lambda v, u: tuple(bwd_call(lap_now, v, u, eff_a, eff_b)),
+            spare_backward,
+            values,
+            upstream,
+        )
         active = first_on | second_on
         fresh = (normed, upstream, hidden, back_pre)
         stores = tuple(

time: 1020 us -> 890 us (0.87)
  Pallas kernels: 269 us -> 114 us
  starting transfers between devices: 57.3 us -> 89.9 us
  local copies, waits for them, and re-layouts: 170 us -> 157 us
    pallas_call x19 -> x8, Pallas kernels: 167 us -> 70.5 us  [bwd_call(): pl.pallas_call(_bwd_kernel, grid_spec=pltpu.PrefetchScalarGridSpec(num_sc...]
    pallas_call x19 -> x8, Pallas kernels: 102 us -> 43.1 us  [fwd_call(): pl.pallas_call(_fwd_kernel, grid_spec=pltpu.PrefetchScalarGridSpec(num_sc...]
    ppermute x38, starting transfers between devices: 57.2 us -> 89.8 us  [shifted(): return lax.ppermute(block, axis, route)]
    squeeze x19 -> x8, local copies, waits for them, and re-layouts: 20.5 us -> 8.61 us  [backward_step(): values = saved_rows[lap_now, micro]]
    unnamed x17 -> x21, local copies, waits for them, and re-layouts: 28.5 us -> 28.9 us
  transfers between devices with their start and end apart: 40 -> 40, of which waited for: 39 -> 39; matrix products, arithmetic and copies ran while one was open for 10% -> 11% of each run, Pallas kernels for 7% -> 4%
where the time goes in v4:
time: 890 us; the launch traced here: 883 us
  waiting for transfers between devices  366 us (41%)
  local copies, waits for them, and re-layouts  157 us (18%)
  other arithmetic  129 us (14%)
  Pallas kernels  114 us (13%)
  starting transfers between devices  89.9 us (10%)
  between operations  14.4 us (2%)
  matrix products  11.7 us (1%)
    ppermute x38, waiting for transfers between devices, shifted(): return lax.ppermute(block, axis, route)  283 us
    dynamic_update_slice x76, other arithmetic, place_item(): lax.dynamic_update_slice(buffer, value[None, None], (lap_now, micro, anch...  97.3 us
    ppermute x38, starting transfers between devices, shifted(): return lax.ppermute(block, axis, route)  89.8 us
    reduce_scatter x2, waiting for transfers between devices, settle(): lax.psum_scatter(joined, 'dp', scatter_dimension=0, tiled=True)  82.5 us
    pallas_call x8, Pallas kernels, bwd_call(): pl.pallas_call(_bwd_kernel, grid_spec=pltpu.PrefetchScalarGridSpec(num_sc...  70.5 us
    pallas_call x8, Pallas kernels, fwd_call(): pl.pallas_call(_fwd_kernel, grid_spec=pltpu.PrefetchScalarGridSpec(num_sc...  43.1 us
    dynamic_slice x76, local copies, waits for them, and re-layouts, backward_step(): buffer[lap_now, micro]  41.2 us
    unnamed x21, local copies, waits for them, and re-layouts  28.9 us
  transfers between devices with their start and end apart: 40, of which 39 were waited for; matrix products, arithmetic and copies ran while one was open for 11% of the time, Pallas kernels for 4%

profile of v4, /device:TPU:0, one launch (start us, length us, event | category | flops | bytes accessed | tf_op | source)
XLA Modules:
  0.0 883.2 jit_solution(2456985133388297095)
XLA Ops:
  7.2 11.4 %copy.34 = bf16[2,1,4096,512]{2,3,0,1:T(8,128)(2,1)} copy(bf16[2,1,4096,512]{3,2,1,0:T(8,128)(2,1)} %param.20) | data formatting | bytes 16777216 | tf_op args[2]
  26.3 12.0 %copy.37 = bf16[2,4096,512]{2,1,0:T(8,128)(2,1)} copy(bf16[2,4096,512]{1,2,0:T(8,128)(2,1)} %bitcast_multiply_fusion.1) | data formatting | bytes 16777216 | tf_op jit(solution)/shard_map/while | solution.py:241
  38.3 12.0 %copy.35 = bf16[2,1,512,4096]{2,3,0,1:T(8,128)(2,1)} copy(bf16[2,1,512,4096]{3,2,1,0:T(8,128)(2,1)} %param.21) | data formatting | bytes 16777216 | tf_op args[3]
  58.1 11.4 %copy.38 = bf16[2,512,4096]{2,1,0:T(8,128)(2,1)} copy(bf16[2,512,4096]{1,2,0:T(8,128)(2,1)} %bitcast_multiply_fusion) | data formatting | bytes 16777216 | tf_op jit(solution)/shard_map/while | solution.py:241
  72.0 298.5 %while.63 = (s32[]{:T(128)}, bf16[64,4096]{1,0:T(8,128)(2,1)S(1)}, bf16[2,4,64,4096]{3,2,1,0:T(8,128)(2,1)}, s32[]{:T(128)}, pred[]{:T(512)}, /*index=5*/bf16[4,...) while((s32[]{:T(128)}, bf16[64,4096]{1,0:T(8,128)(2,1)S(1)}, ...), condition=%wide.region_3.4_spmd, body=%wide.region_0.3_spmd.sunk | while | flops 524309 | bytes 6291851 | solution.py:241
  80.5 9.8 %collective-permute-done = bf16[64,4096]{1,0:T(8,128)(2,1)S(1)} collective-permute-done((bf16[64,4096]{1,0:T(8,128)(2,1)S(1)}, bf16[64,4096]{1,0:T(8,128)(2,1)S(1)}, u32[]{:S(2)}, u32[]{:S(2)}) %collective-permute-start) | collective-permute-done | bytes 524320 | tf_op jit(solution)/shard_map/while/body/eval_jaxpr/ppermute | solution.py:121
  117.3 9.8 %collective-permute-done = bf16[64,4096]{1,0:T(8,128)(2,1)S(1)} collective-permute-done((bf16[64,4096]{1,0:T(8,128)(2,1)S(1)}, bf16[64,4096]{1,0:T(8,128)(2,1)S(1)}, u32[]{:S(2)}, u32[]{:S(2)}) %collective-permute-start) | collective-permute-done | bytes 524320 | tf_op jit(solution)/shard_map/while/body/eval_jaxpr/ppermute | solution.py:121
  135.6 9.8 %collective-permute-done = bf16[64,4096]{1,0:T(8,128)(2,1)S(1)} collective-permute-done((bf16[64,4096]{1,0:T(8,128)(2,1)S(1)}, bf16[64,4096]{1,0:T(8,128)(2,1)S(1)}, u32[]{:S(2)}, u32[]{:S(2)}) %collective-permute-start) | collective-permute-done | bytes 524320 | tf_op jit(solution)/shard_map/while/body/eval_jaxpr/ppermute | solution.py:121
  148.7 9.8 %collective-permute-done = bf16[64,4096]{1,0:T(8,128)(2,1)S(1)} collective-permute-done((bf16[64,4096]{1,0:T(8,128)(2,1)S(1)}, bf16[64,4096]{1,0:T(8,128)(2,1)S(1)}, u32[]{:S(2)}, u32[]{:S(2)}) %collective-permute-start) | collective-permute-done | bytes 524320 | tf_op jit(solution)/shard_map/while/body/eval_jaxpr/ppermute | solution.py:121
  187.8 11.4 %collective-permute-done = bf16[64,4096]{1,0:T(8,128)(2,1)S(1)} collective-permute-done((bf16[64,4096]{1,0:T(8,128)(2,1)S(1)}, bf16[64,4096]{1,0:T(8,128)(2,1)S(1)}, u32[]{:S(2)}, u32[]{:S(2)}) %collective-permute-start) | collective-permute-done | bytes 524320 | tf_op jit(solution)/shard_map/while/body/eval_jaxpr/ppermute | solution.py:121
  207.7 9.8 %collective-permute-done = bf16[64,4096]{1,0:T(8,128)(2,1)S(1)} collective-permute-done((bf16[64,4096]{1,0:T(8,128)(2,1)S(1)}, bf16[64,4096]{1,0:T(8,128)(2,1)S(1)}, u32[]{:S(2)}, u32[]{:S(2)}) %collective-permute-start) | collective-permute-done | bytes 524320 | tf_op jit(solution)/shard_map/while/body/eval_jaxpr/ppermute | solution.py:121
  226.1 9.8 %collective-permute-done = bf16[64,4096]{1,0:T(8,128)(2,1)S(1)} collective-permute-done((bf16[64,4096]{1,0:T(8,128)(2,1)S(1)}, bf16[64,4096]{1,0:T(8,128)(2,1)S(1)}, u32[]{:S(2)}, u32[]{:S(2)}) %collective-permute-start) | collective-permute-done | bytes 524320 | tf_op jit(solution)/shard_map/while/body/eval_jaxpr/ppermute | solution.py:121
  262.8 9.8 %collective-permute-done = bf16[64,4096]{1,0:T(8,128)(2,1)S(1)} collective-permute-done((bf16[64,4096]{1,0:T(8,128)(2,1)S(1)}, bf16[64,4096]{1,0:T(8,128)(2,1)S(1)}, u32[]{:S(2)}, u32[]{:S(2)}) %collective-permute-start) | collective-permute-done | bytes 524320 | tf_op jit(solution)/shard_map/while/body/eval_jaxpr/ppermute | solution.py:121
  315.0 11.4 %collective-permute-done = bf16[64,4096]{1,0:T(8,128)(2,1)S(1)} collective-permute-done((bf16[64,4096]{1,0:T(8,128)(2,1)S(1)}, bf16[64,4096]{1,0:T(8,128)(2,1)S(1)}, u32[]{:S(2)}, u32[]{:S(2)}) %collective-permute-start) | collective-permute-done | bytes 524320 | tf_op jit(solution)/shard_map/while/body/eval_jaxpr/ppermute | solution.py:121
  329.6 11.5 %collective-permute-done = bf16[64,4096]{1,0:T(8,128)(2,1)S(1)} collective-permute-done((bf16[64,4096]{1,0:T(8,128)(2,1)S(1)}, bf16[64,4096]{1,0:T(8,128)(2,1)S(1)}, u32[]{:S(2)}, u32[]{:S(2)}) %collective-permute-start) | collective-permute-done | bytes 524320 | tf_op jit(solution)/shard_map/while/body/eval_jaxpr/ppermute | solution.py:121
  344.3 11.4 %collective-permute-done = bf16[64,4096]{1,0:T(8,128)(2,1)S(1)} collective-permute-done((bf16[64,4096]{1,0:T(8,128)(2,1)S(1)}, bf16[64,4096]{1,0:T(8,128)(2,1)S(1)}, u32[]{:S(2)}, u32[]{:S(2)}) %collective-permute-start) | collective-permute-done | bytes 524320 | tf_op jit(solution)/shard_map/while/body/eval_jaxpr/ppermute | solution.py:121
  359.0 11.4 %collective-permute-done = bf16[64,4096]{1,0:T(8,128)(2,1)S(1)} collective-permute-done((bf16[64,4096]{1,0:T(8,128)(2,1)S(1)}, bf16[64,4096]{1,0:T(8,128)(2,1)S(1)}, u32[]{:S(2)}, u32[]{:S(2)}) %collective-permute-start) | collective-permute-done | bytes 524320 | tf_op jit(solution)/shard_map/while/body/eval_jaxpr/ppermute | solution.py:121
  375.7 215.3 %while.64 = (s32[]{:T(128)}, bf16[64,4096]{1,0:T(8,128)(2,1)S(1)}, bf16[2,4,64,4096]{3,2,1,0:T(8,128)(2,1)}, bf16[2,4,64,4096]{3,2,1,0:T(8,128)(2,1)}, bf16[2,4,...) while((s32[]{:T(128)}, bf16[64,4096]{1,0:T(8,128)(2,1)S(1)}, ...), condition=%wide.region_7.8_spmd, body=%wide.region_4.7_spmd.sunk | while | flops 851986 | bytes 10226137 | solution.py:299
  398.0 12.9 %collective-permute-start.1 = (bf16[64,4096]{1,0:T(8,128)(2,1)S(1)}, bf16[64,4096]{1,0:T(8,128)(2,1)S(1)}, u32[]{:S(2)}, u32[]{:S(2)}) collective-permute-start(bf16[64,4096]{1,0:T(8,128)(2,1)S(1)} %get-tuple-element.1209), channel_id=1, source_target_pairs={{16,0},{32,16},{48,32},{64,48},{80,64},{96,80},{112,96},{0,112},{1... | collective-permute-start | bytes 1572872 | tf_op jit(solution)/shard_map/while/body/eval_jaxpr/ppermute | solution.py:121
  420.8 12.9 %collective-permute-start.1 = (bf16[64,4096]{1,0:T(8,128)(2,1)S(1)}, bf16[64,4096]{1,0:T(8,128)(2,1)S(1)}, u32[]{:S(2)}, u32[]{:S(2)}) collective-permute-start(bf16[64,4096]{1,0:T(8,128)(2,1)S(1)} %get-tuple-element.1209), channel_id=1, source_target_pairs={{16,0},{32,16},{48,32},{64,48},{80,64},{96,80},{112,96},{0,112},{1... | collective-permute-start | bytes 1572872 | tf_op jit(solution)/shard_map/while/body/eval_jaxpr/ppermute | solution.py:121
  443.7 12.9 %collective-permute-start.1 = (bf16[64,4096]{1,0:T(8,128)(2,1)S(1)}, bf16[64,4096]{1,0:T(8,128)(2,1)S(1)}, u32[]{:S(2)}, u32[]{:S(2)}) collective-permute-start(bf16[64,4096]{1,0:T(8,128)(2,1)S(1)} %get-tuple-element.1209), channel_id=1, source_target_pairs={{16,0},{32,16},{48,32},{64,48},{80,64},{96,80},{112,96},{0,112},{1... | collective-permute-start | bytes 1572872 | tf_op jit(solution)/shard_map/while/body/eval_jaxpr/ppermute | solution.py:121
  505.8 9.9 %conditional.7 = ((bf16[64,4096]{1,0:T(8,128)(2,1)S(1)}, bf16[64,4096]{1,0:T(8,128)(2,1)S(1)}, bf16[64,512]{1,0:T(8,128)(2,1)S(1)}, bf16[64,512]{1,0:T(8,128)(2,1)S(1)})) conditional(s32[]{:T(128)} %convert_element_type.188, () %tuple.160, (s32[]{:T(128)}, bf16[2,4,64,4096]{3,2,1,0:T(8,128)(2,1)}, s32[]{:T(128)}, bf16[64,4096]{1,0:T(8,128)(2,1)S(1)}, ...), branch_computations={%region_5.5_spmd, %region_6.6_spmd} | conditional | bytes 1179696 | solution.py:269
  525.5 9.9 %conditional.7 = ((bf16[64,4096]{1,0:T(8,128)(2,1)S(1)}, bf16[64,4096]{1,0:T(8,128)(2,1)S(1)}, bf16[64,512]{1,0:T(8,128)(2,1)S(1)}, bf16[64,512]{1,0:T(8,128)(2,1)S(1)})) conditional(s32[]{:T(128)} %convert_element_type.188, () %tuple.160, (s32[]{:T(128)}, bf16[2,4,64,4096]{3,2,1,0:T(8,128)(2,1)}, s32[]{:T(128)}, bf16[64,4096]{1,0:T(8,128)(2,1)S(1)}, ...), branch_computations={%region_5.5_spmd, %region_6.6_spmd} | conditional | bytes 1179696 | solution.py:269
  548.4 9.9 %conditional.7 = ((bf16[64,4096]{1,0:T(8,128)(2,1)S(1)}, bf16[64,4096]{1,0:T(8,128)(2,1)S(1)}, bf16[64,512]{1,0:T(8,128)(2,1)S(1)}, bf16[64,512]{1,0:T(8,128)(2,1)S(1)})) conditional(s32[]{:T(128)} %convert_element_type.188, () %tuple.160, (s32[]{:T(128)}, bf16[2,4,64,4096]{3,2,1,0:T(8,128)(2,1)}, s32[]{:T(128)}, bf16[64,4096]{1,0:T(8,128)(2,1)S(1)}, ...), branch_computations={%region_5.5_spmd, %region_6.6_spmd} | conditional | bytes 1179696 | solution.py:269
  571.3 9.9 %conditional.7 = ((bf16[64,4096]{1,0:T(8,128)(2,1)S(1)}, bf16[64,4096]{1,0:T(8,128)(2,1)S(1)}, bf16[64,512]{1,0:T(8,128)(2,1)S(1)}, bf16[64,512]{1,0:T(8,128)(2,1)S(1)})) conditional(s32[]{:T(128)} %convert_element_type.188, () %tuple.160, (s32[]{:T(128)}, bf16[2,4,64,4096]{3,2,1,0:T(8,128)(2,1)}, s32[]{:T(128)}, bf16[64,4096]{1,0:T(8,128)(2,1)S(1)}, ...), branch_computations={%region_5.5_spmd, %region_6.6_spmd} | conditional | bytes 1179696 | solution.py:269
  616.5 143.5 %while.65 = (s32[]{:T(128)}, bf16[64,4096]{1,0:T(8,128)(2,1)S(1)}, bf16[2,4,64,4096]{3,2,1,0:T(8,128)(2,1)}, bf16[2,4,64,4096]{3,2,1,0:T(8,128)(2,1)}, bf16[2,4,...) while((s32[]{:T(128)}, bf16[64,4096]{1,0:T(8,128)(2,1)S(1)}, ...), condition=%wide.region_11.12_spmd, body=%wide.region_8.11_spmd.sunk | while | flops 851987 | bytes 10226157 | solution.py:301
  619.9 12.9 %collective-permute-start.2 = (bf16[64,4096]{1,0:T(8,128)(2,1)S(1)}, bf16[64,4096]{1,0:T(8,128)(2,1)S(1)}, u32[]{:S(2)}, u32[]{:S(2)}) collective-permute-start(bf16[64,4096]{1,0:T(8,128)(2,1)S(1)} %get-tuple-element.1229), channel_id=1, source_target_pairs={{16,0},{32,16},{48,32},{64,48},{80,64},{96,80},{112,96},{0,112},{1... | collective-permute-start | bytes 1572872 | tf_op jit(solution)/shard_map/while/body/eval_jaxpr/ppermute | solution.py:121
  682.7 10.1 %conditional.8 = ((bf16[64,4096]{1,0:T(8,128)(2,1)S(1)}, bf16[64,4096]{1,0:T(8,128)(2,1)S(1)}, bf16[64,512]{1,0:T(8,128)(2,1)S(1)}, bf16[64,512]{1,0:T(8,128)(2,1)S(1)})) conditional(s32[]{:T(128)} %convert_element_type.189, () %tuple.165, (s32[]{:T(128)}, bf16[2,4,64,4096]{3,2,1,0:T(8,128)(2,1)}, s32[]{:T(128)}, bf16[64,4096]{1,0:T(8,128)(2,1)S(1)}, ...), branch_computations={%region_9.9_spmd, %region_10.10_spmd} | conditional | bytes 1179696 | solution.py:269
  702.7 9.9 %conditional.8 = ((bf16[64,4096]{1,0:T(8,128)(2,1)S(1)}, bf16[64,4096]{1,0:T(8,128)(2,1)S(1)}, bf16[64,512]{1,0:T(8,128)(2,1)S(1)}, bf16[64,512]{1,0:T(8,128)(2,1)S(1)})) conditional(s32[]{:T(128)} %convert_element_type.189, () %tuple.165, (s32[]{:T(128)}, bf16[2,4,64,4096]{3,2,1,0:T(8,128)(2,1)}, s32[]{:T(128)}, bf16[64,4096]{1,0:T(8,128)(2,1)S(1)}, ...), branch_computations={%region_9.9_spmd, %region_10.10_spmd} | conditional | bytes 1179696 | solution.py:269
  722.5 9.9 %conditional.8 = ((bf16[64,4096]{1,0:T(8,128)(2,1)S(1)}, bf16[64,4096]{1,0:T(8,128)(2,1)S(1)}, bf16[64,512]{1,0:T(8,128)(2,1)S(1)}, bf16[64,512]{1,0:T(8,128)(2,1)S(1)})) conditional(s32[]{:T(128)} %convert_element_type.189, () %tuple.165, (s32[]{:T(128)}, bf16[2,4,64,4096]{3,2,1,0:T(8,128)(2,1)}, s32[]{:T(128)}, bf16[64,4096]{1,0:T(8,128)(2,1)S(1)}, ...), branch_computations={%region_9.9_spmd, %region_10.10_spmd} | conditional | bytes 1179696 | solution.py:269
  743.4 9.9 %conditional.8 = ((bf16[64,4096]{1,0:T(8,128)(2,1)S(1)}, bf16[64,4096]{1,0:T(8,128)(2,1)S(1)}, bf16[64,512]{1,0:T(8,128)(2,1)S(1)}, bf16[64,512]{1,0:T(8,128)(2,1)S(1)})) conditional(s32[]{:T(128)} %convert_element_type.189, () %tuple.165, (s32[]{:T(128)}, bf16[2,4,64,4096]{3,2,1,0:T(8,128)(2,1)}, s32[]{:T(128)}, bf16[64,4096]{1,0:T(8,128)(2,1)S(1)}, ...), branch_computations={%region_9.9_spmd, %region_10.10_spmd} | conditional | bytes 1179696 | solution.py:269
  789.1 82.5 %reduce-scatter.3.cloned.1.call-done = bf16[512,512]{1,0:T(8,128)(2,1)} async-done(((bf16[8192,512]{1,0:T(8,128)(2,1)}), bf16[512,512]{1,0:T(8,128)(2,1)}) %reduce-scatter.3.cloned.1.call-update) | async-done | bytes 524304 | tf_op jit(solution)/shard_map/reduce_scatter | solution.py:185
  (422 shorter events, 605.5 us)
Async XLA Ops:
  7.2 779.5 %reduce-scatter.5.cloned.1.call-start = ((), (), s32[]{:S(2)}) async-start(), calls=%async_computation.3 | async-start | bytes 8912896 | tf_op jit(solution)/shard_map/reduce_scatter | solution.py:185
  80.5 9.8 %collective-permute-start = (bf16[64,4096]{1,0:T(8,128)(2,1)S(1)}, bf16[64,4096]{1,0:T(8,128)(2,1)S(1)}, u32[]{:S(2)}, u32[]{:S(2)}) collective-permute-start(bf16[64,4096]{1,0:T(8,128)(2,1)S(1)} %get-tuple-element.1399), channel_id=1, source_target_pairs={{112,0},{0,16},{16,32},{32,48},{48,64},{64,80},{80,96},{96,112},{1... | collective-permute-start | bytes 1572872 | tf_op jit(solution)/shard_map/while/body/eval_jaxpr/ppermute | solution.py:121
  98.9 9.8 %collective-permute-start = (bf16[64,4096]{1,0:T(8,128)(2,1)S(1)}, bf16[64,4096]{1,0:T(8,128)(2,1)S(1)}, u32[]{:S(2)}, u32[]{:S(2)}) collective-permute-start(bf16[64,4096]{1,0:T(8,128)(2,1)S(1)} %get-tuple-element.1399), channel_id=1, source_target_pairs={{112,0},{0,16},{16,32},{32,48},{48,64},{64,80},{80,96},{96,112},{1... | collective-permute-start | bytes 1572872 | tf_op jit(solution)/shard_map/while/body/eval_jaxpr/ppermute | solution.py:121
  117.2 9.8 %collective-permute-start = (bf16[64,4096]{1,0:T(8,128)(2,1)S(1)}, bf16[64,4096]{1,0:T(8,128)(2,1)S(1)}, u32[]{:S(2)}, u32[]{:S(2)}) collective-permute-start(bf16[64,4096]{1,0:T(8,128)(2,1)S(1)} %get-tuple-element.1399), channel_id=1, source_target_pairs={{112,0},{0,16},{16,32},{32,48},{48,64},{64,80},{80,96},{96,112},{1... | collective-permute-start | bytes 1572872 | tf_op jit(solution)/shard_map/while/body/eval_jaxpr/ppermute | solution.py:121
  135.6 9.8 %collective-permute-start = (bf16[64,4096]{1,0:T(8,128)(2,1)S(1)}, bf16[64,4096]{1,0:T(8,128)(2,1)S(1)}, u32[]{:S(2)}, u32[]{:S(2)}) collective-permute-start(bf16[64,4096]{1,0:T(8,128)(2,1)S(1)} %get-tuple-element.1399), channel_id=1, source_target_pairs={{112,0},{0,16},{16,32},{32,48},{48,64},{64,80},{80,96},{96,112},{1... | collective-permute-start | bytes 1572872 | tf_op jit(solution)/shard_map/while/body/eval_jaxpr/ppermute | solution.py:121
  148.6 9.8 %collective-permute-start = (bf16[64,4096]{1,0:T(8,128)(2,1)S(1)}, bf16[64,4096]{1,0:T(8,128)(2,1)S(1)}, u32[]{:S(2)}, u32[]{:S(2)}) collective-permute-start(bf16[64,4096]{1,0:T(8,128)(2,1)S(1)} %get-tuple-element.1399), channel_id=1, source_target_pairs={{112,0},{0,16},{16,32},{32,48},{48,64},{64,80},{80,96},{96,112},{1... | collective-permute-start | bytes 1572872 | tf_op jit(solution)/shard_map/while/body/eval_jaxpr/ppermute | solution.py:121
  161.7 9.8 %collective-permute-start = (bf16[64,4096]{1,0:T(8,128)(2,1)S(1)}, bf16[64,4096]{1,0:T(8,128)(2,1)S(1)}, u32[]{:S(2)}, u32[]{:S(2)}) collective-permute-start(bf16[64,4096]{1,0:T(8,128)(2,1)S(1)} %get-tuple-element.1399), channel_id=1, source_target_pairs={{112,0},{0,16},{16,32},{32,48},{48,64},{64,80},{80,96},{96,112},{1... | collective-permute-start | bytes 1572872 | tf_op jit(solution)/shard_map/while/body/eval_jaxpr/ppermute | solution.py:121
  174.7 9.8 %collective-permute-start = (bf16[64,4096]{1,0:T(8,128)(2,1)S(1)}, bf16[64,4096]{1,0:T(8,128)(2,1)S(1)}, u32[]{:S(2)}, u32[]{:S(2)}) collective-permute-start(bf16[64,4096]{1,0:T(8,128)(2,1)S(1)} %get-tuple-element.1399), channel_id=1, source_target_pairs={{112,0},{0,16},{16,32},{32,48},{48,64},{64,80},{80,96},{96,112},{1... | collective-permute-start | bytes 1572872 | tf_op jit(solution)/shard_map/while/body/eval_jaxpr/ppermute | solution.py:121
  187.7 11.5 %collective-permute-start = (bf16[64,4096]{1,0:T(8,128)(2,1)S(1)}, bf16[64,4096]{1,0:T(8,128)(2,1)S(1)}, u32[]{:S(2)}, u32[]{:S(2)}) collective-permute-start(bf16[64,4096]{1,0:T(8,128)(2,1)S(1)} %get-tuple-element.1399), channel_id=1, source_target_pairs={{112,0},{0,16},{16,32},{32,48},{48,64},{64,80},{80,96},{96,112},{1... | collective-permute-start | bytes 1572872 | tf_op jit(solution)/shard_map/while/body/eval_jaxpr/ppermute | solution.py:121
  207.7 9.8 %collective-permute-start = (bf16[64,4096]{1,0:T(8,128)(2,1)S(1)}, bf16[64,4096]{1,0:T(8,128)(2,1)S(1)}, u32[]{:S(2)}, u32[]{:S(2)}) collective-permute-start(bf16[64,4096]{1,0:T(8,128)(2,1)S(1)} %get-tuple-element.1399), channel_id=1, source_target_pairs={{112,0},{0,16},{16,32},{32,48},{48,64},{64,80},{80,96},{96,112},{1... | collective-permute-start | bytes 1572872 | tf_op jit(solution)/shard_map/while/body/eval_jaxpr/ppermute | solution.py:121
  226.1 9.8 %collective-permute-start = (bf16[64,4096]{1,0:T(8,128)(2,1)S(1)}, bf16[64,4096]{1,0:T(8,128)(2,1)S(1)}, u32[]{:S(2)}, u32[]{:S(2)}) collective-permute-start(bf16[64,4096]{1,0:T(8,128)(2,1)S(1)} %get-tuple-element.1399), channel_id=1, source_target_pairs={{112,0},{0,16},{16,32},{32,48},{48,64},{64,80},{80,96},{96,112},{1... | collective-permute-start | bytes 1572872 | tf_op jit(solution)/shard_map/while/body/eval_jaxpr/ppermute | solution.py:121
  244.5 9.8 %collective-permute-start = (bf16[64,4096]{1,0:T(8,128)(2,1)S(1)}, bf16[64,4096]{1,0:T(8,128)(2,1)S(1)}, u32[]{:S(2)}, u32[]{:S(2)}) collective-permute-start(bf16[64,4096]{1,0:T(8,128)(2,1)S(1)} %get-tuple-element.1399), channel_id=1, source_target_pairs={{112,0},{0,16},{16,32},{32,48},{48,64},{64,80},{80,96},{96,112},{1... | collective-permute-start | bytes 1572872 | tf_op jit(solution)/shard_map/while/body/eval_jaxpr/ppermute | solution.py:121
  262.8 9.8 %collective-permute-start = (bf16[64,4096]{1,0:T(8,128)(2,1)S(1)}, bf16[64,4096]{1,0:T(8,128)(2,1)S(1)}, u32[]{:S(2)}, u32[]{:S(2)}) collective-permute-start(bf16[64,4096]{1,0:T(8,128)(2,1)S(1)} %get-tuple-element.1399), channel_id=1, source_target_pairs={{112,0},{0,16},{16,32},{32,48},{48,64},{64,80},{80,96},{96,112},{1... | collective-permute-start | bytes 1572872 | tf_op jit(solution)/shard_map/while/body/eval_jaxpr/ppermute | solution.py:121
  275.9 9.8 %collective-permute-start = (bf16[64,4096]{1,0:T(8,128)(2,1)S(1)}, bf16[64,4096]{1,0:T(8,128)(2,1)S(1)}, u32[]{:S(2)}, u32[]{:S(2)}) collective-permute-start(bf16[64,4096]{1,0:T(8,128)(2,1)S(1)} %get-tuple-element.1399), channel_id=1, source_target_pairs={{112,0},{0,16},{16,32},{32,48},{48,64},{64,80},{80,96},{96,112},{1... | collective-permute-start | bytes 1572872 | tf_op jit(solution)/shard_map/while/body/eval_jaxpr/ppermute | solution.py:121
  288.9 9.8 %collective-permute-start = (bf16[64,4096]{1,0:T(8,128)(2,1)S(1)}, bf16[64,4096]{1,0:T(8,128)(2,1)S(1)}, u32[]{:S(2)}, u32[]{:S(2)}) collective-permute-start(bf16[64,4096]{1,0:T(8,128)(2,1)S(1)} %get-tuple-element.1399), channel_id=1, source_target_pairs={{112,0},{0,16},{16,32},{32,48},{48,64},{64,80},{80,96},{96,112},{1... | collective-permute-start | bytes 1572872 | tf_op jit(solution)/shard_map/while/body/eval_jaxpr/ppermute | solution.py:121
  314.9 11.5 %collective-permute-start = (bf16[64,4096]{1,0:T(8,128)(2,1)S(1)}, bf16[64,4096]{1,0:T(8,128)(2,1)S(1)}, u32[]{:S(2)}, u32[]{:S(2)}) collective-permute-start(bf16[64,4096]{1,0:T(8,128)(2,1)S(1)} %get-tuple-element.1399), channel_id=1, source_target_pairs={{112,0},{0,16},{16,32},{32,48},{48,64},{64,80},{80,96},{96,112},{1... | collective-permute-start | bytes 1572872 | tf_op jit(solution)/shard_map/while/body/eval_jaxpr/ppermute | solution.py:121
  329.6 11.5 %collective-permute-start = (bf16[64,4096]{1,0:T(8,128)(2,1)S(1)}, bf16[64,4096]{1,0:T(8,128)(2,1)S(1)}, u32[]{:S(2)}, u32[]{:S(2)}) collective-permute-start(bf16[64,4096]{1,0:T(8,128)(2,1)S(1)} %get-tuple-element.1399), channel_id=1, source_target_pairs={{112,0},{0,16},{16,32},{32,48},{48,64},{64,80},{80,96},{96,112},{1... | collective-permute-start | bytes 1572872 | tf_op jit(solution)/shard_map/while/body/eval_jaxpr/ppermute | solution.py:121
  344.3 11.5 %collective-permute-start = (bf16[64,4096]{1,0:T(8,128)(2,1)S(1)}, bf16[64,4096]{1,0:T(8,128)(2,1)S(1)}, u32[]{:S(2)}, u32[]{:S(2)}) collective-permute-start(bf16[64,4096]{1,0:T(8,128)(2,1)S(1)} %get-tuple-element.1399), channel_id=1, source_target_pairs={{112,0},{0,16},{16,32},{32,48},{48,64},{64,80},{80,96},{96,112},{1... | collective-permute-start | bytes 1572872 | tf_op jit(solution)/shard_map/while/body/eval_jaxpr/ppermute | solution.py:121
  359.0 11.5 %collective-permute-start = (bf16[64,4096]{1,0:T(8,128)(2,1)S(1)}, bf16[64,4096]{1,0:T(8,128)(2,1)S(1)}, u32[]{:S(2)}, u32[]{:S(2)}) collective-permute-start(bf16[64,4096]{1,0:T(8,128)(2,1)S(1)} %get-tuple-element.1399), channel_id=1, source_target_pairs={{112,0},{0,16},{16,32},{32,48},{48,64},{64,80},{80,96},{96,112},{1... | collective-permute-start | bytes 1572872 | tf_op jit(solution)/shard_map/while/body/eval_jaxpr/ppermute | solution.py:121
  379.0 15.7 %collective-permute-start.1 = (bf16[64,4096]{1,0:T(8,128)(2,1)S(1)}, bf16[64,4096]{1,0:T(8,128)(2,1)S(1)}, u32[]{:S(2)}, u32[]{:S(2)}) collective-permute-start(bf16[64,4096]{1,0:T(8,128)(2,1)S(1)} %get-tuple-element.1209), channel_id=1, source_target_pairs={{16,0},{32,16},{48,32},{64,48},{80,64},{96,80},{112,96},{0,112},{1... | collective-permute-start | bytes 1572872 | tf_op jit(solution)/shard_map/while/body/eval_jaxpr/ppermute | solution.py:121
  398.0 19.6 %collective-permute-start.1 = (bf16[64,4096]{1,0:T(8,128)(2,1)S(1)}, bf16[64,4096]{1,0:T(8,128)(2,1)S(1)}, u32[]{:S(2)}, u32[]{:S(2)}) collective-permute-start(bf16[64,4096]{1,0:T(8,128)(2,1)S(1)} %get-tuple-element.1209), channel_id=1, source_target_pairs={{16,0},{32,16},{48,32},{64,48},{80,64},{96,80},{112,96},{0,112},{1... | collective-permute-start | bytes 1572872 | tf_op jit(solution)/shard_map/while/body/eval_jaxpr/ppermute | solution.py:121
  420.8 19.6 %collective-permute-start.1 = (bf16[64,4096]{1,0:T(8,128)(2,1)S(1)}, bf16[64,4096]{1,0:T(8,128)(2,1)S(1)}, u32[]{:S(2)}, u32[]{:S(2)}) collective-permute-start(bf16[64,4096]{1,0:T(8,128)(2,1)S(1)} %get-tuple-element.1209), channel_id=1, source_target_pairs={{16,0},{32,16},{48,32},{64,48},{80,64},{96,80},{112,96},{0,112},{1... | collective-permute-start | bytes 1572872 | tf_op jit(solution)/shard_map/while/body/eval_jaxpr/ppermute | solution.py:121
  443.7 19.6 %collective-permute-start.1 = (bf16[64,4096]{1,0:T(8,128)(2,1)S(1)}, bf16[64,4096]{1,0:T(8,128)(2,1)S(1)}, u32[]{:S(2)}, u32[]{:S(2)}) collective-permute-start(bf16[64,4096]{1,0:T(8,128)(2,1)S(1)} %get-tuple-element.1209), channel_id=1, source_target_pairs={{16,0},{32,16},{48,32},{64,48},{80,64},{96,80},{112,96},{0,112},{1... | collective-permute-start | bytes 1572872 | tf_op jit(solution)/shard_map/while/body/eval_jaxpr/ppermute | solution.py:121
  466.6 9.8 %collective-permute-start.1 = (bf16[64,4096]{1,0:T(8,128)(2,1)S(1)}, bf16[64,4096]{1,0:T(8,128)(2,1)S(1)}, u32[]{:S(2)}, u32[]{:S(2)}) collective-permute-start(bf16[64,4096]{1,0:T(8,128)(2,1)S(1)} %get-tuple-element.1209), channel_id=1, source_target_pairs={{16,0},{32,16},{48,32},{64,48},{80,64},{96,80},{112,96},{0,112},{1... | collective-permute-start | bytes 1572872 | tf_op jit(solution)/shard_map/while/body/eval_jaxpr/ppermute | solution.py:121
  479.7 9.8 %collective-permute-start.1 = (bf16[64,4096]{1,0:T(8,128)(2,1)S(1)}, bf16[64,4096]{1,0:T(8,128)(2,1)S(1)}, u32[]{:S(2)}, u32[]{:S(2)}) collective-permute-start(bf16[64,4096]{1,0:T(8,128)(2,1)S(1)} %get-tuple-element.1209), channel_id=1, source_target_pairs={{16,0},{32,16},{48,32},{64,48},{80,64},{96,80},{112,96},{0,112},{1... | collective-permute-start | bytes 1572872 | tf_op jit(solution)/shard_map/while/body/eval_jaxpr/ppermute | solution.py:121
  492.8 9.8 %collective-permute-start.1 = (bf16[64,4096]{1,0:T(8,128)(2,1)S(1)}, bf16[64,4096]{1,0:T(8,128)(2,1)S(1)}, u32[]{:S(2)}, u32[]{:S(2)}) collective-permute-start(bf16[64,4096]{1,0:T(8,128)(2,1)S(1)} %get-tuple-element.1209), channel_id=1, source_target_pairs={{16,0},{32,16},{48,32},{64,48},{80,64},{96,80},{112,96},{0,112},{1... | collective-permute-start | bytes 1572872 | tf_op jit(solution)/shard_map/while/body/eval_jaxpr/ppermute | solution.py:121
  535.4 9.8 %collective-permute-start.1 = (bf16[64,4096]{1,0:T(8,128)(2,1)S(1)}, bf16[64,4096]{1,0:T(8,128)(2,1)S(1)}, u32[]{:S(2)}, u32[]{:S(2)}) collective-permute-start(bf16[64,4096]{1,0:T(8,128)(2,1)S(1)} %get-tuple-element.1209), channel_id=1, source_target_pairs={{16,0},{32,16},{48,32},{64,48},{80,64},{96,80},{112,96},{0,112},{1... | collective-permute-start | bytes 1572872 | tf_op jit(solution)/shard_map/while/body/eval_jaxpr/ppermute | solution.py:121
  616.5 255.1 %reduce-scatter.3.cloned.1.call-start = ((), (), s32[]{:S(2)}) async-start(), calls=%async_computation.2 | async-start | bytes 8912896 | tf_op jit(solution)/shard_map/reduce_scatter | solution.py:185
  619.9 19.6 %collective-permute-start.2 = (bf16[64,4096]{1,0:T(8,128)(2,1)S(1)}, bf16[64,4096]{1,0:T(8,128)(2,1)S(1)}, u32[]{:S(2)}, u32[]{:S(2)}) collective-permute-start(bf16[64,4096]{1,0:T(8,128)(2,1)S(1)} %get-tuple-element.1229), channel_id=1, source_target_pairs={{16,0},{32,16},{48,32},{64,48},{80,64},{96,80},{112,96},{0,112},{1... | collective-permute-start | bytes 1572872 | tf_op jit(solution)/shard_map/while/body/eval_jaxpr/ppermute | solution.py:121
  642.7 10.2 %collective-permute-start.2 = (bf16[64,4096]{1,0:T(8,128)(2,1)S(1)}, bf16[64,4096]{1,0:T(8,128)(2,1)S(1)}, u32[]{:S(2)}, u32[]{:S(2)}) collective-permute-start(bf16[64,4096]{1,0:T(8,128)(2,1)S(1)} %get-tuple-element.1229), channel_id=1, source_target_pairs={{16,0},{32,16},{48,32},{64,48},{80,64},{96,80},{112,96},{0,112},{1... | collective-permute-start | bytes 1572872 | tf_op jit(solution)/shard_map/while/body/eval_jaxpr/ppermute | solution.py:121
  656.2 9.8 %collective-permute-start.2 = (bf16[64,4096]{1,0:T(8,128)(2,1)S(1)}, bf16[64,4096]{1,0:T(8,128)(2,1)S(1)}, u32[]{:S(2)}, u32[]{:S(2)}) collective-permute-start(bf16[64,4096]{1,0:T(8,128)(2,1)S(1)} %get-tuple-element.1229), channel_id=1, source_target_pairs={{16,0},{32,16},{48,32},{64,48},{80,64},{96,80},{112,96},{0,112},{1... | collective-permute-start | bytes 1572872 | tf_op jit(solution)/shard_map/while/body/eval_jaxpr/ppermute | solution.py:121
  669.4 10.2 %collective-permute-start.2 = (bf16[64,4096]{1,0:T(8,128)(2,1)S(1)}, bf16[64,4096]{1,0:T(8,128)(2,1)S(1)}, u32[]{:S(2)}, u32[]{:S(2)}) collective-permute-start(bf16[64,4096]{1,0:T(8,128)(2,1)S(1)} %get-tuple-element.1229), channel_id=1, source_target_pairs={{16,0},{32,16},{48,32},{64,48},{80,64},{96,80},{112,96},{0,112},{1... | collective-permute-start | bytes 1572872 | tf_op jit(solution)/shard_map/while/body/eval_jaxpr/ppermute | solution.py:121
  (14 other events, 95.2 us)
Sparse Core Ops, SparseCore 0:
  616.6 88.7 reduce-scatter.4
  782.3 89.1 reduce-scatter.2

commit v5 on v3

--- a/solution.py
+++ b/solution.py
@@ -8,17 +8,23 @@
 BLK = 64
 SPLIT = 1
 TK = 128
+TKB = 256
 
 
 EPS = 1e-05
 
 
-def _fwd_kernel(lap_ref, x_ref, ea_ref, eb_ref, o_ref, n_scr, acc_scr):
+VMEM_LIMIT = 48 * 1024 * 1024
+
+
+def _fwd_kernel(sc_ref, mi_ref, inc_ref, ea_ref, eb_ref, saved_in, o_ref, saved_ref, n_scr, acc_scr):
     k = pl.program_id(0)
 
     @pl.when(k == 0)
     def _():
-        wide = x_ref[...].astype(jnp.float32)
+        values = jnp.where(sc_ref[2] == 1, mi_ref[...], inc_ref[...])
+        saved_ref[...] = values
+        wide = values.astype(jnp.float32)
         inv = lax.rsqrt(jnp.mean(wide * wide, axis=-1, keepdims=True) + EPS)
         n_scr[...] = (wide * inv).astype(jnp.bfloat16)
         acc_scr[...] = wide
@@ -32,8 +38,8 @@
         o_ref[...] = acc_scr[...].astype(o_ref.dtype)
 
 
-def fwd_call(lap, x, ea_all, eb_all):
-    rows, width = x.shape
+def fwd_call(sc, micro_inputs, incoming, ea_all, eb_all, saved):
+    rows, width = incoming.shape
     inner = ea_all.shape[-1]
     return pl.pallas_call(
         _fwd_kernel,
@@ -41,23 +47,34 @@
             num_scalar_prefetch=1,
             grid=(inner // TK,),
             in_specs=[
-                pl.BlockSpec((rows, width), lambda k, lp: (0, 0)),
-                pl.BlockSpec((None, width, TK), lambda k, lp: (lp[0], 0, k)),
-                pl.BlockSpec((None, TK, width), lambda k, lp: (lp[0], k, 0)),
+                pl.BlockSpec((None, rows, width), lambda k, s: (s[1], 0, 0)),
+                pl.BlockSpec((rows, width), lambda k, s: (0, 0)),
+                pl.BlockSpec((None, width, TK), lambda k, s: (s[0], 0, k)),
+                pl.BlockSpec((None, TK, width), lambda k, s: (s[0], k, 0)),
+                pl.BlockSpec(memory_space=pl.ANY),
             ],
-            out_specs=pl.BlockSpec((rows, width), lambda k, lp: (0, 0)),
+            out_specs=[
+                pl.BlockSpec((rows, width), lambda k, s: (0, 0)),
+                pl.BlockSpec((None, None, rows, width), lambda k, s: (s[0], s[1], 0, 0)),
+            ],
             scratch_shapes=[pltpu.VMEM((rows, width), jnp.bfloat16), pltpu.VMEM((rows, width), jnp.float32)],
         ),
-        out_shape=jax.ShapeDtypeStruct((rows, width), jnp.bfloat16),
-        compiler_params=pltpu.CompilerParams(dimension_semantics=("arbitrary",), vmem_limit_bytes=48 * 1024 * 1024)
-    )(jnp.reshape(lap, (1,)).astype(jnp.int32), x, ea_all, eb_all)
-
-
-def _bwd_kernel(lap_ref, x_ref, g_ref, ea_ref, eb_ref, down_ref, normed_ref, hidden_ref, bp_ref, gn_scr):
+        out_shape=[
+            jax.ShapeDtypeStruct((rows, width), jnp.bfloat16),
+            jax.ShapeDtypeStruct(saved.shape, saved.dtype),
+        ],
+        input_output_aliases={5: 1},
+        compiler_params=pltpu.CompilerParams(dimension_semantics=("arbitrary",), vmem_limit_bytes=VMEM_LIMIT),
+    )(sc, micro_inputs, incoming, ea_all, eb_all, saved)
+
+
+def _bwd_kernel(sc_ref, x_ref, cot_ref, inc_ref, ea_ref, eb_ref, n_in, u_in, h_in, b_in,
+                down_ref, normed_ref, up_ref, hidden_ref, bp_ref, gn_scr):
     k = pl.program_id(0)
 
     @pl.when(k == 0)
     def _():
+        up_ref[...] = jnp.where(sc_ref[2] == 1, cot_ref[...], inc_ref[...])
         wide = x_ref[...].astype(jnp.float32)
         inv = lax.rsqrt(jnp.mean(wide * wide, axis=-1, keepdims=True) + EPS)
         normed_ref[...] = (wide * inv).astype(jnp.bfloat16)
@@ -67,7 +84,7 @@
     p = jnp.dot(normed_ref[...], ea, preferred_element_type=jnp.float32)
     sg = jax.nn.sigmoid(p)
     hidden_ref[...] = (p * sg).astype(jnp.bfloat16)
-    gh = lax.dot_general(g_ref[...], eb_ref[...], (((1,), (1,)), ((), ())), preferred_element_type=jnp.float32)
+    gh = lax.dot_general(up_ref[...], eb_ref[...], (((1,), (1,)), ((), ())), preferred_element_type=jnp.float32)
     gp = (gh * sg * (1.0 + p * (1.0 - sg))).astype(jnp.bfloat16)
     bp_ref[...] = gp
     gn_scr[...] += lax.dot_general(gp, ea, (((1,), (1,)), ((), ())), preferred_element_type=jnp.float32)
@@ -79,36 +96,38 @@
         scaled = wide * inv
         gn = gn_scr[...]
         center = jnp.mean(gn * scaled, axis=-1, keepdims=True)
-        down_ref[...] = (g_ref[...].astype(jnp.float32) + inv * (gn - scaled * center)).astype(down_ref.dtype)
-
-
-def bwd_call(lap, x, g, ea_all, eb_all):
-    rows, width = x.shape
+        down_ref[...] = (up_ref[...].astype(jnp.float32) + inv * (gn - scaled * center)).astype(down_ref.dtype)
+
+
+def bwd_call(sc, saved, cotangent, incoming, ea_all, eb_all, stores):
+    rows, width = incoming.shape
     inner = ea_all.shape[-1]
-    full = pl.BlockSpec((rows, width), lambda k, lp: (0, 0))
-    part = pl.BlockSpec((rows, TK), lambda k, lp: (0, k))
-    return pl.pallas_call(
+    here = lambda k, s: (s[0], s[1], 0, 0)
+    wide_slot = pl.BlockSpec((None, None, rows, width), here)
+    part_slot = pl.BlockSpec((None, None, rows, TKB), lambda k, s: (s[0], s[1], 0, k))
+    anywhere = pl.BlockSpec(memory_space=pl.ANY)
+    outs = pl.pallas_call(
         _bwd_kernel,
         grid_spec=pltpu.PrefetchScalarGridSpec(
             num_scalar_prefetch=1,
-            grid=(inner // TK,),
+            grid=(inner // TKB,),
             in_specs=[
-                full,
-                full,
-                pl.BlockSpec((None, width, TK), lambda k, lp: (lp[0], 0, k)),
-                pl.BlockSpec((None, TK, width), lambda k, lp: (lp[0], k, 0)),
+                wide_slot,
+                pl.BlockSpec((None, rows, width), lambda k, s: (s[1], 0, 0)),
+                pl.BlockSpec((rows, width), lambda k, s: (0, 0)),
+                pl.BlockSpec((None, width, TKB), lambda k, s: (s[0], 0, k)),
+                pl.BlockSpec((None, TKB, width), lambda k, s: (s[0], k, 0)),
+                anywhere, anywhere, anywhere, anywhere,
             ],
-            out_specs=[full, full, part, part],
+            out_specs=[pl.BlockSpec((rows, width), lambda k, s: (0, 0)), wide_slot, wide_slot, part_slot, part_slot],
             scratch_shapes=[pltpu.VMEM((rows, width), jnp.float32)],
         ),
-        out_shape=[
-            jax.ShapeDtypeStruct((rows, width), jnp.bfloat16),
-            jax.ShapeDtypeStruct((rows, width), jnp.bfloat16),
-            jax.ShapeDtypeStruct((rows, inner), jnp.bfloat16),
-            jax.ShapeDtypeStruct((rows, inner), jnp.bfloat16),
-        ],
-        compiler_params=pltpu.CompilerParams(dimension_semantics=("arbitrary",), vmem_limit_bytes=48 * 1024 * 1024)
-    )(jnp.reshape(lap, (1,)).astype(jnp.int32), x, g, ea_all, eb_all)
+        out_shape=[jax.ShapeDtypeStruct((rows, width), jnp.bfloat16)]
+        + [jax.ShapeDtypeStruct(b.shape, b.dtype) for b in stores],
+        input_output_aliases={6: 1, 7: 2, 8: 3, 9: 4},
+        compiler_params=pltpu.CompilerParams(dimension_semantics=("arbitrary",), vmem_limit_bytes=VMEM_LIMIT),
+    )(sc, saved, cotangent, incoming, ea_all, eb_all, *stores)
+    return outs[0], tuple(outs[1:])
 
 
 def shortened(shard):
@@ -219,11 +238,16 @@
         second_on = (second_micro >= 0) & (second_micro < batches)
         lap_now = second_on.astype(jnp.int32)
         micro = jnp.clip(jnp.where(second_on, second_micro, first_micro), 0, batches - 1)
-        values = jnp.where((here == 0) & (lap_now == 0), micro_inputs[micro], incoming)
-        branch = first_on.astype(jnp.int32) + 2 * second_on.astype(jnp.int32)
-        result = fwd_call(lap_now, values, eff_a, eff_b)
-        keep = jnp.where(first_on | second_on, values, saved[lap_now, micro])
-        saved = place_item(saved, lap_now, micro, keep)
+        use_inputs = ((here == 0) & (lap_now == 0)).astype(jnp.int32)
+        table = jnp.stack([lap_now, micro, use_inputs, jnp.int32(0)]).astype(jnp.int32)
+
+        def active(inc, kept):
+            return tuple(fwd_call(table, micro_inputs, inc, eff_a, eff_b, kept))
+
+        def idle(inc, kept):
+            return (jnp.zeros_like(inc), kept)
+
+        result, saved = lax.cond(first_on | second_on, active, idle, incoming, saved)
         incoming = jax.tree.map(
             lambda part, own: part.astype(own.dtype),
             shifted(shortened(result), "section", 1),
@@ -256,20 +280,16 @@
         second_on = (second_micro >= 0) & (second_micro < batches)
         lap_now = jnp.where(first_on, 0, 1).astype(jnp.int32)
         micro = jnp.clip(jnp.where(first_on, first_micro, second_micro), 0, batches - 1)
-        upstream = jnp.where(
-            (here == sections - 1) & (lap_now == 1), out_cotangent[micro], incoming
-        )
-        values = saved_rows[lap_now, micro]
-        branch = first_on.astype(jnp.int32) + 2 * second_on.astype(jnp.int32)
-        downstream, normed, hidden, back_pre = bwd_call(lap_now, values, upstream, eff_a, eff_b)
-        active = first_on | second_on
-        fresh = (normed, upstream, hidden, back_pre)
-        stores = tuple(
-            (
-                place_item(buffer, lap_now, micro, jnp.where(active, item, buffer[lap_now, micro]))
-                for buffer, item in zip(stores, fresh)
-            )
-        )
+        use_cotangent = ((here == sections - 1) & (lap_now == 1)).astype(jnp.int32)
+        table = jnp.stack([lap_now, micro, use_cotangent, jnp.int32(0)]).astype(jnp.int32)
+
+        def active(inc, kept):
+            return bwd_call(table, saved_rows, out_cotangent, inc, eff_a, eff_b, kept)
+
+        def idle(inc, kept):
+            return (jnp.zeros_like(inc), kept)
+
+        downstream, stores = lax.cond(first_on | second_on, active, idle, incoming, stores)
         incoming = jax.tree.map(
             lambda part, own: part.astype(own.dtype),
             shifted(shortened(downstream), "section", -1),

time: 1020 us -> 792 us (0.78)
  Pallas kernels: 269 us -> 132 us
  other arithmetic: 130 us -> 34.8 us
  local copies, waits for them, and re-layouts: 170 us -> 95.7 us
  waiting for transfers between devices: 356 us -> 415 us
  starting transfers between devices: 57.3 us -> 86.2 us
    dynamic_update_slice x76 -> x0, other arithmetic: 97.8 us -> none  [place_item(): lax.dynamic_update_slice(buffer, value[None, None], (lap_now, micro, anch...]
    pallas_call x19 -> x8, Pallas kernels: 167 us -> 78.1 us  [bwd_call(): pl.pallas_call(_bwd_kernel, grid_spec=pltpu.PrefetchScalarGridSpec(num_sc...]
    dynamic_slice x95 -> x0, local copies, waits for them, and re-layouts: 61.7 us -> none  [the longest x76 41.3 us: backward_step(): buffer[lap_now, micro]]
    ppermute x38, waiting for transfers between devices: 274 us -> 333 us  [shifted(): return lax.ppermute(block, axis, route)]
    pallas_call x19 -> x8, Pallas kernels: 102 us -> 54 us  [fwd_call(): pl.pallas_call(_fwd_kernel, grid_spec=pltpu.PrefetchScalarGridSpec(num_sc...]
    ppermute x38, starting transfers between devices: 57.2 us -> 86.1 us  [shifted(): return lax.ppermute(block, axis, route)]
    squeeze x19 -> x0, local copies, waits for them, and re-layouts: 20.5 us -> none  [backward_step(): values = saved_rows[lap_now, micro]]
    another operation x5 -> x29, local copies, waits for them, and re-layouts: 7.58 us -> 18 us
  transfers between devices with their start and end apart: 40 -> 40, of which waited for: 39 -> 39; matrix products, arithmetic and copies ran while one was open for 10% -> 4% of each run, Pallas kernels for 7% -> 5%
where the time goes in v5:
time: 792 us; the launch traced here: 791 us
  waiting for transfers between devices  415 us (52%)
  Pallas kernels  132 us (17%)
  local copies, waits for them, and re-layouts  95.7 us (12%)
  starting transfers between devices  86.2 us (11%)
  other arithmetic  34.8 us (4%)
  between operations  14.4 us (2%)
  matrix products  11.7 us (1%)
    ppermute x38, waiting for transfers between devices, shifted(): return lax.ppermute(block, axis, route)  333 us
    ppermute x38, starting transfers between devices, shifted(): return lax.ppermute(block, axis, route)  86.1 us
    reduce_scatter x2, waiting for transfers between devices, settle(): lax.psum_scatter(joined, 'dp', scatter_dimension=0, tiled=True)  81.7 us
    pallas_call x8, Pallas kernels, bwd_call(): pl.pallas_call(_bwd_kernel, grid_spec=pltpu.PrefetchScalarGridSpec(num_sc...  78.1 us
    pallas_call x8, Pallas kernels, fwd_call(): pl.pallas_call(_fwd_kernel, grid_spec=pltpu.PrefetchScalarGridSpec(num_sc...  54 us
    unnamed x25, local copies, waits for them, and re-layouts  28.9 us
    while x2, local copies, waits for them, and re-layouts, on_device(): lax.fori_loop(0, batches + 2 * sections - 1, forward_step, (start_rows, s...  23.4 us
    another operation x29, local copies, waits for them, and re-layouts  18 us
  transfers between devices with their start and end apart: 40, of which 39 were waited for; matrix products, arithmetic and copies ran while one was open for 4% of the time, Pallas kernels for 5%

profile of v5, /device:TPU:0, one launch (start us, length us, event | category | flops | bytes accessed | tf_op | source)
XLA Modules:
  0.0 790.7 jit_solution(17473674002617271215)
XLA Ops:
  7.2 11.4 %copy.43 = bf16[2,1,4096,512]{2,3,0,1:T(8,128)(2,1)} copy(bf16[2,1,4096,512]{3,2,1,0:T(8,128)(2,1)} %param.20) | data formatting | bytes 16777216 | tf_op args[2]
  26.3 12.0 %copy.46 = bf16[2,4096,512]{2,1,0:T(8,128)(2,1)} copy(bf16[2,4096,512]{1,2,0:T(8,128)(2,1)} %bitcast_multiply_fusion.1) | data formatting | bytes 16777216 | tf_op jit(solution)/shard_map/while | solution.py:260
  38.3 12.0 %copy.44 = bf16[2,1,512,4096]{2,3,0,1:T(8,128)(2,1)} copy(bf16[2,1,512,4096]{3,2,1,0:T(8,128)(2,1)} %param.21) | data formatting | bytes 16777216 | tf_op args[3]
  58.1 11.4 %copy.47 = bf16[2,512,4096]{2,1,0:T(8,128)(2,1)} copy(bf16[2,512,4096]{1,2,0:T(8,128)(2,1)} %bitcast_multiply_fusion) | data formatting | bytes 16777216 | tf_op jit(solution)/shard_map/while | solution.py:260
  72.0 257.7 %while.66 = (s32[]{:T(128)}, bf16[64,4096]{1,0:T(8,128)(2,1)S(1)}, bf16[2,4,64,4096]{3,2,1,0:T(8,128)(2,1)}, s32[]{:T(128)}, pred[]{:T(512)}, /*index=5*/bf16[4,...) while((s32[]{:T(128)}, bf16[64,4096]{1,0:T(8,128)(2,1)S(1)}, ...), condition=%wide.region_3.4_spmd, body=%wide.region_0.3_spmd.sunk | while | flops 31 | bytes 2621852 | solution.py:260
  78.8 9.8 %collective-permute-done = bf16[64,4096]{1,0:T(8,128)(2,1)S(1)} collective-permute-done((bf16[64,4096]{1,0:T(8,128)(2,1)S(1)}, bf16[64,4096]{1,0:T(8,128)(2,1)S(1)}, u32[]{:S(2)}, u32[]{:S(2)}) %collective-permute-start) | collective-permute-done | bytes 524320 | tf_op jit(solution)/shard_map/while/body/eval_jaxpr/ppermute | solution.py:140
  95.4 9.8 %collective-permute-done = bf16[64,4096]{1,0:T(8,128)(2,1)S(1)} collective-permute-done((bf16[64,4096]{1,0:T(8,128)(2,1)S(1)}, bf16[64,4096]{1,0:T(8,128)(2,1)S(1)}, u32[]{:S(2)}, u32[]{:S(2)}) %collective-permute-start) | collective-permute-done | bytes 524320 | tf_op jit(solution)/shard_map/while/body/eval_jaxpr/ppermute | solution.py:140
  112.1 9.8 %collective-permute-done = bf16[64,4096]{1,0:T(8,128)(2,1)S(1)} collective-permute-done((bf16[64,4096]{1,0:T(8,128)(2,1)S(1)}, bf16[64,4096]{1,0:T(8,128)(2,1)S(1)}, u32[]{:S(2)}, u32[]{:S(2)}) %collective-permute-start) | collective-permute-done | bytes 524320 | tf_op jit(solution)/shard_map/while/body/eval_jaxpr/ppermute | solution.py:140
  128.7 9.8 %collective-permute-done = bf16[64,4096]{1,0:T(8,128)(2,1)S(1)} collective-permute-done((bf16[64,4096]{1,0:T(8,128)(2,1)S(1)}, bf16[64,4096]{1,0:T(8,128)(2,1)S(1)}, u32[]{:S(2)}, u32[]{:S(2)}) %collective-permute-start) | collective-permute-done | bytes 524320 | tf_op jit(solution)/shard_map/while/body/eval_jaxpr/ppermute | solution.py:140
  138.7 9.8 %collective-permute-done = bf16[64,4096]{1,0:T(8,128)(2,1)S(1)} collective-permute-done((bf16[64,4096]{1,0:T(8,128)(2,1)S(1)}, bf16[64,4096]{1,0:T(8,128)(2,1)S(1)}, u32[]{:S(2)}, u32[]{:S(2)}) %collective-permute-start) | collective-permute-done | bytes 524320 | tf_op jit(solution)/shard_map/while/body/eval_jaxpr/ppermute | solution.py:140
  148.7 9.8 %collective-permute-done = bf16[64,4096]{1,0:T(8,128)(2,1)S(1)} collective-permute-done((bf16[64,4096]{1,0:T(8,128)(2,1)S(1)}, bf16[64,4096]{1,0:T(8,128)(2,1)S(1)}, u32[]{:S(2)}, u32[]{:S(2)}) %collective-permute-start) | collective-permute-done | bytes 524320 | tf_op jit(solution)/shard_map/while/body/eval_jaxpr/ppermute | solution.py:140
  168.6 12.8 %collective-permute-done = bf16[64,4096]{1,0:T(8,128)(2,1)S(1)} collective-permute-done((bf16[64,4096]{1,0:T(8,128)(2,1)S(1)}, bf16[64,4096]{1,0:T(8,128)(2,1)S(1)}, u32[]{:S(2)}, u32[]{:S(2)}) %collective-permute-start) | collective-permute-done | bytes 524320 | tf_op jit(solution)/shard_map/while/body/eval_jaxpr/ppermute | solution.py:140
  188.2 9.8 %collective-permute-done = bf16[64,4096]{1,0:T(8,128)(2,1)S(1)} collective-permute-done((bf16[64,4096]{1,0:T(8,128)(2,1)S(1)}, bf16[64,4096]{1,0:T(8,128)(2,1)S(1)}, u32[]{:S(2)}, u32[]{:S(2)}) %collective-permute-start) | collective-permute-done | bytes 524320 | tf_op jit(solution)/shard_map/while/body/eval_jaxpr/ppermute | solution.py:140
  204.8 9.8 %collective-permute-done = bf16[64,4096]{1,0:T(8,128)(2,1)S(1)} collective-permute-done((bf16[64,4096]{1,0:T(8,128)(2,1)S(1)}, bf16[64,4096]{1,0:T(8,128)(2,1)S(1)}, u32[]{:S(2)}, u32[]{:S(2)}) %collective-permute-start) | collective-permute-done | bytes 524320 | tf_op jit(solution)/shard_map/while/body/eval_jaxpr/ppermute | solution.py:140
  221.5 9.8 %collective-permute-done = bf16[64,4096]{1,0:T(8,128)(2,1)S(1)} collective-permute-done((bf16[64,4096]{1,0:T(8,128)(2,1)S(1)}, bf16[64,4096]{1,0:T(8,128)(2,1)S(1)}, u32[]{:S(2)}, u32[]{:S(2)}) %collective-permute-start) | collective-permute-done | bytes 524320 | tf_op jit(solution)/shard_map/while/body/eval_jaxpr/ppermute | solution.py:140
  238.1 9.8 %collective-permute-done = bf16[64,4096]{1,0:T(8,128)(2,1)S(1)} collective-permute-done((bf16[64,4096]{1,0:T(8,128)(2,1)S(1)}, bf16[64,4096]{1,0:T(8,128)(2,1)S(1)}, u32[]{:S(2)}, u32[]{:S(2)}) %collective-permute-start) | collective-permute-done | bytes 524320 | tf_op jit(solution)/shard_map/while/body/eval_jaxpr/ppermute | solution.py:140
  248.1 9.8 %collective-permute-done = bf16[64,4096]{1,0:T(8,128)(2,1)S(1)} collective-permute-done((bf16[64,4096]{1,0:T(8,128)(2,1)S(1)}, bf16[64,4096]{1,0:T(8,128)(2,1)S(1)}, u32[]{:S(2)}, u32[]{:S(2)}) %collective-permute-start) | collective-permute-done | bytes 524320 | tf_op jit(solution)/shard_map/while/body/eval_jaxpr/ppermute | solution.py:140
  258.1 9.8 %collective-permute-done = bf16[64,4096]{1,0:T(8,128)(2,1)S(1)} collective-permute-done((bf16[64,4096]{1,0:T(8,128)(2,1)S(1)}, bf16[64,4096]{1,0:T(8,128)(2,1)S(1)}, u32[]{:S(2)}, u32[]{:S(2)}) %collective-permute-start) | collective-permute-done | bytes 524320 | tf_op jit(solution)/shard_map/while/body/eval_jaxpr/ppermute | solution.py:140
  278.0 12.8 %collective-permute-done = bf16[64,4096]{1,0:T(8,128)(2,1)S(1)} collective-permute-done((bf16[64,4096]{1,0:T(8,128)(2,1)S(1)}, bf16[64,4096]{1,0:T(8,128)(2,1)S(1)}, u32[]{:S(2)}, u32[]{:S(2)}) %collective-permute-start) | collective-permute-done | bytes 524320 | tf_op jit(solution)/shard_map/while/body/eval_jaxpr/ppermute | solution.py:140
  290.9 12.8 %collective-permute-done = bf16[64,4096]{1,0:T(8,128)(2,1)S(1)} collective-permute-done((bf16[64,4096]{1,0:T(8,128)(2,1)S(1)}, bf16[64,4096]{1,0:T(8,128)(2,1)S(1)}, u32[]{:S(2)}, u32[]{:S(2)}) %collective-permute-start) | collective-permute-done | bytes 524320 | tf_op jit(solution)/shard_map/while/body/eval_jaxpr/ppermute | solution.py:140
  303.9 12.8 %collective-permute-done = bf16[64,4096]{1,0:T(8,128)(2,1)S(1)} collective-permute-done((bf16[64,4096]{1,0:T(8,128)(2,1)S(1)}, bf16[64,4096]{1,0:T(8,128)(2,1)S(1)}, u32[]{:S(2)}, u32[]{:S(2)}) %collective-permute-start) | collective-permute-done | bytes 524320 | tf_op jit(solution)/shard_map/while/body/eval_jaxpr/ppermute | solution.py:140
  316.9 12.8 %collective-permute-done = bf16[64,4096]{1,0:T(8,128)(2,1)S(1)} collective-permute-done((bf16[64,4096]{1,0:T(8,128)(2,1)S(1)}, bf16[64,4096]{1,0:T(8,128)(2,1)S(1)}, u32[]{:S(2)}, u32[]{:S(2)}) %collective-permute-start) | collective-permute-done | bytes 524320 | tf_op jit(solution)/shard_map/while/body/eval_jaxpr/ppermute | solution.py:140
  335.7 185.6 %while.67 = (s32[]{:T(128)}, bf16[64,4096]{1,0:T(8,128)(2,1)}, bf16[2,4,64,4096]{3,2,1,0:T(8,128)(2,1)}, bf16[2,4,64,4096]{3,2,1,0:T(8,128)(2,1)}, bf16[2,4,64,5...) while((s32[]{:T(128)}, bf16[64,4096]{1,0:T(8,128)(2,1)}, ...), condition=%wide.region_7.8_spmd, body=%wide.region_4.7_spmd.sunk | while | flops 31 | bytes 2621980 | solution.py:308
  352.7 12.0 %collective-permute-start.1 = (bf16[64,4096]{1,0:T(8,128)(2,1)}, bf16[64,4096]{1,0:T(8,128)(2,1)}, u32[]{:S(2)}, u32[]{:S(2)}) collective-permute-start(bf16[64,4096]{1,0:T(8,128)(2,1)} %get-tuple-element.1236), channel_id=1, source_target_pairs={{16,0},{32,16},{48,32},{64,48},{80,64},{96,80},{112,96},{0,112},{1... | collective-permute-start | bytes 1572872 | tf_op jit(solution)/shard_map/while/body/eval_jaxpr/ppermute | solution.py:140
  372.6 12.0 %collective-permute-start.1 = (bf16[64,4096]{1,0:T(8,128)(2,1)}, bf16[64,4096]{1,0:T(8,128)(2,1)}, u32[]{:S(2)}, u32[]{:S(2)}) collective-permute-start(bf16[64,4096]{1,0:T(8,128)(2,1)} %get-tuple-element.1236), channel_id=1, source_target_pairs={{16,0},{32,16},{48,32},{64,48},{80,64},{96,80},{112,96},{0,112},{1... | collective-permute-start | bytes 1572872 | tf_op jit(solution)/shard_map/while/body/eval_jaxpr/ppermute | solution.py:140
  392.6 12.0 %collective-permute-start.1 = (bf16[64,4096]{1,0:T(8,128)(2,1)}, bf16[64,4096]{1,0:T(8,128)(2,1)}, u32[]{:S(2)}, u32[]{:S(2)}) collective-permute-start(bf16[64,4096]{1,0:T(8,128)(2,1)} %get-tuple-element.1236), channel_id=1, source_target_pairs={{16,0},{32,16},{48,32},{64,48},{80,64},{96,80},{112,96},{0,112},{1... | collective-permute-start | bytes 1572872 | tf_op jit(solution)/shard_map/while/body/eval_jaxpr/ppermute | solution.py:140
  546.9 121.4 %while.68 = (s32[]{:T(128)}, bf16[64,4096]{1,0:T(8,128)(2,1)}, bf16[2,4,64,4096]{3,2,1,0:T(8,128)(2,1)}, bf16[2,4,64,4096]{3,2,1,0:T(8,128)(2,1)}, bf16[2,4,64,5...) while((s32[]{:T(128)}, bf16[64,4096]{1,0:T(8,128)(2,1)}, ...), condition=%wide.region_11.12_spmd, body=%wide.region_8.11_spmd.sunk | while | flops 32 | bytes 2622000 | solution.py:310
  547.8 12.0 %collective-permute-start.2 = (bf16[64,4096]{1,0:T(8,128)(2,1)}, bf16[64,4096]{1,0:T(8,128)(2,1)}, u32[]{:S(2)}, u32[]{:S(2)}) collective-permute-start(bf16[64,4096]{1,0:T(8,128)(2,1)} %get-tuple-element.1253), channel_id=1, source_target_pairs={{16,0},{32,16},{48,32},{64,48},{80,64},{96,80},{112,96},{0,112},{1... | collective-permute-start | bytes 1572872 | tf_op jit(solution)/shard_map/while/body/eval_jaxpr/ppermute | solution.py:140
  617.5 10.1 %conditional.8 = ((bf16[64,4096]{1,0:T(8,128)(2,1)}, bf16[2,4,64,4096]{3,2,1,0:T(8,128)(2,1)}, bf16[2,4,64,4096]{3,2,1,0:T(8,128)(2,1)}, bf16[2,4,64,512]{3,2,1,0:T(8,128)(2,1)S(1)}, bf16[2,4,64,512]{3,2,1,0:T(8,128)(2,1)S(1)})) conditional(s32[]{:T(128)} %convert_element_type.213, (bf16[2,4,64,4096]{3,2,1,0:T(8,128)(2,1)}, ...), branch_computations={%region_9.9_spmd, %region_10.10_spmd} | conditional | bytes 524338 | solution.py:292
  617.5 10.1 %branch_1_fun.5 = (bf16[64,4096]{1,0:T(8,128)(2,1)}, bf16[2,4,64,4096]{3,2,1,0:T(8,128)(2,1)}, bf16[2,4,64,4096]{3,2,1,0:T(8,128)(2,1)}, bf16[2,4,64,512]{3,2,1,0:T(8,128)(2,1)S(1)}, bf16[2,4,64,512]{3,2,1,0:T(8,128)(2,1)S(1)}) custom-call(s32[4]{0:T(128)S(1)} %get-tuple-element.853.sc_ref, ...), custom_call_target="tpu_custom_call", output_to_operand_aliasing={{1}: (6, {}), {2}: (7, {}), {3}: (8, {}), {4}: (9, {})} | custom-call | tf_op jit(solution)/shard_map/while/body/eval_jaxpr/cond/branch_1_fun/pallas_call | solution.py:109
  634.7 9.7 %conditional.8 = ((bf16[64,4096]{1,0:T(8,128)(2,1)}, bf16[2,4,64,4096]{3,2,1,0:T(8,128)(2,1)}, bf16[2,4,64,4096]{3,2,1,0:T(8,128)(2,1)}, bf16[2,4,64,512]{3,2,1,0:T(8,128)(2,1)S(1)}, bf16[2,4,64,512]{3,2,1,0:T(8,128)(2,1)S(1)})) conditional(s32[]{:T(128)} %convert_element_type.213, (bf16[2,4,64,4096]{3,2,1,0:T(8,128)(2,1)}, ...), branch_computations={%region_9.9_spmd, %region_10.10_spmd} | conditional | bytes 524338 | solution.py:292
  697.3 81.7 %reduce-scatter.3.cloned.1.call-done = bf16[512,512]{1,0:T(8,128)(2,1)} async-done(((bf16[8192,512]{1,0:T(8,128)(2,1)}), bf16[512,512]{1,0:T(8,128)(2,1)}) %reduce-scatter.3.cloned.1.call-update) | async-done | bytes 524304 | tf_op jit(solution)/shard_map/reduce_scatter | solution.py:204
  (252 shorter events, 529.5 us)
Async XLA Ops:
  7.2 687.7 %reduce-scatter.5.cloned.1.call-start = ((), (), s32[]{:S(2)}) async-start(), calls=%async_computation.3 | async-start | bytes 8912896 | tf_op jit(solution)/shard_map/reduce_scatter | solution.py:204
  78.8 9.8 %collective-permute-start = (bf16[64,4096]{1,0:T(8,128)(2,1)S(1)}, bf16[64,4096]{1,0:T(8,128)(2,1)S(1)}, u32[]{:S(2)}, u32[]{:S(2)}) collective-permute-start(bf16[64,4096]{1,0:T(8,128)(2,1)S(1)} %get-tuple-element.1222), channel_id=1, source_target_pairs={{112,0},{0,16},{16,32},{32,48},{48,64},{64,80},{80,96},{96,112},{1... | collective-permute-start | bytes 1572872 | tf_op jit(solution)/shard_map/while/body/eval_jaxpr/ppermute | solution.py:140
  95.4 9.8 %collective-permute-start = (bf16[64,4096]{1,0:T(8,128)(2,1)S(1)}, bf16[64,4096]{1,0:T(8,128)(2,1)S(1)}, u32[]{:S(2)}, u32[]{:S(2)}) collective-permute-start(bf16[64,4096]{1,0:T(8,128)(2,1)S(1)} %get-tuple-element.1222), channel_id=1, source_target_pairs={{112,0},{0,16},{16,32},{32,48},{48,64},{64,80},{80,96},{96,112},{1... | collective-permute-start | bytes 1572872 | tf_op jit(solution)/shard_map/while/body/eval_jaxpr/ppermute | solution.py:140
  112.1 9.8 %collective-permute-start = (bf16[64,4096]{1,0:T(8,128)(2,1)S(1)}, bf16[64,4096]{1,0:T(8,128)(2,1)S(1)}, u32[]{:S(2)}, u32[]{:S(2)}) collective-permute-start(bf16[64,4096]{1,0:T(8,128)(2,1)S(1)} %get-tuple-element.1222), channel_id=1, source_target_pairs={{112,0},{0,16},{16,32},{32,48},{48,64},{64,80},{80,96},{96,112},{1... | collective-permute-start | bytes 1572872 | tf_op jit(solution)/shard_map/while/body/eval_jaxpr/ppermute | solution.py:140
  128.7 9.8 %collective-permute-start = (bf16[64,4096]{1,0:T(8,128)(2,1)S(1)}, bf16[64,4096]{1,0:T(8,128)(2,1)S(1)}, u32[]{:S(2)}, u32[]{:S(2)}) collective-permute-start(bf16[64,4096]{1,0:T(8,128)(2,1)S(1)} %get-tuple-element.1222), channel_id=1, source_target_pairs={{112,0},{0,16},{16,32},{32,48},{48,64},{64,80},{80,96},{96,112},{1... | collective-permute-start | bytes 1572872 | tf_op jit(solution)/shard_map/while/body/eval_jaxpr/ppermute | solution.py:140
  138.7 9.8 %collective-permute-start = (bf16[64,4096]{1,0:T(8,128)(2,1)S(1)}, bf16[64,4096]{1,0:T(8,128)(2,1)S(1)}, u32[]{:S(2)}, u32[]{:S(2)}) collective-permute-start(bf16[64,4096]{1,0:T(8,128)(2,1)S(1)} %get-tuple-element.1222), channel_id=1, source_target_pairs={{112,0},{0,16},{16,32},{32,48},{48,64},{64,80},{80,96},{96,112},{1... | collective-permute-start | bytes 1572872 | tf_op jit(solution)/shard_map/while/body/eval_jaxpr/ppermute | solution.py:140
  148.7 9.8 %collective-permute-start = (bf16[64,4096]{1,0:T(8,128)(2,1)S(1)}, bf16[64,4096]{1,0:T(8,128)(2,1)S(1)}, u32[]{:S(2)}, u32[]{:S(2)}) collective-permute-start(bf16[64,4096]{1,0:T(8,128)(2,1)S(1)} %get-tuple-element.1222), channel_id=1, source_target_pairs={{112,0},{0,16},{16,32},{32,48},{48,64},{64,80},{80,96},{96,112},{1... | collective-permute-start | bytes 1572872 | tf_op jit(solution)/shard_map/while/body/eval_jaxpr/ppermute | solution.py:140
  158.6 9.8 %collective-permute-start = (bf16[64,4096]{1,0:T(8,128)(2,1)S(1)}, bf16[64,4096]{1,0:T(8,128)(2,1)S(1)}, u32[]{:S(2)}, u32[]{:S(2)}) collective-permute-start(bf16[64,4096]{1,0:T(8,128)(2,1)S(1)} %get-tuple-element.1222), channel_id=1, source_target_pairs={{112,0},{0,16},{16,32},{32,48},{48,64},{64,80},{80,96},{96,112},{1... | collective-permute-start | bytes 1572872 | tf_op jit(solution)/shard_map/while/body/eval_jaxpr/ppermute | solution.py:140
  168.6 12.8 %collective-permute-start = (bf16[64,4096]{1,0:T(8,128)(2,1)S(1)}, bf16[64,4096]{1,0:T(8,128)(2,1)S(1)}, u32[]{:S(2)}, u32[]{:S(2)}) collective-permute-start(bf16[64,4096]{1,0:T(8,128)(2,1)S(1)} %get-tuple-element.1222), channel_id=1, source_target_pairs={{112,0},{0,16},{16,32},{32,48},{48,64},{64,80},{80,96},{96,112},{1... | collective-permute-start | bytes 1572872 | tf_op jit(solution)/shard_map/while/body/eval_jaxpr/ppermute | solution.py:140
  188.2 9.8 %collective-permute-start = (bf16[64,4096]{1,0:T(8,128)(2,1)S(1)}, bf16[64,4096]{1,0:T(8,128)(2,1)S(1)}, u32[]{:S(2)}, u32[]{:S(2)}) collective-permute-start(bf16[64,4096]{1,0:T(8,128)(2,1)S(1)} %get-tuple-element.1222), channel_id=1, source_target_pairs={{112,0},{0,16},{16,32},{32,48},{48,64},{64,80},{80,96},{96,112},{1... | collective-permute-start | bytes 1572872 | tf_op jit(solution)/shard_map/while/body/eval_jaxpr/ppermute | solution.py:140
  248.1 9.8 %collective-permute-start = (bf16[64,4096]{1,0:T(8,128)(2,1)S(1)}, bf16[64,4096]{1,0:T(8,128)(2,1)S(1)}, u32[]{:S(2)}, u32[]{:S(2)}) collective-permute-start(bf16[64,4096]{1,0:T(8,128)(2,1)S(1)} %get-tuple-element.1222), channel_id=1, source_target_pairs={{112,0},{0,16},{16,32},{32,48},{48,64},{64,80},{80,96},{96,112},{1... | collective-permute-start | bytes 1572872 | tf_op jit(solution)/shard_map/while/body/eval_jaxpr/ppermute | solution.py:140
  258.0 9.8 %collective-permute-start = (bf16[64,4096]{1,0:T(8,128)(2,1)S(1)}, bf16[64,4096]{1,0:T(8,128)(2,1)S(1)}, u32[]{:S(2)}, u32[]{:S(2)}) collective-permute-start(bf16[64,4096]{1,0:T(8,128)(2,1)S(1)} %get-tuple-element.1222), channel_id=1, source_target_pairs={{112,0},{0,16},{16,32},{32,48},{48,64},{64,80},{80,96},{96,112},{1... | collective-permute-start | bytes 1572872 | tf_op jit(solution)/shard_map/while/body/eval_jaxpr/ppermute | solution.py:140
  268.0 9.8 %collective-permute-start = (bf16[64,4096]{1,0:T(8,128)(2,1)S(1)}, bf16[64,4096]{1,0:T(8,128)(2,1)S(1)}, u32[]{:S(2)}, u32[]{:S(2)}) collective-permute-start(bf16[64,4096]{1,0:T(8,128)(2,1)S(1)} %get-tuple-element.1222), channel_id=1, source_target_pairs={{112,0},{0,16},{16,32},{32,48},{48,64},{64,80},{80,96},{96,112},{1... | collective-permute-start | bytes 1572872 | tf_op jit(solution)/shard_map/while/body/eval_jaxpr/ppermute | solution.py:140
  278.0 12.8 %collective-permute-start = (bf16[64,4096]{1,0:T(8,128)(2,1)S(1)}, bf16[64,4096]{1,0:T(8,128)(2,1)S(1)}, u32[]{:S(2)}, u32[]{:S(2)}) collective-permute-start(bf16[64,4096]{1,0:T(8,128)(2,1)S(1)} %get-tuple-element.1222), channel_id=1, source_target_pairs={{112,0},{0,16},{16,32},{32,48},{48,64},{64,80},{80,96},{96,112},{1... | collective-permute-start | bytes 1572872 | tf_op jit(solution)/shard_map/while/body/eval_jaxpr/ppermute | solution.py:140
  290.9 12.8 %collective-permute-start = (bf16[64,4096]{1,0:T(8,128)(2,1)S(1)}, bf16[64,4096]{1,0:T(8,128)(2,1)S(1)}, u32[]{:S(2)}, u32[]{:S(2)}) collective-permute-start(bf16[64,4096]{1,0:T(8,128)(2,1)S(1)} %get-tuple-element.1222), channel_id=1, source_target_pairs={{112,0},{0,16},{16,32},{32,48},{48,64},{64,80},{80,96},{96,112},{1... | collective-permute-start | bytes 1572872 | tf_op jit(solution)/shard_map/while/body/eval_jaxpr/ppermute | solution.py:140
  303.9 12.8 %collective-permute-start = (bf16[64,4096]{1,0:T(8,128)(2,1)S(1)}, bf16[64,4096]{1,0:T(8,128)(2,1)S(1)}, u32[]{:S(2)}, u32[]{:S(2)}) collective-permute-start(bf16[64,4096]{1,0:T(8,128)(2,1)S(1)} %get-tuple-element.1222), channel_id=1, source_target_pairs={{112,0},{0,16},{16,32},{32,48},{48,64},{64,80},{80,96},{96,112},{1... | collective-permute-start | bytes 1572872 | tf_op jit(solution)/shard_map/while/body/eval_jaxpr/ppermute | solution.py:140
  316.8 12.8 %collective-permute-start = (bf16[64,4096]{1,0:T(8,128)(2,1)S(1)}, bf16[64,4096]{1,0:T(8,128)(2,1)S(1)}, u32[]{:S(2)}, u32[]{:S(2)}) collective-permute-start(bf16[64,4096]{1,0:T(8,128)(2,1)S(1)} %get-tuple-element.1222), channel_id=1, source_target_pairs={{112,0},{0,16},{16,32},{32,48},{48,64},{64,80},{80,96},{96,112},{1... | collective-permute-start | bytes 1572872 | tf_op jit(solution)/shard_map/while/body/eval_jaxpr/ppermute | solution.py:140
  336.6 15.2 %collective-permute-start.1 = (bf16[64,4096]{1,0:T(8,128)(2,1)}, bf16[64,4096]{1,0:T(8,128)(2,1)}, u32[]{:S(2)}, u32[]{:S(2)}) collective-permute-start(bf16[64,4096]{1,0:T(8,128)(2,1)} %get-tuple-element.1236), channel_id=1, source_target_pairs={{16,0},{32,16},{48,32},{64,48},{80,64},{96,80},{112,96},{0,112},{1... | collective-permute-start | bytes 1572872 | tf_op jit(solution)/shard_map/while/body/eval_jaxpr/ppermute | solution.py:140
  352.7 19.0 %collective-permute-start.1 = (bf16[64,4096]{1,0:T(8,128)(2,1)}, bf16[64,4096]{1,0:T(8,128)(2,1)}, u32[]{:S(2)}, u32[]{:S(2)}) collective-permute-start(bf16[64,4096]{1,0:T(8,128)(2,1)} %get-tuple-element.1236), channel_id=1, source_target_pairs={{16,0},{32,16},{48,32},{64,48},{80,64},{96,80},{112,96},{0,112},{1... | collective-permute-start | bytes 1572872 | tf_op jit(solution)/shard_map/while/body/eval_jaxpr/ppermute | solution.py:140
  372.6 19.0 %collective-permute-start.1 = (bf16[64,4096]{1,0:T(8,128)(2,1)}, bf16[64,4096]{1,0:T(8,128)(2,1)}, u32[]{:S(2)}, u32[]{:S(2)}) collective-permute-start(bf16[64,4096]{1,0:T(8,128)(2,1)} %get-tuple-element.1236), channel_id=1, source_target_pairs={{16,0},{32,16},{48,32},{64,48},{80,64},{96,80},{112,96},{0,112},{1... | collective-permute-start | bytes 1572872 | tf_op jit(solution)/shard_map/while/body/eval_jaxpr/ppermute | solution.py:140
  392.6 19.0 %collective-permute-start.1 = (bf16[64,4096]{1,0:T(8,128)(2,1)}, bf16[64,4096]{1,0:T(8,128)(2,1)}, u32[]{:S(2)}, u32[]{:S(2)}) collective-permute-start(bf16[64,4096]{1,0:T(8,128)(2,1)} %get-tuple-element.1236), channel_id=1, source_target_pairs={{16,0},{32,16},{48,32},{64,48},{80,64},{96,80},{112,96},{0,112},{1... | collective-permute-start | bytes 1572872 | tf_op jit(solution)/shard_map/while/body/eval_jaxpr/ppermute | solution.py:140
  412.5 10.1 %collective-permute-start.1 = (bf16[64,4096]{1,0:T(8,128)(2,1)}, bf16[64,4096]{1,0:T(8,128)(2,1)}, u32[]{:S(2)}, u32[]{:S(2)}) collective-permute-start(bf16[64,4096]{1,0:T(8,128)(2,1)} %get-tuple-element.1236), channel_id=1, source_target_pairs={{16,0},{32,16},{48,32},{64,48},{80,64},{96,80},{112,96},{0,112},{1... | collective-permute-start | bytes 1572872 | tf_op jit(solution)/shard_map/while/body/eval_jaxpr/ppermute | solution.py:140
  423.6 10.1 %collective-permute-start.1 = (bf16[64,4096]{1,0:T(8,128)(2,1)}, bf16[64,4096]{1,0:T(8,128)(2,1)}, u32[]{:S(2)}, u32[]{:S(2)}) collective-permute-start(bf16[64,4096]{1,0:T(8,128)(2,1)} %get-tuple-element.1236), channel_id=1, source_target_pairs={{16,0},{32,16},{48,32},{64,48},{80,64},{96,80},{112,96},{0,112},{1... | collective-permute-start | bytes 1572872 | tf_op jit(solution)/shard_map/while/body/eval_jaxpr/ppermute | solution.py:140
  434.6 10.1 %collective-permute-start.1 = (bf16[64,4096]{1,0:T(8,128)(2,1)}, bf16[64,4096]{1,0:T(8,128)(2,1)}, u32[]{:S(2)}, u32[]{:S(2)}) collective-permute-start(bf16[64,4096]{1,0:T(8,128)(2,1)} %get-tuple-element.1236), channel_id=1, source_target_pairs={{16,0},{32,16},{48,32},{64,48},{80,64},{96,80},{112,96},{0,112},{1... | collective-permute-start | bytes 1572872 | tf_op jit(solution)/shard_map/while/body/eval_jaxpr/ppermute | solution.py:140
  471.3 10.1 %collective-permute-start.1 = (bf16[64,4096]{1,0:T(8,128)(2,1)}, bf16[64,4096]{1,0:T(8,128)(2,1)}, u32[]{:S(2)}, u32[]{:S(2)}) collective-permute-start(bf16[64,4096]{1,0:T(8,128)(2,1)} %get-tuple-element.1236), channel_id=1, source_target_pairs={{16,0},{32,16},{48,32},{64,48},{80,64},{96,80},{112,96},{0,112},{1... | collective-permute-start | bytes 1572872 | tf_op jit(solution)/shard_map/while/body/eval_jaxpr/ppermute | solution.py:140
  491.3 10.1 %collective-permute-start.1 = (bf16[64,4096]{1,0:T(8,128)(2,1)}, bf16[64,4096]{1,0:T(8,128)(2,1)}, u32[]{:S(2)}, u32[]{:S(2)}) collective-permute-start(bf16[64,4096]{1,0:T(8,128)(2,1)} %get-tuple-element.1236), channel_id=1, source_target_pairs={{16,0},{32,16},{48,32},{64,48},{80,64},{96,80},{112,96},{0,112},{1... | collective-permute-start | bytes 1572872 | tf_op jit(solution)/shard_map/while/body/eval_jaxpr/ppermute | solution.py:140
  511.2 10.1 %collective-permute-start.1 = (bf16[64,4096]{1,0:T(8,128)(2,1)}, bf16[64,4096]{1,0:T(8,128)(2,1)}, u32[]{:S(2)}, u32[]{:S(2)}) collective-permute-start(bf16[64,4096]{1,0:T(8,128)(2,1)} %get-tuple-element.1236), channel_id=1, source_target_pairs={{16,0},{32,16},{48,32},{64,48},{80,64},{96,80},{112,96},{0,112},{1... | collective-permute-start | bytes 1572872 | tf_op jit(solution)/shard_map/while/body/eval_jaxpr/ppermute | solution.py:140
  546.8 232.2 %reduce-scatter.3.cloned.1.call-start = ((), (), s32[]{:S(2)}) async-start(), calls=%async_computation.2 | async-start | bytes 8912896 | tf_op jit(solution)/shard_map/reduce_scatter | solution.py:204
  547.8 19.0 %collective-permute-start.2 = (bf16[64,4096]{1,0:T(8,128)(2,1)}, bf16[64,4096]{1,0:T(8,128)(2,1)}, u32[]{:S(2)}, u32[]{:S(2)}) collective-permute-start(bf16[64,4096]{1,0:T(8,128)(2,1)} %get-tuple-element.1253), channel_id=1, source_target_pairs={{16,0},{32,16},{48,32},{64,48},{80,64},{96,80},{112,96},{0,112},{1... | collective-permute-start | bytes 1572872 | tf_op jit(solution)/shard_map/while/body/eval_jaxpr/ppermute | solution.py:140
  567.8 10.1 %collective-permute-start.2 = (bf16[64,4096]{1,0:T(8,128)(2,1)}, bf16[64,4096]{1,0:T(8,128)(2,1)}, u32[]{:S(2)}, u32[]{:S(2)}) collective-permute-start(bf16[64,4096]{1,0:T(8,128)(2,1)} %get-tuple-element.1253), channel_id=1, source_target_pairs={{16,0},{32,16},{48,32},{64,48},{80,64},{96,80},{112,96},{0,112},{1... | collective-permute-start | bytes 1572872 | tf_op jit(solution)/shard_map/while/body/eval_jaxpr/ppermute | solution.py:140
  578.8 10.4 %collective-permute-start.2 = (bf16[64,4096]{1,0:T(8,128)(2,1)}, bf16[64,4096]{1,0:T(8,128)(2,1)}, u32[]{:S(2)}, u32[]{:S(2)}) collective-permute-start(bf16[64,4096]{1,0:T(8,128)(2,1)} %get-tuple-element.1253), channel_id=1, source_target_pairs={{16,0},{32,16},{48,32},{64,48},{80,64},{96,80},{112,96},{0,112},{1... | collective-permute-start | bytes 1572872 | tf_op jit(solution)/shard_map/while/body/eval_jaxpr/ppermute | solution.py:140
  590.2 10.4 %collective-permute-start.2 = (bf16[64,4096]{1,0:T(8,128)(2,1)}, bf16[64,4096]{1,0:T(8,128)(2,1)}, u32[]{:S(2)}, u32[]{:S(2)}) collective-permute-start(bf16[64,4096]{1,0:T(8,128)(2,1)} %get-tuple-element.1253), channel_id=1, source_target_pairs={{16,0},{32,16},{48,32},{64,48},{80,64},{96,80},{112,96},{0,112},{1... | collective-permute-start | bytes 1572872 | tf_op jit(solution)/shard_map/while/body/eval_jaxpr/ppermute | solution.py:140
  (16 other events, 103.2 us)
Sparse Core Ops, SparseCore 0:
  546.9 88.8 reduce-scatter.4
  690.6 88.4 reduce-scatter.2

commit v6 on v5

--- a/solution.py
+++ b/solution.py
@@ -140,6 +140,13 @@
     return lax.ppermute(block, axis, route)
 
 
+def masked(weight, mask):
+    laps, rows, cols = weight.shape
+    tiles = weight.reshape(laps, rows // BLK, BLK, cols // BLK, BLK)
+    keep = mask.astype(weight.dtype)[:, :, None, :, None]
+    return (tiles * keep).reshape(laps, rows, cols)
+
+
 def expand_blocks(mask):
     return jnp.repeat(jnp.repeat(mask, BLK, axis=-2), BLK, axis=-1)
 
@@ -199,10 +206,11 @@
         "rqd,rk->qdk", upstream_all.reshape(rows, groups, span), hidden_all,
         preferred_element_type=jnp.float32,
     )
-    joined = jnp.stack([part_a.astype(jnp.bfloat16), part_b.astype(jnp.bfloat16)], axis=1)
-    joined = joined.reshape(-1, joined.shape[-1])
+    inner = part_a.shape[-1]
+    joined = jnp.concatenate([part_a.astype(jnp.bfloat16), part_b.astype(jnp.bfloat16)], axis=-1)
+    joined = joined.reshape(-1, 2 * inner)
     summed = lax.psum_scatter(joined, "dp", scatter_dimension=0, tiled=True).astype(jnp.float32)
-    sum_a, sum_b = summed[:span], summed[span:]
+    sum_a, sum_b = summed[:, :inner], summed[:, inner:]
     full_a = expand_blocks(mask_a[lap_idx, 0]).astype(jnp.float32)
     full_b = expand_blocks(mask_b[lap_idx, 0]).astype(jnp.float32)
     owned_a = lax.dynamic_slice_in_dim(full_a, owner * span, span, 0)
@@ -218,8 +226,8 @@
     micro_inputs = micro_inputs.reshape(batches, tokens, width)
     out_cotangent = out_cotangent.reshape(batches, tokens, width)
     inner = weight_a.shape[3]
-    eff_a = weight_a[:, 0] * expand_blocks(mask_a[:, 0]).astype(jnp.bfloat16)
-    eff_b = weight_b[:, 0] * expand_blocks(mask_b[:, 0]).astype(jnp.bfloat16)
+    eff_a = masked(weight_a[:, 0], mask_a[:, 0])
+    eff_b = masked(weight_b[:, 0], mask_b[:, 0])
 
     def spare_forward(values):
         return jnp.zeros_like(values)

time: 792 us -> 822 us (1.038)
  local copies, waits for them, and re-layouts: 95.7 us -> 118 us
    mul x0 -> x4, local copies, waits for them, and re-layouts: none -> 57.7 us  [masked(): return (tiles * keep).reshape(laps, rows, cols)]
    while x2 -> x0, local copies, waits for them, and re-layouts: 23.4 us -> none  [on_device(): lax.fori_loop(0, batches + 2 * sections - 1, forward_step, (start_rows, s...]
    reshape x0 -> x2, local copies, waits for them, and re-layouts: none -> 22.9 us  [settle(): joined = joined.reshape(-1, 2 * inner)]
    unnamed x25, local copies, waits for them, and re-layouts: 28.9 us -> 9.22 us
    concatenate x0 -> x2, other arithmetic: none -> 16 us  [settle(): jnp.concatenate([part_a.astype(jnp.bfloat16), part_b.astype(jnp.bfloat16)...]
    another operation x31 -> x29, local copies, waits for them, and re-layouts: 33.1 us -> 18 us
    another operation x2 -> x0, other arithmetic: 13.6 us -> none  [settle(): jnp.stack([part_a.astype(jnp.bfloat16), part_b.astype(jnp.bfloat16)], axi...]
  transfers between devices with their start and end apart: 40 -> 40, of which waited for: 39 -> 39; matrix products, arithmetic and copies ran while one was open for 4% -> 5% of each run, Pallas kernels for 5% -> 5%
where the time goes in v6:
time: 822 us; the launch traced here: 820 us
  waiting for transfers between devices  413 us (50%)
  Pallas kernels  132 us (16%)
  local copies, waits for them, and re-layouts  118 us (14%)
  starting transfers between devices  86.4 us (11%)
  other arithmetic  42.5 us (5%)
  between operations  14.4 us (2%)
  matrix products  13.7 us (2%)
    ppermute x38, waiting for transfers between devices, shifted(): return lax.ppermute(block, axis, route)  333 us
    ppermute x38, starting transfers between devices, shifted(): return lax.ppermute(block, axis, route)  86.3 us
    reduce_scatter x2, waiting for transfers between devices, settle(): lax.psum_scatter(joined, 'dp', scatter_dimension=0, tiled=True)  79.2 us
    pallas_call x8, Pallas kernels, bwd_call(): pl.pallas_call(_bwd_kernel, grid_spec=pltpu.PrefetchScalarGridSpec(num_sc...  78.3 us
    mul x4, local copies, waits for them, and re-layouts, masked(): return (tiles * keep).reshape(laps, rows, cols)  57.7 us
    pallas_call x8, Pallas kernels, fwd_call(): pl.pallas_call(_fwd_kernel, grid_spec=pltpu.PrefetchScalarGridSpec(num_sc...  54 us
    reshape x2, local copies, waits for them, and re-layouts, settle(): joined = joined.reshape(-1, 2 * inner)  22.9 us
    another operation x29, local copies, waits for them, and re-layouts  18 us
  transfers between devices with their start and end apart: 40, of which 39 were waited for; matrix products, arithmetic and copies ran while one was open for 5% of the time, Pallas kernels for 5%

profile of v6, /device:TPU:0, one launch (start us, length us, event | category | flops | bytes accessed | tf_op | source)
XLA Modules:
  0.0 820.2 jit_solution(9579566542687225555)
XLA Ops:
  14.1 22.5 %mul.41 = bf16[2,4096,512]{2,1,0:T(8,128)(2,1)} reshape(bf16[2,64,64,8,64]{4,3,2,1,0:T(8,128)(2,1)} %mul.40) | data formatting | bytes 16777216 | tf_op jit(solution)/shard_map/mul | solution.py:147
  43.2 22.5 %mul.44 = bf16[2,512,4096]{2,1,0:T(8,128)(2,1)} reshape(bf16[2,8,64,64,64]{4,3,2,1,0:T(8,128)(2,1)} %mul.43) | data formatting | bytes 16777216 | tf_op jit(solution)/shard_map/mul | solution.py:147
  86.8 257.7 %while.66 = (s32[]{:T(128)}, bf16[64,4096]{1,0:T(8,128)(2,1)S(1)}, bf16[2,4,64,4096]{3,2,1,0:T(8,128)(2,1)}, s32[]{:T(128)}, pred[]{:T(512)}, /*index=5*/bf16[4,...) while((s32[]{:T(128)}, bf16[64,4096]{1,0:T(8,128)(2,1)S(1)}, ...), condition=%wide.region_3.4_spmd, body=%wide.region_0.3_spmd.sunk | while | flops 31 | bytes 2621852 | solution.py:268
  93.6 9.8 %collective-permute-done = bf16[64,4096]{1,0:T(8,128)(2,1)S(1)} collective-permute-done((bf16[64,4096]{1,0:T(8,128)(2,1)S(1)}, bf16[64,4096]{1,0:T(8,128)(2,1)S(1)}, u32[]{:S(2)}, u32[]{:S(2)}) %collective-permute-start) | collective-permute-done | bytes 524320 | tf_op jit(solution)/shard_map/while/body/eval_jaxpr/ppermute | solution.py:140
  110.2 9.8 %collective-permute-done = bf16[64,4096]{1,0:T(8,128)(2,1)S(1)} collective-permute-done((bf16[64,4096]{1,0:T(8,128)(2,1)S(1)}, bf16[64,4096]{1,0:T(8,128)(2,1)S(1)}, u32[]{:S(2)}, u32[]{:S(2)}) %collective-permute-start) | collective-permute-done | bytes 524320 | tf_op jit(solution)/shard_map/while/body/eval_jaxpr/ppermute | solution.py:140
  126.9 9.8 %collective-permute-done = bf16[64,4096]{1,0:T(8,128)(2,1)S(1)} collective-permute-done((bf16[64,4096]{1,0:T(8,128)(2,1)S(1)}, bf16[64,4096]{1,0:T(8,128)(2,1)S(1)}, u32[]{:S(2)}, u32[]{:S(2)}) %collective-permute-start) | collective-permute-done | bytes 524320 | tf_op jit(solution)/shard_map/while/body/eval_jaxpr/ppermute | solution.py:140
  143.5 9.8 %collective-permute-done = bf16[64,4096]{1,0:T(8,128)(2,1)S(1)} collective-permute-done((bf16[64,4096]{1,0:T(8,128)(2,1)S(1)}, bf16[64,4096]{1,0:T(8,128)(2,1)S(1)}, u32[]{:S(2)}, u32[]{:S(2)}) %collective-permute-start) | collective-permute-done | bytes 524320 | tf_op jit(solution)/shard_map/while/body/eval_jaxpr/ppermute | solution.py:140
  153.5 9.8 %collective-permute-done = bf16[64,4096]{1,0:T(8,128)(2,1)S(1)} collective-permute-done((bf16[64,4096]{1,0:T(8,128)(2,1)S(1)}, bf16[64,4096]{1,0:T(8,128)(2,1)S(1)}, u32[]{:S(2)}, u32[]{:S(2)}) %collective-permute-start) | collective-permute-done | bytes 524320 | tf_op jit(solution)/shard_map/while/body/eval_jaxpr/ppermute | solution.py:140
  163.5 9.8 %collective-permute-done = bf16[64,4096]{1,0:T(8,128)(2,1)S(1)} collective-permute-done((bf16[64,4096]{1,0:T(8,128)(2,1)S(1)}, bf16[64,4096]{1,0:T(8,128)(2,1)S(1)}, u32[]{:S(2)}, u32[]{:S(2)}) %collective-permute-start) | collective-permute-done | bytes 524320 | tf_op jit(solution)/shard_map/while/body/eval_jaxpr/ppermute | solution.py:140
  183.4 12.8 %collective-permute-done = bf16[64,4096]{1,0:T(8,128)(2,1)S(1)} collective-permute-done((bf16[64,4096]{1,0:T(8,128)(2,1)S(1)}, bf16[64,4096]{1,0:T(8,128)(2,1)S(1)}, u32[]{:S(2)}, u32[]{:S(2)}) %collective-permute-start) | collective-permute-done | bytes 524320 | tf_op jit(solution)/shard_map/while/body/eval_jaxpr/ppermute | solution.py:140
  203.0 9.8 %collective-permute-done = bf16[64,4096]{1,0:T(8,128)(2,1)S(1)} collective-permute-done((bf16[64,4096]{1,0:T(8,128)(2,1)S(1)}, bf16[64,4096]{1,0:T(8,128)(2,1)S(1)}, u32[]{:S(2)}, u32[]{:S(2)}) %collective-permute-start) | collective-permute-done | bytes 524320 | tf_op jit(solution)/shard_map/while/body/eval_jaxpr/ppermute | solution.py:140
  219.7 9.8 %collective-permute-done = bf16[64,4096]{1,0:T(8,128)(2,1)S(1)} collective-permute-done((bf16[64,4096]{1,0:T(8,128)(2,1)S(1)}, bf16[64,4096]{1,0:T(8,128)(2,1)S(1)}, u32[]{:S(2)}, u32[]{:S(2)}) %collective-permute-start) | collective-permute-done | bytes 524320 | tf_op jit(solution)/shard_map/while/body/eval_jaxpr/ppermute | solution.py:140
  236.3 9.8 %collective-permute-done = bf16[64,4096]{1,0:T(8,128)(2,1)S(1)} collective-permute-done((bf16[64,4096]{1,0:T(8,128)(2,1)S(1)}, bf16[64,4096]{1,0:T(8,128)(2,1)S(1)}, u32[]{:S(2)}, u32[]{:S(2)}) %collective-permute-start) | collective-permute-done | bytes 524320 | tf_op jit(solution)/shard_map/while/body/eval_jaxpr/ppermute | solution.py:140
  252.9 9.8 %collective-permute-done = bf16[64,4096]{1,0:T(8,128)(2,1)S(1)} collective-permute-done((bf16[64,4096]{1,0:T(8,128)(2,1)S(1)}, bf16[64,4096]{1,0:T(8,128)(2,1)S(1)}, u32[]{:S(2)}, u32[]{:S(2)}) %collective-permute-start) | collective-permute-done | bytes 524320 | tf_op jit(solution)/shard_map/while/body/eval_jaxpr/ppermute | solution.py:140
  262.9 9.8 %collective-permute-done = bf16[64,4096]{1,0:T(8,128)(2,1)S(1)} collective-permute-done((bf16[64,4096]{1,0:T(8,128)(2,1)S(1)}, bf16[64,4096]{1,0:T(8,128)(2,1)S(1)}, u32[]{:S(2)}, u32[]{:S(2)}) %collective-permute-start) | collective-permute-done | bytes 524320 | tf_op jit(solution)/shard_map/while/body/eval_jaxpr/ppermute | solution.py:140
  272.9 9.8 %collective-permute-done = bf16[64,4096]{1,0:T(8,128)(2,1)S(1)} collective-permute-done((bf16[64,4096]{1,0:T(8,128)(2,1)S(1)}, bf16[64,4096]{1,0:T(8,128)(2,1)S(1)}, u32[]{:S(2)}, u32[]{:S(2)}) %collective-permute-start) | collective-permute-done | bytes 524320 | tf_op jit(solution)/shard_map/while/body/eval_jaxpr/ppermute | solution.py:140
  292.8 12.8 %collective-permute-done = bf16[64,4096]{1,0:T(8,128)(2,1)S(1)} collective-permute-done((bf16[64,4096]{1,0:T(8,128)(2,1)S(1)}, bf16[64,4096]{1,0:T(8,128)(2,1)S(1)}, u32[]{:S(2)}, u32[]{:S(2)}) %collective-permute-start) | collective-permute-done | bytes 524320 | tf_op jit(solution)/shard_map/while/body/eval_jaxpr/ppermute | solution.py:140
  305.7 12.8 %collective-permute-done = bf16[64,4096]{1,0:T(8,128)(2,1)S(1)} collective-permute-done((bf16[64,4096]{1,0:T(8,128)(2,1)S(1)}, bf16[64,4096]{1,0:T(8,128)(2,1)S(1)}, u32[]{:S(2)}, u32[]{:S(2)}) %collective-permute-start) | collective-permute-done | bytes 524320 | tf_op jit(solution)/shard_map/while/body/eval_jaxpr/ppermute | solution.py:140
  318.7 12.8 %collective-permute-done = bf16[64,4096]{1,0:T(8,128)(2,1)S(1)} collective-permute-done((bf16[64,4096]{1,0:T(8,128)(2,1)S(1)}, bf16[64,4096]{1,0:T(8,128)(2,1)S(1)}, u32[]{:S(2)}, u32[]{:S(2)}) %collective-permute-start) | collective-permute-done | bytes 524320 | tf_op jit(solution)/shard_map/while/body/eval_jaxpr/ppermute | solution.py:140
  331.6 12.8 %collective-permute-done = bf16[64,4096]{1,0:T(8,128)(2,1)S(1)} collective-permute-done((bf16[64,4096]{1,0:T(8,128)(2,1)S(1)}, bf16[64,4096]{1,0:T(8,128)(2,1)S(1)}, u32[]{:S(2)}, u32[]{:S(2)}) %collective-permute-start) | collective-permute-done | bytes 524320 | tf_op jit(solution)/shard_map/while/body/eval_jaxpr/ppermute | solution.py:140
  350.4 185.7 %while.67 = (s32[]{:T(128)}, bf16[64,4096]{1,0:T(8,128)(2,1)}, bf16[2,4,64,4096]{3,2,1,0:T(8,128)(2,1)}, bf16[2,4,64,4096]{3,2,1,0:T(8,128)(2,1)}, bf16[2,4,64,5...) while((s32[]{:T(128)}, bf16[64,4096]{1,0:T(8,128)(2,1)}, ...), condition=%wide.region_7.8_spmd, body=%wide.region_4.7_spmd.sunk | while | flops 31 | bytes 2621980 | solution.py:316
  367.5 12.0 %collective-permute-start.1 = (bf16[64,4096]{1,0:T(8,128)(2,1)}, bf16[64,4096]{1,0:T(8,128)(2,1)}, u32[]{:S(2)}, u32[]{:S(2)}) collective-permute-start(bf16[64,4096]{1,0:T(8,128)(2,1)} %get-tuple-element.1172), channel_id=1, source_target_pairs={{16,0},{32,16},{48,32},{64,48},{80,64},{96,80},{112,96},{0,112},{1... | collective-permute-start | bytes 1572872 | tf_op jit(solution)/shard_map/while/body/eval_jaxpr/ppermute | solution.py:140
  387.4 12.0 %collective-permute-start.1 = (bf16[64,4096]{1,0:T(8,128)(2,1)}, bf16[64,4096]{1,0:T(8,128)(2,1)}, u32[]{:S(2)}, u32[]{:S(2)}) collective-permute-start(bf16[64,4096]{1,0:T(8,128)(2,1)} %get-tuple-element.1172), channel_id=1, source_target_pairs={{16,0},{32,16},{48,32},{64,48},{80,64},{96,80},{112,96},{0,112},{1... | collective-permute-start | bytes 1572872 | tf_op jit(solution)/shard_map/while/body/eval_jaxpr/ppermute | solution.py:140
  407.4 12.0 %collective-permute-start.1 = (bf16[64,4096]{1,0:T(8,128)(2,1)}, bf16[64,4096]{1,0:T(8,128)(2,1)}, u32[]{:S(2)}, u32[]{:S(2)}) collective-permute-start(bf16[64,4096]{1,0:T(8,128)(2,1)} %get-tuple-element.1172), channel_id=1, source_target_pairs={{16,0},{32,16},{48,32},{64,48},{80,64},{96,80},{112,96},{0,112},{1... | collective-permute-start | bytes 1572872 | tf_op jit(solution)/shard_map/while/body/eval_jaxpr/ppermute | solution.py:140
  554.6 11.4 %copy.41 = bf16[4096,1024]{0,1:T(8,128)(2,1)} copy(bf16[4096,1024]{1,0:T(8,128)(2,1)} %bitcast.119) | data formatting | bytes 16777216 | tf_op jit(solution)/shard_map/reshape | solution.py:211
  566.1 121.8 %while.68 = (s32[]{:T(128)}, bf16[64,4096]{1,0:T(8,128)(2,1)}, bf16[2,4,64,4096]{3,2,1,0:T(8,128)(2,1)}, bf16[2,4,64,4096]{3,2,1,0:T(8,128)(2,1)}, bf16[2,4,64,5...) while((s32[]{:T(128)}, bf16[64,4096]{1,0:T(8,128)(2,1)}, ...), condition=%wide.region_11.12_spmd, body=%wide.region_8.11_spmd.sunk | while | flops 32 | bytes 2622000 | solution.py:318
  567.3 12.0 %collective-permute-start.2 = (bf16[64,4096]{1,0:T(8,128)(2,1)}, bf16[64,4096]{1,0:T(8,128)(2,1)}, u32[]{:S(2)}, u32[]{:S(2)}) collective-permute-start(bf16[64,4096]{1,0:T(8,128)(2,1)} %get-tuple-element.1189), channel_id=1, source_target_pairs={{16,0},{32,16},{48,32},{64,48},{80,64},{96,80},{112,96},{0,112},{1... | collective-permute-start | bytes 1572872 | tf_op jit(solution)/shard_map/while/body/eval_jaxpr/ppermute | solution.py:140
  620.3 9.8 %conditional.8 = ((bf16[64,4096]{1,0:T(8,128)(2,1)}, bf16[2,4,64,4096]{3,2,1,0:T(8,128)(2,1)}, bf16[2,4,64,4096]{3,2,1,0:T(8,128)(2,1)}, bf16[2,4,64,512]{3,2,1,0:T(8,128)(2,1)S(1)}, bf16[2,4,64,512]{3,2,1,0:T(8,128)(2,1)S(1)})) conditional(s32[]{:T(128)} %convert_element_type.201, (bf16[2,4,64,4096]{3,2,1,0:T(8,128)(2,1)}, ...), branch_computations={%region_9.9_spmd, %region_10.10_spmd} | conditional | bytes 524338 | solution.py:300
  637.2 10.1 %conditional.8 = ((bf16[64,4096]{1,0:T(8,128)(2,1)}, bf16[2,4,64,4096]{3,2,1,0:T(8,128)(2,1)}, bf16[2,4,64,4096]{3,2,1,0:T(8,128)(2,1)}, bf16[2,4,64,512]{3,2,1,0:T(8,128)(2,1)S(1)}, bf16[2,4,64,512]{3,2,1,0:T(8,128)(2,1)S(1)})) conditional(s32[]{:T(128)} %convert_element_type.201, (bf16[2,4,64,4096]{3,2,1,0:T(8,128)(2,1)}, ...), branch_computations={%region_9.9_spmd, %region_10.10_spmd} | conditional | bytes 524338 | solution.py:300
  637.2 10.1 %branch_1_fun.5 = (bf16[64,4096]{1,0:T(8,128)(2,1)}, bf16[2,4,64,4096]{3,2,1,0:T(8,128)(2,1)}, bf16[2,4,64,4096]{3,2,1,0:T(8,128)(2,1)}, bf16[2,4,64,512]{3,2,1,0:T(8,128)(2,1)S(1)}, bf16[2,4,64,512]{3,2,1,0:T(8,128)(2,1)S(1)}) custom-call(s32[4]{0:T(128)S(1)} %get-tuple-element.853.sc_ref, ...), custom_call_target="tpu_custom_call", output_to_operand_aliasing={{1}: (6, {}), {2}: (7, {}), {3}: (8, {}), {4}: (9, {})} | custom-call | tf_op jit(solution)/shard_map/while/body/eval_jaxpr/cond/branch_1_fun/pallas_call | solution.py:109
  706.5 11.5 %copy.38 = bf16[4096,1024]{0,1:T(8,128)(2,1)} copy(bf16[4096,1024]{1,0:T(8,128)(2,1)} %bitcast.120) | data formatting | bytes 16777216 | tf_op jit(solution)/shard_map/reshape | solution.py:211
  727.2 79.2 %reduce-scatter.3.cloned.1.call-done = bf16[256,1024]{0,1:T(8,128)(2,1)} async-done(((bf16[4096,1024]{0,1:T(8,128)(2,1)}), bf16[256,1024]{0,1:T(8,128)(2,1)}) %reduce-scatter.3.cloned.1.call-update) | async-done | bytes 524304 | tf_op jit(solution)/shard_map/reduce_scatter | solution.py:212
  (250 shorter events, 540.2 us)
Async XLA Ops:
  7.2 717.0 %reduce-scatter.5.cloned.1.call-start = ((), (), s32[]{:S(2)}) async-start(), calls=%async_computation.3 | async-start | bytes 8912896 | tf_op jit(solution)/shard_map/reduce_scatter | solution.py:212
  93.6 9.8 %collective-permute-start = (bf16[64,4096]{1,0:T(8,128)(2,1)S(1)}, bf16[64,4096]{1,0:T(8,128)(2,1)S(1)}, u32[]{:S(2)}, u32[]{:S(2)}) collective-permute-start(bf16[64,4096]{1,0:T(8,128)(2,1)S(1)} %get-tuple-element.1158), channel_id=1, source_target_pairs={{112,0},{0,16},{16,32},{32,48},{48,64},{64,80},{80,96},{96,112},{1... | collective-permute-start | bytes 1572872 | tf_op jit(solution)/shard_map/while/body/eval_jaxpr/ppermute | solution.py:140
  110.2 9.8 %collective-permute-start = (bf16[64,4096]{1,0:T(8,128)(2,1)S(1)}, bf16[64,4096]{1,0:T(8,128)(2,1)S(1)}, u32[]{:S(2)}, u32[]{:S(2)}) collective-permute-start(bf16[64,4096]{1,0:T(8,128)(2,1)S(1)} %get-tuple-element.1158), channel_id=1, source_target_pairs={{112,0},{0,16},{16,32},{32,48},{48,64},{64,80},{80,96},{96,112},{1... | collective-permute-start | bytes 1572872 | tf_op jit(solution)/shard_map/while/body/eval_jaxpr/ppermute | solution.py:140
  126.9 9.8 %collective-permute-start = (bf16[64,4096]{1,0:T(8,128)(2,1)S(1)}, bf16[64,4096]{1,0:T(8,128)(2,1)S(1)}, u32[]{:S(2)}, u32[]{:S(2)}) collective-permute-start(bf16[64,4096]{1,0:T(8,128)(2,1)S(1)} %get-tuple-element.1158), channel_id=1, source_target_pairs={{112,0},{0,16},{16,32},{32,48},{48,64},{64,80},{80,96},{96,112},{1... | collective-permute-start | bytes 1572872 | tf_op jit(solution)/shard_map/while/body/eval_jaxpr/ppermute | solution.py:140
  143.5 9.8 %collective-permute-start = (bf16[64,4096]{1,0:T(8,128)(2,1)S(1)}, bf16[64,4096]{1,0:T(8,128)(2,1)S(1)}, u32[]{:S(2)}, u32[]{:S(2)}) collective-permute-start(bf16[64,4096]{1,0:T(8,128)(2,1)S(1)} %get-tuple-element.1158), channel_id=1, source_target_pairs={{112,0},{0,16},{16,32},{32,48},{48,64},{64,80},{80,96},{96,112},{1... | collective-permute-start | bytes 1572872 | tf_op jit(solution)/shard_map/while/body/eval_jaxpr/ppermute | solution.py:140
  153.5 9.8 %collective-permute-start = (bf16[64,4096]{1,0:T(8,128)(2,1)S(1)}, bf16[64,4096]{1,0:T(8,128)(2,1)S(1)}, u32[]{:S(2)}, u32[]{:S(2)}) collective-permute-start(bf16[64,4096]{1,0:T(8,128)(2,1)S(1)} %get-tuple-element.1158), channel_id=1, source_target_pairs={{112,0},{0,16},{16,32},{32,48},{48,64},{64,80},{80,96},{96,112},{1... | collective-permute-start | bytes 1572872 | tf_op jit(solution)/shard_map/while/body/eval_jaxpr/ppermute | solution.py:140
  163.5 9.8 %collective-permute-start = (bf16[64,4096]{1,0:T(8,128)(2,1)S(1)}, bf16[64,4096]{1,0:T(8,128)(2,1)S(1)}, u32[]{:S(2)}, u32[]{:S(2)}) collective-permute-start(bf16[64,4096]{1,0:T(8,128)(2,1)S(1)} %get-tuple-element.1158), channel_id=1, source_target_pairs={{112,0},{0,16},{16,32},{32,48},{48,64},{64,80},{80,96},{96,112},{1... | collective-permute-start | bytes 1572872 | tf_op jit(solution)/shard_map/while/body/eval_jaxpr/ppermute | solution.py:140
  173.4 9.8 %collective-permute-start = (bf16[64,4096]{1,0:T(8,128)(2,1)S(1)}, bf16[64,4096]{1,0:T(8,128)(2,1)S(1)}, u32[]{:S(2)}, u32[]{:S(2)}) collective-permute-start(bf16[64,4096]{1,0:T(8,128)(2,1)S(1)} %get-tuple-element.1158), channel_id=1, source_target_pairs={{112,0},{0,16},{16,32},{32,48},{48,64},{64,80},{80,96},{96,112},{1... | collective-permute-start | bytes 1572872 | tf_op jit(solution)/shard_map/while/body/eval_jaxpr/ppermute | solution.py:140
  183.4 12.8 %collective-permute-start = (bf16[64,4096]{1,0:T(8,128)(2,1)S(1)}, bf16[64,4096]{1,0:T(8,128)(2,1)S(1)}, u32[]{:S(2)}, u32[]{:S(2)}) collective-permute-start(bf16[64,4096]{1,0:T(8,128)(2,1)S(1)} %get-tuple-element.1158), channel_id=1, source_target_pairs={{112,0},{0,16},{16,32},{32,48},{48,64},{64,80},{80,96},{96,112},{1... | collective-permute-start | bytes 1572872 | tf_op jit(solution)/shard_map/while/body/eval_jaxpr/ppermute | solution.py:140
  203.0 9.8 %collective-permute-start = (bf16[64,4096]{1,0:T(8,128)(2,1)S(1)}, bf16[64,4096]{1,0:T(8,128)(2,1)S(1)}, u32[]{:S(2)}, u32[]{:S(2)}) collective-permute-start(bf16[64,4096]{1,0:T(8,128)(2,1)S(1)} %get-tuple-element.1158), channel_id=1, source_target_pairs={{112,0},{0,16},{16,32},{32,48},{48,64},{64,80},{80,96},{96,112},{1... | collective-permute-start | bytes 1572872 | tf_op jit(solution)/shard_map/while/body/eval_jaxpr/ppermute | solution.py:140
  262.9 9.8 %collective-permute-start = (bf16[64,4096]{1,0:T(8,128)(2,1)S(1)}, bf16[64,4096]{1,0:T(8,128)(2,1)S(1)}, u32[]{:S(2)}, u32[]{:S(2)}) collective-permute-start(bf16[64,4096]{1,0:T(8,128)(2,1)S(1)} %get-tuple-element.1158), channel_id=1, source_target_pairs={{112,0},{0,16},{16,32},{32,48},{48,64},{64,80},{80,96},{96,112},{1... | collective-permute-start | bytes 1572872 | tf_op jit(solution)/shard_map/while/body/eval_jaxpr/ppermute | solution.py:140
  272.8 9.8 %collective-permute-start = (bf16[64,4096]{1,0:T(8,128)(2,1)S(1)}, bf16[64,4096]{1,0:T(8,128)(2,1)S(1)}, u32[]{:S(2)}, u32[]{:S(2)}) collective-permute-start(bf16[64,4096]{1,0:T(8,128)(2,1)S(1)} %get-tuple-element.1158), channel_id=1, source_target_pairs={{112,0},{0,16},{16,32},{32,48},{48,64},{64,80},{80,96},{96,112},{1... | collective-permute-start | bytes 1572872 | tf_op jit(solution)/shard_map/while/body/eval_jaxpr/ppermute | solution.py:140
  282.8 9.8 %collective-permute-start = (bf16[64,4096]{1,0:T(8,128)(2,1)S(1)}, bf16[64,4096]{1,0:T(8,128)(2,1)S(1)}, u32[]{:S(2)}, u32[]{:S(2)}) collective-permute-start(bf16[64,4096]{1,0:T(8,128)(2,1)S(1)} %get-tuple-element.1158), channel_id=1, source_target_pairs={{112,0},{0,16},{16,32},{32,48},{48,64},{64,80},{80,96},{96,112},{1... | collective-permute-start | bytes 1572872 | tf_op jit(solution)/shard_map/while/body/eval_jaxpr/ppermute | solution.py:140
  292.8 12.8 %collective-permute-start = (bf16[64,4096]{1,0:T(8,128)(2,1)S(1)}, bf16[64,4096]{1,0:T(8,128)(2,1)S(1)}, u32[]{:S(2)}, u32[]{:S(2)}) collective-permute-start(bf16[64,4096]{1,0:T(8,128)(2,1)S(1)} %get-tuple-element.1158), channel_id=1, source_target_pairs={{112,0},{0,16},{16,32},{32,48},{48,64},{64,80},{80,96},{96,112},{1... | collective-permute-start | bytes 1572872 | tf_op jit(solution)/shard_map/while/body/eval_jaxpr/ppermute | solution.py:140
  305.7 12.8 %collective-permute-start = (bf16[64,4096]{1,0:T(8,128)(2,1)S(1)}, bf16[64,4096]{1,0:T(8,128)(2,1)S(1)}, u32[]{:S(2)}, u32[]{:S(2)}) collective-permute-start(bf16[64,4096]{1,0:T(8,128)(2,1)S(1)} %get-tuple-element.1158), channel_id=1, source_target_pairs={{112,0},{0,16},{16,32},{32,48},{48,64},{64,80},{80,96},{96,112},{1... | collective-permute-start | bytes 1572872 | tf_op jit(solution)/shard_map/while/body/eval_jaxpr/ppermute | solution.py:140
  318.7 12.8 %collective-permute-start = (bf16[64,4096]{1,0:T(8,128)(2,1)S(1)}, bf16[64,4096]{1,0:T(8,128)(2,1)S(1)}, u32[]{:S(2)}, u32[]{:S(2)}) collective-permute-start(bf16[64,4096]{1,0:T(8,128)(2,1)S(1)} %get-tuple-element.1158), channel_id=1, source_target_pairs={{112,0},{0,16},{16,32},{32,48},{48,64},{64,80},{80,96},{96,112},{1... | collective-permute-start | bytes 1572872 | tf_op jit(solution)/shard_map/while/body/eval_jaxpr/ppermute | solution.py:140
  331.6 12.8 %collective-permute-start = (bf16[64,4096]{1,0:T(8,128)(2,1)S(1)}, bf16[64,4096]{1,0:T(8,128)(2,1)S(1)}, u32[]{:S(2)}, u32[]{:S(2)}) collective-permute-start(bf16[64,4096]{1,0:T(8,128)(2,1)S(1)} %get-tuple-element.1158), channel_id=1, source_target_pairs={{112,0},{0,16},{16,32},{32,48},{48,64},{64,80},{80,96},{96,112},{1... | collective-permute-start | bytes 1572872 | tf_op jit(solution)/shard_map/while/body/eval_jaxpr/ppermute | solution.py:140
  351.4 15.2 %collective-permute-start.1 = (bf16[64,4096]{1,0:T(8,128)(2,1)}, bf16[64,4096]{1,0:T(8,128)(2,1)}, u32[]{:S(2)}, u32[]{:S(2)}) collective-permute-start(bf16[64,4096]{1,0:T(8,128)(2,1)} %get-tuple-element.1172), channel_id=1, source_target_pairs={{16,0},{32,16},{48,32},{64,48},{80,64},{96,80},{112,96},{0,112},{1... | collective-permute-start | bytes 1572872 | tf_op jit(solution)/shard_map/while/body/eval_jaxpr/ppermute | solution.py:140
  367.5 19.0 %collective-permute-start.1 = (bf16[64,4096]{1,0:T(8,128)(2,1)}, bf16[64,4096]{1,0:T(8,128)(2,1)}, u32[]{:S(2)}, u32[]{:S(2)}) collective-permute-start(bf16[64,4096]{1,0:T(8,128)(2,1)} %get-tuple-element.1172), channel_id=1, source_target_pairs={{16,0},{32,16},{48,32},{64,48},{80,64},{96,80},{112,96},{0,112},{1... | collective-permute-start | bytes 1572872 | tf_op jit(solution)/shard_map/while/body/eval_jaxpr/ppermute | solution.py:140
  387.4 19.0 %collective-permute-start.1 = (bf16[64,4096]{1,0:T(8,128)(2,1)}, bf16[64,4096]{1,0:T(8,128)(2,1)}, u32[]{:S(2)}, u32[]{:S(2)}) collective-permute-start(bf16[64,4096]{1,0:T(8,128)(2,1)} %get-tuple-element.1172), channel_id=1, source_target_pairs={{16,0},{32,16},{48,32},{64,48},{80,64},{96,80},{112,96},{0,112},{1... | collective-permute-start | bytes 1572872 | tf_op jit(solution)/shard_map/while/body/eval_jaxpr/ppermute | solution.py:140
  407.4 19.0 %collective-permute-start.1 = (bf16[64,4096]{1,0:T(8,128)(2,1)}, bf16[64,4096]{1,0:T(8,128)(2,1)}, u32[]{:S(2)}, u32[]{:S(2)}) collective-permute-start(bf16[64,4096]{1,0:T(8,128)(2,1)} %get-tuple-element.1172), channel_id=1, source_target_pairs={{16,0},{32,16},{48,32},{64,48},{80,64},{96,80},{112,96},{0,112},{1... | collective-permute-start | bytes 1572872 | tf_op jit(solution)/shard_map/while/body/eval_jaxpr/ppermute | solution.py:140
  427.3 10.1 %collective-permute-start.1 = (bf16[64,4096]{1,0:T(8,128)(2,1)}, bf16[64,4096]{1,0:T(8,128)(2,1)}, u32[]{:S(2)}, u32[]{:S(2)}) collective-permute-start(bf16[64,4096]{1,0:T(8,128)(2,1)} %get-tuple-element.1172), channel_id=1, source_target_pairs={{16,0},{32,16},{48,32},{64,48},{80,64},{96,80},{112,96},{0,112},{1... | collective-permute-start | bytes 1572872 | tf_op jit(solution)/shard_map/while/body/eval_jaxpr/ppermute | solution.py:140
  438.4 10.1 %collective-permute-start.1 = (bf16[64,4096]{1,0:T(8,128)(2,1)}, bf16[64,4096]{1,0:T(8,128)(2,1)}, u32[]{:S(2)}, u32[]{:S(2)}) collective-permute-start(bf16[64,4096]{1,0:T(8,128)(2,1)} %get-tuple-element.1172), channel_id=1, source_target_pairs={{16,0},{32,16},{48,32},{64,48},{80,64},{96,80},{112,96},{0,112},{1... | collective-permute-start | bytes 1572872 | tf_op jit(solution)/shard_map/while/body/eval_jaxpr/ppermute | solution.py:140
  449.4 10.1 %collective-permute-start.1 = (bf16[64,4096]{1,0:T(8,128)(2,1)}, bf16[64,4096]{1,0:T(8,128)(2,1)}, u32[]{:S(2)}, u32[]{:S(2)}) collective-permute-start(bf16[64,4096]{1,0:T(8,128)(2,1)} %get-tuple-element.1172), channel_id=1, source_target_pairs={{16,0},{32,16},{48,32},{64,48},{80,64},{96,80},{112,96},{0,112},{1... | collective-permute-start | bytes 1572872 | tf_op jit(solution)/shard_map/while/body/eval_jaxpr/ppermute | solution.py:140
  486.2 10.1 %collective-permute-start.1 = (bf16[64,4096]{1,0:T(8,128)(2,1)}, bf16[64,4096]{1,0:T(8,128)(2,1)}, u32[]{:S(2)}, u32[]{:S(2)}) collective-permute-start(bf16[64,4096]{1,0:T(8,128)(2,1)} %get-tuple-element.1172), channel_id=1, source_target_pairs={{16,0},{32,16},{48,32},{64,48},{80,64},{96,80},{112,96},{0,112},{1... | collective-permute-start | bytes 1572872 | tf_op jit(solution)/shard_map/while/body/eval_jaxpr/ppermute | solution.py:140
  506.1 10.1 %collective-permute-start.1 = (bf16[64,4096]{1,0:T(8,128)(2,1)}, bf16[64,4096]{1,0:T(8,128)(2,1)}, u32[]{:S(2)}, u32[]{:S(2)}) collective-permute-start(bf16[64,4096]{1,0:T(8,128)(2,1)} %get-tuple-element.1172), channel_id=1, source_target_pairs={{16,0},{32,16},{48,32},{64,48},{80,64},{96,80},{112,96},{0,112},{1... | collective-permute-start | bytes 1572872 | tf_op jit(solution)/shard_map/while/body/eval_jaxpr/ppermute | solution.py:140
  526.0 10.1 %collective-permute-start.1 = (bf16[64,4096]{1,0:T(8,128)(2,1)}, bf16[64,4096]{1,0:T(8,128)(2,1)}, u32[]{:S(2)}, u32[]{:S(2)}) collective-permute-start(bf16[64,4096]{1,0:T(8,128)(2,1)} %get-tuple-element.1172), channel_id=1, source_target_pairs={{16,0},{32,16},{48,32},{64,48},{80,64},{96,80},{112,96},{0,112},{1... | collective-permute-start | bytes 1572872 | tf_op jit(solution)/shard_map/while/body/eval_jaxpr/ppermute | solution.py:140
  566.0 240.4 %reduce-scatter.3.cloned.1.call-start = ((), (), s32[]{:S(2)}) async-start(), calls=%async_computation.2 | async-start | bytes 8912896 | tf_op jit(solution)/shard_map/reduce_scatter | solution.py:212
  567.3 19.0 %collective-permute-start.2 = (bf16[64,4096]{1,0:T(8,128)(2,1)}, bf16[64,4096]{1,0:T(8,128)(2,1)}, u32[]{:S(2)}, u32[]{:S(2)}) collective-permute-start(bf16[64,4096]{1,0:T(8,128)(2,1)} %get-tuple-element.1189), channel_id=1, source_target_pairs={{16,0},{32,16},{48,32},{64,48},{80,64},{96,80},{112,96},{0,112},{1... | collective-permute-start | bytes 1572872 | tf_op jit(solution)/shard_map/while/body/eval_jaxpr/ppermute | solution.py:140
  587.2 10.4 %collective-permute-start.2 = (bf16[64,4096]{1,0:T(8,128)(2,1)}, bf16[64,4096]{1,0:T(8,128)(2,1)}, u32[]{:S(2)}, u32[]{:S(2)}) collective-permute-start(bf16[64,4096]{1,0:T(8,128)(2,1)} %get-tuple-element.1189), channel_id=1, source_target_pairs={{16,0},{32,16},{48,32},{64,48},{80,64},{96,80},{112,96},{0,112},{1... | collective-permute-start | bytes 1572872 | tf_op jit(solution)/shard_map/while/body/eval_jaxpr/ppermute | solution.py:140
  598.6 10.3 %collective-permute-start.2 = (bf16[64,4096]{1,0:T(8,128)(2,1)}, bf16[64,4096]{1,0:T(8,128)(2,1)}, u32[]{:S(2)}, u32[]{:S(2)}) collective-permute-start(bf16[64,4096]{1,0:T(8,128)(2,1)} %get-tuple-element.1189), channel_id=1, source_target_pairs={{16,0},{32,16},{48,32},{64,48},{80,64},{96,80},{112,96},{0,112},{1... | collective-permute-start | bytes 1572872 | tf_op jit(solution)/shard_map/while/body/eval_jaxpr/ppermute | solution.py:140
  609.8 10.4 %collective-permute-start.2 = (bf16[64,4096]{1,0:T(8,128)(2,1)}, bf16[64,4096]{1,0:T(8,128)(2,1)}, u32[]{:S(2)}, u32[]{:S(2)}) collective-permute-start(bf16[64,4096]{1,0:T(8,128)(2,1)} %get-tuple-element.1189), channel_id=1, source_target_pairs={{16,0},{32,16},{48,32},{64,48},{80,64},{96,80},{112,96},{0,112},{1... | collective-permute-start | bytes 1572872 | tf_op jit(solution)/shard_map/while/body/eval_jaxpr/ppermute | solution.py:140
  (17 other events, 114.7 us)
Sparse Core Ops, SparseCore 0:
  566.2 88.6 reduce-scatter.4
  718.2 88.2 reduce-scatter.2

commit v7 on v6

--- a/solution.py
+++ b/solution.py
@@ -9,6 +9,7 @@
 SPLIT = 1
 TK = 128
 TKB = 256
+LANES = 128
 
 
 EPS = 1e-05
@@ -140,11 +141,39 @@
     return lax.ppermute(block, axis, route)
 
 
+def _mask_kernel(m_ref, w_ref, o_ref, *, sub_rows, sub_blocks, groups):
+    lap = pl.program_id(0)
+    rb = pl.program_id(1)
+    half = lax.broadcasted_iota(jnp.int32, (1, LANES), 1) < BLK
+    for s in range(sub_blocks):
+        row = rb * sub_blocks + s
+        pieces = [
+            jnp.where(half, m_ref[lap, row, 2 * v], m_ref[lap, row, 2 * v + 1]).astype(jnp.float32)
+            for v in range(groups)
+        ]
+        keep = jnp.concatenate(pieces, axis=1) if groups > 1 else pieces[0]
+        lo = s * sub_rows
+        block = w_ref[lo:lo + sub_rows, :].astype(jnp.float32)
+        o_ref[lo:lo + sub_rows, :] = (block * keep).astype(o_ref.dtype)
+
+
 def masked(weight, mask):
     laps, rows, cols = weight.shape
-    tiles = weight.reshape(laps, rows // BLK, BLK, cols // BLK, BLK)
-    keep = mask.astype(weight.dtype)[:, :, None, :, None]
-    return (tiles * keep).reshape(laps, rows, cols)
+    tile_rows = 512 if cols <= 512 else 128
+    sub_blocks = tile_rows // BLK
+    groups = cols // LANES
+    kernel = lambda m, w, o: _mask_kernel(m, w, o, sub_rows=BLK, sub_blocks=sub_blocks, groups=groups)
+    return pl.pallas_call(
+        kernel,
+        grid_spec=pltpu.PrefetchScalarGridSpec(
+            num_scalar_prefetch=1,
+            grid=(laps, rows // tile_rows),
+            in_specs=[pl.BlockSpec((None, tile_rows, cols), lambda l, r, m: (l, r, 0))],
+            out_specs=pl.BlockSpec((None, tile_rows, cols), lambda l, r, m: (l, r, 0)),
+        ),
+        out_shape=jax.ShapeDtypeStruct(weight.shape, weight.dtype),
+        compiler_params=pltpu.CompilerParams(dimension_semantics=("arbitrary", "arbitrary"), vmem_limit_bytes=VMEM_LIMIT),
+    )(mask.astype(jnp.int32), weight)
 
 
 def expand_blocks(mask):
@@ -197,18 +226,14 @@
     groups = lax.axis_size("dp")
     owner = lax.axis_index("dp")
     span = normed_all.shape[1] // groups
-    rows = normed_all.shape[0]
-    part_a = jnp.einsum(
-        "rqd,rk->qdk", normed_all.reshape(rows, groups, span), back_all,
-        preferred_element_type=jnp.float32,
-    )
-    part_b = jnp.einsum(
-        "rqd,rk->qdk", upstream_all.reshape(rows, groups, span), hidden_all,
-        preferred_element_type=jnp.float32,
-    )
-    inner = part_a.shape[-1]
-    joined = jnp.concatenate([part_a.astype(jnp.bfloat16), part_b.astype(jnp.bfloat16)], axis=-1)
-    joined = joined.reshape(-1, 2 * inner)
+    part_a = lax.dot_general(
+        normed_all, back_all, (((0,), (0,)), ((), ())), preferred_element_type=jnp.float32
+    )
+    part_b = lax.dot_general(
+        upstream_all, hidden_all, (((0,), (0,)), ((), ())), preferred_element_type=jnp.float32
+    )
+    inner = part_a.shape[1]
+    joined = jnp.concatenate([part_a.astype(jnp.bfloat16), part_b.astype(jnp.bfloat16)], axis=1)
     summed = lax.psum_scatter(joined, "dp", scatter_dimension=0, tiled=True).astype(jnp.float32)
     sum_a, sum_b = summed[:, :inner], summed[:, inner:]
     full_a = expand_blocks(mask_a[lap_idx, 0]).astype(jnp.float32)

time: 822 us -> 742 us (0.903)
  local copies, waits for them, and re-layouts: 118 us -> 28.2 us
  Pallas kernels: 132 us -> 157 us
  other arithmetic: 42.5 us -> 25.1 us
    mul x4 -> x0, local copies, waits for them, and re-layouts: 57.7 us -> none  [masked(): return (tiles * keep).reshape(laps, rows, cols)]
    pallas_call x0 -> x2, Pallas kernels: none -> 24.3 us  [masked(): pl.pallas_call(kernel, grid_spec=pltpu.PrefetchScalarGridSpec(num_scalar_...]
    reshape x2 -> x0, local copies, waits for them, and re-layouts: 22.9 us -> none  [settle(): joined = joined.reshape(-1, 2 * inner)]
    mul x2 -> x0, other arithmetic: 16.4 us -> none  [masked(): return (tiles * keep).reshape(laps, rows, cols)]
  transfers between devices with their start and end apart: 40 -> 40, of which waited for: 39 -> 39; matrix products, arithmetic and copies ran while one was open for 5% -> 4% of each run, Pallas kernels for 5% -> 5%
where the time goes in v7:
time: 742 us; the launch traced here: 741 us
  waiting for transfers between devices  413 us (56%)
  Pallas kernels  157 us (21%)
  starting transfers between devices  86.7 us (12%)
  local copies, waits for them, and re-layouts  28.2 us (4%)
  other arithmetic  25.1 us (3%)
  matrix products  16.5 us (2%)
  between operations  14.3 us (2%)
    ppermute x38, waiting for transfers between devices, shifted(): return lax.ppermute(block, axis, route)  333 us
    ppermute x38, starting transfers between devices, shifted(): return lax.ppermute(block, axis, route)  86.5 us
    reduce_scatter x2, waiting for transfers between devices, settle(): lax.psum_scatter(joined, 'dp', scatter_dimension=0, tiled=True)  79.2 us
    pallas_call x8, Pallas kernels, bwd_call(): pl.pallas_call(_bwd_kernel, grid_spec=pltpu.PrefetchScalarGridSpec(num_sc...  78.3 us
    pallas_call x8, Pallas kernels, fwd_call(): pl.pallas_call(_fwd_kernel, grid_spec=pltpu.PrefetchScalarGridSpec(num_sc...  54.1 us
    pallas_call x2, Pallas kernels, masked(): pl.pallas_call(kernel, grid_spec=pltpu.PrefetchScalarGridSpec(num_scalar_...  24.3 us
    another operation x29, local copies, waits for them, and re-layouts  18 us
    concatenate x2, other arithmetic, settle(): jnp.concatenate([part_a.astype(jnp.bfloat16), part_b.astype(jnp.bfloat16)...  15.7 us
  transfers between devices with their start and end apart: 40, of which 39 were waited for; matrix products, arithmetic and copies ran while one was open for 4% of the time, Pallas kernels for 5%

profile of v7, /device:TPU:0, one launch (start us, length us, event | category | flops | bytes accessed | tf_op | source)
XLA Modules:
  0.0 740.7 jit_solution(3123874399970644984)
XLA Ops:
  8.0 14.2 %shard_map.77 = bf16[2,4096,512]{2,1,0:T(8,128)(2,1)} custom-call(s32[2,64,8]{2,1,0:T(8,128)S(1)} %bitcast.109, bf16[2,4096,512]{2,1,0:T(8,128)(2,1)} %bitcast.115), custom_call_target="tpu_custom_call" | custom-call | tf_op jit(solution)/shard_map/pallas_call | solution.py:166
  22.2 10.2 %shard_map.78 = bf16[2,512,4096]{2,1,0:T(8,128)(2,1)} custom-call(s32[2,8,64]{2,1,0:T(8,128)S(1)} %bitcast.110, bf16[2,512,4096]{2,1,0:T(8,128)(2,1)} %bitcast.116), custom_call_target="tpu_custom_call" | custom-call | tf_op jit(solution)/shard_map/pallas_call | solution.py:166
  35.0 257.8 %while.66 = (s32[]{:T(128)}, bf16[64,4096]{1,0:T(8,128)(2,1)S(1)}, bf16[2,4,64,4096]{3,2,1,0:T(8,128)(2,1)}, s32[]{:T(128)}, pred[]{:T(512)}, /*index=5*/bf16[4,...) while((s32[]{:T(128)}, bf16[64,4096]{1,0:T(8,128)(2,1)S(1)}, ...), condition=%wide.region_3.4_spmd, body=%wide.region_0.3_spmd.sunk | while | flops 31 | bytes 2621852 | solution.py:293
  41.8 9.8 %collective-permute-done = bf16[64,4096]{1,0:T(8,128)(2,1)S(1)} collective-permute-done((bf16[64,4096]{1,0:T(8,128)(2,1)S(1)}, bf16[64,4096]{1,0:T(8,128)(2,1)S(1)}, u32[]{:S(2)}, u32[]{:S(2)}) %collective-permute-start) | collective-permute-done | bytes 524320 | tf_op jit(solution)/shard_map/while/body/eval_jaxpr/ppermute | solution.py:141
  58.4 9.8 %collective-permute-done = bf16[64,4096]{1,0:T(8,128)(2,1)S(1)} collective-permute-done((bf16[64,4096]{1,0:T(8,128)(2,1)S(1)}, bf16[64,4096]{1,0:T(8,128)(2,1)S(1)}, u32[]{:S(2)}, u32[]{:S(2)}) %collective-permute-start) | collective-permute-done | bytes 524320 | tf_op jit(solution)/shard_map/while/body/eval_jaxpr/ppermute | solution.py:141
  75.1 9.8 %collective-permute-done = bf16[64,4096]{1,0:T(8,128)(2,1)S(1)} collective-permute-done((bf16[64,4096]{1,0:T(8,128)(2,1)S(1)}, bf16[64,4096]{1,0:T(8,128)(2,1)S(1)}, u32[]{:S(2)}, u32[]{:S(2)}) %collective-permute-start) | collective-permute-done | bytes 524320 | tf_op jit(solution)/shard_map/while/body/eval_jaxpr/ppermute | solution.py:141
  91.8 9.8 %collective-permute-done = bf16[64,4096]{1,0:T(8,128)(2,1)S(1)} collective-permute-done((bf16[64,4096]{1,0:T(8,128)(2,1)S(1)}, bf16[64,4096]{1,0:T(8,128)(2,1)S(1)}, u32[]{:S(2)}, u32[]{:S(2)}) %collective-permute-start) | collective-permute-done | bytes 524320 | tf_op jit(solution)/shard_map/while/body/eval_jaxpr/ppermute | solution.py:141
  101.7 9.8 %collective-permute-done = bf16[64,4096]{1,0:T(8,128)(2,1)S(1)} collective-permute-done((bf16[64,4096]{1,0:T(8,128)(2,1)S(1)}, bf16[64,4096]{1,0:T(8,128)(2,1)S(1)}, u32[]{:S(2)}, u32[]{:S(2)}) %collective-permute-start) | collective-permute-done | bytes 524320 | tf_op jit(solution)/shard_map/while/body/eval_jaxpr/ppermute | solution.py:141
  111.7 9.8 %collective-permute-done = bf16[64,4096]{1,0:T(8,128)(2,1)S(1)} collective-permute-done((bf16[64,4096]{1,0:T(8,128)(2,1)S(1)}, bf16[64,4096]{1,0:T(8,128)(2,1)S(1)}, u32[]{:S(2)}, u32[]{:S(2)}) %collective-permute-start) | collective-permute-done | bytes 524320 | tf_op jit(solution)/shard_map/while/body/eval_jaxpr/ppermute | solution.py:141
  131.6 12.8 %collective-permute-done = bf16[64,4096]{1,0:T(8,128)(2,1)S(1)} collective-permute-done((bf16[64,4096]{1,0:T(8,128)(2,1)S(1)}, bf16[64,4096]{1,0:T(8,128)(2,1)S(1)}, u32[]{:S(2)}, u32[]{:S(2)}) %collective-permute-start) | collective-permute-done | bytes 524320 | tf_op jit(solution)/shard_map/while/body/eval_jaxpr/ppermute | solution.py:141
  151.3 9.8 %collective-permute-done = bf16[64,4096]{1,0:T(8,128)(2,1)S(1)} collective-permute-done((bf16[64,4096]{1,0:T(8,128)(2,1)S(1)}, bf16[64,4096]{1,0:T(8,128)(2,1)S(1)}, u32[]{:S(2)}, u32[]{:S(2)}) %collective-permute-start) | collective-permute-done | bytes 524320 | tf_op jit(solution)/shard_map/while/body/eval_jaxpr/ppermute | solution.py:141
  167.9 9.8 %collective-permute-done = bf16[64,4096]{1,0:T(8,128)(2,1)S(1)} collective-permute-done((bf16[64,4096]{1,0:T(8,128)(2,1)S(1)}, bf16[64,4096]{1,0:T(8,128)(2,1)S(1)}, u32[]{:S(2)}, u32[]{:S(2)}) %collective-permute-start) | collective-permute-done | bytes 524320 | tf_op jit(solution)/shard_map/while/body/eval_jaxpr/ppermute | solution.py:141
  184.6 9.8 %collective-permute-done = bf16[64,4096]{1,0:T(8,128)(2,1)S(1)} collective-permute-done((bf16[64,4096]{1,0:T(8,128)(2,1)S(1)}, bf16[64,4096]{1,0:T(8,128)(2,1)S(1)}, u32[]{:S(2)}, u32[]{:S(2)}) %collective-permute-start) | collective-permute-done | bytes 524320 | tf_op jit(solution)/shard_map/while/body/eval_jaxpr/ppermute | solution.py:141
  201.2 9.8 %collective-permute-done = bf16[64,4096]{1,0:T(8,128)(2,1)S(1)} collective-permute-done((bf16[64,4096]{1,0:T(8,128)(2,1)S(1)}, bf16[64,4096]{1,0:T(8,128)(2,1)S(1)}, u32[]{:S(2)}, u32[]{:S(2)}) %collective-permute-start) | collective-permute-done | bytes 524320 | tf_op jit(solution)/shard_map/while/body/eval_jaxpr/ppermute | solution.py:141
  211.2 9.8 %collective-permute-done = bf16[64,4096]{1,0:T(8,128)(2,1)S(1)} collective-permute-done((bf16[64,4096]{1,0:T(8,128)(2,1)S(1)}, bf16[64,4096]{1,0:T(8,128)(2,1)S(1)}, u32[]{:S(2)}, u32[]{:S(2)}) %collective-permute-start) | collective-permute-done | bytes 524320 | tf_op jit(solution)/shard_map/while/body/eval_jaxpr/ppermute | solution.py:141
  221.2 9.8 %collective-permute-done = bf16[64,4096]{1,0:T(8,128)(2,1)S(1)} collective-permute-done((bf16[64,4096]{1,0:T(8,128)(2,1)S(1)}, bf16[64,4096]{1,0:T(8,128)(2,1)S(1)}, u32[]{:S(2)}, u32[]{:S(2)}) %collective-permute-start) | collective-permute-done | bytes 524320 | tf_op jit(solution)/shard_map/while/body/eval_jaxpr/ppermute | solution.py:141
  241.1 12.8 %collective-permute-done = bf16[64,4096]{1,0:T(8,128)(2,1)S(1)} collective-permute-done((bf16[64,4096]{1,0:T(8,128)(2,1)S(1)}, bf16[64,4096]{1,0:T(8,128)(2,1)S(1)}, u32[]{:S(2)}, u32[]{:S(2)}) %collective-permute-start) | collective-permute-done | bytes 524320 | tf_op jit(solution)/shard_map/while/body/eval_jaxpr/ppermute | solution.py:141
  254.0 12.8 %collective-permute-done = bf16[64,4096]{1,0:T(8,128)(2,1)S(1)} collective-permute-done((bf16[64,4096]{1,0:T(8,128)(2,1)S(1)}, bf16[64,4096]{1,0:T(8,128)(2,1)S(1)}, u32[]{:S(2)}, u32[]{:S(2)}) %collective-permute-start) | collective-permute-done | bytes 524320 | tf_op jit(solution)/shard_map/while/body/eval_jaxpr/ppermute | solution.py:141
  267.0 12.8 %collective-permute-done = bf16[64,4096]{1,0:T(8,128)(2,1)S(1)} collective-permute-done((bf16[64,4096]{1,0:T(8,128)(2,1)S(1)}, bf16[64,4096]{1,0:T(8,128)(2,1)S(1)}, u32[]{:S(2)}, u32[]{:S(2)}) %collective-permute-start) | collective-permute-done | bytes 524320 | tf_op jit(solution)/shard_map/while/body/eval_jaxpr/ppermute | solution.py:141
  280.0 12.8 %collective-permute-done = bf16[64,4096]{1,0:T(8,128)(2,1)S(1)} collective-permute-done((bf16[64,4096]{1,0:T(8,128)(2,1)S(1)}, bf16[64,4096]{1,0:T(8,128)(2,1)S(1)}, u32[]{:S(2)}, u32[]{:S(2)}) %collective-permute-start) | collective-permute-done | bytes 524320 | tf_op jit(solution)/shard_map/while/body/eval_jaxpr/ppermute | solution.py:141
  298.7 185.7 %while.67 = (s32[]{:T(128)}, bf16[64,4096]{1,0:T(8,128)(2,1)}, bf16[2,4,64,4096]{3,2,1,0:T(8,128)(2,1)}, bf16[2,4,64,4096]{3,2,1,0:T(8,128)(2,1)}, bf16[2,4,64,5...) while((s32[]{:T(128)}, bf16[64,4096]{1,0:T(8,128)(2,1)}, ...), condition=%wide.region_7.8_spmd, body=%wide.region_4.7_spmd.sunk | while | flops 31 | bytes 2621980 | solution.py:341
  315.7 12.0 %collective-permute-start.1 = (bf16[64,4096]{1,0:T(8,128)(2,1)}, bf16[64,4096]{1,0:T(8,128)(2,1)}, u32[]{:S(2)}, u32[]{:S(2)}) collective-permute-start(bf16[64,4096]{1,0:T(8,128)(2,1)} %get-tuple-element.1172), channel_id=1, source_target_pairs={{16,0},{32,16},{48,32},{64,48},{80,64},{96,80},{112,96},{0,112},{1... | collective-permute-start | bytes 1572872 | tf_op jit(solution)/shard_map/while/body/eval_jaxpr/ppermute | solution.py:141
  335.6 12.0 %collective-permute-start.1 = (bf16[64,4096]{1,0:T(8,128)(2,1)}, bf16[64,4096]{1,0:T(8,128)(2,1)}, u32[]{:S(2)}, u32[]{:S(2)}) collective-permute-start(bf16[64,4096]{1,0:T(8,128)(2,1)} %get-tuple-element.1172), channel_id=1, source_target_pairs={{16,0},{32,16},{48,32},{64,48},{80,64},{96,80},{112,96},{0,112},{1... | collective-permute-start | bytes 1572872 | tf_op jit(solution)/shard_map/while/body/eval_jaxpr/ppermute | solution.py:141
  355.6 12.0 %collective-permute-start.1 = (bf16[64,4096]{1,0:T(8,128)(2,1)}, bf16[64,4096]{1,0:T(8,128)(2,1)}, u32[]{:S(2)}, u32[]{:S(2)}) collective-permute-start(bf16[64,4096]{1,0:T(8,128)(2,1)} %get-tuple-element.1172), channel_id=1, source_target_pairs={{16,0},{32,16},{48,32},{64,48},{80,64},{96,80},{112,96},{0,112},{1... | collective-permute-start | bytes 1572872 | tf_op jit(solution)/shard_map/while/body/eval_jaxpr/ppermute | solution.py:141
  464.6 9.7 %conditional.7 = ((bf16[64,4096]{1,0:T(8,128)(2,1)}, bf16[2,4,64,4096]{3,2,1,0:T(8,128)(2,1)}, bf16[2,4,64,4096]{3,2,1,0:T(8,128)(2,1)}, bf16[2,4,64,512]{3,2,1,0:T(8,128)(2,1)S(1)}, bf16[2,4,64,512]{3,2,1,0:T(8,128)(2,1)S(1)})) conditional(s32[]{:T(128)} %convert_element_type.174, (bf16[2,4,64,4096]{3,2,1,0:T(8,128)(2,1)}, ...), branch_computations={%region_5.5_spmd, %region_6.6_spmd} | conditional | bytes 524338 | solution.py:325
  500.8 121.7 %while.68 = (s32[]{:T(128)}, bf16[64,4096]{1,0:T(8,128)(2,1)}, bf16[2,4,64,4096]{3,2,1,0:T(8,128)(2,1)}, bf16[2,4,64,4096]{3,2,1,0:T(8,128)(2,1)}, bf16[2,4,64,5...) while((s32[]{:T(128)}, bf16[64,4096]{1,0:T(8,128)(2,1)}, ...), condition=%wide.region_11.12_spmd, body=%wide.region_8.11_spmd.sunk | while | flops 32 | bytes 2622000 | solution.py:343
  501.7 12.0 %collective-permute-start.2 = (bf16[64,4096]{1,0:T(8,128)(2,1)}, bf16[64,4096]{1,0:T(8,128)(2,1)}, u32[]{:S(2)}, u32[]{:S(2)}) collective-permute-start(bf16[64,4096]{1,0:T(8,128)(2,1)} %get-tuple-element.1189), channel_id=1, source_target_pairs={{16,0},{32,16},{48,32},{64,48},{80,64},{96,80},{112,96},{0,112},{1... | collective-permute-start | bytes 1572872 | tf_op jit(solution)/shard_map/while/body/eval_jaxpr/ppermute | solution.py:141
  554.8 9.8 %conditional.8 = ((bf16[64,4096]{1,0:T(8,128)(2,1)}, bf16[2,4,64,4096]{3,2,1,0:T(8,128)(2,1)}, bf16[2,4,64,4096]{3,2,1,0:T(8,128)(2,1)}, bf16[2,4,64,512]{3,2,1,0:T(8,128)(2,1)S(1)}, bf16[2,4,64,512]{3,2,1,0:T(8,128)(2,1)S(1)})) conditional(s32[]{:T(128)} %convert_element_type.175, (bf16[2,4,64,4096]{3,2,1,0:T(8,128)(2,1)}, ...), branch_computations={%region_9.9_spmd, %region_10.10_spmd} | conditional | bytes 524338 | solution.py:325
  554.8 9.8 %branch_1_fun.5 = (bf16[64,4096]{1,0:T(8,128)(2,1)}, bf16[2,4,64,4096]{3,2,1,0:T(8,128)(2,1)}, bf16[2,4,64,4096]{3,2,1,0:T(8,128)(2,1)}, bf16[2,4,64,512]{3,2,1,0:T(8,128)(2,1)S(1)}, bf16[2,4,64,512]{3,2,1,0:T(8,128)(2,1)S(1)}) custom-call(s32[4]{0:T(128)S(1)} %get-tuple-element.853.sc_ref, ...), custom_call_target="tpu_custom_call", output_to_operand_aliasing={{1}: (6, {}), {2}: (7, {}), {3}: (8, {}), {4}: (9, {})} | custom-call | tf_op jit(solution)/shard_map/while/body/eval_jaxpr/cond/branch_1_fun/pallas_call | solution.py:110
  571.7 10.1 %conditional.8 = ((bf16[64,4096]{1,0:T(8,128)(2,1)}, bf16[2,4,64,4096]{3,2,1,0:T(8,128)(2,1)}, bf16[2,4,64,4096]{3,2,1,0:T(8,128)(2,1)}, bf16[2,4,64,512]{3,2,1,0:T(8,128)(2,1)S(1)}, bf16[2,4,64,512]{3,2,1,0:T(8,128)(2,1)S(1)})) conditional(s32[]{:T(128)} %convert_element_type.175, (bf16[2,4,64,4096]{3,2,1,0:T(8,128)(2,1)}, ...), branch_computations={%region_9.9_spmd, %region_10.10_spmd} | conditional | bytes 524338 | solution.py:325
  571.7 10.1 %branch_1_fun.5 = (bf16[64,4096]{1,0:T(8,128)(2,1)}, bf16[2,4,64,4096]{3,2,1,0:T(8,128)(2,1)}, bf16[2,4,64,4096]{3,2,1,0:T(8,128)(2,1)}, bf16[2,4,64,512]{3,2,1,0:T(8,128)(2,1)S(1)}, bf16[2,4,64,512]{3,2,1,0:T(8,128)(2,1)S(1)}) custom-call(s32[4]{0:T(128)S(1)} %get-tuple-element.853.sc_ref, ...), custom_call_target="tpu_custom_call", output_to_operand_aliasing={{1}: (6, {}), {2}: (7, {}), {3}: (8, {}), {4}: (9, {})} | custom-call | tf_op jit(solution)/shard_map/while/body/eval_jaxpr/cond/branch_1_fun/pallas_call | solution.py:110
  647.7 79.2 %reduce-scatter.3.cloned.1.call-done = bf16[256,1024]{0,1:T(8,128)(2,1)} async-done(((bf16[4096,1024]{0,1:T(8,128)(2,1)}), bf16[256,1024]{0,1:T(8,128)(2,1)}) %reduce-scatter.3.cloned.1.call-update) | async-done | bytes 524304 | tf_op jit(solution)/shard_map/reduce_scatter | solution.py:237
  (228 shorter events, 485.0 us)
Async XLA Ops:
  7.2 637.6 %reduce-scatter.5.cloned.1.call-start = ((), (), s32[]{:S(2)}) async-start(), calls=%async_computation.3 | async-start | bytes 8912896 | tf_op jit(solution)/shard_map/reduce_scatter | solution.py:237
  41.8 9.8 %collective-permute-start = (bf16[64,4096]{1,0:T(8,128)(2,1)S(1)}, bf16[64,4096]{1,0:T(8,128)(2,1)S(1)}, u32[]{:S(2)}, u32[]{:S(2)}) collective-permute-start(bf16[64,4096]{1,0:T(8,128)(2,1)S(1)} %get-tuple-element.1158), channel_id=1, source_target_pairs={{112,0},{0,16},{16,32},{32,48},{48,64},{64,80},{80,96},{96,112},{1... | collective-permute-start | bytes 1572872 | tf_op jit(solution)/shard_map/while/body/eval_jaxpr/ppermute | solution.py:141
  58.4 9.8 %collective-permute-start = (bf16[64,4096]{1,0:T(8,128)(2,1)S(1)}, bf16[64,4096]{1,0:T(8,128)(2,1)S(1)}, u32[]{:S(2)}, u32[]{:S(2)}) collective-permute-start(bf16[64,4096]{1,0:T(8,128)(2,1)S(1)} %get-tuple-element.1158), channel_id=1, source_target_pairs={{112,0},{0,16},{16,32},{32,48},{48,64},{64,80},{80,96},{96,112},{1... | collective-permute-start | bytes 1572872 | tf_op jit(solution)/shard_map/while/body/eval_jaxpr/ppermute | solution.py:141
  75.1 9.8 %collective-permute-start = (bf16[64,4096]{1,0:T(8,128)(2,1)S(1)}, bf16[64,4096]{1,0:T(8,128)(2,1)S(1)}, u32[]{:S(2)}, u32[]{:S(2)}) collective-permute-start(bf16[64,4096]{1,0:T(8,128)(2,1)S(1)} %get-tuple-element.1158), channel_id=1, source_target_pairs={{112,0},{0,16},{16,32},{32,48},{48,64},{64,80},{80,96},{96,112},{1... | collective-permute-start | bytes 1572872 | tf_op jit(solution)/shard_map/while/body/eval_jaxpr/ppermute | solution.py:141
  91.8 9.8 %collective-permute-start = (bf16[64,4096]{1,0:T(8,128)(2,1)S(1)}, bf16[64,4096]{1,0:T(8,128)(2,1)S(1)}, u32[]{:S(2)}, u32[]{:S(2)}) collective-permute-start(bf16[64,4096]{1,0:T(8,128)(2,1)S(1)} %get-tuple-element.1158), channel_id=1, source_target_pairs={{112,0},{0,16},{16,32},{32,48},{48,64},{64,80},{80,96},{96,112},{1... | collective-permute-start | bytes 1572872 | tf_op jit(solution)/shard_map/while/body/eval_jaxpr/ppermute | solution.py:141
  101.7 9.8 %collective-permute-start = (bf16[64,4096]{1,0:T(8,128)(2,1)S(1)}, bf16[64,4096]{1,0:T(8,128)(2,1)S(1)}, u32[]{:S(2)}, u32[]{:S(2)}) collective-permute-start(bf16[64,4096]{1,0:T(8,128)(2,1)S(1)} %get-tuple-element.1158), channel_id=1, source_target_pairs={{112,0},{0,16},{16,32},{32,48},{48,64},{64,80},{80,96},{96,112},{1... | collective-permute-start | bytes 1572872 | tf_op jit(solution)/shard_map/while/body/eval_jaxpr/ppermute | solution.py:141
  111.7 9.8 %collective-permute-start = (bf16[64,4096]{1,0:T(8,128)(2,1)S(1)}, bf16[64,4096]{1,0:T(8,128)(2,1)S(1)}, u32[]{:S(2)}, u32[]{:S(2)}) collective-permute-start(bf16[64,4096]{1,0:T(8,128)(2,1)S(1)} %get-tuple-element.1158), channel_id=1, source_target_pairs={{112,0},{0,16},{16,32},{32,48},{48,64},{64,80},{80,96},{96,112},{1... | collective-permute-start | bytes 1572872 | tf_op jit(solution)/shard_map/while/body/eval_jaxpr/ppermute | solution.py:141
  121.6 9.8 %collective-permute-start = (bf16[64,4096]{1,0:T(8,128)(2,1)S(1)}, bf16[64,4096]{1,0:T(8,128)(2,1)S(1)}, u32[]{:S(2)}, u32[]{:S(2)}) collective-permute-start(bf16[64,4096]{1,0:T(8,128)(2,1)S(1)} %get-tuple-element.1158), channel_id=1, source_target_pairs={{112,0},{0,16},{16,32},{32,48},{48,64},{64,80},{80,96},{96,112},{1... | collective-permute-start | bytes 1572872 | tf_op jit(solution)/shard_map/while/body/eval_jaxpr/ppermute | solution.py:141
  131.6 12.8 %collective-permute-start = (bf16[64,4096]{1,0:T(8,128)(2,1)S(1)}, bf16[64,4096]{1,0:T(8,128)(2,1)S(1)}, u32[]{:S(2)}, u32[]{:S(2)}) collective-permute-start(bf16[64,4096]{1,0:T(8,128)(2,1)S(1)} %get-tuple-element.1158), channel_id=1, source_target_pairs={{112,0},{0,16},{16,32},{32,48},{48,64},{64,80},{80,96},{96,112},{1... | collective-permute-start | bytes 1572872 | tf_op jit(solution)/shard_map/while/body/eval_jaxpr/ppermute | solution.py:141
  151.3 9.8 %collective-permute-start = (bf16[64,4096]{1,0:T(8,128)(2,1)S(1)}, bf16[64,4096]{1,0:T(8,128)(2,1)S(1)}, u32[]{:S(2)}, u32[]{:S(2)}) collective-permute-start(bf16[64,4096]{1,0:T(8,128)(2,1)S(1)} %get-tuple-element.1158), channel_id=1, source_target_pairs={{112,0},{0,16},{16,32},{32,48},{48,64},{64,80},{80,96},{96,112},{1... | collective-permute-start | bytes 1572872 | tf_op jit(solution)/shard_map/while/body/eval_jaxpr/ppermute | solution.py:141
  211.2 9.8 %collective-permute-start = (bf16[64,4096]{1,0:T(8,128)(2,1)S(1)}, bf16[64,4096]{1,0:T(8,128)(2,1)S(1)}, u32[]{:S(2)}, u32[]{:S(2)}) collective-permute-start(bf16[64,4096]{1,0:T(8,128)(2,1)S(1)} %get-tuple-element.1158), channel_id=1, source_target_pairs={{112,0},{0,16},{16,32},{32,48},{48,64},{64,80},{80,96},{96,112},{1... | collective-permute-start | bytes 1572872 | tf_op jit(solution)/shard_map/while/body/eval_jaxpr/ppermute | solution.py:141
  221.1 9.8 %collective-permute-start = (bf16[64,4096]{1,0:T(8,128)(2,1)S(1)}, bf16[64,4096]{1,0:T(8,128)(2,1)S(1)}, u32[]{:S(2)}, u32[]{:S(2)}) collective-permute-start(bf16[64,4096]{1,0:T(8,128)(2,1)S(1)} %get-tuple-element.1158), channel_id=1, source_target_pairs={{112,0},{0,16},{16,32},{32,48},{48,64},{64,80},{80,96},{96,112},{1... | collective-permute-start | bytes 1572872 | tf_op jit(solution)/shard_map/while/body/eval_jaxpr/ppermute | solution.py:141
  231.1 9.8 %collective-permute-start = (bf16[64,4096]{1,0:T(8,128)(2,1)S(1)}, bf16[64,4096]{1,0:T(8,128)(2,1)S(1)}, u32[]{:S(2)}, u32[]{:S(2)}) collective-permute-start(bf16[64,4096]{1,0:T(8,128)(2,1)S(1)} %get-tuple-element.1158), channel_id=1, source_target_pairs={{112,0},{0,16},{16,32},{32,48},{48,64},{64,80},{80,96},{96,112},{1... | collective-permute-start | bytes 1572872 | tf_op jit(solution)/shard_map/while/body/eval_jaxpr/ppermute | solution.py:141
  241.1 12.8 %collective-permute-start = (bf16[64,4096]{1,0:T(8,128)(2,1)S(1)}, bf16[64,4096]{1,0:T(8,128)(2,1)S(1)}, u32[]{:S(2)}, u32[]{:S(2)}) collective-permute-start(bf16[64,4096]{1,0:T(8,128)(2,1)S(1)} %get-tuple-element.1158), channel_id=1, source_target_pairs={{112,0},{0,16},{16,32},{32,48},{48,64},{64,80},{80,96},{96,112},{1... | collective-permute-start | bytes 1572872 | tf_op jit(solution)/shard_map/while/body/eval_jaxpr/ppermute | solution.py:141
  254.0 12.8 %collective-permute-start = (bf16[64,4096]{1,0:T(8,128)(2,1)S(1)}, bf16[64,4096]{1,0:T(8,128)(2,1)S(1)}, u32[]{:S(2)}, u32[]{:S(2)}) collective-permute-start(bf16[64,4096]{1,0:T(8,128)(2,1)S(1)} %get-tuple-element.1158), channel_id=1, source_target_pairs={{112,0},{0,16},{16,32},{32,48},{48,64},{64,80},{80,96},{96,112},{1... | collective-permute-start | bytes 1572872 | tf_op jit(solution)/shard_map/while/body/eval_jaxpr/ppermute | solution.py:141
  267.0 12.9 %collective-permute-start = (bf16[64,4096]{1,0:T(8,128)(2,1)S(1)}, bf16[64,4096]{1,0:T(8,128)(2,1)S(1)}, u32[]{:S(2)}, u32[]{:S(2)}) collective-permute-start(bf16[64,4096]{1,0:T(8,128)(2,1)S(1)} %get-tuple-element.1158), channel_id=1, source_target_pairs={{112,0},{0,16},{16,32},{32,48},{48,64},{64,80},{80,96},{96,112},{1... | collective-permute-start | bytes 1572872 | tf_op jit(solution)/shard_map/while/body/eval_jaxpr/ppermute | solution.py:141
  280.0 12.8 %collective-permute-start = (bf16[64,4096]{1,0:T(8,128)(2,1)S(1)}, bf16[64,4096]{1,0:T(8,128)(2,1)S(1)}, u32[]{:S(2)}, u32[]{:S(2)}) collective-permute-start(bf16[64,4096]{1,0:T(8,128)(2,1)S(1)} %get-tuple-element.1158), channel_id=1, source_target_pairs={{112,0},{0,16},{16,32},{32,48},{48,64},{64,80},{80,96},{96,112},{1... | collective-permute-start | bytes 1572872 | tf_op jit(solution)/shard_map/while/body/eval_jaxpr/ppermute | solution.py:141
  299.6 15.2 %collective-permute-start.1 = (bf16[64,4096]{1,0:T(8,128)(2,1)}, bf16[64,4096]{1,0:T(8,128)(2,1)}, u32[]{:S(2)}, u32[]{:S(2)}) collective-permute-start(bf16[64,4096]{1,0:T(8,128)(2,1)} %get-tuple-element.1172), channel_id=1, source_target_pairs={{16,0},{32,16},{48,32},{64,48},{80,64},{96,80},{112,96},{0,112},{1... | collective-permute-start | bytes 1572872 | tf_op jit(solution)/shard_map/while/body/eval_jaxpr/ppermute | solution.py:141
  315.7 19.0 %collective-permute-start.1 = (bf16[64,4096]{1,0:T(8,128)(2,1)}, bf16[64,4096]{1,0:T(8,128)(2,1)}, u32[]{:S(2)}, u32[]{:S(2)}) collective-permute-start(bf16[64,4096]{1,0:T(8,128)(2,1)} %get-tuple-element.1172), channel_id=1, source_target_pairs={{16,0},{32,16},{48,32},{64,48},{80,64},{96,80},{112,96},{0,112},{1... | collective-permute-start | bytes 1572872 | tf_op jit(solution)/shard_map/while/body/eval_jaxpr/ppermute | solution.py:141
  335.6 19.0 %collective-permute-start.1 = (bf16[64,4096]{1,0:T(8,128)(2,1)}, bf16[64,4096]{1,0:T(8,128)(2,1)}, u32[]{:S(2)}, u32[]{:S(2)}) collective-permute-start(bf16[64,4096]{1,0:T(8,128)(2,1)} %get-tuple-element.1172), channel_id=1, source_target_pairs={{16,0},{32,16},{48,32},{64,48},{80,64},{96,80},{112,96},{0,112},{1... | collective-permute-start | bytes 1572872 | tf_op jit(solution)/shard_map/while/body/eval_jaxpr/ppermute | solution.py:141
  355.6 19.0 %collective-permute-start.1 = (bf16[64,4096]{1,0:T(8,128)(2,1)}, bf16[64,4096]{1,0:T(8,128)(2,1)}, u32[]{:S(2)}, u32[]{:S(2)}) collective-permute-start(bf16[64,4096]{1,0:T(8,128)(2,1)} %get-tuple-element.1172), channel_id=1, source_target_pairs={{16,0},{32,16},{48,32},{64,48},{80,64},{96,80},{112,96},{0,112},{1... | collective-permute-start | bytes 1572872 | tf_op jit(solution)/shard_map/while/body/eval_jaxpr/ppermute | solution.py:141
  375.5 10.1 %collective-permute-start.1 = (bf16[64,4096]{1,0:T(8,128)(2,1)}, bf16[64,4096]{1,0:T(8,128)(2,1)}, u32[]{:S(2)}, u32[]{:S(2)}) collective-permute-start(bf16[64,4096]{1,0:T(8,128)(2,1)} %get-tuple-element.1172), channel_id=1, source_target_pairs={{16,0},{32,16},{48,32},{64,48},{80,64},{96,80},{112,96},{0,112},{1... | collective-permute-start | bytes 1572872 | tf_op jit(solution)/shard_map/while/body/eval_jaxpr/ppermute | solution.py:141
  386.6 10.1 %collective-permute-start.1 = (bf16[64,4096]{1,0:T(8,128)(2,1)}, bf16[64,4096]{1,0:T(8,128)(2,1)}, u32[]{:S(2)}, u32[]{:S(2)}) collective-permute-start(bf16[64,4096]{1,0:T(8,128)(2,1)} %get-tuple-element.1172), channel_id=1, source_target_pairs={{16,0},{32,16},{48,32},{64,48},{80,64},{96,80},{112,96},{0,112},{1... | collective-permute-start | bytes 1572872 | tf_op jit(solution)/shard_map/while/body/eval_jaxpr/ppermute | solution.py:141
  397.6 10.1 %collective-permute-start.1 = (bf16[64,4096]{1,0:T(8,128)(2,1)}, bf16[64,4096]{1,0:T(8,128)(2,1)}, u32[]{:S(2)}, u32[]{:S(2)}) collective-permute-start(bf16[64,4096]{1,0:T(8,128)(2,1)} %get-tuple-element.1172), channel_id=1, source_target_pairs={{16,0},{32,16},{48,32},{64,48},{80,64},{96,80},{112,96},{0,112},{1... | collective-permute-start | bytes 1572872 | tf_op jit(solution)/shard_map/while/body/eval_jaxpr/ppermute | solution.py:141
  434.4 10.2 %collective-permute-start.1 = (bf16[64,4096]{1,0:T(8,128)(2,1)}, bf16[64,4096]{1,0:T(8,128)(2,1)}, u32[]{:S(2)}, u32[]{:S(2)}) collective-permute-start(bf16[64,4096]{1,0:T(8,128)(2,1)} %get-tuple-element.1172), channel_id=1, source_target_pairs={{16,0},{32,16},{48,32},{64,48},{80,64},{96,80},{112,96},{0,112},{1... | collective-permute-start | bytes 1572872 | tf_op jit(solution)/shard_map/while/body/eval_jaxpr/ppermute | solution.py:141
  454.4 10.1 %collective-permute-start.1 = (bf16[64,4096]{1,0:T(8,128)(2,1)}, bf16[64,4096]{1,0:T(8,128)(2,1)}, u32[]{:S(2)}, u32[]{:S(2)}) collective-permute-start(bf16[64,4096]{1,0:T(8,128)(2,1)} %get-tuple-element.1172), channel_id=1, source_target_pairs={{16,0},{32,16},{48,32},{64,48},{80,64},{96,80},{112,96},{0,112},{1... | collective-permute-start | bytes 1572872 | tf_op jit(solution)/shard_map/while/body/eval_jaxpr/ppermute | solution.py:141
  474.3 10.1 %collective-permute-start.1 = (bf16[64,4096]{1,0:T(8,128)(2,1)}, bf16[64,4096]{1,0:T(8,128)(2,1)}, u32[]{:S(2)}, u32[]{:S(2)}) collective-permute-start(bf16[64,4096]{1,0:T(8,128)(2,1)} %get-tuple-element.1172), channel_id=1, source_target_pairs={{16,0},{32,16},{48,32},{64,48},{80,64},{96,80},{112,96},{0,112},{1... | collective-permute-start | bytes 1572872 | tf_op jit(solution)/shard_map/while/body/eval_jaxpr/ppermute | solution.py:141
  500.5 226.4 %reduce-scatter.3.cloned.1.call-start = ((), (), s32[]{:S(2)}) async-start(), calls=%async_computation.2 | async-start | bytes 8912896 | tf_op jit(solution)/shard_map/reduce_scatter | solution.py:237
  501.7 19.0 %collective-permute-start.2 = (bf16[64,4096]{1,0:T(8,128)(2,1)}, bf16[64,4096]{1,0:T(8,128)(2,1)}, u32[]{:S(2)}, u32[]{:S(2)}) collective-permute-start(bf16[64,4096]{1,0:T(8,128)(2,1)} %get-tuple-element.1189), channel_id=1, source_target_pairs={{16,0},{32,16},{48,32},{64,48},{80,64},{96,80},{112,96},{0,112},{1... | collective-permute-start | bytes 1572872 | tf_op jit(solution)/shard_map/while/body/eval_jaxpr/ppermute | solution.py:141
  521.7 10.4 %collective-permute-start.2 = (bf16[64,4096]{1,0:T(8,128)(2,1)}, bf16[64,4096]{1,0:T(8,128)(2,1)}, u32[]{:S(2)}, u32[]{:S(2)}) collective-permute-start(bf16[64,4096]{1,0:T(8,128)(2,1)} %get-tuple-element.1189), channel_id=1, source_target_pairs={{16,0},{32,16},{48,32},{64,48},{80,64},{96,80},{112,96},{0,112},{1... | collective-permute-start | bytes 1572872 | tf_op jit(solution)/shard_map/while/body/eval_jaxpr/ppermute | solution.py:141
  533.0 10.4 %collective-permute-start.2 = (bf16[64,4096]{1,0:T(8,128)(2,1)}, bf16[64,4096]{1,0:T(8,128)(2,1)}, u32[]{:S(2)}, u32[]{:S(2)}) collective-permute-start(bf16[64,4096]{1,0:T(8,128)(2,1)} %get-tuple-element.1189), channel_id=1, source_target_pairs={{16,0},{32,16},{48,32},{64,48},{80,64},{96,80},{112,96},{0,112},{1... | collective-permute-start | bytes 1572872 | tf_op jit(solution)/shard_map/while/body/eval_jaxpr/ppermute | solution.py:141
  544.3 10.4 %collective-permute-start.2 = (bf16[64,4096]{1,0:T(8,128)(2,1)}, bf16[64,4096]{1,0:T(8,128)(2,1)}, u32[]{:S(2)}, u32[]{:S(2)}) collective-permute-start(bf16[64,4096]{1,0:T(8,128)(2,1)} %get-tuple-element.1189), channel_id=1, source_target_pairs={{16,0},{32,16},{48,32},{64,48},{80,64},{96,80},{112,96},{0,112},{1... | collective-permute-start | bytes 1572872 | tf_op jit(solution)/shard_map/while/body/eval_jaxpr/ppermute | solution.py:141
  (16 other events, 99.5 us)
Sparse Core Ops, SparseCore 0:
  500.7 88.6 reduce-scatter.4
  638.7 88.1 reduce-scatter.2

commit v8 on v7

--- a/solution.py
+++ b/solution.py
@@ -3,7 +3,7 @@
 from jax import lax
 from jax.experimental import pallas as pl
 from jax.experimental.pallas import tpu as pltpu
-from jax.sharding import PartitionSpec as P
+from jax.sharding import Mesh, PartitionSpec as P
 
 BLK = 64
 SPLIT = 1
@@ -219,12 +219,12 @@
     return lax.dynamic_update_slice(buffer, value[None, None], (lap_now, micro, anchor, anchor))
 
 
-def settle(lap_idx, stores, mask_a, mask_b):
+def settle(lap_idx, stores, mask_a, mask_b, staged):
     normed_all, upstream_all, hidden_all, back_all = [
         buffer[lap_idx].reshape(-1, buffer.shape[-1]) for buffer in stores
     ]
-    groups = lax.axis_size("dp")
-    owner = lax.axis_index("dp")
+    groups = lax.axis_size("dz") * lax.axis_size("dy")
+    owner = lax.axis_index("dz") * lax.axis_size("dy") + lax.axis_index("dy")
     span = normed_all.shape[1] // groups
     part_a = lax.dot_general(
         normed_all, back_all, (((0,), (0,)), ((), ())), preferred_element_type=jnp.float32
@@ -234,7 +234,12 @@
     )
     inner = part_a.shape[1]
     joined = jnp.concatenate([part_a.astype(jnp.bfloat16), part_b.astype(jnp.bfloat16)], axis=1)
-    summed = lax.psum_scatter(joined, "dp", scatter_dimension=0, tiled=True).astype(jnp.float32)
+    if staged:
+        outer = lax.psum_scatter(joined, "dz", scatter_dimension=0, tiled=True)
+        summed = lax.psum_scatter(outer, "dy", scatter_dimension=0, tiled=True)
+    else:
+        summed = lax.psum_scatter(joined, ("dz", "dy"), scatter_dimension=0, tiled=True)
+    summed = summed.astype(jnp.float32)
     sum_a, sum_b = summed[:, :inner], summed[:, inner:]
     full_a = expand_blocks(mask_a[lap_idx, 0]).astype(jnp.float32)
     full_b = expand_blocks(mask_b[lap_idx, 0]).astype(jnp.float32)
@@ -339,18 +344,24 @@
     middle = batches + sections - 1
     finish = batches + 2 * sections - 1
     carry = lax.fori_loop(0, middle, backward_step, (start_rows, stores))
-    later_one = settle(1, carry[1], mask_a, mask_b)
+    later_one = settle(1, carry[1], mask_a, mask_b, True)
     carry = lax.fori_loop(middle, finish, backward_step, carry)
-    later_zero = settle(0, carry[1], mask_a, mask_b)
+    later_zero = settle(0, carry[1], mask_a, mask_b, True)
     grad_a = jnp.stack([later_zero[0], later_one[0]])[:, None]
     grad_b = jnp.stack([later_zero[1], later_one[1]])[:, None]
     return (grad_a, grad_b)
 
 
 def solution(mesh):
+    grid = mesh.devices
+    outer = len({device.coords[2] for device in grid[0]})
+    if grid.shape[1] % outer:
+        outer = 1
+    split = Mesh(grid.reshape(grid.shape[0], outer, grid.shape[1] // outer), ("section", "dz", "dy"))
+    rows = ("dz", "dy")
     placed = (
-        P(None, "dp", None),
-        P(None, "dp", None),
+        P(None, rows, None),
+        P(None, rows, None),
         P(None, "section", None, None),
         P(None, "section", None, None),
         P(None, "section", None, None),
@@ -358,8 +369,8 @@
     )
     return jax.shard_map(
         on_device,
-        mesh=mesh,
+        mesh=split,
         in_specs=placed,
-        out_specs=(P(None, "section", "dp", None), P(None, "section", None, "dp")),
+        out_specs=(P(None, "section", rows, None), P(None, "section", None, rows)),
         check_vma=False,
     )

time: 742 us -> 800 us (1.078)
  waiting for transfers between devices: 413 us -> 472 us
    reduce_scatter x2 -> x4, waiting for transfers between devices: 79.2 us -> 138 us  [the longest x2 82.7 us: settle(): outer = lax.psum_scatter(joined, 'dz', scatter_dimension=0, tiled=True)]
  transfers between devices with their start and end apart: 40 -> 42, of which waited for: 39 -> 41; matrix products, arithmetic and copies ran while one was open for 4% -> 4% of each run, Pallas kernels for 5% -> 5%
where the time goes in v8:
time: 800 us; the launch traced here: 799 us
  waiting for transfers between devices  472 us (59%)
  Pallas kernels  156 us (20%)
  starting transfers between devices  86.9 us (11%)
  local copies, waits for them, and re-layouts  27.5 us (3%)
  other arithmetic  25.1 us (3%)
  matrix products  16.5 us (2%)
  between operations  14 us (2%)
    ppermute x38, waiting for transfers between devices, shifted(): return lax.ppermute(block, axis, route)  333 us
    ppermute x38, starting transfers between devices, shifted(): return lax.ppermute(block, axis, route)  86.5 us
    reduce_scatter x2, waiting for transfers between devices, settle(): outer = lax.psum_scatter(joined, 'dz', scatter_dimension=0, tiled=True)  82.7 us
    pallas_call x8, Pallas kernels, bwd_call(): pl.pallas_call(_bwd_kernel, grid_spec=pltpu.PrefetchScalarGridSpec(num_sc...  77.9 us
    reduce_scatter x2, waiting for transfers between devices, settle(): summed = lax.psum_scatter(outer, 'dy', scatter_dimension=0, tiled=True)  55 us
    pallas_call x8, Pallas kernels, fwd_call(): pl.pallas_call(_fwd_kernel, grid_spec=pltpu.PrefetchScalarGridSpec(num_sc...  54.1 us
    pallas_call x2, Pallas kernels, masked(): pl.pallas_call(kernel, grid_spec=pltpu.PrefetchScalarGridSpec(num_scalar_...  24.3 us
    another operation x29, local copies, waits for them, and re-layouts  18 us
  transfers between devices with their start and end apart: 42, of which 41 were waited for; matrix products, arithmetic and copies ran while one was open for 4% of the time, Pallas kernels for 5%

profile of v8, /device:TPU:0, one launch (start us, length us, event | category | flops | bytes accessed | tf_op | source)
XLA Modules:
  0.0 798.7 jit_solution(2498333559493093052)
XLA Ops:
  8.0 14.2 %shard_map.77 = bf16[2,4096,512]{2,1,0:T(8,128)(2,1)} custom-call(s32[2,64,8]{2,1,0:T(8,128)S(1)} %bitcast.109, bf16[2,4096,512]{2,1,0:T(8,128)(2,1)} %bitcast.115), custom_call_target="tpu_custom_call" | custom-call | tf_op jit(solution)/shard_map/pallas_call | solution.py:166
  22.2 10.2 %shard_map.78 = bf16[2,512,4096]{2,1,0:T(8,128)(2,1)} custom-call(s32[2,8,64]{2,1,0:T(8,128)S(1)} %bitcast.110, bf16[2,512,4096]{2,1,0:T(8,128)(2,1)} %bitcast.116), custom_call_target="tpu_custom_call" | custom-call | tf_op jit(solution)/shard_map/pallas_call | solution.py:166
  35.0 257.8 %while.66 = (s32[]{:T(128)}, bf16[64,4096]{1,0:T(8,128)(2,1)S(1)}, bf16[2,4,64,4096]{3,2,1,0:T(8,128)(2,1)}, s32[]{:T(128)}, pred[]{:T(512)}, /*index=5*/bf16[4,...) while((s32[]{:T(128)}, bf16[64,4096]{1,0:T(8,128)(2,1)S(1)}, ...), condition=%wide.region_3.4_spmd, body=%wide.region_0.3_spmd.sunk | while | flops 31 | bytes 2621852 | solution.py:298
  41.8 9.8 %collective-permute-done = bf16[64,4096]{1,0:T(8,128)(2,1)S(1)} collective-permute-done((bf16[64,4096]{1,0:T(8,128)(2,1)S(1)}, bf16[64,4096]{1,0:T(8,128)(2,1)S(1)}, u32[]{:S(2)}, u32[]{:S(2)}) %collective-permute-start) | collective-permute-done | bytes 524320 | tf_op jit(solution)/shard_map/while/body/eval_jaxpr/ppermute | solution.py:141
  58.4 9.8 %collective-permute-done = bf16[64,4096]{1,0:T(8,128)(2,1)S(1)} collective-permute-done((bf16[64,4096]{1,0:T(8,128)(2,1)S(1)}, bf16[64,4096]{1,0:T(8,128)(2,1)S(1)}, u32[]{:S(2)}, u32[]{:S(2)}) %collective-permute-start) | collective-permute-done | bytes 524320 | tf_op jit(solution)/shard_map/while/body/eval_jaxpr/ppermute | solution.py:141
  75.1 9.8 %collective-permute-done = bf16[64,4096]{1,0:T(8,128)(2,1)S(1)} collective-permute-done((bf16[64,4096]{1,0:T(8,128)(2,1)S(1)}, bf16[64,4096]{1,0:T(8,128)(2,1)S(1)}, u32[]{:S(2)}, u32[]{:S(2)}) %collective-permute-start) | collective-permute-done | bytes 524320 | tf_op jit(solution)/shard_map/while/body/eval_jaxpr/ppermute | solution.py:141
  91.8 9.8 %collective-permute-done = bf16[64,4096]{1,0:T(8,128)(2,1)S(1)} collective-permute-done((bf16[64,4096]{1,0:T(8,128)(2,1)S(1)}, bf16[64,4096]{1,0:T(8,128)(2,1)S(1)}, u32[]{:S(2)}, u32[]{:S(2)}) %collective-permute-start) | collective-permute-done | bytes 524320 | tf_op jit(solution)/shard_map/while/body/eval_jaxpr/ppermute | solution.py:141
  101.7 9.8 %collective-permute-done = bf16[64,4096]{1,0:T(8,128)(2,1)S(1)} collective-permute-done((bf16[64,4096]{1,0:T(8,128)(2,1)S(1)}, bf16[64,4096]{1,0:T(8,128)(2,1)S(1)}, u32[]{:S(2)}, u32[]{:S(2)}) %collective-permute-start) | collective-permute-done | bytes 524320 | tf_op jit(solution)/shard_map/while/body/eval_jaxpr/ppermute | solution.py:141
  111.7 9.8 %collective-permute-done = bf16[64,4096]{1,0:T(8,128)(2,1)S(1)} collective-permute-done((bf16[64,4096]{1,0:T(8,128)(2,1)S(1)}, bf16[64,4096]{1,0:T(8,128)(2,1)S(1)}, u32[]{:S(2)}, u32[]{:S(2)}) %collective-permute-start) | collective-permute-done | bytes 524320 | tf_op jit(solution)/shard_map/while/body/eval_jaxpr/ppermute | solution.py:141
  131.6 12.8 %collective-permute-done = bf16[64,4096]{1,0:T(8,128)(2,1)S(1)} collective-permute-done((bf16[64,4096]{1,0:T(8,128)(2,1)S(1)}, bf16[64,4096]{1,0:T(8,128)(2,1)S(1)}, u32[]{:S(2)}, u32[]{:S(2)}) %collective-permute-start) | collective-permute-done | bytes 524320 | tf_op jit(solution)/shard_map/while/body/eval_jaxpr/ppermute | solution.py:141
  151.3 9.8 %collective-permute-done = bf16[64,4096]{1,0:T(8,128)(2,1)S(1)} collective-permute-done((bf16[64,4096]{1,0:T(8,128)(2,1)S(1)}, bf16[64,4096]{1,0:T(8,128)(2,1)S(1)}, u32[]{:S(2)}, u32[]{:S(2)}) %collective-permute-start) | collective-permute-done | bytes 524320 | tf_op jit(solution)/shard_map/while/body/eval_jaxpr/ppermute | solution.py:141
  167.9 9.8 %collective-permute-done = bf16[64,4096]{1,0:T(8,128)(2,1)S(1)} collective-permute-done((bf16[64,4096]{1,0:T(8,128)(2,1)S(1)}, bf16[64,4096]{1,0:T(8,128)(2,1)S(1)}, u32[]{:S(2)}, u32[]{:S(2)}) %collective-permute-start) | collective-permute-done | bytes 524320 | tf_op jit(solution)/shard_map/while/body/eval_jaxpr/ppermute | solution.py:141
  184.6 9.8 %collective-permute-done = bf16[64,4096]{1,0:T(8,128)(2,1)S(1)} collective-permute-done((bf16[64,4096]{1,0:T(8,128)(2,1)S(1)}, bf16[64,4096]{1,0:T(8,128)(2,1)S(1)}, u32[]{:S(2)}, u32[]{:S(2)}) %collective-permute-start) | collective-permute-done | bytes 524320 | tf_op jit(solution)/shard_map/while/body/eval_jaxpr/ppermute | solution.py:141
  201.2 9.8 %collective-permute-done = bf16[64,4096]{1,0:T(8,128)(2,1)S(1)} collective-permute-done((bf16[64,4096]{1,0:T(8,128)(2,1)S(1)}, bf16[64,4096]{1,0:T(8,128)(2,1)S(1)}, u32[]{:S(2)}, u32[]{:S(2)}) %collective-permute-start) | collective-permute-done | bytes 524320 | tf_op jit(solution)/shard_map/while/body/eval_jaxpr/ppermute | solution.py:141
  211.2 9.8 %collective-permute-done = bf16[64,4096]{1,0:T(8,128)(2,1)S(1)} collective-permute-done((bf16[64,4096]{1,0:T(8,128)(2,1)S(1)}, bf16[64,4096]{1,0:T(8,128)(2,1)S(1)}, u32[]{:S(2)}, u32[]{:S(2)}) %collective-permute-start) | collective-permute-done | bytes 524320 | tf_op jit(solution)/shard_map/while/body/eval_jaxpr/ppermute | solution.py:141
  221.2 9.8 %collective-permute-done = bf16[64,4096]{1,0:T(8,128)(2,1)S(1)} collective-permute-done((bf16[64,4096]{1,0:T(8,128)(2,1)S(1)}, bf16[64,4096]{1,0:T(8,128)(2,1)S(1)}, u32[]{:S(2)}, u32[]{:S(2)}) %collective-permute-start) | collective-permute-done | bytes 524320 | tf_op jit(solution)/shard_map/while/body/eval_jaxpr/ppermute | solution.py:141
  241.1 12.8 %collective-permute-done = bf16[64,4096]{1,0:T(8,128)(2,1)S(1)} collective-permute-done((bf16[64,4096]{1,0:T(8,128)(2,1)S(1)}, bf16[64,4096]{1,0:T(8,128)(2,1)S(1)}, u32[]{:S(2)}, u32[]{:S(2)}) %collective-permute-start) | collective-permute-done | bytes 524320 | tf_op jit(solution)/shard_map/while/body/eval_jaxpr/ppermute | solution.py:141
  254.0 12.8 %collective-permute-done = bf16[64,4096]{1,0:T(8,128)(2,1)S(1)} collective-permute-done((bf16[64,4096]{1,0:T(8,128)(2,1)S(1)}, bf16[64,4096]{1,0:T(8,128)(2,1)S(1)}, u32[]{:S(2)}, u32[]{:S(2)}) %collective-permute-start) | collective-permute-done | bytes 524320 | tf_op jit(solution)/shard_map/while/body/eval_jaxpr/ppermute | solution.py:141
  267.0 12.8 %collective-permute-done = bf16[64,4096]{1,0:T(8,128)(2,1)S(1)} collective-permute-done((bf16[64,4096]{1,0:T(8,128)(2,1)S(1)}, bf16[64,4096]{1,0:T(8,128)(2,1)S(1)}, u32[]{:S(2)}, u32[]{:S(2)}) %collective-permute-start) | collective-permute-done | bytes 524320 | tf_op jit(solution)/shard_map/while/body/eval_jaxpr/ppermute | solution.py:141
  280.0 12.8 %collective-permute-done = bf16[64,4096]{1,0:T(8,128)(2,1)S(1)} collective-permute-done((bf16[64,4096]{1,0:T(8,128)(2,1)S(1)}, bf16[64,4096]{1,0:T(8,128)(2,1)S(1)}, u32[]{:S(2)}, u32[]{:S(2)}) %collective-permute-start) | collective-permute-done | bytes 524320 | tf_op jit(solution)/shard_map/while/body/eval_jaxpr/ppermute | solution.py:141
  298.7 185.7 %while.67 = (s32[]{:T(128)}, bf16[64,4096]{1,0:T(8,128)(2,1)}, bf16[2,4,64,4096]{3,2,1,0:T(8,128)(2,1)}, bf16[2,4,64,4096]{3,2,1,0:T(8,128)(2,1)}, bf16[2,4,64,5...) while((s32[]{:T(128)}, bf16[64,4096]{1,0:T(8,128)(2,1)}, ...), condition=%wide.region_7.8_spmd, body=%wide.region_4.7_spmd.sunk | while | flops 31 | bytes 2621980 | solution.py:346
  315.7 12.0 %collective-permute-start.1 = (bf16[64,4096]{1,0:T(8,128)(2,1)}, bf16[64,4096]{1,0:T(8,128)(2,1)}, u32[]{:S(2)}, u32[]{:S(2)}) collective-permute-start(bf16[64,4096]{1,0:T(8,128)(2,1)} %get-tuple-element.1172), channel_id=1, source_target_pairs={{16,0},{32,16},{48,32},{64,48},{80,64},{96,80},{112,96},{0,112},{1... | collective-permute-start | bytes 1572872 | tf_op jit(solution)/shard_map/while/body/eval_jaxpr/ppermute | solution.py:141
  335.6 12.0 %collective-permute-start.1 = (bf16[64,4096]{1,0:T(8,128)(2,1)}, bf16[64,4096]{1,0:T(8,128)(2,1)}, u32[]{:S(2)}, u32[]{:S(2)}) collective-permute-start(bf16[64,4096]{1,0:T(8,128)(2,1)} %get-tuple-element.1172), channel_id=1, source_target_pairs={{16,0},{32,16},{48,32},{64,48},{80,64},{96,80},{112,96},{0,112},{1... | collective-permute-start | bytes 1572872 | tf_op jit(solution)/shard_map/while/body/eval_jaxpr/ppermute | solution.py:141
  355.6 12.0 %collective-permute-start.1 = (bf16[64,4096]{1,0:T(8,128)(2,1)}, bf16[64,4096]{1,0:T(8,128)(2,1)}, u32[]{:S(2)}, u32[]{:S(2)}) collective-permute-start(bf16[64,4096]{1,0:T(8,128)(2,1)} %get-tuple-element.1172), channel_id=1, source_target_pairs={{16,0},{32,16},{48,32},{64,48},{80,64},{96,80},{112,96},{0,112},{1... | collective-permute-start | bytes 1572872 | tf_op jit(solution)/shard_map/while/body/eval_jaxpr/ppermute | solution.py:141
  464.6 9.7 %conditional.7 = ((bf16[64,4096]{1,0:T(8,128)(2,1)}, bf16[2,4,64,4096]{3,2,1,0:T(8,128)(2,1)}, bf16[2,4,64,4096]{3,2,1,0:T(8,128)(2,1)}, bf16[2,4,64,512]{3,2,1,0:T(8,128)(2,1)S(1)}, bf16[2,4,64,512]{3,2,1,0:T(8,128)(2,1)S(1)})) conditional(s32[]{:T(128)} %convert_element_type.174, (bf16[2,4,64,4096]{3,2,1,0:T(8,128)(2,1)}, ...), branch_computations={%region_5.5_spmd, %region_6.6_spmd} | conditional | bytes 524338 | solution.py:330
  500.8 121.4 %while.68 = (s32[]{:T(128)}, bf16[64,4096]{1,0:T(8,128)(2,1)}, bf16[2,4,64,4096]{3,2,1,0:T(8,128)(2,1)}, bf16[2,4,64,4096]{3,2,1,0:T(8,128)(2,1)}, bf16[2,4,64,5...) while((s32[]{:T(128)}, bf16[64,4096]{1,0:T(8,128)(2,1)}, ...), condition=%wide.region_11.12_spmd, body=%wide.region_8.11_spmd.sunk | while | flops 32 | bytes 2622000 | solution.py:348
  501.7 12.0 %collective-permute-start.2 = (bf16[64,4096]{1,0:T(8,128)(2,1)}, bf16[64,4096]{1,0:T(8,128)(2,1)}, u32[]{:S(2)}, u32[]{:S(2)}) collective-permute-start(bf16[64,4096]{1,0:T(8,128)(2,1)} %get-tuple-element.1189), channel_id=1, source_target_pairs={{16,0},{32,16},{48,32},{64,48},{80,64},{96,80},{112,96},{0,112},{1... | collective-permute-start | bytes 1572872 | tf_op jit(solution)/shard_map/while/body/eval_jaxpr/ppermute | solution.py:141
  554.8 9.9 %conditional.8 = ((bf16[64,4096]{1,0:T(8,128)(2,1)}, bf16[2,4,64,4096]{3,2,1,0:T(8,128)(2,1)}, bf16[2,4,64,4096]{3,2,1,0:T(8,128)(2,1)}, bf16[2,4,64,512]{3,2,1,0:T(8,128)(2,1)S(1)}, bf16[2,4,64,512]{3,2,1,0:T(8,128)(2,1)S(1)})) conditional(s32[]{:T(128)} %convert_element_type.175, (bf16[2,4,64,4096]{3,2,1,0:T(8,128)(2,1)}, ...), branch_computations={%region_9.9_spmd, %region_10.10_spmd} | conditional | bytes 524338 | solution.py:330
  554.8 9.9 %branch_1_fun.5 = (bf16[64,4096]{1,0:T(8,128)(2,1)}, bf16[2,4,64,4096]{3,2,1,0:T(8,128)(2,1)}, bf16[2,4,64,4096]{3,2,1,0:T(8,128)(2,1)}, bf16[2,4,64,512]{3,2,1,0:T(8,128)(2,1)S(1)}, bf16[2,4,64,512]{3,2,1,0:T(8,128)(2,1)S(1)}) custom-call(s32[4]{0:T(128)S(1)} %get-tuple-element.853.sc_ref, ...), custom_call_target="tpu_custom_call", output_to_operand_aliasing={{1}: (6, {}), {2}: (7, {}), {3}: (8, {}), {4}: (9, {})} | custom-call | tf_op jit(solution)/shard_map/while/body/eval_jaxpr/cond/branch_1_fun/pallas_call | solution.py:110
  639.1 82.7 %reduce-scatter.5.cloned.1.call-done = bf16[1024,1024]{0,1:T(8,128)(2,1)} async-done(((bf16[4096,1024]{0,1:T(8,128)(2,1)}), bf16[1024,1024]{0,1:T(8,128)(2,1)}) %reduce-scatter.5.cloned.1.call-update) | async-done | bytes 2097168 | tf_op jit(solution)/shard_map/reduce_scatter | solution.py:238
  727.3 26.2 %reduce-scatter.11.cloned.1.call-done = bf16[256,1024]{0,1:T(8,128)(2,1)} async-done(((bf16[1024,1024]{0,1:T(8,128)(2,1)}), bf16[256,1024]{0,1:T(8,128)(2,1)}) %reduce-scatter.11.cloned.1.call-update) | async-done | bytes 524304 | tf_op jit(solution)/shard_map/reduce_scatter | solution.py:239
  756.5 28.7 %reduce-scatter.7.cloned.1.call-done = bf16[256,1024]{0,1:T(8,128)(2,1)} async-done(((bf16[1024,1024]{0,1:T(8,128)(2,1)}), bf16[256,1024]{0,1:T(8,128)(2,1)}) %reduce-scatter.7.cloned.1.call-update) | async-done | bytes 524304 | tf_op jit(solution)/shard_map/reduce_scatter | solution.py:239
  (234 shorter events, 504.6 us)
Async XLA Ops:
  7.2 631.2 %reduce-scatter.9.cloned.1.call-start = ((), (), s32[]{:S(2)}) async-start(), calls=%async_computation.6 | async-start | bytes 10485760 | tf_op jit(solution)/shard_map/reduce_scatter | solution.py:238
  41.8 9.8 %collective-permute-start = (bf16[64,4096]{1,0:T(8,128)(2,1)S(1)}, bf16[64,4096]{1,0:T(8,128)(2,1)S(1)}, u32[]{:S(2)}, u32[]{:S(2)}) collective-permute-start(bf16[64,4096]{1,0:T(8,128)(2,1)S(1)} %get-tuple-element.1158), channel_id=1, source_target_pairs={{112,0},{0,16},{16,32},{32,48},{48,64},{64,80},{80,96},{96,112},{1... | collective-permute-start | bytes 1572872 | tf_op jit(solution)/shard_map/while/body/eval_jaxpr/ppermute | solution.py:141
  58.4 9.8 %collective-permute-start = (bf16[64,4096]{1,0:T(8,128)(2,1)S(1)}, bf16[64,4096]{1,0:T(8,128)(2,1)S(1)}, u32[]{:S(2)}, u32[]{:S(2)}) collective-permute-start(bf16[64,4096]{1,0:T(8,128)(2,1)S(1)} %get-tuple-element.1158), channel_id=1, source_target_pairs={{112,0},{0,16},{16,32},{32,48},{48,64},{64,80},{80,96},{96,112},{1... | collective-permute-start | bytes 1572872 | tf_op jit(solution)/shard_map/while/body/eval_jaxpr/ppermute | solution.py:141
  101.7 9.8 %collective-permute-start = (bf16[64,4096]{1,0:T(8,128)(2,1)S(1)}, bf16[64,4096]{1,0:T(8,128)(2,1)S(1)}, u32[]{:S(2)}, u32[]{:S(2)}) collective-permute-start(bf16[64,4096]{1,0:T(8,128)(2,1)S(1)} %get-tuple-element.1158), channel_id=1, source_target_pairs={{112,0},{0,16},{16,32},{32,48},{48,64},{64,80},{80,96},{96,112},{1... | collective-permute-start | bytes 1572872 | tf_op jit(solution)/shard_map/while/body/eval_jaxpr/ppermute | solution.py:141
  111.7 9.8 %collective-permute-start = (bf16[64,4096]{1,0:T(8,128)(2,1)S(1)}, bf16[64,4096]{1,0:T(8,128)(2,1)S(1)}, u32[]{:S(2)}, u32[]{:S(2)}) collective-permute-start(bf16[64,4096]{1,0:T(8,128)(2,1)S(1)} %get-tuple-element.1158), channel_id=1, source_target_pairs={{112,0},{0,16},{16,32},{32,48},{48,64},{64,80},{80,96},{96,112},{1... | collective-permute-start | bytes 1572872 | tf_op jit(solution)/shard_map/while/body/eval_jaxpr/ppermute | solution.py:141
  121.6 9.8 %collective-permute-start = (bf16[64,4096]{1,0:T(8,128)(2,1)S(1)}, bf16[64,4096]{1,0:T(8,128)(2,1)S(1)}, u32[]{:S(2)}, u32[]{:S(2)}) collective-permute-start(bf16[64,4096]{1,0:T(8,128)(2,1)S(1)} %get-tuple-element.1158), channel_id=1, source_target_pairs={{112,0},{0,16},{16,32},{32,48},{48,64},{64,80},{80,96},{96,112},{1... | collective-permute-start | bytes 1572872 | tf_op jit(solution)/shard_map/while/body/eval_jaxpr/ppermute | solution.py:141
  131.6 12.8 %collective-permute-start = (bf16[64,4096]{1,0:T(8,128)(2,1)S(1)}, bf16[64,4096]{1,0:T(8,128)(2,1)S(1)}, u32[]{:S(2)}, u32[]{:S(2)}) collective-permute-start(bf16[64,4096]{1,0:T(8,128)(2,1)S(1)} %get-tuple-element.1158), channel_id=1, source_target_pairs={{112,0},{0,16},{16,32},{32,48},{48,64},{64,80},{80,96},{96,112},{1... | collective-permute-start | bytes 1572872 | tf_op jit(solution)/shard_map/while/body/eval_jaxpr/ppermute | solution.py:141
  167.9 9.8 %collective-permute-start = (bf16[64,4096]{1,0:T(8,128)(2,1)S(1)}, bf16[64,4096]{1,0:T(8,128)(2,1)S(1)}, u32[]{:S(2)}, u32[]{:S(2)}) collective-permute-start(bf16[64,4096]{1,0:T(8,128)(2,1)S(1)} %get-tuple-element.1158), channel_id=1, source_target_pairs={{112,0},{0,16},{16,32},{32,48},{48,64},{64,80},{80,96},{96,112},{1... | collective-permute-start | bytes 1572872 | tf_op jit(solution)/shard_map/while/body/eval_jaxpr/ppermute | solution.py:141
  211.2 9.8 %collective-permute-start = (bf16[64,4096]{1,0:T(8,128)(2,1)S(1)}, bf16[64,4096]{1,0:T(8,128)(2,1)S(1)}, u32[]{:S(2)}, u32[]{:S(2)}) collective-permute-start(bf16[64,4096]{1,0:T(8,128)(2,1)S(1)} %get-tuple-element.1158), channel_id=1, source_target_pairs={{112,0},{0,16},{16,32},{32,48},{48,64},{64,80},{80,96},{96,112},{1... | collective-permute-start | bytes 1572872 | tf_op jit(solution)/shard_map/while/body/eval_jaxpr/ppermute | solution.py:141
  221.1 9.8 %collective-permute-start = (bf16[64,4096]{1,0:T(8,128)(2,1)S(1)}, bf16[64,4096]{1,0:T(8,128)(2,1)S(1)}, u32[]{:S(2)}, u32[]{:S(2)}) collective-permute-start(bf16[64,4096]{1,0:T(8,128)(2,1)S(1)} %get-tuple-element.1158), channel_id=1, source_target_pairs={{112,0},{0,16},{16,32},{32,48},{48,64},{64,80},{80,96},{96,112},{1... | collective-permute-start | bytes 1572872 | tf_op jit(solution)/shard_map/while/body/eval_jaxpr/ppermute | solution.py:141
  231.1 9.8 %collective-permute-start = (bf16[64,4096]{1,0:T(8,128)(2,1)S(1)}, bf16[64,4096]{1,0:T(8,128)(2,1)S(1)}, u32[]{:S(2)}, u32[]{:S(2)}) collective-permute-start(bf16[64,4096]{1,0:T(8,128)(2,1)S(1)} %get-tuple-element.1158), channel_id=1, source_target_pairs={{112,0},{0,16},{16,32},{32,48},{48,64},{64,80},{80,96},{96,112},{1... | collective-permute-start | bytes 1572872 | tf_op jit(solution)/shard_map/while/body/eval_jaxpr/ppermute | solution.py:141
  241.1 12.8 %collective-permute-start = (bf16[64,4096]{1,0:T(8,128)(2,1)S(1)}, bf16[64,4096]{1,0:T(8,128)(2,1)S(1)}, u32[]{:S(2)}, u32[]{:S(2)}) collective-permute-start(bf16[64,4096]{1,0:T(8,128)(2,1)S(1)} %get-tuple-element.1158), channel_id=1, source_target_pairs={{112,0},{0,16},{16,32},{32,48},{48,64},{64,80},{80,96},{96,112},{1... | collective-permute-start | bytes 1572872 | tf_op jit(solution)/shard_map/while/body/eval_jaxpr/ppermute | solution.py:141
  254.0 12.8 %collective-permute-start = (bf16[64,4096]{1,0:T(8,128)(2,1)S(1)}, bf16[64,4096]{1,0:T(8,128)(2,1)S(1)}, u32[]{:S(2)}, u32[]{:S(2)}) collective-permute-start(bf16[64,4096]{1,0:T(8,128)(2,1)S(1)} %get-tuple-element.1158), channel_id=1, source_target_pairs={{112,0},{0,16},{16,32},{32,48},{48,64},{64,80},{80,96},{96,112},{1... | collective-permute-start | bytes 1572872 | tf_op jit(solution)/shard_map/while/body/eval_jaxpr/ppermute | solution.py:141
  267.0 12.9 %collective-permute-start = (bf16[64,4096]{1,0:T(8,128)(2,1)S(1)}, bf16[64,4096]{1,0:T(8,128)(2,1)S(1)}, u32[]{:S(2)}, u32[]{:S(2)}) collective-permute-start(bf16[64,4096]{1,0:T(8,128)(2,1)S(1)} %get-tuple-element.1158), channel_id=1, source_target_pairs={{112,0},{0,16},{16,32},{32,48},{48,64},{64,80},{80,96},{96,112},{1... | collective-permute-start | bytes 1572872 | tf_op jit(solution)/shard_map/while/body/eval_jaxpr/ppermute | solution.py:141
  280.0 12.8 %collective-permute-start = (bf16[64,4096]{1,0:T(8,128)(2,1)S(1)}, bf16[64,4096]{1,0:T(8,128)(2,1)S(1)}, u32[]{:S(2)}, u32[]{:S(2)}) collective-permute-start(bf16[64,4096]{1,0:T(8,128)(2,1)S(1)} %get-tuple-element.1158), channel_id=1, source_target_pairs={{112,0},{0,16},{16,32},{32,48},{48,64},{64,80},{80,96},{96,112},{1... | collective-permute-start | bytes 1572872 | tf_op jit(solution)/shard_map/while/body/eval_jaxpr/ppermute | solution.py:141
  299.6 15.2 %collective-permute-start.1 = (bf16[64,4096]{1,0:T(8,128)(2,1)}, bf16[64,4096]{1,0:T(8,128)(2,1)}, u32[]{:S(2)}, u32[]{:S(2)}) collective-permute-start(bf16[64,4096]{1,0:T(8,128)(2,1)} %get-tuple-element.1172), channel_id=1, source_target_pairs={{16,0},{32,16},{48,32},{64,48},{80,64},{96,80},{112,96},{0,112},{1... | collective-permute-start | bytes 1572872 | tf_op jit(solution)/shard_map/while/body/eval_jaxpr/ppermute | solution.py:141
  315.7 19.0 %collective-permute-start.1 = (bf16[64,4096]{1,0:T(8,128)(2,1)}, bf16[64,4096]{1,0:T(8,128)(2,1)}, u32[]{:S(2)}, u32[]{:S(2)}) collective-permute-start(bf16[64,4096]{1,0:T(8,128)(2,1)} %get-tuple-element.1172), channel_id=1, source_target_pairs={{16,0},{32,16},{48,32},{64,48},{80,64},{96,80},{112,96},{0,112},{1... | collective-permute-start | bytes 1572872 | tf_op jit(solution)/shard_map/while/body/eval_jaxpr/ppermute | solution.py:141
  335.6 19.0 %collective-permute-start.1 = (bf16[64,4096]{1,0:T(8,128)(2,1)}, bf16[64,4096]{1,0:T(8,128)(2,1)}, u32[]{:S(2)}, u32[]{:S(2)}) collective-permute-start(bf16[64,4096]{1,0:T(8,128)(2,1)} %get-tuple-element.1172), channel_id=1, source_target_pairs={{16,0},{32,16},{48,32},{64,48},{80,64},{96,80},{112,96},{0,112},{1... | collective-permute-start | bytes 1572872 | tf_op jit(solution)/shard_map/while/body/eval_jaxpr/ppermute | solution.py:141
  355.6 19.0 %collective-permute-start.1 = (bf16[64,4096]{1,0:T(8,128)(2,1)}, bf16[64,4096]{1,0:T(8,128)(2,1)}, u32[]{:S(2)}, u32[]{:S(2)}) collective-permute-start(bf16[64,4096]{1,0:T(8,128)(2,1)} %get-tuple-element.1172), channel_id=1, source_target_pairs={{16,0},{32,16},{48,32},{64,48},{80,64},{96,80},{112,96},{0,112},{1... | collective-permute-start | bytes 1572872 | tf_op jit(solution)/shard_map/while/body/eval_jaxpr/ppermute | solution.py:141
  375.5 10.1 %collective-permute-start.1 = (bf16[64,4096]{1,0:T(8,128)(2,1)}, bf16[64,4096]{1,0:T(8,128)(2,1)}, u32[]{:S(2)}, u32[]{:S(2)}) collective-permute-start(bf16[64,4096]{1,0:T(8,128)(2,1)} %get-tuple-element.1172), channel_id=1, source_target_pairs={{16,0},{32,16},{48,32},{64,48},{80,64},{96,80},{112,96},{0,112},{1... | collective-permute-start | bytes 1572872 | tf_op jit(solution)/shard_map/while/body/eval_jaxpr/ppermute | solution.py:141
  386.6 10.1 %collective-permute-start.1 = (bf16[64,4096]{1,0:T(8,128)(2,1)}, bf16[64,4096]{1,0:T(8,128)(2,1)}, u32[]{:S(2)}, u32[]{:S(2)}) collective-permute-start(bf16[64,4096]{1,0:T(8,128)(2,1)} %get-tuple-element.1172), channel_id=1, source_target_pairs={{16,0},{32,16},{48,32},{64,48},{80,64},{96,80},{112,96},{0,112},{1... | collective-permute-start | bytes 1572872 | tf_op jit(solution)/shard_map/while/body/eval_jaxpr/ppermute | solution.py:141
  397.6 10.1 %collective-permute-start.1 = (bf16[64,4096]{1,0:T(8,128)(2,1)}, bf16[64,4096]{1,0:T(8,128)(2,1)}, u32[]{:S(2)}, u32[]{:S(2)}) collective-permute-start(bf16[64,4096]{1,0:T(8,128)(2,1)} %get-tuple-element.1172), channel_id=1, source_target_pairs={{16,0},{32,16},{48,32},{64,48},{80,64},{96,80},{112,96},{0,112},{1... | collective-permute-start | bytes 1572872 | tf_op jit(solution)/shard_map/while/body/eval_jaxpr/ppermute | solution.py:141
  434.4 10.2 %collective-permute-start.1 = (bf16[64,4096]{1,0:T(8,128)(2,1)}, bf16[64,4096]{1,0:T(8,128)(2,1)}, u32[]{:S(2)}, u32[]{:S(2)}) collective-permute-start(bf16[64,4096]{1,0:T(8,128)(2,1)} %get-tuple-element.1172), channel_id=1, source_target_pairs={{16,0},{32,16},{48,32},{64,48},{80,64},{96,80},{112,96},{0,112},{1... | collective-permute-start | bytes 1572872 | tf_op jit(solution)/shard_map/while/body/eval_jaxpr/ppermute | solution.py:141
  454.4 10.1 %collective-permute-start.1 = (bf16[64,4096]{1,0:T(8,128)(2,1)}, bf16[64,4096]{1,0:T(8,128)(2,1)}, u32[]{:S(2)}, u32[]{:S(2)}) collective-permute-start(bf16[64,4096]{1,0:T(8,128)(2,1)} %get-tuple-element.1172), channel_id=1, source_target_pairs={{16,0},{32,16},{48,32},{64,48},{80,64},{96,80},{112,96},{0,112},{1... | collective-permute-start | bytes 1572872 | tf_op jit(solution)/shard_map/while/body/eval_jaxpr/ppermute | solution.py:141
  474.3 10.1 %collective-permute-start.1 = (bf16[64,4096]{1,0:T(8,128)(2,1)}, bf16[64,4096]{1,0:T(8,128)(2,1)}, u32[]{:S(2)}, u32[]{:S(2)}) collective-permute-start(bf16[64,4096]{1,0:T(8,128)(2,1)} %get-tuple-element.1172), channel_id=1, source_target_pairs={{16,0},{32,16},{48,32},{64,48},{80,64},{96,80},{112,96},{0,112},{1... | collective-permute-start | bytes 1572872 | tf_op jit(solution)/shard_map/while/body/eval_jaxpr/ppermute | solution.py:141
  500.5 221.2 %reduce-scatter.5.cloned.1.call-start = ((), (), s32[]{:S(2)}) async-start(), calls=%async_computation.4 | async-start | bytes 10485760 | tf_op jit(solution)/shard_map/reduce_scatter | solution.py:238
  501.7 19.0 %collective-permute-start.2 = (bf16[64,4096]{1,0:T(8,128)(2,1)}, bf16[64,4096]{1,0:T(8,128)(2,1)}, u32[]{:S(2)}, u32[]{:S(2)}) collective-permute-start(bf16[64,4096]{1,0:T(8,128)(2,1)} %get-tuple-element.1189), channel_id=1, source_target_pairs={{16,0},{32,16},{48,32},{64,48},{80,64},{96,80},{112,96},{0,112},{1... | collective-permute-start | bytes 1572872 | tf_op jit(solution)/shard_map/while/body/eval_jaxpr/ppermute | solution.py:141
  521.7 10.4 %collective-permute-start.2 = (bf16[64,4096]{1,0:T(8,128)(2,1)}, bf16[64,4096]{1,0:T(8,128)(2,1)}, u32[]{:S(2)}, u32[]{:S(2)}) collective-permute-start(bf16[64,4096]{1,0:T(8,128)(2,1)} %get-tuple-element.1189), channel_id=1, source_target_pairs={{16,0},{32,16},{48,32},{64,48},{80,64},{96,80},{112,96},{0,112},{1... | collective-permute-start | bytes 1572872 | tf_op jit(solution)/shard_map/while/body/eval_jaxpr/ppermute | solution.py:141
  533.0 10.4 %collective-permute-start.2 = (bf16[64,4096]{1,0:T(8,128)(2,1)}, bf16[64,4096]{1,0:T(8,128)(2,1)}, u32[]{:S(2)}, u32[]{:S(2)}) collective-permute-start(bf16[64,4096]{1,0:T(8,128)(2,1)} %get-tuple-element.1189), channel_id=1, source_target_pairs={{16,0},{32,16},{48,32},{64,48},{80,64},{96,80},{112,96},{0,112},{1... | collective-permute-start | bytes 1572872 | tf_op jit(solution)/shard_map/while/body/eval_jaxpr/ppermute | solution.py:141
  544.3 10.4 %collective-permute-start.2 = (bf16[64,4096]{1,0:T(8,128)(2,1)}, bf16[64,4096]{1,0:T(8,128)(2,1)}, u32[]{:S(2)}, u32[]{:S(2)}) collective-permute-start(bf16[64,4096]{1,0:T(8,128)(2,1)} %get-tuple-element.1189), channel_id=1, source_target_pairs={{16,0},{32,16},{48,32},{64,48},{80,64},{96,80},{112,96},{0,112},{1... | collective-permute-start | bytes 1572872 | tf_op jit(solution)/shard_map/while/body/eval_jaxpr/ppermute | solution.py:141
  638.3 115.2 %reduce-scatter.11.cloned.1.call-start = ((), (), s32[]{:S(2)}) async-start(), calls=%async_computation.7 | async-start | bytes 2621440 | tf_op jit(solution)/shard_map/reduce_scatter | solution.py:239
  639.0 146.2 %reduce-scatter.7.cloned.1.call-start = ((), (), s32[]{:S(2)}) async-start(), calls=%async_computation.5 | async-start | bytes 2621440 | tf_op jit(solution)/shard_map/reduce_scatter | solution.py:239
  (18 other events, 284.7 us)
Sparse Core Ops, SparseCore 0:
  500.7 83.3 reduce-scatter.8
  638.4 83.3 reduce-scatter.4
  724.2 29.2 reduce-scatter.10
  755.8 29.4 reduce-scatter.6

commit v9 on v7

--- a/solution.py
+++ b/solution.py
@@ -8,7 +8,7 @@
 BLK = 64
 SPLIT = 1
 TK = 128
-TKB = 256
+TKB = 512
 LANES = 128
 
 

time: 742 us -> 733 us (0.988)
  no operation moved by 1% of the time
where the time goes in v9:
time: 733 us; the launch traced here: 732 us
  waiting for transfers between devices  413 us (56%)
  Pallas kernels  151 us (21%)
  starting transfers between devices  82.9 us (11%)
  local copies, waits for them, and re-layouts  28.2 us (4%)
  other arithmetic  25.1 us (3%)
  matrix products  16.5 us (2%)
  between operations  14.3 us (2%)
    ppermute x38, waiting for transfers between devices, shifted(): return lax.ppermute(block, axis, route)  333 us
    ppermute x38, starting transfers between devices, shifted(): return lax.ppermute(block, axis, route)  82.7 us
    reduce_scatter x2, waiting for transfers between devices, settle(): lax.psum_scatter(joined, 'dp', scatter_dimension=0, tiled=True)  79.7 us
    pallas_call x8, Pallas kernels, bwd_call(): pl.pallas_call(_bwd_kernel, grid_spec=pltpu.PrefetchScalarGridSpec(num_sc...  72.9 us
    pallas_call x8, Pallas kernels, fwd_call(): pl.pallas_call(_fwd_kernel, grid_spec=pltpu.PrefetchScalarGridSpec(num_sc...  54.1 us
    pallas_call x2, Pallas kernels, masked(): pl.pallas_call(kernel, grid_spec=pltpu.PrefetchScalarGridSpec(num_scalar_...  24.3 us
    another operation x29, local copies, waits for them, and re-layouts  18 us
    concatenate x2, other arithmetic, settle(): jnp.concatenate([part_a.astype(jnp.bfloat16), part_b.astype(jnp.bfloat16)...  15.7 us
  transfers between devices with their start and end apart: 40, of which 39 were waited for; matrix products, arithmetic and copies ran while one was open for 4% of the time, Pallas kernels for 5%

profile of v9, /device:TPU:0, one launch (start us, length us, event | category | flops | bytes accessed | tf_op | source)
XLA Modules:
  0.0 732.0 jit_solution(17813161094820627094)
XLA Ops:
  8.0 14.2 %shard_map.77 = bf16[2,4096,512]{2,1,0:T(8,128)(2,1)} custom-call(s32[2,64,8]{2,1,0:T(8,128)S(1)} %bitcast.109, bf16[2,4096,512]{2,1,0:T(8,128)(2,1)} %bitcast.115), custom_call_target="tpu_custom_call" | custom-call | tf_op jit(solution)/shard_map/pallas_call | solution.py:166
  22.2 10.2 %shard_map.78 = bf16[2,512,4096]{2,1,0:T(8,128)(2,1)} custom-call(s32[2,8,64]{2,1,0:T(8,128)S(1)} %bitcast.110, bf16[2,512,4096]{2,1,0:T(8,128)(2,1)} %bitcast.116), custom_call_target="tpu_custom_call" | custom-call | tf_op jit(solution)/shard_map/pallas_call | solution.py:166
  35.0 257.8 %while.66 = (s32[]{:T(128)}, bf16[64,4096]{1,0:T(8,128)(2,1)S(1)}, bf16[2,4,64,4096]{3,2,1,0:T(8,128)(2,1)}, s32[]{:T(128)}, pred[]{:T(512)}, /*index=5*/bf16[4,...) while((s32[]{:T(128)}, bf16[64,4096]{1,0:T(8,128)(2,1)S(1)}, ...), condition=%wide.region_3.4_spmd, body=%wide.region_0.3_spmd.sunk | while | flops 31 | bytes 2621852 | solution.py:293
  41.8 9.8 %collective-permute-done = bf16[64,4096]{1,0:T(8,128)(2,1)S(1)} collective-permute-done((bf16[64,4096]{1,0:T(8,128)(2,1)S(1)}, bf16[64,4096]{1,0:T(8,128)(2,1)S(1)}, u32[]{:S(2)}, u32[]{:S(2)}) %collective-permute-start) | collective-permute-done | bytes 524320 | tf_op jit(solution)/shard_map/while/body/eval_jaxpr/ppermute | solution.py:141
  58.4 9.8 %collective-permute-done = bf16[64,4096]{1,0:T(8,128)(2,1)S(1)} collective-permute-done((bf16[64,4096]{1,0:T(8,128)(2,1)S(1)}, bf16[64,4096]{1,0:T(8,128)(2,1)S(1)}, u32[]{:S(2)}, u32[]{:S(2)}) %collective-permute-start) | collective-permute-done | bytes 524320 | tf_op jit(solution)/shard_map/while/body/eval_jaxpr/ppermute | solution.py:141
  75.1 9.8 %collective-permute-done = bf16[64,4096]{1,0:T(8,128)(2,1)S(1)} collective-permute-done((bf16[64,4096]{1,0:T(8,128)(2,1)S(1)}, bf16[64,4096]{1,0:T(8,128)(2,1)S(1)}, u32[]{:S(2)}, u32[]{:S(2)}) %collective-permute-start) | collective-permute-done | bytes 524320 | tf_op jit(solution)/shard_map/while/body/eval_jaxpr/ppermute | solution.py:141
  91.8 9.8 %collective-permute-done = bf16[64,4096]{1,0:T(8,128)(2,1)S(1)} collective-permute-done((bf16[64,4096]{1,0:T(8,128)(2,1)S(1)}, bf16[64,4096]{1,0:T(8,128)(2,1)S(1)}, u32[]{:S(2)}, u32[]{:S(2)}) %collective-permute-start) | collective-permute-done | bytes 524320 | tf_op jit(solution)/shard_map/while/body/eval_jaxpr/ppermute | solution.py:141
  101.7 9.8 %collective-permute-done = bf16[64,4096]{1,0:T(8,128)(2,1)S(1)} collective-permute-done((bf16[64,4096]{1,0:T(8,128)(2,1)S(1)}, bf16[64,4096]{1,0:T(8,128)(2,1)S(1)}, u32[]{:S(2)}, u32[]{:S(2)}) %collective-permute-start) | collective-permute-done | bytes 524320 | tf_op jit(solution)/shard_map/while/body/eval_jaxpr/ppermute | solution.py:141
  111.7 9.8 %collective-permute-done = bf16[64,4096]{1,0:T(8,128)(2,1)S(1)} collective-permute-done((bf16[64,4096]{1,0:T(8,128)(2,1)S(1)}, bf16[64,4096]{1,0:T(8,128)(2,1)S(1)}, u32[]{:S(2)}, u32[]{:S(2)}) %collective-permute-start) | collective-permute-done | bytes 524320 | tf_op jit(solution)/shard_map/while/body/eval_jaxpr/ppermute | solution.py:141
  122.3 9.2 %collective-permute-done = bf16[64,4096]{1,0:T(8,128)(2,1)S(1)} collective-permute-done((bf16[64,4096]{1,0:T(8,128)(2,1)S(1)}, bf16[64,4096]{1,0:T(8,128)(2,1)S(1)}, u32[]{:S(2)}, u32[]{:S(2)}) %collective-permute-start) | collective-permute-done | bytes 524320 | tf_op jit(solution)/shard_map/while/body/eval_jaxpr/ppermute | solution.py:141
  131.6 12.8 %collective-permute-done = bf16[64,4096]{1,0:T(8,128)(2,1)S(1)} collective-permute-done((bf16[64,4096]{1,0:T(8,128)(2,1)S(1)}, bf16[64,4096]{1,0:T(8,128)(2,1)S(1)}, u32[]{:S(2)}, u32[]{:S(2)}) %collective-permute-start) | collective-permute-done | bytes 524320 | tf_op jit(solution)/shard_map/while/body/eval_jaxpr/ppermute | solution.py:141
  151.3 9.8 %collective-permute-done = bf16[64,4096]{1,0:T(8,128)(2,1)S(1)} collective-permute-done((bf16[64,4096]{1,0:T(8,128)(2,1)S(1)}, bf16[64,4096]{1,0:T(8,128)(2,1)S(1)}, u32[]{:S(2)}, u32[]{:S(2)}) %collective-permute-start) | collective-permute-done | bytes 524320 | tf_op jit(solution)/shard_map/while/body/eval_jaxpr/ppermute | solution.py:141
  167.9 9.8 %collective-permute-done = bf16[64,4096]{1,0:T(8,128)(2,1)S(1)} collective-permute-done((bf16[64,4096]{1,0:T(8,128)(2,1)S(1)}, bf16[64,4096]{1,0:T(8,128)(2,1)S(1)}, u32[]{:S(2)}, u32[]{:S(2)}) %collective-permute-start) | collective-permute-done | bytes 524320 | tf_op jit(solution)/shard_map/while/body/eval_jaxpr/ppermute | solution.py:141
  184.6 9.8 %collective-permute-done = bf16[64,4096]{1,0:T(8,128)(2,1)S(1)} collective-permute-done((bf16[64,4096]{1,0:T(8,128)(2,1)S(1)}, bf16[64,4096]{1,0:T(8,128)(2,1)S(1)}, u32[]{:S(2)}, u32[]{:S(2)}) %collective-permute-start) | collective-permute-done | bytes 524320 | tf_op jit(solution)/shard_map/while/body/eval_jaxpr/ppermute | solution.py:141
  201.2 9.8 %collective-permute-done = bf16[64,4096]{1,0:T(8,128)(2,1)S(1)} collective-permute-done((bf16[64,4096]{1,0:T(8,128)(2,1)S(1)}, bf16[64,4096]{1,0:T(8,128)(2,1)S(1)}, u32[]{:S(2)}, u32[]{:S(2)}) %collective-permute-start) | collective-permute-done | bytes 524320 | tf_op jit(solution)/shard_map/while/body/eval_jaxpr/ppermute | solution.py:141
  211.2 9.8 %collective-permute-done = bf16[64,4096]{1,0:T(8,128)(2,1)S(1)} collective-permute-done((bf16[64,4096]{1,0:T(8,128)(2,1)S(1)}, bf16[64,4096]{1,0:T(8,128)(2,1)S(1)}, u32[]{:S(2)}, u32[]{:S(2)}) %collective-permute-start) | collective-permute-done | bytes 524320 | tf_op jit(solution)/shard_map/while/body/eval_jaxpr/ppermute | solution.py:141
  221.2 9.8 %collective-permute-done = bf16[64,4096]{1,0:T(8,128)(2,1)S(1)} collective-permute-done((bf16[64,4096]{1,0:T(8,128)(2,1)S(1)}, bf16[64,4096]{1,0:T(8,128)(2,1)S(1)}, u32[]{:S(2)}, u32[]{:S(2)}) %collective-permute-start) | collective-permute-done | bytes 524320 | tf_op jit(solution)/shard_map/while/body/eval_jaxpr/ppermute | solution.py:141
  231.7 9.2 %collective-permute-done = bf16[64,4096]{1,0:T(8,128)(2,1)S(1)} collective-permute-done((bf16[64,4096]{1,0:T(8,128)(2,1)S(1)}, bf16[64,4096]{1,0:T(8,128)(2,1)S(1)}, u32[]{:S(2)}, u32[]{:S(2)}) %collective-permute-start) | collective-permute-done | bytes 524320 | tf_op jit(solution)/shard_map/while/body/eval_jaxpr/ppermute | solution.py:141
  241.1 12.8 %collective-permute-done = bf16[64,4096]{1,0:T(8,128)(2,1)S(1)} collective-permute-done((bf16[64,4096]{1,0:T(8,128)(2,1)S(1)}, bf16[64,4096]{1,0:T(8,128)(2,1)S(1)}, u32[]{:S(2)}, u32[]{:S(2)}) %collective-permute-start) | collective-permute-done | bytes 524320 | tf_op jit(solution)/shard_map/while/body/eval_jaxpr/ppermute | solution.py:141
  254.0 12.8 %collective-permute-done = bf16[64,4096]{1,0:T(8,128)(2,1)S(1)} collective-permute-done((bf16[64,4096]{1,0:T(8,128)(2,1)S(1)}, bf16[64,4096]{1,0:T(8,128)(2,1)S(1)}, u32[]{:S(2)}, u32[]{:S(2)}) %collective-permute-start) | collective-permute-done | bytes 524320 | tf_op jit(solution)/shard_map/while/body/eval_jaxpr/ppermute | solution.py:141
  267.0 12.8 %collective-permute-done = bf16[64,4096]{1,0:T(8,128)(2,1)S(1)} collective-permute-done((bf16[64,4096]{1,0:T(8,128)(2,1)S(1)}, bf16[64,4096]{1,0:T(8,128)(2,1)S(1)}, u32[]{:S(2)}, u32[]{:S(2)}) %collective-permute-start) | collective-permute-done | bytes 524320 | tf_op jit(solution)/shard_map/while/body/eval_jaxpr/ppermute | solution.py:141
  280.0 12.8 %collective-permute-done = bf16[64,4096]{1,0:T(8,128)(2,1)S(1)} collective-permute-done((bf16[64,4096]{1,0:T(8,128)(2,1)S(1)}, bf16[64,4096]{1,0:T(8,128)(2,1)S(1)}, u32[]{:S(2)}, u32[]{:S(2)}) %collective-permute-start) | collective-permute-done | bytes 524320 | tf_op jit(solution)/shard_map/while/body/eval_jaxpr/ppermute | solution.py:141
  298.7 180.2 %while.67 = (s32[]{:T(128)}, bf16[64,4096]{1,0:T(8,128)(2,1)}, bf16[2,4,64,4096]{3,2,1,0:T(8,128)(2,1)}, bf16[2,4,64,4096]{3,2,1,0:T(8,128)(2,1)}, bf16[2,4,64,5...) while((s32[]{:T(128)}, bf16[64,4096]{1,0:T(8,128)(2,1)}, ...), condition=%wide.region_7.8_spmd, body=%wide.region_4.7_spmd.sunk | while | flops 31 | bytes 2621980 | solution.py:341
  315.0 11.3 %collective-permute-start.1 = (bf16[64,4096]{1,0:T(8,128)(2,1)}, bf16[64,4096]{1,0:T(8,128)(2,1)}, u32[]{:S(2)}, u32[]{:S(2)}) collective-permute-start(bf16[64,4096]{1,0:T(8,128)(2,1)} %get-tuple-element.1172), channel_id=1, source_target_pairs={{16,0},{32,16},{48,32},{64,48},{80,64},{96,80},{112,96},{0,112},{1... | collective-permute-start | bytes 1572872 | tf_op jit(solution)/shard_map/while/body/eval_jaxpr/ppermute | solution.py:141
  334.3 11.3 %collective-permute-start.1 = (bf16[64,4096]{1,0:T(8,128)(2,1)}, bf16[64,4096]{1,0:T(8,128)(2,1)}, u32[]{:S(2)}, u32[]{:S(2)}) collective-permute-start(bf16[64,4096]{1,0:T(8,128)(2,1)} %get-tuple-element.1172), channel_id=1, source_target_pairs={{16,0},{32,16},{48,32},{64,48},{80,64},{96,80},{112,96},{0,112},{1... | collective-permute-start | bytes 1572872 | tf_op jit(solution)/shard_map/while/body/eval_jaxpr/ppermute | solution.py:141
  353.5 11.3 %collective-permute-start.1 = (bf16[64,4096]{1,0:T(8,128)(2,1)}, bf16[64,4096]{1,0:T(8,128)(2,1)}, u32[]{:S(2)}, u32[]{:S(2)}) collective-permute-start(bf16[64,4096]{1,0:T(8,128)(2,1)} %get-tuple-element.1172), channel_id=1, source_target_pairs={{16,0},{32,16},{48,32},{64,48},{80,64},{96,80},{112,96},{0,112},{1... | collective-permute-start | bytes 1572872 | tf_op jit(solution)/shard_map/while/body/eval_jaxpr/ppermute | solution.py:141
  495.3 118.1 %while.68 = (s32[]{:T(128)}, bf16[64,4096]{1,0:T(8,128)(2,1)}, bf16[2,4,64,4096]{3,2,1,0:T(8,128)(2,1)}, bf16[2,4,64,4096]{3,2,1,0:T(8,128)(2,1)}, bf16[2,4,64,5...) while((s32[]{:T(128)}, bf16[64,4096]{1,0:T(8,128)(2,1)}, ...), condition=%wide.region_11.12_spmd, body=%wide.region_8.11_spmd.sunk | while | flops 32 | bytes 2622000 | solution.py:343
  496.2 11.3 %collective-permute-start.2 = (bf16[64,4096]{1,0:T(8,128)(2,1)}, bf16[64,4096]{1,0:T(8,128)(2,1)}, u32[]{:S(2)}, u32[]{:S(2)}) collective-permute-start(bf16[64,4096]{1,0:T(8,128)(2,1)} %get-tuple-element.1189), channel_id=1, source_target_pairs={{16,0},{32,16},{48,32},{64,48},{80,64},{96,80},{112,96},{0,112},{1... | collective-permute-start | bytes 1572872 | tf_op jit(solution)/shard_map/while/body/eval_jaxpr/ppermute | solution.py:141
  564.4 9.4 %conditional.8 = ((bf16[64,4096]{1,0:T(8,128)(2,1)}, bf16[2,4,64,4096]{3,2,1,0:T(8,128)(2,1)}, bf16[2,4,64,4096]{3,2,1,0:T(8,128)(2,1)}, bf16[2,4,64,512]{3,2,1,0:T(8,128)(2,1)S(1)}, bf16[2,4,64,512]{3,2,1,0:T(8,128)(2,1)S(1)})) conditional(s32[]{:T(128)} %convert_element_type.175, (bf16[2,4,64,4096]{3,2,1,0:T(8,128)(2,1)}, ...), branch_computations={%region_9.9_spmd, %region_10.10_spmd} | conditional | bytes 524338 | solution.py:325
  564.4 9.4 %branch_1_fun.5 = (bf16[64,4096]{1,0:T(8,128)(2,1)}, bf16[2,4,64,4096]{3,2,1,0:T(8,128)(2,1)}, bf16[2,4,64,4096]{3,2,1,0:T(8,128)(2,1)}, bf16[2,4,64,512]{3,2,1,0:T(8,128)(2,1)S(1)}, bf16[2,4,64,512]{3,2,1,0:T(8,128)(2,1)S(1)}) custom-call(s32[4]{0:T(128)S(1)} %get-tuple-element.853.sc_ref, ...), custom_call_target="tpu_custom_call", output_to_operand_aliasing={{1}: (6, {}), {2}: (7, {}), {3}: (8, {}), {4}: (9, {})} | custom-call | tf_op jit(solution)/shard_map/while/body/eval_jaxpr/cond/branch_1_fun/pallas_call | solution.py:110
  580.9 9.2 %conditional.8 = ((bf16[64,4096]{1,0:T(8,128)(2,1)}, bf16[2,4,64,4096]{3,2,1,0:T(8,128)(2,1)}, bf16[2,4,64,4096]{3,2,1,0:T(8,128)(2,1)}, bf16[2,4,64,512]{3,2,1,0:T(8,128)(2,1)S(1)}, bf16[2,4,64,512]{3,2,1,0:T(8,128)(2,1)S(1)})) conditional(s32[]{:T(128)} %convert_element_type.175, (bf16[2,4,64,4096]{3,2,1,0:T(8,128)(2,1)}, ...), branch_computations={%region_9.9_spmd, %region_10.10_spmd} | conditional | bytes 524338 | solution.py:325
  638.6 79.7 %reduce-scatter.3.cloned.1.call-done = bf16[256,1024]{0,1:T(8,128)(2,1)} async-done(((bf16[4096,1024]{0,1:T(8,128)(2,1)}), bf16[256,1024]{0,1:T(8,128)(2,1)}) %reduce-scatter.3.cloned.1.call-update) | async-done | bytes 524304 | tf_op jit(solution)/shard_map/reduce_scatter | solution.py:237
  (228 shorter events, 476.4 us)
Async XLA Ops:
  7.2 628.4 %reduce-scatter.5.cloned.1.call-start = ((), (), s32[]{:S(2)}) async-start(), calls=%async_computation.3 | async-start | bytes 8912896 | tf_op jit(solution)/shard_map/reduce_scatter | solution.py:237
  41.8 9.8 %collective-permute-start = (bf16[64,4096]{1,0:T(8,128)(2,1)S(1)}, bf16[64,4096]{1,0:T(8,128)(2,1)S(1)}, u32[]{:S(2)}, u32[]{:S(2)}) collective-permute-start(bf16[64,4096]{1,0:T(8,128)(2,1)S(1)} %get-tuple-element.1158), channel_id=1, source_target_pairs={{112,0},{0,16},{16,32},{32,48},{48,64},{64,80},{80,96},{96,112},{1... | collective-permute-start | bytes 1572872 | tf_op jit(solution)/shard_map/while/body/eval_jaxpr/ppermute | solution.py:141
  58.4 9.8 %collective-permute-start = (bf16[64,4096]{1,0:T(8,128)(2,1)S(1)}, bf16[64,4096]{1,0:T(8,128)(2,1)S(1)}, u32[]{:S(2)}, u32[]{:S(2)}) collective-permute-start(bf16[64,4096]{1,0:T(8,128)(2,1)S(1)} %get-tuple-element.1158), channel_id=1, source_target_pairs={{112,0},{0,16},{16,32},{32,48},{48,64},{64,80},{80,96},{96,112},{1... | collective-permute-start | bytes 1572872 | tf_op jit(solution)/shard_map/while/body/eval_jaxpr/ppermute | solution.py:141
  75.1 9.8 %collective-permute-start = (bf16[64,4096]{1,0:T(8,128)(2,1)S(1)}, bf16[64,4096]{1,0:T(8,128)(2,1)S(1)}, u32[]{:S(2)}, u32[]{:S(2)}) collective-permute-start(bf16[64,4096]{1,0:T(8,128)(2,1)S(1)} %get-tuple-element.1158), channel_id=1, source_target_pairs={{112,0},{0,16},{16,32},{32,48},{48,64},{64,80},{80,96},{96,112},{1... | collective-permute-start | bytes 1572872 | tf_op jit(solution)/shard_map/while/body/eval_jaxpr/ppermute | solution.py:141
  91.8 9.8 %collective-permute-start = (bf16[64,4096]{1,0:T(8,128)(2,1)S(1)}, bf16[64,4096]{1,0:T(8,128)(2,1)S(1)}, u32[]{:S(2)}, u32[]{:S(2)}) collective-permute-start(bf16[64,4096]{1,0:T(8,128)(2,1)S(1)} %get-tuple-element.1158), channel_id=1, source_target_pairs={{112,0},{0,16},{16,32},{32,48},{48,64},{64,80},{80,96},{96,112},{1... | collective-permute-start | bytes 1572872 | tf_op jit(solution)/shard_map/while/body/eval_jaxpr/ppermute | solution.py:141
  101.7 9.8 %collective-permute-start = (bf16[64,4096]{1,0:T(8,128)(2,1)S(1)}, bf16[64,4096]{1,0:T(8,128)(2,1)S(1)}, u32[]{:S(2)}, u32[]{:S(2)}) collective-permute-start(bf16[64,4096]{1,0:T(8,128)(2,1)S(1)} %get-tuple-element.1158), channel_id=1, source_target_pairs={{112,0},{0,16},{16,32},{32,48},{48,64},{64,80},{80,96},{96,112},{1... | collective-permute-start | bytes 1572872 | tf_op jit(solution)/shard_map/while/body/eval_jaxpr/ppermute | solution.py:141
  111.7 9.8 %collective-permute-start = (bf16[64,4096]{1,0:T(8,128)(2,1)S(1)}, bf16[64,4096]{1,0:T(8,128)(2,1)S(1)}, u32[]{:S(2)}, u32[]{:S(2)}) collective-permute-start(bf16[64,4096]{1,0:T(8,128)(2,1)S(1)} %get-tuple-element.1158), channel_id=1, source_target_pairs={{112,0},{0,16},{16,32},{32,48},{48,64},{64,80},{80,96},{96,112},{1... | collective-permute-start | bytes 1572872 | tf_op jit(solution)/shard_map/while/body/eval_jaxpr/ppermute | solution.py:141
  121.6 9.8 %collective-permute-start = (bf16[64,4096]{1,0:T(8,128)(2,1)S(1)}, bf16[64,4096]{1,0:T(8,128)(2,1)S(1)}, u32[]{:S(2)}, u32[]{:S(2)}) collective-permute-start(bf16[64,4096]{1,0:T(8,128)(2,1)S(1)} %get-tuple-element.1158), channel_id=1, source_target_pairs={{112,0},{0,16},{16,32},{32,48},{48,64},{64,80},{80,96},{96,112},{1... | collective-permute-start | bytes 1572872 | tf_op jit(solution)/shard_map/while/body/eval_jaxpr/ppermute | solution.py:141
  131.6 12.8 %collective-permute-start = (bf16[64,4096]{1,0:T(8,128)(2,1)S(1)}, bf16[64,4096]{1,0:T(8,128)(2,1)S(1)}, u32[]{:S(2)}, u32[]{:S(2)}) collective-permute-start(bf16[64,4096]{1,0:T(8,128)(2,1)S(1)} %get-tuple-element.1158), channel_id=1, source_target_pairs={{112,0},{0,16},{16,32},{32,48},{48,64},{64,80},{80,96},{96,112},{1... | collective-permute-start | bytes 1572872 | tf_op jit(solution)/shard_map/while/body/eval_jaxpr/ppermute | solution.py:141
  151.3 9.8 %collective-permute-start = (bf16[64,4096]{1,0:T(8,128)(2,1)S(1)}, bf16[64,4096]{1,0:T(8,128)(2,1)S(1)}, u32[]{:S(2)}, u32[]{:S(2)}) collective-permute-start(bf16[64,4096]{1,0:T(8,128)(2,1)S(1)} %get-tuple-element.1158), channel_id=1, source_target_pairs={{112,0},{0,16},{16,32},{32,48},{48,64},{64,80},{80,96},{96,112},{1... | collective-permute-start | bytes 1572872 | tf_op jit(solution)/shard_map/while/body/eval_jaxpr/ppermute | solution.py:141
  211.2 9.8 %collective-permute-start = (bf16[64,4096]{1,0:T(8,128)(2,1)S(1)}, bf16[64,4096]{1,0:T(8,128)(2,1)S(1)}, u32[]{:S(2)}, u32[]{:S(2)}) collective-permute-start(bf16[64,4096]{1,0:T(8,128)(2,1)S(1)} %get-tuple-element.1158), channel_id=1, source_target_pairs={{112,0},{0,16},{16,32},{32,48},{48,64},{64,80},{80,96},{96,112},{1... | collective-permute-start | bytes 1572872 | tf_op jit(solution)/shard_map/while/body/eval_jaxpr/ppermute | solution.py:141
  221.1 9.8 %collective-permute-start = (bf16[64,4096]{1,0:T(8,128)(2,1)S(1)}, bf16[64,4096]{1,0:T(8,128)(2,1)S(1)}, u32[]{:S(2)}, u32[]{:S(2)}) collective-permute-start(bf16[64,4096]{1,0:T(8,128)(2,1)S(1)} %get-tuple-element.1158), channel_id=1, source_target_pairs={{112,0},{0,16},{16,32},{32,48},{48,64},{64,80},{80,96},{96,112},{1... | collective-permute-start | bytes 1572872 | tf_op jit(solution)/shard_map/while/body/eval_jaxpr/ppermute | solution.py:141
  231.1 9.8 %collective-permute-start = (bf16[64,4096]{1,0:T(8,128)(2,1)S(1)}, bf16[64,4096]{1,0:T(8,128)(2,1)S(1)}, u32[]{:S(2)}, u32[]{:S(2)}) collective-permute-start(bf16[64,4096]{1,0:T(8,128)(2,1)S(1)} %get-tuple-element.1158), channel_id=1, source_target_pairs={{112,0},{0,16},{16,32},{32,48},{48,64},{64,80},{80,96},{96,112},{1... | collective-permute-start | bytes 1572872 | tf_op jit(solution)/shard_map/while/body/eval_jaxpr/ppermute | solution.py:141
  241.1 12.8 %collective-permute-start = (bf16[64,4096]{1,0:T(8,128)(2,1)S(1)}, bf16[64,4096]{1,0:T(8,128)(2,1)S(1)}, u32[]{:S(2)}, u32[]{:S(2)}) collective-permute-start(bf16[64,4096]{1,0:T(8,128)(2,1)S(1)} %get-tuple-element.1158), channel_id=1, source_target_pairs={{112,0},{0,16},{16,32},{32,48},{48,64},{64,80},{80,96},{96,112},{1... | collective-permute-start | bytes 1572872 | tf_op jit(solution)/shard_map/while/body/eval_jaxpr/ppermute | solution.py:141
  254.0 12.8 %collective-permute-start = (bf16[64,4096]{1,0:T(8,128)(2,1)S(1)}, bf16[64,4096]{1,0:T(8,128)(2,1)S(1)}, u32[]{:S(2)}, u32[]{:S(2)}) collective-permute-start(bf16[64,4096]{1,0:T(8,128)(2,1)S(1)} %get-tuple-element.1158), channel_id=1, source_target_pairs={{112,0},{0,16},{16,32},{32,48},{48,64},{64,80},{80,96},{96,112},{1... | collective-permute-start | bytes 1572872 | tf_op jit(solution)/shard_map/while/body/eval_jaxpr/ppermute | solution.py:141
  267.0 12.9 %collective-permute-start = (bf16[64,4096]{1,0:T(8,128)(2,1)S(1)}, bf16[64,4096]{1,0:T(8,128)(2,1)S(1)}, u32[]{:S(2)}, u32[]{:S(2)}) collective-permute-start(bf16[64,4096]{1,0:T(8,128)(2,1)S(1)} %get-tuple-element.1158), channel_id=1, source_target_pairs={{112,0},{0,16},{16,32},{32,48},{48,64},{64,80},{80,96},{96,112},{1... | collective-permute-start | bytes 1572872 | tf_op jit(solution)/shard_map/while/body/eval_jaxpr/ppermute | solution.py:141
  280.0 12.8 %collective-permute-start = (bf16[64,4096]{1,0:T(8,128)(2,1)S(1)}, bf16[64,4096]{1,0:T(8,128)(2,1)S(1)}, u32[]{:S(2)}, u32[]{:S(2)}) collective-permute-start(bf16[64,4096]{1,0:T(8,128)(2,1)S(1)} %get-tuple-element.1158), channel_id=1, source_target_pairs={{112,0},{0,16},{16,32},{32,48},{48,64},{64,80},{80,96},{96,112},{1... | collective-permute-start | bytes 1572872 | tf_op jit(solution)/shard_map/while/body/eval_jaxpr/ppermute | solution.py:141
  299.6 14.5 %collective-permute-start.1 = (bf16[64,4096]{1,0:T(8,128)(2,1)}, bf16[64,4096]{1,0:T(8,128)(2,1)}, u32[]{:S(2)}, u32[]{:S(2)}) collective-permute-start(bf16[64,4096]{1,0:T(8,128)(2,1)} %get-tuple-element.1172), channel_id=1, source_target_pairs={{16,0},{32,16},{48,32},{64,48},{80,64},{96,80},{112,96},{0,112},{1... | collective-permute-start | bytes 1572872 | tf_op jit(solution)/shard_map/while/body/eval_jaxpr/ppermute | solution.py:141
  315.0 18.3 %collective-permute-start.1 = (bf16[64,4096]{1,0:T(8,128)(2,1)}, bf16[64,4096]{1,0:T(8,128)(2,1)}, u32[]{:S(2)}, u32[]{:S(2)}) collective-permute-start(bf16[64,4096]{1,0:T(8,128)(2,1)} %get-tuple-element.1172), channel_id=1, source_target_pairs={{16,0},{32,16},{48,32},{64,48},{80,64},{96,80},{112,96},{0,112},{1... | collective-permute-start | bytes 1572872 | tf_op jit(solution)/shard_map/while/body/eval_jaxpr/ppermute | solution.py:141
  334.3 18.3 %collective-permute-start.1 = (bf16[64,4096]{1,0:T(8,128)(2,1)}, bf16[64,4096]{1,0:T(8,128)(2,1)}, u32[]{:S(2)}, u32[]{:S(2)}) collective-permute-start(bf16[64,4096]{1,0:T(8,128)(2,1)} %get-tuple-element.1172), channel_id=1, source_target_pairs={{16,0},{32,16},{48,32},{64,48},{80,64},{96,80},{112,96},{0,112},{1... | collective-permute-start | bytes 1572872 | tf_op jit(solution)/shard_map/while/body/eval_jaxpr/ppermute | solution.py:141
  353.5 18.3 %collective-permute-start.1 = (bf16[64,4096]{1,0:T(8,128)(2,1)}, bf16[64,4096]{1,0:T(8,128)(2,1)}, u32[]{:S(2)}, u32[]{:S(2)}) collective-permute-start(bf16[64,4096]{1,0:T(8,128)(2,1)} %get-tuple-element.1172), channel_id=1, source_target_pairs={{16,0},{32,16},{48,32},{64,48},{80,64},{96,80},{112,96},{0,112},{1... | collective-permute-start | bytes 1572872 | tf_op jit(solution)/shard_map/while/body/eval_jaxpr/ppermute | solution.py:141
  372.8 10.1 %collective-permute-start.1 = (bf16[64,4096]{1,0:T(8,128)(2,1)}, bf16[64,4096]{1,0:T(8,128)(2,1)}, u32[]{:S(2)}, u32[]{:S(2)}) collective-permute-start(bf16[64,4096]{1,0:T(8,128)(2,1)} %get-tuple-element.1172), channel_id=1, source_target_pairs={{16,0},{32,16},{48,32},{64,48},{80,64},{96,80},{112,96},{0,112},{1... | collective-permute-start | bytes 1572872 | tf_op jit(solution)/shard_map/while/body/eval_jaxpr/ppermute | solution.py:141
  383.8 10.1 %collective-permute-start.1 = (bf16[64,4096]{1,0:T(8,128)(2,1)}, bf16[64,4096]{1,0:T(8,128)(2,1)}, u32[]{:S(2)}, u32[]{:S(2)}) collective-permute-start(bf16[64,4096]{1,0:T(8,128)(2,1)} %get-tuple-element.1172), channel_id=1, source_target_pairs={{16,0},{32,16},{48,32},{64,48},{80,64},{96,80},{112,96},{0,112},{1... | collective-permute-start | bytes 1572872 | tf_op jit(solution)/shard_map/while/body/eval_jaxpr/ppermute | solution.py:141
  394.9 10.1 %collective-permute-start.1 = (bf16[64,4096]{1,0:T(8,128)(2,1)}, bf16[64,4096]{1,0:T(8,128)(2,1)}, u32[]{:S(2)}, u32[]{:S(2)}) collective-permute-start(bf16[64,4096]{1,0:T(8,128)(2,1)} %get-tuple-element.1172), channel_id=1, source_target_pairs={{16,0},{32,16},{48,32},{64,48},{80,64},{96,80},{112,96},{0,112},{1... | collective-permute-start | bytes 1572872 | tf_op jit(solution)/shard_map/while/body/eval_jaxpr/ppermute | solution.py:141
  430.3 10.1 %collective-permute-start.1 = (bf16[64,4096]{1,0:T(8,128)(2,1)}, bf16[64,4096]{1,0:T(8,128)(2,1)}, u32[]{:S(2)}, u32[]{:S(2)}) collective-permute-start(bf16[64,4096]{1,0:T(8,128)(2,1)} %get-tuple-element.1172), channel_id=1, source_target_pairs={{16,0},{32,16},{48,32},{64,48},{80,64},{96,80},{112,96},{0,112},{1... | collective-permute-start | bytes 1572872 | tf_op jit(solution)/shard_map/while/body/eval_jaxpr/ppermute | solution.py:141
  449.5 10.1 %collective-permute-start.1 = (bf16[64,4096]{1,0:T(8,128)(2,1)}, bf16[64,4096]{1,0:T(8,128)(2,1)}, u32[]{:S(2)}, u32[]{:S(2)}) collective-permute-start(bf16[64,4096]{1,0:T(8,128)(2,1)} %get-tuple-element.1172), channel_id=1, source_target_pairs={{16,0},{32,16},{48,32},{64,48},{80,64},{96,80},{112,96},{0,112},{1... | collective-permute-start | bytes 1572872 | tf_op jit(solution)/shard_map/while/body/eval_jaxpr/ppermute | solution.py:141
  468.8 10.1 %collective-permute-start.1 = (bf16[64,4096]{1,0:T(8,128)(2,1)}, bf16[64,4096]{1,0:T(8,128)(2,1)}, u32[]{:S(2)}, u32[]{:S(2)}) collective-permute-start(bf16[64,4096]{1,0:T(8,128)(2,1)} %get-tuple-element.1172), channel_id=1, source_target_pairs={{16,0},{32,16},{48,32},{64,48},{80,64},{96,80},{112,96},{0,112},{1... | collective-permute-start | bytes 1572872 | tf_op jit(solution)/shard_map/while/body/eval_jaxpr/ppermute | solution.py:141
  495.0 223.3 %reduce-scatter.3.cloned.1.call-start = ((), (), s32[]{:S(2)}) async-start(), calls=%async_computation.2 | async-start | bytes 8912896 | tf_op jit(solution)/shard_map/reduce_scatter | solution.py:237
  496.2 18.3 %collective-permute-start.2 = (bf16[64,4096]{1,0:T(8,128)(2,1)}, bf16[64,4096]{1,0:T(8,128)(2,1)}, u32[]{:S(2)}, u32[]{:S(2)}) collective-permute-start(bf16[64,4096]{1,0:T(8,128)(2,1)} %get-tuple-element.1189), channel_id=1, source_target_pairs={{16,0},{32,16},{48,32},{64,48},{80,64},{96,80},{112,96},{0,112},{1... | collective-permute-start | bytes 1572872 | tf_op jit(solution)/shard_map/while/body/eval_jaxpr/ppermute | solution.py:141
  515.5 10.1 %collective-permute-start.2 = (bf16[64,4096]{1,0:T(8,128)(2,1)}, bf16[64,4096]{1,0:T(8,128)(2,1)}, u32[]{:S(2)}, u32[]{:S(2)}) collective-permute-start(bf16[64,4096]{1,0:T(8,128)(2,1)} %get-tuple-element.1189), channel_id=1, source_target_pairs={{16,0},{32,16},{48,32},{64,48},{80,64},{96,80},{112,96},{0,112},{1... | collective-permute-start | bytes 1572872 | tf_op jit(solution)/shard_map/while/body/eval_jaxpr/ppermute | solution.py:141
  526.5 10.4 %collective-permute-start.2 = (bf16[64,4096]{1,0:T(8,128)(2,1)}, bf16[64,4096]{1,0:T(8,128)(2,1)}, u32[]{:S(2)}, u32[]{:S(2)}) collective-permute-start(bf16[64,4096]{1,0:T(8,128)(2,1)} %get-tuple-element.1189), channel_id=1, source_target_pairs={{16,0},{32,16},{48,32},{64,48},{80,64},{96,80},{112,96},{0,112},{1... | collective-permute-start | bytes 1572872 | tf_op jit(solution)/shard_map/while/body/eval_jaxpr/ppermute | solution.py:141
  537.9 10.3 %collective-permute-start.2 = (bf16[64,4096]{1,0:T(8,128)(2,1)}, bf16[64,4096]{1,0:T(8,128)(2,1)}, u32[]{:S(2)}, u32[]{:S(2)}) collective-permute-start(bf16[64,4096]{1,0:T(8,128)(2,1)} %get-tuple-element.1189), channel_id=1, source_target_pairs={{16,0},{32,16},{48,32},{64,48},{80,64},{96,80},{112,96},{0,112},{1... | collective-permute-start | bytes 1572872 | tf_op jit(solution)/shard_map/while/body/eval_jaxpr/ppermute | solution.py:141
  (16 other events, 99.5 us)
Sparse Core Ops, SparseCore 0:
  495.2 88.5 reduce-scatter.4
  629.6 88.6 reduce-scatter.2

commit v10 on v9

--- a/solution.py
+++ b/solution.py
@@ -226,14 +226,16 @@
     groups = lax.axis_size("dp")
     owner = lax.axis_index("dp")
     span = normed_all.shape[1] // groups
-    part_a = lax.dot_general(
-        normed_all, back_all, (((0,), (0,)), ((), ())), preferred_element_type=jnp.float32
-    )
-    part_b = lax.dot_general(
-        upstream_all, hidden_all, (((0,), (0,)), ((), ())), preferred_element_type=jnp.float32
-    )
-    inner = part_a.shape[1]
-    joined = jnp.concatenate([part_a.astype(jnp.bfloat16), part_b.astype(jnp.bfloat16)], axis=1)
+    inner = back_all.shape[1]
+    left = jnp.concatenate([normed_all, upstream_all], axis=0)
+    blank = jnp.zeros_like(back_all)
+    right = jnp.concatenate(
+        [jnp.concatenate([back_all, blank], axis=1), jnp.concatenate([blank, hidden_all], axis=1)],
+        axis=0,
+    )
+    joined = lax.dot_general(
+        left, right, (((0,), (0,)), ((), ())), preferred_element_type=jnp.float32
+    ).astype(jnp.bfloat16)
     summed = lax.psum_scatter(joined, "dp", scatter_dimension=0, tiled=True).astype(jnp.float32)
     sum_a, sum_b = summed[:, :inner], summed[:, inner:]
     full_a = expand_blocks(mask_a[lap_idx, 0]).astype(jnp.float32)

time: 733 us -> 719 us (0.981)
  other arithmetic: 25.1 us -> 6.65 us
    concatenate x2 -> x0, other arithmetic: 15.7 us -> none  [settle(): jnp.concatenate([part_a.astype(jnp.bfloat16), part_b.astype(jnp.bfloat16)...]
    dot_general x4 -> x2, matrix products: 16.5 us -> 13.7 us  [settle(): lax.dot_general(left, right, (((0,), (0,)), ((), ())), preferred_element_...]
  transfers between devices with their start and end apart: 40 -> 40, of which waited for: 39 -> 39; matrix products, arithmetic and copies ran while one was open for 4% -> 3% of each run, Pallas kernels for 5% -> 5%
where the time goes in v10:
time: 719 us; the launch traced here: 718 us
  waiting for transfers between devices  415 us (58%)
  Pallas kernels  151 us (21%)
  starting transfers between devices  83.1 us (12%)
  local copies, waits for them, and re-layouts  32.7 us (5%)
  between operations  14.3 us (2%)
  matrix products  13.7 us (2%)
    ppermute x38, waiting for transfers between devices, shifted(): return lax.ppermute(block, axis, route)  333 us
    ppermute x38, starting transfers between devices, shifted(): return lax.ppermute(block, axis, route)  82.8 us
    reduce_scatter x2, waiting for transfers between devices, settle(): lax.psum_scatter(joined, 'dp', scatter_dimension=0, tiled=True)  81.8 us
    pallas_call x8, Pallas kernels, bwd_call(): pl.pallas_call(_bwd_kernel, grid_spec=pltpu.PrefetchScalarGridSpec(num_sc...  72.9 us
    pallas_call x8, Pallas kernels, fwd_call(): pl.pallas_call(_fwd_kernel, grid_spec=pltpu.PrefetchScalarGridSpec(num_sc...  54.1 us
    pallas_call x2, Pallas kernels, masked(): pl.pallas_call(kernel, grid_spec=pltpu.PrefetchScalarGridSpec(num_scalar_...  24.3 us
    another operation x29, local copies, waits for them, and re-layouts  18 us
  transfers between devices with their start and end apart: 40, of which 39 were waited for; matrix products, arithmetic and copies ran while one was open for 3% of the time, Pallas kernels for 5%

profile of v10, /device:TPU:0, one launch (start us, length us, event | category | flops | bytes accessed | tf_op | source)
XLA Modules:
  0.0 717.6 jit_solution(9026115525484911706)
XLA Ops:
  8.0 14.2 %shard_map.77 = bf16[2,4096,512]{2,1,0:T(8,128)(2,1)} custom-call(s32[2,64,8]{2,1,0:T(8,128)S(1)} %bitcast.85, bf16[2,4096,512]{2,1,0:T(8,128)(2,1)} %bitcast.91), custom_call_target="tpu_custom_call" | custom-call | tf_op jit(solution)/shard_map/pallas_call | solution.py:166
  22.2 10.2 %shard_map.78 = bf16[2,512,4096]{2,1,0:T(8,128)(2,1)} custom-call(s32[2,8,64]{2,1,0:T(8,128)S(1)} %bitcast.86, bf16[2,512,4096]{2,1,0:T(8,128)(2,1)} %bitcast.92), custom_call_target="tpu_custom_call" | custom-call | tf_op jit(solution)/shard_map/pallas_call | solution.py:166
  35.0 257.9 %while.66 = (s32[]{:T(128)}, bf16[64,4096]{1,0:T(8,128)(2,1)S(1)}, bf16[2,4,64,4096]{3,2,1,0:T(8,128)(2,1)}, s32[]{:T(128)}, pred[]{:T(512)}, /*index=5*/bf16[4,...) while((s32[]{:T(128)}, bf16[64,4096]{1,0:T(8,128)(2,1)S(1)}, ...), condition=%wide.region_3.4_spmd, body=%wide.region_0.3_spmd.sunk | while | flops 31 | bytes 2621852 | solution.py:295
  41.8 9.8 %collective-permute-done = bf16[64,4096]{1,0:T(8,128)(2,1)S(1)} collective-permute-done((bf16[64,4096]{1,0:T(8,128)(2,1)S(1)}, bf16[64,4096]{1,0:T(8,128)(2,1)S(1)}, u32[]{:S(2)}, u32[]{:S(2)}) %collective-permute-start) | collective-permute-done | bytes 524320 | tf_op jit(solution)/shard_map/while/body/eval_jaxpr/ppermute | solution.py:141
  58.5 9.8 %collective-permute-done = bf16[64,4096]{1,0:T(8,128)(2,1)S(1)} collective-permute-done((bf16[64,4096]{1,0:T(8,128)(2,1)S(1)}, bf16[64,4096]{1,0:T(8,128)(2,1)S(1)}, u32[]{:S(2)}, u32[]{:S(2)}) %collective-permute-start) | collective-permute-done | bytes 524320 | tf_op jit(solution)/shard_map/while/body/eval_jaxpr/ppermute | solution.py:141
  75.1 9.8 %collective-permute-done = bf16[64,4096]{1,0:T(8,128)(2,1)S(1)} collective-permute-done((bf16[64,4096]{1,0:T(8,128)(2,1)S(1)}, bf16[64,4096]{1,0:T(8,128)(2,1)S(1)}, u32[]{:S(2)}, u32[]{:S(2)}) %collective-permute-start) | collective-permute-done | bytes 524320 | tf_op jit(solution)/shard_map/while/body/eval_jaxpr/ppermute | solution.py:141
  91.8 9.8 %collective-permute-done = bf16[64,4096]{1,0:T(8,128)(2,1)S(1)} collective-permute-done((bf16[64,4096]{1,0:T(8,128)(2,1)S(1)}, bf16[64,4096]{1,0:T(8,128)(2,1)S(1)}, u32[]{:S(2)}, u32[]{:S(2)}) %collective-permute-start) | collective-permute-done | bytes 524320 | tf_op jit(solution)/shard_map/while/body/eval_jaxpr/ppermute | solution.py:141
  101.8 9.8 %collective-permute-done = bf16[64,4096]{1,0:T(8,128)(2,1)S(1)} collective-permute-done((bf16[64,4096]{1,0:T(8,128)(2,1)S(1)}, bf16[64,4096]{1,0:T(8,128)(2,1)S(1)}, u32[]{:S(2)}, u32[]{:S(2)}) %collective-permute-start) | collective-permute-done | bytes 524320 | tf_op jit(solution)/shard_map/while/body/eval_jaxpr/ppermute | solution.py:141
  111.7 9.8 %collective-permute-done = bf16[64,4096]{1,0:T(8,128)(2,1)S(1)} collective-permute-done((bf16[64,4096]{1,0:T(8,128)(2,1)S(1)}, bf16[64,4096]{1,0:T(8,128)(2,1)S(1)}, u32[]{:S(2)}, u32[]{:S(2)}) %collective-permute-start) | collective-permute-done | bytes 524320 | tf_op jit(solution)/shard_map/while/body/eval_jaxpr/ppermute | solution.py:141
  122.3 9.2 %collective-permute-done = bf16[64,4096]{1,0:T(8,128)(2,1)S(1)} collective-permute-done((bf16[64,4096]{1,0:T(8,128)(2,1)S(1)}, bf16[64,4096]{1,0:T(8,128)(2,1)S(1)}, u32[]{:S(2)}, u32[]{:S(2)}) %collective-permute-start) | collective-permute-done | bytes 524320 | tf_op jit(solution)/shard_map/while/body/eval_jaxpr/ppermute | solution.py:141
  131.7 12.8 %collective-permute-done = bf16[64,4096]{1,0:T(8,128)(2,1)S(1)} collective-permute-done((bf16[64,4096]{1,0:T(8,128)(2,1)S(1)}, bf16[64,4096]{1,0:T(8,128)(2,1)S(1)}, u32[]{:S(2)}, u32[]{:S(2)}) %collective-permute-start) | collective-permute-done | bytes 524320 | tf_op jit(solution)/shard_map/while/body/eval_jaxpr/ppermute | solution.py:141
  151.3 9.8 %collective-permute-done = bf16[64,4096]{1,0:T(8,128)(2,1)S(1)} collective-permute-done((bf16[64,4096]{1,0:T(8,128)(2,1)S(1)}, bf16[64,4096]{1,0:T(8,128)(2,1)S(1)}, u32[]{:S(2)}, u32[]{:S(2)}) %collective-permute-start) | collective-permute-done | bytes 524320 | tf_op jit(solution)/shard_map/while/body/eval_jaxpr/ppermute | solution.py:141
  167.9 9.8 %collective-permute-done = bf16[64,4096]{1,0:T(8,128)(2,1)S(1)} collective-permute-done((bf16[64,4096]{1,0:T(8,128)(2,1)S(1)}, bf16[64,4096]{1,0:T(8,128)(2,1)S(1)}, u32[]{:S(2)}, u32[]{:S(2)}) %collective-permute-start) | collective-permute-done | bytes 524320 | tf_op jit(solution)/shard_map/while/body/eval_jaxpr/ppermute | solution.py:141
  184.6 9.8 %collective-permute-done = bf16[64,4096]{1,0:T(8,128)(2,1)S(1)} collective-permute-done((bf16[64,4096]{1,0:T(8,128)(2,1)S(1)}, bf16[64,4096]{1,0:T(8,128)(2,1)S(1)}, u32[]{:S(2)}, u32[]{:S(2)}) %collective-permute-start) | collective-permute-done | bytes 524320 | tf_op jit(solution)/shard_map/while/body/eval_jaxpr/ppermute | solution.py:141
  201.3 9.8 %collective-permute-done = bf16[64,4096]{1,0:T(8,128)(2,1)S(1)} collective-permute-done((bf16[64,4096]{1,0:T(8,128)(2,1)S(1)}, bf16[64,4096]{1,0:T(8,128)(2,1)S(1)}, u32[]{:S(2)}, u32[]{:S(2)}) %collective-permute-start) | collective-permute-done | bytes 524320 | tf_op jit(solution)/shard_map/while/body/eval_jaxpr/ppermute | solution.py:141
  211.3 9.8 %collective-permute-done = bf16[64,4096]{1,0:T(8,128)(2,1)S(1)} collective-permute-done((bf16[64,4096]{1,0:T(8,128)(2,1)S(1)}, bf16[64,4096]{1,0:T(8,128)(2,1)S(1)}, u32[]{:S(2)}, u32[]{:S(2)}) %collective-permute-start) | collective-permute-done | bytes 524320 | tf_op jit(solution)/shard_map/while/body/eval_jaxpr/ppermute | solution.py:141
  221.2 9.8 %collective-permute-done = bf16[64,4096]{1,0:T(8,128)(2,1)S(1)} collective-permute-done((bf16[64,4096]{1,0:T(8,128)(2,1)S(1)}, bf16[64,4096]{1,0:T(8,128)(2,1)S(1)}, u32[]{:S(2)}, u32[]{:S(2)}) %collective-permute-start) | collective-permute-done | bytes 524320 | tf_op jit(solution)/shard_map/while/body/eval_jaxpr/ppermute | solution.py:141
  231.7 9.2 %collective-permute-done = bf16[64,4096]{1,0:T(8,128)(2,1)S(1)} collective-permute-done((bf16[64,4096]{1,0:T(8,128)(2,1)S(1)}, bf16[64,4096]{1,0:T(8,128)(2,1)S(1)}, u32[]{:S(2)}, u32[]{:S(2)}) %collective-permute-start) | collective-permute-done | bytes 524320 | tf_op jit(solution)/shard_map/while/body/eval_jaxpr/ppermute | solution.py:141
  241.1 12.8 %collective-permute-done = bf16[64,4096]{1,0:T(8,128)(2,1)S(1)} collective-permute-done((bf16[64,4096]{1,0:T(8,128)(2,1)S(1)}, bf16[64,4096]{1,0:T(8,128)(2,1)S(1)}, u32[]{:S(2)}, u32[]{:S(2)}) %collective-permute-start) | collective-permute-done | bytes 524320 | tf_op jit(solution)/shard_map/while/body/eval_jaxpr/ppermute | solution.py:141
  254.1 12.8 %collective-permute-done = bf16[64,4096]{1,0:T(8,128)(2,1)S(1)} collective-permute-done((bf16[64,4096]{1,0:T(8,128)(2,1)S(1)}, bf16[64,4096]{1,0:T(8,128)(2,1)S(1)}, u32[]{:S(2)}, u32[]{:S(2)}) %collective-permute-start) | collective-permute-done | bytes 524320 | tf_op jit(solution)/shard_map/while/body/eval_jaxpr/ppermute | solution.py:141
  267.1 12.8 %collective-permute-done = bf16[64,4096]{1,0:T(8,128)(2,1)S(1)} collective-permute-done((bf16[64,4096]{1,0:T(8,128)(2,1)S(1)}, bf16[64,4096]{1,0:T(8,128)(2,1)S(1)}, u32[]{:S(2)}, u32[]{:S(2)}) %collective-permute-start) | collective-permute-done | bytes 524320 | tf_op jit(solution)/shard_map/while/body/eval_jaxpr/ppermute | solution.py:141
  280.1 12.8 %collective-permute-done = bf16[64,4096]{1,0:T(8,128)(2,1)S(1)} collective-permute-done((bf16[64,4096]{1,0:T(8,128)(2,1)S(1)}, bf16[64,4096]{1,0:T(8,128)(2,1)S(1)}, u32[]{:S(2)}, u32[]{:S(2)}) %collective-permute-start) | collective-permute-done | bytes 524320 | tf_op jit(solution)/shard_map/while/body/eval_jaxpr/ppermute | solution.py:141
  298.8 180.2 %while.67 = (s32[]{:T(128)}, bf16[64,4096]{1,0:T(8,128)(2,1)}, bf16[2,4,64,4096]{3,2,1,0:T(8,128)(2,1)}, bf16[2,4,64,4096]{3,2,1,0:T(8,128)(2,1)}, bf16[2,4,64,5...) while((s32[]{:T(128)}, bf16[64,4096]{1,0:T(8,128)(2,1)}, ...), condition=%wide.region_7.8_spmd, body=%wide.region_4.7_spmd.sunk | while | flops 31 | bytes 2621980 | solution.py:343
  315.1 11.3 %collective-permute-start.1 = (bf16[64,4096]{1,0:T(8,128)(2,1)}, bf16[64,4096]{1,0:T(8,128)(2,1)}, u32[]{:S(2)}, u32[]{:S(2)}) collective-permute-start(bf16[64,4096]{1,0:T(8,128)(2,1)} %get-tuple-element.1172), channel_id=1, source_target_pairs={{16,0},{32,16},{48,32},{64,48},{80,64},{96,80},{112,96},{0,112},{1... | collective-permute-start | bytes 1572872 | tf_op jit(solution)/shard_map/while/body/eval_jaxpr/ppermute | solution.py:141
  334.4 11.3 %collective-permute-start.1 = (bf16[64,4096]{1,0:T(8,128)(2,1)}, bf16[64,4096]{1,0:T(8,128)(2,1)}, u32[]{:S(2)}, u32[]{:S(2)}) collective-permute-start(bf16[64,4096]{1,0:T(8,128)(2,1)} %get-tuple-element.1172), channel_id=1, source_target_pairs={{16,0},{32,16},{48,32},{64,48},{80,64},{96,80},{112,96},{0,112},{1... | collective-permute-start | bytes 1572872 | tf_op jit(solution)/shard_map/while/body/eval_jaxpr/ppermute | solution.py:141
  353.6 11.3 %collective-permute-start.1 = (bf16[64,4096]{1,0:T(8,128)(2,1)}, bf16[64,4096]{1,0:T(8,128)(2,1)}, u32[]{:S(2)}, u32[]{:S(2)}) collective-permute-start(bf16[64,4096]{1,0:T(8,128)(2,1)} %get-tuple-element.1172), channel_id=1, source_target_pairs={{16,0},{32,16},{48,32},{64,48},{80,64},{96,80},{112,96},{0,112},{1... | collective-permute-start | bytes 1572872 | tf_op jit(solution)/shard_map/while/body/eval_jaxpr/ppermute | solution.py:141
  489.2 118.2 %while.68 = (s32[]{:T(128)}, bf16[64,4096]{1,0:T(8,128)(2,1)}, bf16[2,4,64,4096]{3,2,1,0:T(8,128)(2,1)}, bf16[2,4,64,4096]{3,2,1,0:T(8,128)(2,1)}, bf16[2,4,64,5...) while((s32[]{:T(128)}, bf16[64,4096]{1,0:T(8,128)(2,1)}, ...), condition=%wide.region_11.12_spmd, body=%wide.region_8.11_spmd.sunk | while | flops 32 | bytes 2622000 | solution.py:345
  490.1 11.3 %collective-permute-start.2 = (bf16[64,4096]{1,0:T(8,128)(2,1)}, bf16[64,4096]{1,0:T(8,128)(2,1)}, u32[]{:S(2)}, u32[]{:S(2)}) collective-permute-start(bf16[64,4096]{1,0:T(8,128)(2,1)} %get-tuple-element.1189), channel_id=1, source_target_pairs={{16,0},{32,16},{48,32},{64,48},{80,64},{96,80},{112,96},{0,112},{1... | collective-permute-start | bytes 1572872 | tf_op jit(solution)/shard_map/while/body/eval_jaxpr/ppermute | solution.py:141
  558.4 9.4 %conditional.8 = ((bf16[64,4096]{1,0:T(8,128)(2,1)}, bf16[2,4,64,4096]{3,2,1,0:T(8,128)(2,1)}, bf16[2,4,64,4096]{3,2,1,0:T(8,128)(2,1)}, bf16[2,4,64,512]{3,2,1,0:T(8,128)(2,1)S(1)}, bf16[2,4,64,512]{3,2,1,0:T(8,128)(2,1)S(1)})) conditional(s32[]{:T(128)} %convert_element_type.165, (bf16[2,4,64,4096]{3,2,1,0:T(8,128)(2,1)}, ...), branch_computations={%region_9.9_spmd, %region_10.10_spmd} | conditional | bytes 524338 | solution.py:327
  558.4 9.4 %branch_1_fun.5 = (bf16[64,4096]{1,0:T(8,128)(2,1)}, bf16[2,4,64,4096]{3,2,1,0:T(8,128)(2,1)}, bf16[2,4,64,4096]{3,2,1,0:T(8,128)(2,1)}, bf16[2,4,64,512]{3,2,1,0:T(8,128)(2,1)S(1)}, bf16[2,4,64,512]{3,2,1,0:T(8,128)(2,1)S(1)}) custom-call(s32[4]{0:T(128)S(1)} %get-tuple-element.853.sc_ref, ...), custom_call_target="tpu_custom_call", output_to_operand_aliasing={{1}: (6, {}), {2}: (7, {}), {3}: (8, {}), {4}: (9, {})} | custom-call | tf_op jit(solution)/shard_map/while/body/eval_jaxpr/cond/branch_1_fun/pallas_call | solution.py:110
  575.0 9.2 %conditional.8 = ((bf16[64,4096]{1,0:T(8,128)(2,1)}, bf16[2,4,64,4096]{3,2,1,0:T(8,128)(2,1)}, bf16[2,4,64,4096]{3,2,1,0:T(8,128)(2,1)}, bf16[2,4,64,512]{3,2,1,0:T(8,128)(2,1)S(1)}, bf16[2,4,64,512]{3,2,1,0:T(8,128)(2,1)S(1)})) conditional(s32[]{:T(128)} %convert_element_type.165, (bf16[2,4,64,4096]{3,2,1,0:T(8,128)(2,1)}, ...), branch_computations={%region_9.9_spmd, %region_10.10_spmd} | conditional | bytes 524338 | solution.py:327
  624.1 81.8 %reduce-scatter.3.cloned.1.call-done = bf16[256,1024]{1,0:T(8,128)(2,1)} async-done(((bf16[4096,1024]{1,0:T(8,128)(2,1)}), bf16[256,1024]{1,0:T(8,128)(2,1)}) %reduce-scatter.3.cloned.1.call-update) | async-done | bytes 524304 | tf_op jit(solution)/shard_map/reduce_scatter | solution.py:239
  (230 shorter events, 459.8 us)
Async XLA Ops:
  7.2 614.5 %reduce-scatter.5.cloned.1.call-start = ((), (), s32[]{:S(2)}) async-start(), calls=%async_computation.3 | async-start | bytes 8912896 | tf_op jit(solution)/shard_map/reduce_scatter | solution.py:239
  41.8 9.8 %collective-permute-start = (bf16[64,4096]{1,0:T(8,128)(2,1)S(1)}, bf16[64,4096]{1,0:T(8,128)(2,1)S(1)}, u32[]{:S(2)}, u32[]{:S(2)}) collective-permute-start(bf16[64,4096]{1,0:T(8,128)(2,1)S(1)} %get-tuple-element.1158), channel_id=1, source_target_pairs={{112,0},{0,16},{16,32},{32,48},{48,64},{64,80},{80,96},{96,112},{1... | collective-permute-start | bytes 1572872 | tf_op jit(solution)/shard_map/while/body/eval_jaxpr/ppermute | solution.py:141
  58.5 9.8 %collective-permute-start = (bf16[64,4096]{1,0:T(8,128)(2,1)S(1)}, bf16[64,4096]{1,0:T(8,128)(2,1)S(1)}, u32[]{:S(2)}, u32[]{:S(2)}) collective-permute-start(bf16[64,4096]{1,0:T(8,128)(2,1)S(1)} %get-tuple-element.1158), channel_id=1, source_target_pairs={{112,0},{0,16},{16,32},{32,48},{48,64},{64,80},{80,96},{96,112},{1... | collective-permute-start | bytes 1572872 | tf_op jit(solution)/shard_map/while/body/eval_jaxpr/ppermute | solution.py:141
  75.1 9.8 %collective-permute-start = (bf16[64,4096]{1,0:T(8,128)(2,1)S(1)}, bf16[64,4096]{1,0:T(8,128)(2,1)S(1)}, u32[]{:S(2)}, u32[]{:S(2)}) collective-permute-start(bf16[64,4096]{1,0:T(8,128)(2,1)S(1)} %get-tuple-element.1158), channel_id=1, source_target_pairs={{112,0},{0,16},{16,32},{32,48},{48,64},{64,80},{80,96},{96,112},{1... | collective-permute-start | bytes 1572872 | tf_op jit(solution)/shard_map/while/body/eval_jaxpr/ppermute | solution.py:141
  91.8 9.8 %collective-permute-start = (bf16[64,4096]{1,0:T(8,128)(2,1)S(1)}, bf16[64,4096]{1,0:T(8,128)(2,1)S(1)}, u32[]{:S(2)}, u32[]{:S(2)}) collective-permute-start(bf16[64,4096]{1,0:T(8,128)(2,1)S(1)} %get-tuple-element.1158), channel_id=1, source_target_pairs={{112,0},{0,16},{16,32},{32,48},{48,64},{64,80},{80,96},{96,112},{1... | collective-permute-start | bytes 1572872 | tf_op jit(solution)/shard_map/while/body/eval_jaxpr/ppermute | solution.py:141
  101.8 9.8 %collective-permute-start = (bf16[64,4096]{1,0:T(8,128)(2,1)S(1)}, bf16[64,4096]{1,0:T(8,128)(2,1)S(1)}, u32[]{:S(2)}, u32[]{:S(2)}) collective-permute-start(bf16[64,4096]{1,0:T(8,128)(2,1)S(1)} %get-tuple-element.1158), channel_id=1, source_target_pairs={{112,0},{0,16},{16,32},{32,48},{48,64},{64,80},{80,96},{96,112},{1... | collective-permute-start | bytes 1572872 | tf_op jit(solution)/shard_map/while/body/eval_jaxpr/ppermute | solution.py:141
  111.7 9.8 %collective-permute-start = (bf16[64,4096]{1,0:T(8,128)(2,1)S(1)}, bf16[64,4096]{1,0:T(8,128)(2,1)S(1)}, u32[]{:S(2)}, u32[]{:S(2)}) collective-permute-start(bf16[64,4096]{1,0:T(8,128)(2,1)S(1)} %get-tuple-element.1158), channel_id=1, source_target_pairs={{112,0},{0,16},{16,32},{32,48},{48,64},{64,80},{80,96},{96,112},{1... | collective-permute-start | bytes 1572872 | tf_op jit(solution)/shard_map/while/body/eval_jaxpr/ppermute | solution.py:141
  121.7 9.8 %collective-permute-start = (bf16[64,4096]{1,0:T(8,128)(2,1)S(1)}, bf16[64,4096]{1,0:T(8,128)(2,1)S(1)}, u32[]{:S(2)}, u32[]{:S(2)}) collective-permute-start(bf16[64,4096]{1,0:T(8,128)(2,1)S(1)} %get-tuple-element.1158), channel_id=1, source_target_pairs={{112,0},{0,16},{16,32},{32,48},{48,64},{64,80},{80,96},{96,112},{1... | collective-permute-start | bytes 1572872 | tf_op jit(solution)/shard_map/while/body/eval_jaxpr/ppermute | solution.py:141
  131.6 12.8 %collective-permute-start = (bf16[64,4096]{1,0:T(8,128)(2,1)S(1)}, bf16[64,4096]{1,0:T(8,128)(2,1)S(1)}, u32[]{:S(2)}, u32[]{:S(2)}) collective-permute-start(bf16[64,4096]{1,0:T(8,128)(2,1)S(1)} %get-tuple-element.1158), channel_id=1, source_target_pairs={{112,0},{0,16},{16,32},{32,48},{48,64},{64,80},{80,96},{96,112},{1... | collective-permute-start | bytes 1572872 | tf_op jit(solution)/shard_map/while/body/eval_jaxpr/ppermute | solution.py:141
  151.3 9.8 %collective-permute-start = (bf16[64,4096]{1,0:T(8,128)(2,1)S(1)}, bf16[64,4096]{1,0:T(8,128)(2,1)S(1)}, u32[]{:S(2)}, u32[]{:S(2)}) collective-permute-start(bf16[64,4096]{1,0:T(8,128)(2,1)S(1)} %get-tuple-element.1158), channel_id=1, source_target_pairs={{112,0},{0,16},{16,32},{32,48},{48,64},{64,80},{80,96},{96,112},{1... | collective-permute-start | bytes 1572872 | tf_op jit(solution)/shard_map/while/body/eval_jaxpr/ppermute | solution.py:141
  211.2 9.8 %collective-permute-start = (bf16[64,4096]{1,0:T(8,128)(2,1)S(1)}, bf16[64,4096]{1,0:T(8,128)(2,1)S(1)}, u32[]{:S(2)}, u32[]{:S(2)}) collective-permute-start(bf16[64,4096]{1,0:T(8,128)(2,1)S(1)} %get-tuple-element.1158), channel_id=1, source_target_pairs={{112,0},{0,16},{16,32},{32,48},{48,64},{64,80},{80,96},{96,112},{1... | collective-permute-start | bytes 1572872 | tf_op jit(solution)/shard_map/while/body/eval_jaxpr/ppermute | solution.py:141
  221.2 9.8 %collective-permute-start = (bf16[64,4096]{1,0:T(8,128)(2,1)S(1)}, bf16[64,4096]{1,0:T(8,128)(2,1)S(1)}, u32[]{:S(2)}, u32[]{:S(2)}) collective-permute-start(bf16[64,4096]{1,0:T(8,128)(2,1)S(1)} %get-tuple-element.1158), channel_id=1, source_target_pairs={{112,0},{0,16},{16,32},{32,48},{48,64},{64,80},{80,96},{96,112},{1... | collective-permute-start | bytes 1572872 | tf_op jit(solution)/shard_map/while/body/eval_jaxpr/ppermute | solution.py:141
  231.2 9.8 %collective-permute-start = (bf16[64,4096]{1,0:T(8,128)(2,1)S(1)}, bf16[64,4096]{1,0:T(8,128)(2,1)S(1)}, u32[]{:S(2)}, u32[]{:S(2)}) collective-permute-start(bf16[64,4096]{1,0:T(8,128)(2,1)S(1)} %get-tuple-element.1158), channel_id=1, source_target_pairs={{112,0},{0,16},{16,32},{32,48},{48,64},{64,80},{80,96},{96,112},{1... | collective-permute-start | bytes 1572872 | tf_op jit(solution)/shard_map/while/body/eval_jaxpr/ppermute | solution.py:141
  241.1 12.8 %collective-permute-start = (bf16[64,4096]{1,0:T(8,128)(2,1)S(1)}, bf16[64,4096]{1,0:T(8,128)(2,1)S(1)}, u32[]{:S(2)}, u32[]{:S(2)}) collective-permute-start(bf16[64,4096]{1,0:T(8,128)(2,1)S(1)} %get-tuple-element.1158), channel_id=1, source_target_pairs={{112,0},{0,16},{16,32},{32,48},{48,64},{64,80},{80,96},{96,112},{1... | collective-permute-start | bytes 1572872 | tf_op jit(solution)/shard_map/while/body/eval_jaxpr/ppermute | solution.py:141
  254.1 12.8 %collective-permute-start = (bf16[64,4096]{1,0:T(8,128)(2,1)S(1)}, bf16[64,4096]{1,0:T(8,128)(2,1)S(1)}, u32[]{:S(2)}, u32[]{:S(2)}) collective-permute-start(bf16[64,4096]{1,0:T(8,128)(2,1)S(1)} %get-tuple-element.1158), channel_id=1, source_target_pairs={{112,0},{0,16},{16,32},{32,48},{48,64},{64,80},{80,96},{96,112},{1... | collective-permute-start | bytes 1572872 | tf_op jit(solution)/shard_map/while/body/eval_jaxpr/ppermute | solution.py:141
  267.0 12.9 %collective-permute-start = (bf16[64,4096]{1,0:T(8,128)(2,1)S(1)}, bf16[64,4096]{1,0:T(8,128)(2,1)S(1)}, u32[]{:S(2)}, u32[]{:S(2)}) collective-permute-start(bf16[64,4096]{1,0:T(8,128)(2,1)S(1)} %get-tuple-element.1158), channel_id=1, source_target_pairs={{112,0},{0,16},{16,32},{32,48},{48,64},{64,80},{80,96},{96,112},{1... | collective-permute-start | bytes 1572872 | tf_op jit(solution)/shard_map/while/body/eval_jaxpr/ppermute | solution.py:141
  280.0 12.8 %collective-permute-start = (bf16[64,4096]{1,0:T(8,128)(2,1)S(1)}, bf16[64,4096]{1,0:T(8,128)(2,1)S(1)}, u32[]{:S(2)}, u32[]{:S(2)}) collective-permute-start(bf16[64,4096]{1,0:T(8,128)(2,1)S(1)} %get-tuple-element.1158), channel_id=1, source_target_pairs={{112,0},{0,16},{16,32},{32,48},{48,64},{64,80},{80,96},{96,112},{1... | collective-permute-start | bytes 1572872 | tf_op jit(solution)/shard_map/while/body/eval_jaxpr/ppermute | solution.py:141
  299.7 14.5 %collective-permute-start.1 = (bf16[64,4096]{1,0:T(8,128)(2,1)}, bf16[64,4096]{1,0:T(8,128)(2,1)}, u32[]{:S(2)}, u32[]{:S(2)}) collective-permute-start(bf16[64,4096]{1,0:T(8,128)(2,1)} %get-tuple-element.1172), channel_id=1, source_target_pairs={{16,0},{32,16},{48,32},{64,48},{80,64},{96,80},{112,96},{0,112},{1... | collective-permute-start | bytes 1572872 | tf_op jit(solution)/shard_map/while/body/eval_jaxpr/ppermute | solution.py:141
  315.1 18.3 %collective-permute-start.1 = (bf16[64,4096]{1,0:T(8,128)(2,1)}, bf16[64,4096]{1,0:T(8,128)(2,1)}, u32[]{:S(2)}, u32[]{:S(2)}) collective-permute-start(bf16[64,4096]{1,0:T(8,128)(2,1)} %get-tuple-element.1172), channel_id=1, source_target_pairs={{16,0},{32,16},{48,32},{64,48},{80,64},{96,80},{112,96},{0,112},{1... | collective-permute-start | bytes 1572872 | tf_op jit(solution)/shard_map/while/body/eval_jaxpr/ppermute | solution.py:141
  334.4 18.3 %collective-permute-start.1 = (bf16[64,4096]{1,0:T(8,128)(2,1)}, bf16[64,4096]{1,0:T(8,128)(2,1)}, u32[]{:S(2)}, u32[]{:S(2)}) collective-permute-start(bf16[64,4096]{1,0:T(8,128)(2,1)} %get-tuple-element.1172), channel_id=1, source_target_pairs={{16,0},{32,16},{48,32},{64,48},{80,64},{96,80},{112,96},{0,112},{1... | collective-permute-start | bytes 1572872 | tf_op jit(solution)/shard_map/while/body/eval_jaxpr/ppermute | solution.py:141
  353.6 18.3 %collective-permute-start.1 = (bf16[64,4096]{1,0:T(8,128)(2,1)}, bf16[64,4096]{1,0:T(8,128)(2,1)}, u32[]{:S(2)}, u32[]{:S(2)}) collective-permute-start(bf16[64,4096]{1,0:T(8,128)(2,1)} %get-tuple-element.1172), channel_id=1, source_target_pairs={{16,0},{32,16},{48,32},{64,48},{80,64},{96,80},{112,96},{0,112},{1... | collective-permute-start | bytes 1572872 | tf_op jit(solution)/shard_map/while/body/eval_jaxpr/ppermute | solution.py:141
  372.9 10.1 %collective-permute-start.1 = (bf16[64,4096]{1,0:T(8,128)(2,1)}, bf16[64,4096]{1,0:T(8,128)(2,1)}, u32[]{:S(2)}, u32[]{:S(2)}) collective-permute-start(bf16[64,4096]{1,0:T(8,128)(2,1)} %get-tuple-element.1172), channel_id=1, source_target_pairs={{16,0},{32,16},{48,32},{64,48},{80,64},{96,80},{112,96},{0,112},{1... | collective-permute-start | bytes 1572872 | tf_op jit(solution)/shard_map/while/body/eval_jaxpr/ppermute | solution.py:141
  383.9 10.1 %collective-permute-start.1 = (bf16[64,4096]{1,0:T(8,128)(2,1)}, bf16[64,4096]{1,0:T(8,128)(2,1)}, u32[]{:S(2)}, u32[]{:S(2)}) collective-permute-start(bf16[64,4096]{1,0:T(8,128)(2,1)} %get-tuple-element.1172), channel_id=1, source_target_pairs={{16,0},{32,16},{48,32},{64,48},{80,64},{96,80},{112,96},{0,112},{1... | collective-permute-start | bytes 1572872 | tf_op jit(solution)/shard_map/while/body/eval_jaxpr/ppermute | solution.py:141
  395.0 10.1 %collective-permute-start.1 = (bf16[64,4096]{1,0:T(8,128)(2,1)}, bf16[64,4096]{1,0:T(8,128)(2,1)}, u32[]{:S(2)}, u32[]{:S(2)}) collective-permute-start(bf16[64,4096]{1,0:T(8,128)(2,1)} %get-tuple-element.1172), channel_id=1, source_target_pairs={{16,0},{32,16},{48,32},{64,48},{80,64},{96,80},{112,96},{0,112},{1... | collective-permute-start | bytes 1572872 | tf_op jit(solution)/shard_map/while/body/eval_jaxpr/ppermute | solution.py:141
  430.3 10.1 %collective-permute-start.1 = (bf16[64,4096]{1,0:T(8,128)(2,1)}, bf16[64,4096]{1,0:T(8,128)(2,1)}, u32[]{:S(2)}, u32[]{:S(2)}) collective-permute-start(bf16[64,4096]{1,0:T(8,128)(2,1)} %get-tuple-element.1172), channel_id=1, source_target_pairs={{16,0},{32,16},{48,32},{64,48},{80,64},{96,80},{112,96},{0,112},{1... | collective-permute-start | bytes 1572872 | tf_op jit(solution)/shard_map/while/body/eval_jaxpr/ppermute | solution.py:141
  449.6 10.1 %collective-permute-start.1 = (bf16[64,4096]{1,0:T(8,128)(2,1)}, bf16[64,4096]{1,0:T(8,128)(2,1)}, u32[]{:S(2)}, u32[]{:S(2)}) collective-permute-start(bf16[64,4096]{1,0:T(8,128)(2,1)} %get-tuple-element.1172), channel_id=1, source_target_pairs={{16,0},{32,16},{48,32},{64,48},{80,64},{96,80},{112,96},{0,112},{1... | collective-permute-start | bytes 1572872 | tf_op jit(solution)/shard_map/while/body/eval_jaxpr/ppermute | solution.py:141
  468.8 10.1 %collective-permute-start.1 = (bf16[64,4096]{1,0:T(8,128)(2,1)}, bf16[64,4096]{1,0:T(8,128)(2,1)}, u32[]{:S(2)}, u32[]{:S(2)}) collective-permute-start(bf16[64,4096]{1,0:T(8,128)(2,1)} %get-tuple-element.1172), channel_id=1, source_target_pairs={{16,0},{32,16},{48,32},{64,48},{80,64},{96,80},{112,96},{0,112},{1... | collective-permute-start | bytes 1572872 | tf_op jit(solution)/shard_map/while/body/eval_jaxpr/ppermute | solution.py:141
  488.9 217.0 %reduce-scatter.3.cloned.1.call-start = ((), (), s32[]{:S(2)}) async-start(), calls=%async_computation.2 | async-start | bytes 8912896 | tf_op jit(solution)/shard_map/reduce_scatter | solution.py:239
  490.1 18.3 %collective-permute-start.2 = (bf16[64,4096]{1,0:T(8,128)(2,1)}, bf16[64,4096]{1,0:T(8,128)(2,1)}, u32[]{:S(2)}, u32[]{:S(2)}) collective-permute-start(bf16[64,4096]{1,0:T(8,128)(2,1)} %get-tuple-element.1189), channel_id=1, source_target_pairs={{16,0},{32,16},{48,32},{64,48},{80,64},{96,80},{112,96},{0,112},{1... | collective-permute-start | bytes 1572872 | tf_op jit(solution)/shard_map/while/body/eval_jaxpr/ppermute | solution.py:141
  509.4 10.1 %collective-permute-start.2 = (bf16[64,4096]{1,0:T(8,128)(2,1)}, bf16[64,4096]{1,0:T(8,128)(2,1)}, u32[]{:S(2)}, u32[]{:S(2)}) collective-permute-start(bf16[64,4096]{1,0:T(8,128)(2,1)} %get-tuple-element.1189), channel_id=1, source_target_pairs={{16,0},{32,16},{48,32},{64,48},{80,64},{96,80},{112,96},{0,112},{1... | collective-permute-start | bytes 1572872 | tf_op jit(solution)/shard_map/while/body/eval_jaxpr/ppermute | solution.py:141
  520.4 10.4 %collective-permute-start.2 = (bf16[64,4096]{1,0:T(8,128)(2,1)}, bf16[64,4096]{1,0:T(8,128)(2,1)}, u32[]{:S(2)}, u32[]{:S(2)}) collective-permute-start(bf16[64,4096]{1,0:T(8,128)(2,1)} %get-tuple-element.1189), channel_id=1, source_target_pairs={{16,0},{32,16},{48,32},{64,48},{80,64},{96,80},{112,96},{0,112},{1... | collective-permute-start | bytes 1572872 | tf_op jit(solution)/shard_map/while/body/eval_jaxpr/ppermute | solution.py:141
  531.8 10.4 %collective-permute-start.2 = (bf16[64,4096]{1,0:T(8,128)(2,1)}, bf16[64,4096]{1,0:T(8,128)(2,1)}, u32[]{:S(2)}, u32[]{:S(2)}) collective-permute-start(bf16[64,4096]{1,0:T(8,128)(2,1)} %get-tuple-element.1189), channel_id=1, source_target_pairs={{16,0},{32,16},{48,32},{64,48},{80,64},{96,80},{112,96},{0,112},{1... | collective-permute-start | bytes 1572872 | tf_op jit(solution)/shard_map/while/body/eval_jaxpr/ppermute | solution.py:141
  (15 other events, 94.0 us)
Sparse Core Ops, SparseCore 0:
  489.1 88.5 reduce-scatter.4
  617.4 88.4 reduce-scatter.2

commit v11 on v10

--- a/solution.py
+++ b/solution.py
@@ -280,7 +280,7 @@
             return tuple(fwd_call(table, micro_inputs, inc, eff_a, eff_b, kept))
 
         def idle(inc, kept):
-            return (jnp.zeros_like(inc), kept)
+            return (inc, kept)
 
         result, saved = lax.cond(first_on | second_on, active, idle, incoming, saved)
         incoming = jax.tree.map(
@@ -322,7 +322,7 @@
             return bwd_call(table, saved_rows, out_cotangent, inc, eff_a, eff_b, kept)
 
         def idle(inc, kept):
-            return (jnp.zeros_like(inc), kept)
+            return (inc, kept)
 
         downstream, stores = lax.cond(first_on | second_on, active, idle, incoming, stores)
         incoming = jax.tree.map(

time: 719 us -> 766 us (1.065)
  local copies, waits for them, and re-layouts: 32.7 us -> 67.9 us
  starting transfers between devices: 83.1 us -> 92 us
    while x0 -> x38, local copies, waits for them, and re-layouts: none -> 36.2 us
    another operation x29 -> x5, local copies, waits for them, and re-layouts: 18 us -> 7.6 us
    ppermute x38, starting transfers between devices: 82.8 us -> 91.7 us  [shifted(): return lax.ppermute(block, axis, route)]
    cond x0 -> x16, local copies, waits for them, and re-layouts: none -> 8.64 us
  transfers between devices with their start and end apart: 40 -> 40, of which waited for: 39 -> 39; matrix products, arithmetic and copies ran while one was open for 3% -> 5% of each run, Pallas kernels for 5% -> 5%
where the time goes in v11:
time: 766 us; the launch traced here: 763 us
  waiting for transfers between devices  418 us (55%)
  Pallas kernels  150 us (20%)
  starting transfers between devices  92 us (12%)
  local copies, waits for them, and re-layouts  67.9 us (9%)
  between operations  14.3 us (2%)
  matrix products  13.6 us (2%)
    ppermute x38, waiting for transfers between devices, shifted(): return lax.ppermute(block, axis, route)  337 us
    ppermute x38, starting transfers between devices, shifted(): return lax.ppermute(block, axis, route)  91.7 us
    reduce_scatter x2, waiting for transfers between devices, settle(): lax.psum_scatter(joined, 'dp', scatter_dimension=0, tiled=True)  81.2 us
    pallas_call x8, Pallas kernels, bwd_call(): pl.pallas_call(_bwd_kernel, grid_spec=pltpu.PrefetchScalarGridSpec(num_sc...  71.2 us
    pallas_call x8, Pallas kernels, fwd_call(): pl.pallas_call(_fwd_kernel, grid_spec=pltpu.PrefetchScalarGridSpec(num_sc...  54.1 us
    while x38, local copies, waits for them, and re-layouts  36.2 us
    pallas_call x2, Pallas kernels, masked(): pl.pallas_call(kernel, grid_spec=pltpu.PrefetchScalarGridSpec(num_scalar_...  24.3 us
  transfers between devices with their start and end apart: 40, of which 39 were waited for; matrix products, arithmetic and copies ran while one was open for 5% of the time, Pallas kernels for 5%

profile of v11, /device:TPU:0, one launch (start us, length us, event | category | flops | bytes accessed | tf_op | source)
XLA Modules:
  0.0 763.2 jit_solution(11446167512608719146)
XLA Ops:
  8.0 14.1 %shard_map.77 = bf16[2,4096,512]{2,1,0:T(8,128)(2,1)} custom-call(s32[2,64,8]{2,1,0:T(8,128)S(1)} %bitcast.85, bf16[2,4096,512]{2,1,0:T(8,128)(2,1)} %bitcast.91), custom_call_target="tpu_custom_call" | custom-call | tf_op jit(solution)/shard_map/pallas_call | solution.py:166
  22.2 10.2 %shard_map.78 = bf16[2,512,4096]{2,1,0:T(8,128)(2,1)} custom-call(s32[2,8,64]{2,1,0:T(8,128)S(1)} %bitcast.86, bf16[2,512,4096]{2,1,0:T(8,128)(2,1)} %bitcast.92), custom_call_target="tpu_custom_call" | custom-call | tf_op jit(solution)/shard_map/pallas_call | solution.py:166
  35.0 259.5 %while.63 = (s32[]{:T(128)}, bf16[64,4096]{1,0:T(8,128)(2,1)S(1)}, bf16[2,4,64,4096]{3,2,1,0:T(8,128)(2,1)}, s32[]{:T(128)}, pred[]{:T(512)}, /*index=5*/bf16[4,...) while((s32[]{:T(128)}, bf16[64,4096]{1,0:T(8,128)(2,1)S(1)}, ...), condition=%wide.region_3.4_spmd, body=%wide.region_0.3_spmd.sunk | while | flops 31 | bytes 4194714 | solution.py:295
  41.8 9.8 %collective-permute-done = bf16[64,4096]{1,0:T(8,128)(2,1)S(1)} collective-permute-done((bf16[64,4096]{1,0:T(8,128)(2,1)S(1)}, bf16[64,4096]{1,0:T(8,128)(2,1)S(1)}, u32[]{:S(2)}, u32[]{:S(2)}) %collective-permute-start) | collective-permute-done | bytes 524320 | tf_op jit(solution)/shard_map/while/body/eval_jaxpr/ppermute | solution.py:141
  58.6 9.8 %collective-permute-done = bf16[64,4096]{1,0:T(8,128)(2,1)S(1)} collective-permute-done((bf16[64,4096]{1,0:T(8,128)(2,1)S(1)}, bf16[64,4096]{1,0:T(8,128)(2,1)S(1)}, u32[]{:S(2)}, u32[]{:S(2)}) %collective-permute-start) | collective-permute-done | bytes 524320 | tf_op jit(solution)/shard_map/while/body/eval_jaxpr/ppermute | solution.py:141
  75.4 9.8 %collective-permute-done = bf16[64,4096]{1,0:T(8,128)(2,1)S(1)} collective-permute-done((bf16[64,4096]{1,0:T(8,128)(2,1)S(1)}, bf16[64,4096]{1,0:T(8,128)(2,1)S(1)}, u32[]{:S(2)}, u32[]{:S(2)}) %collective-permute-start) | collective-permute-done | bytes 524320 | tf_op jit(solution)/shard_map/while/body/eval_jaxpr/ppermute | solution.py:141
  102.1 9.8 %collective-permute-done = bf16[64,4096]{1,0:T(8,128)(2,1)S(1)} collective-permute-done((bf16[64,4096]{1,0:T(8,128)(2,1)S(1)}, bf16[64,4096]{1,0:T(8,128)(2,1)S(1)}, u32[]{:S(2)}, u32[]{:S(2)}) %collective-permute-start) | collective-permute-done | bytes 524320 | tf_op jit(solution)/shard_map/while/body/eval_jaxpr/ppermute | solution.py:141
  112.1 9.8 %collective-permute-done = bf16[64,4096]{1,0:T(8,128)(2,1)S(1)} collective-permute-done((bf16[64,4096]{1,0:T(8,128)(2,1)S(1)}, bf16[64,4096]{1,0:T(8,128)(2,1)S(1)}, u32[]{:S(2)}, u32[]{:S(2)}) %collective-permute-start) | collective-permute-done | bytes 524320 | tf_op jit(solution)/shard_map/while/body/eval_jaxpr/ppermute | solution.py:141
  132.1 12.9 %collective-permute-done = bf16[64,4096]{1,0:T(8,128)(2,1)S(1)} collective-permute-done((bf16[64,4096]{1,0:T(8,128)(2,1)S(1)}, bf16[64,4096]{1,0:T(8,128)(2,1)S(1)}, u32[]{:S(2)}, u32[]{:S(2)}) %collective-permute-start) | collective-permute-done | bytes 524320 | tf_op jit(solution)/shard_map/while/body/eval_jaxpr/ppermute | solution.py:141
  168.7 9.8 %collective-permute-done = bf16[64,4096]{1,0:T(8,128)(2,1)S(1)} collective-permute-done((bf16[64,4096]{1,0:T(8,128)(2,1)S(1)}, bf16[64,4096]{1,0:T(8,128)(2,1)S(1)}, u32[]{:S(2)}, u32[]{:S(2)}) %collective-permute-start) | collective-permute-done | bytes 524320 | tf_op jit(solution)/shard_map/while/body/eval_jaxpr/ppermute | solution.py:141
  212.3 9.8 %collective-permute-done = bf16[64,4096]{1,0:T(8,128)(2,1)S(1)} collective-permute-done((bf16[64,4096]{1,0:T(8,128)(2,1)S(1)}, bf16[64,4096]{1,0:T(8,128)(2,1)S(1)}, u32[]{:S(2)}, u32[]{:S(2)}) %collective-permute-start) | collective-permute-done | bytes 524320 | tf_op jit(solution)/shard_map/while/body/eval_jaxpr/ppermute | solution.py:141
  222.3 9.8 %collective-permute-done = bf16[64,4096]{1,0:T(8,128)(2,1)S(1)} collective-permute-done((bf16[64,4096]{1,0:T(8,128)(2,1)S(1)}, bf16[64,4096]{1,0:T(8,128)(2,1)S(1)}, u32[]{:S(2)}, u32[]{:S(2)}) %collective-permute-start) | collective-permute-done | bytes 524320 | tf_op jit(solution)/shard_map/while/body/eval_jaxpr/ppermute | solution.py:141
  242.2 12.9 %collective-permute-done = bf16[64,4096]{1,0:T(8,128)(2,1)S(1)} collective-permute-done((bf16[64,4096]{1,0:T(8,128)(2,1)S(1)}, bf16[64,4096]{1,0:T(8,128)(2,1)S(1)}, u32[]{:S(2)}, u32[]{:S(2)}) %collective-permute-start) | collective-permute-done | bytes 524320 | tf_op jit(solution)/shard_map/while/body/eval_jaxpr/ppermute | solution.py:141
  255.3 12.9 %collective-permute-done = bf16[64,4096]{1,0:T(8,128)(2,1)S(1)} collective-permute-done((bf16[64,4096]{1,0:T(8,128)(2,1)S(1)}, bf16[64,4096]{1,0:T(8,128)(2,1)S(1)}, u32[]{:S(2)}, u32[]{:S(2)}) %collective-permute-start) | collective-permute-done | bytes 524320 | tf_op jit(solution)/shard_map/while/body/eval_jaxpr/ppermute | solution.py:141
  268.4 12.9 %collective-permute-done = bf16[64,4096]{1,0:T(8,128)(2,1)S(1)} collective-permute-done((bf16[64,4096]{1,0:T(8,128)(2,1)S(1)}, bf16[64,4096]{1,0:T(8,128)(2,1)S(1)}, u32[]{:S(2)}, u32[]{:S(2)}) %collective-permute-start) | collective-permute-done | bytes 524320 | tf_op jit(solution)/shard_map/while/body/eval_jaxpr/ppermute | solution.py:141
  281.5 12.9 %collective-permute-done = bf16[64,4096]{1,0:T(8,128)(2,1)S(1)} collective-permute-done((bf16[64,4096]{1,0:T(8,128)(2,1)S(1)}, bf16[64,4096]{1,0:T(8,128)(2,1)S(1)}, u32[]{:S(2)}, u32[]{:S(2)}) %collective-permute-start) | collective-permute-done | bytes 524320 | tf_op jit(solution)/shard_map/while/body/eval_jaxpr/ppermute | solution.py:141
  300.4 205.4 %while.64 = (s32[]{:T(128)}, bf16[64,4096]{1,0:T(8,128)(2,1)}, bf16[2,4,64,4096]{3,2,1,0:T(8,128)(2,1)}, bf16[2,4,64,4096]{3,2,1,0:T(8,128)(2,1)}, bf16[2,4,64,5...) while((s32[]{:T(128)}, bf16[64,4096]{1,0:T(8,128)(2,1)}, ...), condition=%wide.region_7.8_spmd, body=%wide.region_4.7_spmd.sunk | while | flops 31 | bytes 4194810 | solution.py:343
  318.6 13.0 %collective-permute-start.1 = (bf16[64,4096]{1,0:T(8,128)(2,1)}, bf16[64,4096]{1,0:T(8,128)(2,1)}, u32[]{:S(2)}, u32[]{:S(2)}) collective-permute-start(bf16[64,4096]{1,0:T(8,128)(2,1)} %get-tuple-element.1171), channel_id=1, source_target_pairs={{16,0},{32,16},{48,32},{64,48},{80,64},{96,80},{112,96},{0,112},{1... | collective-permute-start | bytes 1572872 | tf_op jit(solution)/shard_map/while/body/eval_jaxpr/ppermute | solution.py:141
  340.7 13.0 %collective-permute-start.1 = (bf16[64,4096]{1,0:T(8,128)(2,1)}, bf16[64,4096]{1,0:T(8,128)(2,1)}, u32[]{:S(2)}, u32[]{:S(2)}) collective-permute-start(bf16[64,4096]{1,0:T(8,128)(2,1)} %get-tuple-element.1171), channel_id=1, source_target_pairs={{16,0},{32,16},{48,32},{64,48},{80,64},{96,80},{112,96},{0,112},{1... | collective-permute-start | bytes 1572872 | tf_op jit(solution)/shard_map/while/body/eval_jaxpr/ppermute | solution.py:141
  362.7 13.0 %collective-permute-start.1 = (bf16[64,4096]{1,0:T(8,128)(2,1)}, bf16[64,4096]{1,0:T(8,128)(2,1)}, u32[]{:S(2)}, u32[]{:S(2)}) collective-permute-start(bf16[64,4096]{1,0:T(8,128)(2,1)} %get-tuple-element.1171), channel_id=1, source_target_pairs={{16,0},{32,16},{48,32},{64,48},{80,64},{96,80},{112,96},{0,112},{1... | collective-permute-start | bytes 1572872 | tf_op jit(solution)/shard_map/while/body/eval_jaxpr/ppermute | solution.py:141
  420.9 9.9 %conditional.7 = ((bf16[64,4096]{1,0:T(8,128)(2,1)}, bf16[2,4,64,4096]{3,2,1,0:T(8,128)(2,1)}, bf16[2,4,64,4096]{3,2,1,0:T(8,128)(2,1)}, bf16[2,4,64,512]{3,2,1,0:T(8,128)(2,1)S(1)}, bf16[2,4,64,512]{3,2,1,0:T(8,128)(2,1)S(1)})) conditional(s32[]{:T(128)} %convert_element_type.164, (bf16[64,4096]{1,0:T(8,128)(2,1)}, ...), branch_computations={%region_5.5_spmd, %region_6.6_spmd} | conditional | bytes 1048584 | solution.py:327
  439.8 9.9 %conditional.7 = ((bf16[64,4096]{1,0:T(8,128)(2,1)}, bf16[2,4,64,4096]{3,2,1,0:T(8,128)(2,1)}, bf16[2,4,64,4096]{3,2,1,0:T(8,128)(2,1)}, bf16[2,4,64,512]{3,2,1,0:T(8,128)(2,1)S(1)}, bf16[2,4,64,512]{3,2,1,0:T(8,128)(2,1)S(1)})) conditional(s32[]{:T(128)} %convert_element_type.164, (bf16[64,4096]{1,0:T(8,128)(2,1)}, ...), branch_computations={%region_5.5_spmd, %region_6.6_spmd} | conditional | bytes 1048584 | solution.py:327
  461.8 9.9 %conditional.7 = ((bf16[64,4096]{1,0:T(8,128)(2,1)}, bf16[2,4,64,4096]{3,2,1,0:T(8,128)(2,1)}, bf16[2,4,64,4096]{3,2,1,0:T(8,128)(2,1)}, bf16[2,4,64,512]{3,2,1,0:T(8,128)(2,1)S(1)}, bf16[2,4,64,512]{3,2,1,0:T(8,128)(2,1)S(1)})) conditional(s32[]{:T(128)} %convert_element_type.164, (bf16[64,4096]{1,0:T(8,128)(2,1)}, ...), branch_computations={%region_5.5_spmd, %region_6.6_spmd} | conditional | bytes 1048584 | solution.py:327
  483.8 9.9 %conditional.7 = ((bf16[64,4096]{1,0:T(8,128)(2,1)}, bf16[2,4,64,4096]{3,2,1,0:T(8,128)(2,1)}, bf16[2,4,64,4096]{3,2,1,0:T(8,128)(2,1)}, bf16[2,4,64,512]{3,2,1,0:T(8,128)(2,1)S(1)}, bf16[2,4,64,512]{3,2,1,0:T(8,128)(2,1)S(1)})) conditional(s32[]{:T(128)} %convert_element_type.164, (bf16[64,4096]{1,0:T(8,128)(2,1)}, ...), branch_computations={%region_5.5_spmd, %region_6.6_spmd} | conditional | bytes 1048584 | solution.py:327
  515.9 137.7 %while.65 = (s32[]{:T(128)}, bf16[64,4096]{1,0:T(8,128)(2,1)}, bf16[2,4,64,4096]{3,2,1,0:T(8,128)(2,1)}, bf16[2,4,64,4096]{3,2,1,0:T(8,128)(2,1)}, bf16[2,4,64,5...) while((s32[]{:T(128)}, bf16[64,4096]{1,0:T(8,128)(2,1)}, ...), condition=%wide.region_11.12_spmd, body=%wide.region_8.11_spmd.sunk | while | flops 32 | bytes 4194830 | solution.py:345
  516.0 13.0 %collective-permute-start.2 = (bf16[64,4096]{1,0:T(8,128)(2,1)}, bf16[64,4096]{1,0:T(8,128)(2,1)}, u32[]{:S(2)}, u32[]{:S(2)}) collective-permute-start(bf16[64,4096]{1,0:T(8,128)(2,1)} %get-tuple-element.1188), channel_id=1, source_target_pairs={{16,0},{32,16},{48,32},{64,48},{80,64},{96,80},{112,96},{0,112},{1... | collective-permute-start | bytes 1572872 | tf_op jit(solution)/shard_map/while/body/eval_jaxpr/ppermute | solution.py:141
  574.9 10.0 %conditional.8 = ((bf16[64,4096]{1,0:T(8,128)(2,1)}, bf16[2,4,64,4096]{3,2,1,0:T(8,128)(2,1)}, bf16[2,4,64,4096]{3,2,1,0:T(8,128)(2,1)}, bf16[2,4,64,512]{3,2,1,0:T(8,128)(2,1)S(1)}, bf16[2,4,64,512]{3,2,1,0:T(8,128)(2,1)S(1)})) conditional(s32[]{:T(128)} %convert_element_type.165, (bf16[64,4096]{1,0:T(8,128)(2,1)}, ...), branch_computations={%region_9.9_spmd, %region_10.10_spmd} | conditional | bytes 1048584 | solution.py:327
  593.9 10.0 %conditional.8 = ((bf16[64,4096]{1,0:T(8,128)(2,1)}, bf16[2,4,64,4096]{3,2,1,0:T(8,128)(2,1)}, bf16[2,4,64,4096]{3,2,1,0:T(8,128)(2,1)}, bf16[2,4,64,512]{3,2,1,0:T(8,128)(2,1)S(1)}, bf16[2,4,64,512]{3,2,1,0:T(8,128)(2,1)S(1)})) conditional(s32[]{:T(128)} %convert_element_type.165, (bf16[64,4096]{1,0:T(8,128)(2,1)}, ...), branch_computations={%region_9.9_spmd, %region_10.10_spmd} | conditional | bytes 1048584 | solution.py:327
  612.9 9.9 %conditional.8 = ((bf16[64,4096]{1,0:T(8,128)(2,1)}, bf16[2,4,64,4096]{3,2,1,0:T(8,128)(2,1)}, bf16[2,4,64,4096]{3,2,1,0:T(8,128)(2,1)}, bf16[2,4,64,512]{3,2,1,0:T(8,128)(2,1)S(1)}, bf16[2,4,64,512]{3,2,1,0:T(8,128)(2,1)S(1)})) conditional(s32[]{:T(128)} %convert_element_type.165, (bf16[64,4096]{1,0:T(8,128)(2,1)}, ...), branch_computations={%region_9.9_spmd, %region_10.10_spmd} | conditional | bytes 1048584 | solution.py:327
  622.8 10.0 %collective-permute-done.2 = bf16[64,4096]{1,0:T(8,128)(2,1)} collective-permute-done((bf16[64,4096]{1,0:T(8,128)(2,1)}, bf16[64,4096]{1,0:T(8,128)(2,1)}, u32[]{:S(2)}, u32[]{:S(2)}) %collective-permute-start.2) | collective-permute-done | bytes 524320 | tf_op jit(solution)/shard_map/while/body/eval_jaxpr/ppermute | solution.py:141
  634.8 9.9 %conditional.8 = ((bf16[64,4096]{1,0:T(8,128)(2,1)}, bf16[2,4,64,4096]{3,2,1,0:T(8,128)(2,1)}, bf16[2,4,64,4096]{3,2,1,0:T(8,128)(2,1)}, bf16[2,4,64,512]{3,2,1,0:T(8,128)(2,1)S(1)}, bf16[2,4,64,512]{3,2,1,0:T(8,128)(2,1)S(1)})) conditional(s32[]{:T(128)} %convert_element_type.165, (bf16[64,4096]{1,0:T(8,128)(2,1)}, ...), branch_computations={%region_9.9_spmd, %region_10.10_spmd} | conditional | bytes 1048584 | solution.py:327
  670.4 81.2 %reduce-scatter.3.cloned.1.call-done = bf16[256,1024]{1,0:T(8,128)(2,1)} async-done(((bf16[4096,1024]{1,0:T(8,128)(2,1)}), bf16[256,1024]{1,0:T(8,128)(2,1)}) %reduce-scatter.3.cloned.1.call-update) | async-done | bytes 524304 | tf_op jit(solution)/shard_map/reduce_scatter | solution.py:239
  (262 shorter events, 491.3 us)
Async XLA Ops:
  7.2 660.8 %reduce-scatter.5.cloned.1.call-start = ((), (), s32[]{:S(2)}) async-start(), calls=%async_computation.3 | async-start | bytes 8912896 | tf_op jit(solution)/shard_map/reduce_scatter | solution.py:239
  41.8 9.8 %collective-permute-start = (bf16[64,4096]{1,0:T(8,128)(2,1)S(1)}, bf16[64,4096]{1,0:T(8,128)(2,1)S(1)}, u32[]{:S(2)}, u32[]{:S(2)}) collective-permute-start(bf16[64,4096]{1,0:T(8,128)(2,1)S(1)} %get-tuple-element.1157), channel_id=1, source_target_pairs={{112,0},{0,16},{16,32},{32,48},{48,64},{64,80},{80,96},{96,112},{1... | collective-permute-start | bytes 1572872 | tf_op jit(solution)/shard_map/while/body/eval_jaxpr/ppermute | solution.py:141
  58.6 9.8 %collective-permute-start = (bf16[64,4096]{1,0:T(8,128)(2,1)S(1)}, bf16[64,4096]{1,0:T(8,128)(2,1)S(1)}, u32[]{:S(2)}, u32[]{:S(2)}) collective-permute-start(bf16[64,4096]{1,0:T(8,128)(2,1)S(1)} %get-tuple-element.1157), channel_id=1, source_target_pairs={{112,0},{0,16},{16,32},{32,48},{48,64},{64,80},{80,96},{96,112},{1... | collective-permute-start | bytes 1572872 | tf_op jit(solution)/shard_map/while/body/eval_jaxpr/ppermute | solution.py:141
  75.4 9.8 %collective-permute-start = (bf16[64,4096]{1,0:T(8,128)(2,1)S(1)}, bf16[64,4096]{1,0:T(8,128)(2,1)S(1)}, u32[]{:S(2)}, u32[]{:S(2)}) collective-permute-start(bf16[64,4096]{1,0:T(8,128)(2,1)S(1)} %get-tuple-element.1157), channel_id=1, source_target_pairs={{112,0},{0,16},{16,32},{32,48},{48,64},{64,80},{80,96},{96,112},{1... | collective-permute-start | bytes 1572872 | tf_op jit(solution)/shard_map/while/body/eval_jaxpr/ppermute | solution.py:141
  102.1 9.8 %collective-permute-start = (bf16[64,4096]{1,0:T(8,128)(2,1)S(1)}, bf16[64,4096]{1,0:T(8,128)(2,1)S(1)}, u32[]{:S(2)}, u32[]{:S(2)}) collective-permute-start(bf16[64,4096]{1,0:T(8,128)(2,1)S(1)} %get-tuple-element.1157), channel_id=1, source_target_pairs={{112,0},{0,16},{16,32},{32,48},{48,64},{64,80},{80,96},{96,112},{1... | collective-permute-start | bytes 1572872 | tf_op jit(solution)/shard_map/while/body/eval_jaxpr/ppermute | solution.py:141
  112.1 9.8 %collective-permute-start = (bf16[64,4096]{1,0:T(8,128)(2,1)S(1)}, bf16[64,4096]{1,0:T(8,128)(2,1)S(1)}, u32[]{:S(2)}, u32[]{:S(2)}) collective-permute-start(bf16[64,4096]{1,0:T(8,128)(2,1)S(1)} %get-tuple-element.1157), channel_id=1, source_target_pairs={{112,0},{0,16},{16,32},{32,48},{48,64},{64,80},{80,96},{96,112},{1... | collective-permute-start | bytes 1572872 | tf_op jit(solution)/shard_map/while/body/eval_jaxpr/ppermute | solution.py:141
  122.1 9.8 %collective-permute-start = (bf16[64,4096]{1,0:T(8,128)(2,1)S(1)}, bf16[64,4096]{1,0:T(8,128)(2,1)S(1)}, u32[]{:S(2)}, u32[]{:S(2)}) collective-permute-start(bf16[64,4096]{1,0:T(8,128)(2,1)S(1)} %get-tuple-element.1157), channel_id=1, source_target_pairs={{112,0},{0,16},{16,32},{32,48},{48,64},{64,80},{80,96},{96,112},{1... | collective-permute-start | bytes 1572872 | tf_op jit(solution)/shard_map/while/body/eval_jaxpr/ppermute | solution.py:141
  132.1 12.9 %collective-permute-start = (bf16[64,4096]{1,0:T(8,128)(2,1)S(1)}, bf16[64,4096]{1,0:T(8,128)(2,1)S(1)}, u32[]{:S(2)}, u32[]{:S(2)}) collective-permute-start(bf16[64,4096]{1,0:T(8,128)(2,1)S(1)} %get-tuple-element.1157), channel_id=1, source_target_pairs={{112,0},{0,16},{16,32},{32,48},{48,64},{64,80},{80,96},{96,112},{1... | collective-permute-start | bytes 1572872 | tf_op jit(solution)/shard_map/while/body/eval_jaxpr/ppermute | solution.py:141
  168.7 9.8 %collective-permute-start = (bf16[64,4096]{1,0:T(8,128)(2,1)S(1)}, bf16[64,4096]{1,0:T(8,128)(2,1)S(1)}, u32[]{:S(2)}, u32[]{:S(2)}) collective-permute-start(bf16[64,4096]{1,0:T(8,128)(2,1)S(1)} %get-tuple-element.1157), channel_id=1, source_target_pairs={{112,0},{0,16},{16,32},{32,48},{48,64},{64,80},{80,96},{96,112},{1... | collective-permute-start | bytes 1572872 | tf_op jit(solution)/shard_map/while/body/eval_jaxpr/ppermute | solution.py:141
  212.3 9.8 %collective-permute-start = (bf16[64,4096]{1,0:T(8,128)(2,1)S(1)}, bf16[64,4096]{1,0:T(8,128)(2,1)S(1)}, u32[]{:S(2)}, u32[]{:S(2)}) collective-permute-start(bf16[64,4096]{1,0:T(8,128)(2,1)S(1)} %get-tuple-element.1157), channel_id=1, source_target_pairs={{112,0},{0,16},{16,32},{32,48},{48,64},{64,80},{80,96},{96,112},{1... | collective-permute-start | bytes 1572872 | tf_op jit(solution)/shard_map/while/body/eval_jaxpr/ppermute | solution.py:141
  222.3 9.8 %collective-permute-start = (bf16[64,4096]{1,0:T(8,128)(2,1)S(1)}, bf16[64,4096]{1,0:T(8,128)(2,1)S(1)}, u32[]{:S(2)}, u32[]{:S(2)}) collective-permute-start(bf16[64,4096]{1,0:T(8,128)(2,1)S(1)} %get-tuple-element.1157), channel_id=1, source_target_pairs={{112,0},{0,16},{16,32},{32,48},{48,64},{64,80},{80,96},{96,112},{1... | collective-permute-start | bytes 1572872 | tf_op jit(solution)/shard_map/while/body/eval_jaxpr/ppermute | solution.py:141
  232.2 9.8 %collective-permute-start = (bf16[64,4096]{1,0:T(8,128)(2,1)S(1)}, bf16[64,4096]{1,0:T(8,128)(2,1)S(1)}, u32[]{:S(2)}, u32[]{:S(2)}) collective-permute-start(bf16[64,4096]{1,0:T(8,128)(2,1)S(1)} %get-tuple-element.1157), channel_id=1, source_target_pairs={{112,0},{0,16},{16,32},{32,48},{48,64},{64,80},{80,96},{96,112},{1... | collective-permute-start | bytes 1572872 | tf_op jit(solution)/shard_map/while/body/eval_jaxpr/ppermute | solution.py:141
  242.2 12.9 %collective-permute-start = (bf16[64,4096]{1,0:T(8,128)(2,1)S(1)}, bf16[64,4096]{1,0:T(8,128)(2,1)S(1)}, u32[]{:S(2)}, u32[]{:S(2)}) collective-permute-start(bf16[64,4096]{1,0:T(8,128)(2,1)S(1)} %get-tuple-element.1157), channel_id=1, source_target_pairs={{112,0},{0,16},{16,32},{32,48},{48,64},{64,80},{80,96},{96,112},{1... | collective-permute-start | bytes 1572872 | tf_op jit(solution)/shard_map/while/body/eval_jaxpr/ppermute | solution.py:141
  255.3 12.9 %collective-permute-start = (bf16[64,4096]{1,0:T(8,128)(2,1)S(1)}, bf16[64,4096]{1,0:T(8,128)(2,1)S(1)}, u32[]{:S(2)}, u32[]{:S(2)}) collective-permute-start(bf16[64,4096]{1,0:T(8,128)(2,1)S(1)} %get-tuple-element.1157), channel_id=1, source_target_pairs={{112,0},{0,16},{16,32},{32,48},{48,64},{64,80},{80,96},{96,112},{1... | collective-permute-start | bytes 1572872 | tf_op jit(solution)/shard_map/while/body/eval_jaxpr/ppermute | solution.py:141
  268.4 12.9 %collective-permute-start = (bf16[64,4096]{1,0:T(8,128)(2,1)S(1)}, bf16[64,4096]{1,0:T(8,128)(2,1)S(1)}, u32[]{:S(2)}, u32[]{:S(2)}) collective-permute-start(bf16[64,4096]{1,0:T(8,128)(2,1)S(1)} %get-tuple-element.1157), channel_id=1, source_target_pairs={{112,0},{0,16},{16,32},{32,48},{48,64},{64,80},{80,96},{96,112},{1... | collective-permute-start | bytes 1572872 | tf_op jit(solution)/shard_map/while/body/eval_jaxpr/ppermute | solution.py:141
  281.5 12.9 %collective-permute-start = (bf16[64,4096]{1,0:T(8,128)(2,1)S(1)}, bf16[64,4096]{1,0:T(8,128)(2,1)S(1)}, u32[]{:S(2)}, u32[]{:S(2)}) collective-permute-start(bf16[64,4096]{1,0:T(8,128)(2,1)S(1)} %get-tuple-element.1157), channel_id=1, source_target_pairs={{112,0},{0,16},{16,32},{32,48},{48,64},{64,80},{80,96},{96,112},{1... | collective-permute-start | bytes 1572872 | tf_op jit(solution)/shard_map/while/body/eval_jaxpr/ppermute | solution.py:141
  300.5 16.2 %collective-permute-start.1 = (bf16[64,4096]{1,0:T(8,128)(2,1)}, bf16[64,4096]{1,0:T(8,128)(2,1)}, u32[]{:S(2)}, u32[]{:S(2)}) collective-permute-start(bf16[64,4096]{1,0:T(8,128)(2,1)} %get-tuple-element.1171), channel_id=1, source_target_pairs={{16,0},{32,16},{48,32},{64,48},{80,64},{96,80},{112,96},{0,112},{1... | collective-permute-start | bytes 1572872 | tf_op jit(solution)/shard_map/while/body/eval_jaxpr/ppermute | solution.py:141
  318.6 20.1 %collective-permute-start.1 = (bf16[64,4096]{1,0:T(8,128)(2,1)}, bf16[64,4096]{1,0:T(8,128)(2,1)}, u32[]{:S(2)}, u32[]{:S(2)}) collective-permute-start(bf16[64,4096]{1,0:T(8,128)(2,1)} %get-tuple-element.1171), channel_id=1, source_target_pairs={{16,0},{32,16},{48,32},{64,48},{80,64},{96,80},{112,96},{0,112},{1... | collective-permute-start | bytes 1572872 | tf_op jit(solution)/shard_map/while/body/eval_jaxpr/ppermute | solution.py:141
  340.7 20.1 %collective-permute-start.1 = (bf16[64,4096]{1,0:T(8,128)(2,1)}, bf16[64,4096]{1,0:T(8,128)(2,1)}, u32[]{:S(2)}, u32[]{:S(2)}) collective-permute-start(bf16[64,4096]{1,0:T(8,128)(2,1)} %get-tuple-element.1171), channel_id=1, source_target_pairs={{16,0},{32,16},{48,32},{64,48},{80,64},{96,80},{112,96},{0,112},{1... | collective-permute-start | bytes 1572872 | tf_op jit(solution)/shard_map/while/body/eval_jaxpr/ppermute | solution.py:141
  362.7 20.1 %collective-permute-start.1 = (bf16[64,4096]{1,0:T(8,128)(2,1)}, bf16[64,4096]{1,0:T(8,128)(2,1)}, u32[]{:S(2)}, u32[]{:S(2)}) collective-permute-start(bf16[64,4096]{1,0:T(8,128)(2,1)} %get-tuple-element.1171), channel_id=1, source_target_pairs={{16,0},{32,16},{48,32},{64,48},{80,64},{96,80},{112,96},{0,112},{1... | collective-permute-start | bytes 1572872 | tf_op jit(solution)/shard_map/while/body/eval_jaxpr/ppermute | solution.py:141
  384.7 10.1 %collective-permute-start.1 = (bf16[64,4096]{1,0:T(8,128)(2,1)}, bf16[64,4096]{1,0:T(8,128)(2,1)}, u32[]{:S(2)}, u32[]{:S(2)}) collective-permute-start(bf16[64,4096]{1,0:T(8,128)(2,1)} %get-tuple-element.1171), channel_id=1, source_target_pairs={{16,0},{32,16},{48,32},{64,48},{80,64},{96,80},{112,96},{0,112},{1... | collective-permute-start | bytes 1572872 | tf_op jit(solution)/shard_map/while/body/eval_jaxpr/ppermute | solution.py:141
  396.8 10.1 %collective-permute-start.1 = (bf16[64,4096]{1,0:T(8,128)(2,1)}, bf16[64,4096]{1,0:T(8,128)(2,1)}, u32[]{:S(2)}, u32[]{:S(2)}) collective-permute-start(bf16[64,4096]{1,0:T(8,128)(2,1)} %get-tuple-element.1171), channel_id=1, source_target_pairs={{16,0},{32,16},{48,32},{64,48},{80,64},{96,80},{112,96},{0,112},{1... | collective-permute-start | bytes 1572872 | tf_op jit(solution)/shard_map/while/body/eval_jaxpr/ppermute | solution.py:141
  408.8 10.1 %collective-permute-start.1 = (bf16[64,4096]{1,0:T(8,128)(2,1)}, bf16[64,4096]{1,0:T(8,128)(2,1)}, u32[]{:S(2)}, u32[]{:S(2)}) collective-permute-start(bf16[64,4096]{1,0:T(8,128)(2,1)} %get-tuple-element.1171), channel_id=1, source_target_pairs={{16,0},{32,16},{48,32},{64,48},{80,64},{96,80},{112,96},{0,112},{1... | collective-permute-start | bytes 1572872 | tf_op jit(solution)/shard_map/while/body/eval_jaxpr/ppermute | solution.py:141
  449.7 10.1 %collective-permute-start.1 = (bf16[64,4096]{1,0:T(8,128)(2,1)}, bf16[64,4096]{1,0:T(8,128)(2,1)}, u32[]{:S(2)}, u32[]{:S(2)}) collective-permute-start(bf16[64,4096]{1,0:T(8,128)(2,1)} %get-tuple-element.1171), channel_id=1, source_target_pairs={{16,0},{32,16},{48,32},{64,48},{80,64},{96,80},{112,96},{0,112},{1... | collective-permute-start | bytes 1572872 | tf_op jit(solution)/shard_map/while/body/eval_jaxpr/ppermute | solution.py:141
  471.8 10.1 %collective-permute-start.1 = (bf16[64,4096]{1,0:T(8,128)(2,1)}, bf16[64,4096]{1,0:T(8,128)(2,1)}, u32[]{:S(2)}, u32[]{:S(2)}) collective-permute-start(bf16[64,4096]{1,0:T(8,128)(2,1)} %get-tuple-element.1171), channel_id=1, source_target_pairs={{16,0},{32,16},{48,32},{64,48},{80,64},{96,80},{112,96},{0,112},{1... | collective-permute-start | bytes 1572872 | tf_op jit(solution)/shard_map/while/body/eval_jaxpr/ppermute | solution.py:141
  493.8 10.1 %collective-permute-start.1 = (bf16[64,4096]{1,0:T(8,128)(2,1)}, bf16[64,4096]{1,0:T(8,128)(2,1)}, u32[]{:S(2)}, u32[]{:S(2)}) collective-permute-start(bf16[64,4096]{1,0:T(8,128)(2,1)} %get-tuple-element.1171), channel_id=1, source_target_pairs={{16,0},{32,16},{48,32},{64,48},{80,64},{96,80},{112,96},{0,112},{1... | collective-permute-start | bytes 1572872 | tf_op jit(solution)/shard_map/while/body/eval_jaxpr/ppermute | solution.py:141
  515.7 235.9 %reduce-scatter.3.cloned.1.call-start = ((), (), s32[]{:S(2)}) async-start(), calls=%async_computation.2 | async-start | bytes 8912896 | tf_op jit(solution)/shard_map/reduce_scatter | solution.py:239
  516.0 20.1 %collective-permute-start.2 = (bf16[64,4096]{1,0:T(8,128)(2,1)}, bf16[64,4096]{1,0:T(8,128)(2,1)}, u32[]{:S(2)}, u32[]{:S(2)}) collective-permute-start(bf16[64,4096]{1,0:T(8,128)(2,1)} %get-tuple-element.1188), channel_id=1, source_target_pairs={{16,0},{32,16},{48,32},{64,48},{80,64},{96,80},{112,96},{0,112},{1... | collective-permute-start | bytes 1572872 | tf_op jit(solution)/shard_map/while/body/eval_jaxpr/ppermute | solution.py:141
  538.1 10.4 %collective-permute-start.2 = (bf16[64,4096]{1,0:T(8,128)(2,1)}, bf16[64,4096]{1,0:T(8,128)(2,1)}, u32[]{:S(2)}, u32[]{:S(2)}) collective-permute-start(bf16[64,4096]{1,0:T(8,128)(2,1)} %get-tuple-element.1188), channel_id=1, source_target_pairs={{16,0},{32,16},{48,32},{64,48},{80,64},{96,80},{112,96},{0,112},{1... | collective-permute-start | bytes 1572872 | tf_op jit(solution)/shard_map/while/body/eval_jaxpr/ppermute | solution.py:141
  550.5 10.4 %collective-permute-start.2 = (bf16[64,4096]{1,0:T(8,128)(2,1)}, bf16[64,4096]{1,0:T(8,128)(2,1)}, u32[]{:S(2)}, u32[]{:S(2)}) collective-permute-start(bf16[64,4096]{1,0:T(8,128)(2,1)} %get-tuple-element.1188), channel_id=1, source_target_pairs={{16,0},{32,16},{48,32},{64,48},{80,64},{96,80},{112,96},{0,112},{1... | collective-permute-start | bytes 1572872 | tf_op jit(solution)/shard_map/while/body/eval_jaxpr/ppermute | solution.py:141
  562.8 10.1 %collective-permute-start.2 = (bf16[64,4096]{1,0:T(8,128)(2,1)}, bf16[64,4096]{1,0:T(8,128)(2,1)}, u32[]{:S(2)}, u32[]{:S(2)}) collective-permute-start(bf16[64,4096]{1,0:T(8,128)(2,1)} %get-tuple-element.1188), channel_id=1, source_target_pairs={{16,0},{32,16},{48,32},{64,48},{80,64},{96,80},{112,96},{0,112},{1... | collective-permute-start | bytes 1572872 | tf_op jit(solution)/shard_map/while/body/eval_jaxpr/ppermute | solution.py:141
  622.8 10.0 %collective-permute-start.2 = (bf16[64,4096]{1,0:T(8,128)(2,1)}, bf16[64,4096]{1,0:T(8,128)(2,1)}, u32[]{:S(2)}, u32[]{:S(2)}) collective-permute-start(bf16[64,4096]{1,0:T(8,128)(2,1)} %get-tuple-element.1188), channel_id=1, source_target_pairs={{16,0},{32,16},{48,32},{64,48},{80,64},{96,80},{112,96},{0,112},{1... | collective-permute-start | bytes 1572872 | tf_op jit(solution)/shard_map/while/body/eval_jaxpr/ppermute | solution.py:141
  (15 other events, 96.8 us)
Sparse Core Ops, SparseCore 0:
  515.8 88.6 reduce-scatter.4
  663.6 87.8 reduce-scatter.2

commit v12 on v10

--- a/solution.py
+++ b/solution.py
@@ -219,7 +219,7 @@
     return lax.dynamic_update_slice(buffer, value[None, None], (lap_now, micro, anchor, anchor))
 
 
-def settle(lap_idx, stores, mask_a, mask_b):
+def settle(lap_idx, stores, mask_a, mask_b, exchange):
     normed_all, upstream_all, hidden_all, back_all = [
         buffer[lap_idx].reshape(-1, buffer.shape[-1]) for buffer in stores
     ]
@@ -236,7 +236,12 @@
     joined = lax.dot_general(
         left, right, (((0,), (0,)), ((), ())), preferred_element_type=jnp.float32
     ).astype(jnp.bfloat16)
-    summed = lax.psum_scatter(joined, "dp", scatter_dimension=0, tiled=True).astype(jnp.float32)
+    if exchange:
+        blocks = joined.reshape(groups, span, joined.shape[-1])
+        received = lax.all_to_all(blocks, "dp", 0, 0)
+        summed = jnp.sum(received.astype(jnp.float32), axis=0)
+    else:
+        summed = lax.psum_scatter(joined, "dp", scatter_dimension=0, tiled=True).astype(jnp.float32)
     sum_a, sum_b = summed[:, :inner], summed[:, inner:]
     full_a = expand_blocks(mask_a[lap_idx, 0]).astype(jnp.float32)
     full_b = expand_blocks(mask_b[lap_idx, 0]).astype(jnp.float32)
@@ -341,9 +346,9 @@
     middle = batches + sections - 1
     finish = batches + 2 * sections - 1
     carry = lax.fori_loop(0, middle, backward_step, (start_rows, stores))
-    later_one = settle(1, carry[1], mask_a, mask_b)
+    later_one = settle(1, carry[1], mask_a, mask_b, False)
     carry = lax.fori_loop(middle, finish, backward_step, carry)
-    later_zero = settle(0, carry[1], mask_a, mask_b)
+    later_zero = settle(0, carry[1], mask_a, mask_b, True)
     grad_a = jnp.stack([later_zero[0], later_one[0]])[:, None]
     grad_b = jnp.stack([later_zero[1], later_one[1]])[:, None]
     return (grad_a, grad_b)

time: 719 us -> 767 us (1.067)
  waiting for transfers between devices: 415 us -> 451 us
  starting transfers between devices: 83.1 us -> 91.2 us
    all_to_all x0 -> x1, waiting for transfers between devices: none -> 118 us  [settle(): received = lax.all_to_all(blocks, 'dp', 0, 0)]
    reduce_scatter x2 -> x1, waiting for transfers between devices: 81.8 us -> 0.02 us  [settle(): lax.psum_scatter(joined, 'dp', scatter_dimension=0, tiled=True)]
    all_to_all x0 -> x1, starting transfers between devices: none -> 8.32 us  [settle(): received = lax.all_to_all(blocks, 'dp', 0, 0)]
where the time goes in v12:
time: 767 us; the launch traced here: 765 us
  waiting for transfers between devices  451 us (59%)
  Pallas kernels  151 us (20%)
  starting transfers between devices  91.2 us (12%)
  local copies, waits for them, and re-layouts  32 us (4%)
  between operations  14.4 us (2%)
  matrix products  13.8 us (2%)
  other arithmetic  11 us (1%)
    ppermute x38, waiting for transfers between devices, shifted(): return lax.ppermute(block, axis, route)  333 us
    all_to_all x1, waiting for transfers between devices, settle(): received = lax.all_to_all(blocks, 'dp', 0, 0)  118 us
    ppermute x38, starting transfers between devices, shifted(): return lax.ppermute(block, axis, route)  82.8 us
    pallas_call x8, Pallas kernels, bwd_call(): pl.pallas_call(_bwd_kernel, grid_spec=pltpu.PrefetchScalarGridSpec(num_sc...  72.9 us
    pallas_call x8, Pallas kernels, fwd_call(): pl.pallas_call(_fwd_kernel, grid_spec=pltpu.PrefetchScalarGridSpec(num_sc...  54 us
    pallas_call x2, Pallas kernels, masked(): pl.pallas_call(kernel, grid_spec=pltpu.PrefetchScalarGridSpec(num_scalar_...  24.3 us
    another operation x29, local copies, waits for them, and re-layouts  18 us
  transfers between devices with their start and end apart: 40, of which 39 were waited for; matrix products, arithmetic and copies ran while one was open for 3% of the time, Pallas kernels for 5%

profile of v12, /device:TPU:0, one launch (start us, length us, event | category | flops | bytes accessed | tf_op | source)
XLA Modules:
  0.0 765.5 jit_solution(6145807197175055973)
XLA Ops:
  8.0 14.2 %shard_map.77 = bf16[2,4096,512]{2,1,0:T(8,128)(2,1)} custom-call(s32[2,64,8]{2,1,0:T(8,128)S(1)} %bitcast.86, bf16[2,4096,512]{2,1,0:T(8,128)(2,1)} %bitcast.92), custom_call_target="tpu_custom_call" | custom-call | tf_op jit(solution)/shard_map/pallas_call | solution.py:166
  22.2 10.2 %shard_map.78 = bf16[2,512,4096]{2,1,0:T(8,128)(2,1)} custom-call(s32[2,8,64]{2,1,0:T(8,128)S(1)} %bitcast.87, bf16[2,512,4096]{2,1,0:T(8,128)(2,1)} %bitcast.94), custom_call_target="tpu_custom_call" | custom-call | tf_op jit(solution)/shard_map/pallas_call | solution.py:166
  35.0 257.8 %while.66 = (s32[]{:T(128)}, bf16[64,4096]{1,0:T(8,128)(2,1)S(1)}, bf16[2,4,64,4096]{3,2,1,0:T(8,128)(2,1)}, s32[]{:T(128)}, pred[]{:T(512)}, /*index=5*/bf16[4,...) while((s32[]{:T(128)}, bf16[64,4096]{1,0:T(8,128)(2,1)S(1)}, ...), condition=%wide.region_3.4_spmd, body=%wide.region_0.3_spmd.sunk | while | flops 31 | bytes 2621852 | solution.py:300
  41.8 9.8 %collective-permute-done = bf16[64,4096]{1,0:T(8,128)(2,1)S(1)} collective-permute-done((bf16[64,4096]{1,0:T(8,128)(2,1)S(1)}, bf16[64,4096]{1,0:T(8,128)(2,1)S(1)}, u32[]{:S(2)}, u32[]{:S(2)}) %collective-permute-start) | collective-permute-done | bytes 524320 | tf_op jit(solution)/shard_map/while/body/eval_jaxpr/ppermute | solution.py:141
  58.4 9.8 %collective-permute-done = bf16[64,4096]{1,0:T(8,128)(2,1)S(1)} collective-permute-done((bf16[64,4096]{1,0:T(8,128)(2,1)S(1)}, bf16[64,4096]{1,0:T(8,128)(2,1)S(1)}, u32[]{:S(2)}, u32[]{:S(2)}) %collective-permute-start) | collective-permute-done | bytes 524320 | tf_op jit(solution)/shard_map/while/body/eval_jaxpr/ppermute | solution.py:141
  75.1 9.8 %collective-permute-done = bf16[64,4096]{1,0:T(8,128)(2,1)S(1)} collective-permute-done((bf16[64,4096]{1,0:T(8,128)(2,1)S(1)}, bf16[64,4096]{1,0:T(8,128)(2,1)S(1)}, u32[]{:S(2)}, u32[]{:S(2)}) %collective-permute-start) | collective-permute-done | bytes 524320 | tf_op jit(solution)/shard_map/while/body/eval_jaxpr/ppermute | solution.py:141
  91.7 9.8 %collective-permute-done = bf16[64,4096]{1,0:T(8,128)(2,1)S(1)} collective-permute-done((bf16[64,4096]{1,0:T(8,128)(2,1)S(1)}, bf16[64,4096]{1,0:T(8,128)(2,1)S(1)}, u32[]{:S(2)}, u32[]{:S(2)}) %collective-permute-start) | collective-permute-done | bytes 524320 | tf_op jit(solution)/shard_map/while/body/eval_jaxpr/ppermute | solution.py:141
  101.7 9.8 %collective-permute-done = bf16[64,4096]{1,0:T(8,128)(2,1)S(1)} collective-permute-done((bf16[64,4096]{1,0:T(8,128)(2,1)S(1)}, bf16[64,4096]{1,0:T(8,128)(2,1)S(1)}, u32[]{:S(2)}, u32[]{:S(2)}) %collective-permute-start) | collective-permute-done | bytes 524320 | tf_op jit(solution)/shard_map/while/body/eval_jaxpr/ppermute | solution.py:141
  111.7 9.8 %collective-permute-done = bf16[64,4096]{1,0:T(8,128)(2,1)S(1)} collective-permute-done((bf16[64,4096]{1,0:T(8,128)(2,1)S(1)}, bf16[64,4096]{1,0:T(8,128)(2,1)S(1)}, u32[]{:S(2)}, u32[]{:S(2)}) %collective-permute-start) | collective-permute-done | bytes 524320 | tf_op jit(solution)/shard_map/while/body/eval_jaxpr/ppermute | solution.py:141
  122.2 9.2 %collective-permute-done = bf16[64,4096]{1,0:T(8,128)(2,1)S(1)} collective-permute-done((bf16[64,4096]{1,0:T(8,128)(2,1)S(1)}, bf16[64,4096]{1,0:T(8,128)(2,1)S(1)}, u32[]{:S(2)}, u32[]{:S(2)}) %collective-permute-start) | collective-permute-done | bytes 524320 | tf_op jit(solution)/shard_map/while/body/eval_jaxpr/ppermute | solution.py:141
  131.6 12.8 %collective-permute-done = bf16[64,4096]{1,0:T(8,128)(2,1)S(1)} collective-permute-done((bf16[64,4096]{1,0:T(8,128)(2,1)S(1)}, bf16[64,4096]{1,0:T(8,128)(2,1)S(1)}, u32[]{:S(2)}, u32[]{:S(2)}) %collective-permute-start) | collective-permute-done | bytes 524320 | tf_op jit(solution)/shard_map/while/body/eval_jaxpr/ppermute | solution.py:141
  151.2 9.8 %collective-permute-done = bf16[64,4096]{1,0:T(8,128)(2,1)S(1)} collective-permute-done((bf16[64,4096]{1,0:T(8,128)(2,1)S(1)}, bf16[64,4096]{1,0:T(8,128)(2,1)S(1)}, u32[]{:S(2)}, u32[]{:S(2)}) %collective-permute-start) | collective-permute-done | bytes 524320 | tf_op jit(solution)/shard_map/while/body/eval_jaxpr/ppermute | solution.py:141
  167.9 9.8 %collective-permute-done = bf16[64,4096]{1,0:T(8,128)(2,1)S(1)} collective-permute-done((bf16[64,4096]{1,0:T(8,128)(2,1)S(1)}, bf16[64,4096]{1,0:T(8,128)(2,1)S(1)}, u32[]{:S(2)}, u32[]{:S(2)}) %collective-permute-start) | collective-permute-done | bytes 524320 | tf_op jit(solution)/shard_map/while/body/eval_jaxpr/ppermute | solution.py:141
  184.5 9.8 %collective-permute-done = bf16[64,4096]{1,0:T(8,128)(2,1)S(1)} collective-permute-done((bf16[64,4096]{1,0:T(8,128)(2,1)S(1)}, bf16[64,4096]{1,0:T(8,128)(2,1)S(1)}, u32[]{:S(2)}, u32[]{:S(2)}) %collective-permute-start) | collective-permute-done | bytes 524320 | tf_op jit(solution)/shard_map/while/body/eval_jaxpr/ppermute | solution.py:141
  201.2 9.8 %collective-permute-done = bf16[64,4096]{1,0:T(8,128)(2,1)S(1)} collective-permute-done((bf16[64,4096]{1,0:T(8,128)(2,1)S(1)}, bf16[64,4096]{1,0:T(8,128)(2,1)S(1)}, u32[]{:S(2)}, u32[]{:S(2)}) %collective-permute-start) | collective-permute-done | bytes 524320 | tf_op jit(solution)/shard_map/while/body/eval_jaxpr/ppermute | solution.py:141
  211.2 9.8 %collective-permute-done = bf16[64,4096]{1,0:T(8,128)(2,1)S(1)} collective-permute-done((bf16[64,4096]{1,0:T(8,128)(2,1)S(1)}, bf16[64,4096]{1,0:T(8,128)(2,1)S(1)}, u32[]{:S(2)}, u32[]{:S(2)}) %collective-permute-start) | collective-permute-done | bytes 524320 | tf_op jit(solution)/shard_map/while/body/eval_jaxpr/ppermute | solution.py:141
  221.1 9.8 %collective-permute-done = bf16[64,4096]{1,0:T(8,128)(2,1)S(1)} collective-permute-done((bf16[64,4096]{1,0:T(8,128)(2,1)S(1)}, bf16[64,4096]{1,0:T(8,128)(2,1)S(1)}, u32[]{:S(2)}, u32[]{:S(2)}) %collective-permute-start) | collective-permute-done | bytes 524320 | tf_op jit(solution)/shard_map/while/body/eval_jaxpr/ppermute | solution.py:141
  231.7 9.2 %collective-permute-done = bf16[64,4096]{1,0:T(8,128)(2,1)S(1)} collective-permute-done((bf16[64,4096]{1,0:T(8,128)(2,1)S(1)}, bf16[64,4096]{1,0:T(8,128)(2,1)S(1)}, u32[]{:S(2)}, u32[]{:S(2)}) %collective-permute-start) | collective-permute-done | bytes 524320 | tf_op jit(solution)/shard_map/while/body/eval_jaxpr/ppermute | solution.py:141
  241.1 12.8 %collective-permute-done = bf16[64,4096]{1,0:T(8,128)(2,1)S(1)} collective-permute-done((bf16[64,4096]{1,0:T(8,128)(2,1)S(1)}, bf16[64,4096]{1,0:T(8,128)(2,1)S(1)}, u32[]{:S(2)}, u32[]{:S(2)}) %collective-permute-start) | collective-permute-done | bytes 524320 | tf_op jit(solution)/shard_map/while/body/eval_jaxpr/ppermute | solution.py:141
  254.0 12.8 %collective-permute-done = bf16[64,4096]{1,0:T(8,128)(2,1)S(1)} collective-permute-done((bf16[64,4096]{1,0:T(8,128)(2,1)S(1)}, bf16[64,4096]{1,0:T(8,128)(2,1)S(1)}, u32[]{:S(2)}, u32[]{:S(2)}) %collective-permute-start) | collective-permute-done | bytes 524320 | tf_op jit(solution)/shard_map/while/body/eval_jaxpr/ppermute | solution.py:141
  267.0 12.8 %collective-permute-done = bf16[64,4096]{1,0:T(8,128)(2,1)S(1)} collective-permute-done((bf16[64,4096]{1,0:T(8,128)(2,1)S(1)}, bf16[64,4096]{1,0:T(8,128)(2,1)S(1)}, u32[]{:S(2)}, u32[]{:S(2)}) %collective-permute-start) | collective-permute-done | bytes 524320 | tf_op jit(solution)/shard_map/while/body/eval_jaxpr/ppermute | solution.py:141
  280.0 12.8 %collective-permute-done = bf16[64,4096]{1,0:T(8,128)(2,1)S(1)} collective-permute-done((bf16[64,4096]{1,0:T(8,128)(2,1)S(1)}, bf16[64,4096]{1,0:T(8,128)(2,1)S(1)}, u32[]{:S(2)}, u32[]{:S(2)}) %collective-permute-start) | collective-permute-done | bytes 524320 | tf_op jit(solution)/shard_map/while/body/eval_jaxpr/ppermute | solution.py:141
  298.7 180.2 %while.67 = (s32[]{:T(128)}, bf16[64,4096]{1,0:T(8,128)(2,1)}, bf16[2,4,64,4096]{3,2,1,0:T(8,128)(2,1)}, bf16[2,4,64,4096]{3,2,1,0:T(8,128)(2,1)}, bf16[2,4,64,5...) while((s32[]{:T(128)}, bf16[64,4096]{1,0:T(8,128)(2,1)}, ...), condition=%wide.region_7.8_spmd, body=%wide.region_4.7_spmd.sunk | while | flops 31 | bytes 2621980 | solution.py:348
  315.0 11.3 %collective-permute-start.1 = (bf16[64,4096]{1,0:T(8,128)(2,1)}, bf16[64,4096]{1,0:T(8,128)(2,1)}, u32[]{:S(2)}, u32[]{:S(2)}) collective-permute-start(bf16[64,4096]{1,0:T(8,128)(2,1)} %get-tuple-element.1172), channel_id=1, source_target_pairs={{16,0},{32,16},{48,32},{64,48},{80,64},{96,80},{112,96},{0,112},{1... | collective-permute-start | bytes 1572872 | tf_op jit(solution)/shard_map/while/body/eval_jaxpr/ppermute | solution.py:141
  334.3 11.3 %collective-permute-start.1 = (bf16[64,4096]{1,0:T(8,128)(2,1)}, bf16[64,4096]{1,0:T(8,128)(2,1)}, u32[]{:S(2)}, u32[]{:S(2)}) collective-permute-start(bf16[64,4096]{1,0:T(8,128)(2,1)} %get-tuple-element.1172), channel_id=1, source_target_pairs={{16,0},{32,16},{48,32},{64,48},{80,64},{96,80},{112,96},{0,112},{1... | collective-permute-start | bytes 1572872 | tf_op jit(solution)/shard_map/while/body/eval_jaxpr/ppermute | solution.py:141
  353.5 11.3 %collective-permute-start.1 = (bf16[64,4096]{1,0:T(8,128)(2,1)}, bf16[64,4096]{1,0:T(8,128)(2,1)}, u32[]{:S(2)}, u32[]{:S(2)}) collective-permute-start(bf16[64,4096]{1,0:T(8,128)(2,1)} %get-tuple-element.1172), channel_id=1, source_target_pairs={{16,0},{32,16},{48,32},{64,48},{80,64},{96,80},{112,96},{0,112},{1... | collective-permute-start | bytes 1572872 | tf_op jit(solution)/shard_map/while/body/eval_jaxpr/ppermute | solution.py:141
  488.8 118.2 %while.68 = (s32[]{:T(128)}, bf16[64,4096]{1,0:T(8,128)(2,1)}, bf16[2,4,64,4096]{3,2,1,0:T(8,128)(2,1)}, bf16[2,4,64,4096]{3,2,1,0:T(8,128)(2,1)}, bf16[2,4,64,5...) while((s32[]{:T(128)}, bf16[64,4096]{1,0:T(8,128)(2,1)}, ...), condition=%wide.region_11.12_spmd, body=%wide.region_8.11_spmd.sunk | while | flops 32 | bytes 2622000 | solution.py:350
  489.8 11.3 %collective-permute-start.2 = (bf16[64,4096]{1,0:T(8,128)(2,1)}, bf16[64,4096]{1,0:T(8,128)(2,1)}, u32[]{:S(2)}, u32[]{:S(2)}) collective-permute-start(bf16[64,4096]{1,0:T(8,128)(2,1)} %get-tuple-element.1189), channel_id=1, source_target_pairs={{16,0},{32,16},{48,32},{64,48},{80,64},{96,80},{112,96},{0,112},{1... | collective-permute-start | bytes 1572872 | tf_op jit(solution)/shard_map/while/body/eval_jaxpr/ppermute | solution.py:141
  558.1 9.4 %conditional.8 = ((bf16[64,4096]{1,0:T(8,128)(2,1)}, bf16[2,4,64,4096]{3,2,1,0:T(8,128)(2,1)}, bf16[2,4,64,4096]{3,2,1,0:T(8,128)(2,1)}, bf16[2,4,64,512]{3,2,1,0:T(8,128)(2,1)S(1)}, bf16[2,4,64,512]{3,2,1,0:T(8,128)(2,1)S(1)})) conditional(s32[]{:T(128)} %convert_element_type.166, (bf16[2,4,64,4096]{3,2,1,0:T(8,128)(2,1)}, ...), branch_computations={%region_9.9_spmd, %region_10.10_spmd} | conditional | bytes 524338 | solution.py:332
  558.1 9.4 %branch_1_fun.5 = (bf16[64,4096]{1,0:T(8,128)(2,1)}, bf16[2,4,64,4096]{3,2,1,0:T(8,128)(2,1)}, bf16[2,4,64,4096]{3,2,1,0:T(8,128)(2,1)}, bf16[2,4,64,512]{3,2,1,0:T(8,128)(2,1)S(1)}, bf16[2,4,64,512]{3,2,1,0:T(8,128)(2,1)S(1)}) custom-call(s32[4]{0:T(128)S(1)} %get-tuple-element.853.sc_ref, ...), custom_call_target="tpu_custom_call", output_to_operand_aliasing={{1}: (6, {}), {2}: (7, {}), {3}: (8, {}), {4}: (9, {})} | custom-call | tf_op jit(solution)/shard_map/while/body/eval_jaxpr/cond/branch_1_fun/pallas_call | solution.py:110
  574.6 9.2 %conditional.8 = ((bf16[64,4096]{1,0:T(8,128)(2,1)}, bf16[2,4,64,4096]{3,2,1,0:T(8,128)(2,1)}, bf16[2,4,64,4096]{3,2,1,0:T(8,128)(2,1)}, bf16[2,4,64,512]{3,2,1,0:T(8,128)(2,1)S(1)}, bf16[2,4,64,512]{3,2,1,0:T(8,128)(2,1)S(1)})) conditional(s32[]{:T(128)} %convert_element_type.166, (bf16[2,4,64,4096]{3,2,1,0:T(8,128)(2,1)}, ...), branch_computations={%region_9.9_spmd, %region_10.10_spmd} | conditional | bytes 524338 | solution.py:332
  629.1 117.9 %all-to-all-done = bf16[16,256,1024]{2,1,0:T(8,128)(2,1)} async-done(((bf16[16,256,1024]{2,1,0:T(8,128)(2,1)}), bf16[16,256,1024]{2,1,0:T(8,128)(2,1)}, u32[]{:S(2)}, u32[]{:S(2)}) %all-to-all-start) | async-done | bytes 8388640 | tf_op jit(solution)/shard_map/all_to_all | solution.py:241
  (229 shorter events, 471.5 us)
Async XLA Ops:
  7.2 746.6 %reduce-scatter.2.cloned.1.call-start = ((), (), s32[]{:S(2)}) async-start(), calls=%async_computation.2 | async-start | bytes 8912896 | tf_op jit(solution)/shard_map/reduce_scatter | solution.py:244
  41.8 9.8 %collective-permute-start = (bf16[64,4096]{1,0:T(8,128)(2,1)S(1)}, bf16[64,4096]{1,0:T(8,128)(2,1)S(1)}, u32[]{:S(2)}, u32[]{:S(2)}) collective-permute-start(bf16[64,4096]{1,0:T(8,128)(2,1)S(1)} %get-tuple-element.1158), channel_id=1, source_target_pairs={{112,0},{0,16},{16,32},{32,48},{48,64},{64,80},{80,96},{96,112},{1... | collective-permute-start | bytes 1572872 | tf_op jit(solution)/shard_map/while/body/eval_jaxpr/ppermute | solution.py:141
  58.4 9.8 %collective-permute-start = (bf16[64,4096]{1,0:T(8,128)(2,1)S(1)}, bf16[64,4096]{1,0:T(8,128)(2,1)S(1)}, u32[]{:S(2)}, u32[]{:S(2)}) collective-permute-start(bf16[64,4096]{1,0:T(8,128)(2,1)S(1)} %get-tuple-element.1158), channel_id=1, source_target_pairs={{112,0},{0,16},{16,32},{32,48},{48,64},{64,80},{80,96},{96,112},{1... | collective-permute-start | bytes 1572872 | tf_op jit(solution)/shard_map/while/body/eval_jaxpr/ppermute | solution.py:141
  75.1 9.8 %collective-permute-start = (bf16[64,4096]{1,0:T(8,128)(2,1)S(1)}, bf16[64,4096]{1,0:T(8,128)(2,1)S(1)}, u32[]{:S(2)}, u32[]{:S(2)}) collective-permute-start(bf16[64,4096]{1,0:T(8,128)(2,1)S(1)} %get-tuple-element.1158), channel_id=1, source_target_pairs={{112,0},{0,16},{16,32},{32,48},{48,64},{64,80},{80,96},{96,112},{1... | collective-permute-start | bytes 1572872 | tf_op jit(solution)/shard_map/while/body/eval_jaxpr/ppermute | solution.py:141
  91.7 9.8 %collective-permute-start = (bf16[64,4096]{1,0:T(8,128)(2,1)S(1)}, bf16[64,4096]{1,0:T(8,128)(2,1)S(1)}, u32[]{:S(2)}, u32[]{:S(2)}) collective-permute-start(bf16[64,4096]{1,0:T(8,128)(2,1)S(1)} %get-tuple-element.1158), channel_id=1, source_target_pairs={{112,0},{0,16},{16,32},{32,48},{48,64},{64,80},{80,96},{96,112},{1... | collective-permute-start | bytes 1572872 | tf_op jit(solution)/shard_map/while/body/eval_jaxpr/ppermute | solution.py:141
  101.7 9.8 %collective-permute-start = (bf16[64,4096]{1,0:T(8,128)(2,1)S(1)}, bf16[64,4096]{1,0:T(8,128)(2,1)S(1)}, u32[]{:S(2)}, u32[]{:S(2)}) collective-permute-start(bf16[64,4096]{1,0:T(8,128)(2,1)S(1)} %get-tuple-element.1158), channel_id=1, source_target_pairs={{112,0},{0,16},{16,32},{32,48},{48,64},{64,80},{80,96},{96,112},{1... | collective-permute-start | bytes 1572872 | tf_op jit(solution)/shard_map/while/body/eval_jaxpr/ppermute | solution.py:141
  111.7 9.8 %collective-permute-start = (bf16[64,4096]{1,0:T(8,128)(2,1)S(1)}, bf16[64,4096]{1,0:T(8,128)(2,1)S(1)}, u32[]{:S(2)}, u32[]{:S(2)}) collective-permute-start(bf16[64,4096]{1,0:T(8,128)(2,1)S(1)} %get-tuple-element.1158), channel_id=1, source_target_pairs={{112,0},{0,16},{16,32},{32,48},{48,64},{64,80},{80,96},{96,112},{1... | collective-permute-start | bytes 1572872 | tf_op jit(solution)/shard_map/while/body/eval_jaxpr/ppermute | solution.py:141
  121.6 9.8 %collective-permute-start = (bf16[64,4096]{1,0:T(8,128)(2,1)S(1)}, bf16[64,4096]{1,0:T(8,128)(2,1)S(1)}, u32[]{:S(2)}, u32[]{:S(2)}) collective-permute-start(bf16[64,4096]{1,0:T(8,128)(2,1)S(1)} %get-tuple-element.1158), channel_id=1, source_target_pairs={{112,0},{0,16},{16,32},{32,48},{48,64},{64,80},{80,96},{96,112},{1... | collective-permute-start | bytes 1572872 | tf_op jit(solution)/shard_map/while/body/eval_jaxpr/ppermute | solution.py:141
  131.6 12.8 %collective-permute-start = (bf16[64,4096]{1,0:T(8,128)(2,1)S(1)}, bf16[64,4096]{1,0:T(8,128)(2,1)S(1)}, u32[]{:S(2)}, u32[]{:S(2)}) collective-permute-start(bf16[64,4096]{1,0:T(8,128)(2,1)S(1)} %get-tuple-element.1158), channel_id=1, source_target_pairs={{112,0},{0,16},{16,32},{32,48},{48,64},{64,80},{80,96},{96,112},{1... | collective-permute-start | bytes 1572872 | tf_op jit(solution)/shard_map/while/body/eval_jaxpr/ppermute | solution.py:141
  151.2 9.8 %collective-permute-start = (bf16[64,4096]{1,0:T(8,128)(2,1)S(1)}, bf16[64,4096]{1,0:T(8,128)(2,1)S(1)}, u32[]{:S(2)}, u32[]{:S(2)}) collective-permute-start(bf16[64,4096]{1,0:T(8,128)(2,1)S(1)} %get-tuple-element.1158), channel_id=1, source_target_pairs={{112,0},{0,16},{16,32},{32,48},{48,64},{64,80},{80,96},{96,112},{1... | collective-permute-start | bytes 1572872 | tf_op jit(solution)/shard_map/while/body/eval_jaxpr/ppermute | solution.py:141
  211.1 9.8 %collective-permute-start = (bf16[64,4096]{1,0:T(8,128)(2,1)S(1)}, bf16[64,4096]{1,0:T(8,128)(2,1)S(1)}, u32[]{:S(2)}, u32[]{:S(2)}) collective-permute-start(bf16[64,4096]{1,0:T(8,128)(2,1)S(1)} %get-tuple-element.1158), channel_id=1, source_target_pairs={{112,0},{0,16},{16,32},{32,48},{48,64},{64,80},{80,96},{96,112},{1... | collective-permute-start | bytes 1572872 | tf_op jit(solution)/shard_map/while/body/eval_jaxpr/ppermute | solution.py:141
  221.1 9.8 %collective-permute-start = (bf16[64,4096]{1,0:T(8,128)(2,1)S(1)}, bf16[64,4096]{1,0:T(8,128)(2,1)S(1)}, u32[]{:S(2)}, u32[]{:S(2)}) collective-permute-start(bf16[64,4096]{1,0:T(8,128)(2,1)S(1)} %get-tuple-element.1158), channel_id=1, source_target_pairs={{112,0},{0,16},{16,32},{32,48},{48,64},{64,80},{80,96},{96,112},{1... | collective-permute-start | bytes 1572872 | tf_op jit(solution)/shard_map/while/body/eval_jaxpr/ppermute | solution.py:141
  231.1 9.8 %collective-permute-start = (bf16[64,4096]{1,0:T(8,128)(2,1)S(1)}, bf16[64,4096]{1,0:T(8,128)(2,1)S(1)}, u32[]{:S(2)}, u32[]{:S(2)}) collective-permute-start(bf16[64,4096]{1,0:T(8,128)(2,1)S(1)} %get-tuple-element.1158), channel_id=1, source_target_pairs={{112,0},{0,16},{16,32},{32,48},{48,64},{64,80},{80,96},{96,112},{1... | collective-permute-start | bytes 1572872 | tf_op jit(solution)/shard_map/while/body/eval_jaxpr/ppermute | solution.py:141
  241.0 12.8 %collective-permute-start = (bf16[64,4096]{1,0:T(8,128)(2,1)S(1)}, bf16[64,4096]{1,0:T(8,128)(2,1)S(1)}, u32[]{:S(2)}, u32[]{:S(2)}) collective-permute-start(bf16[64,4096]{1,0:T(8,128)(2,1)S(1)} %get-tuple-element.1158), channel_id=1, source_target_pairs={{112,0},{0,16},{16,32},{32,48},{48,64},{64,80},{80,96},{96,112},{1... | collective-permute-start | bytes 1572872 | tf_op jit(solution)/shard_map/while/body/eval_jaxpr/ppermute | solution.py:141
  254.0 12.8 %collective-permute-start = (bf16[64,4096]{1,0:T(8,128)(2,1)S(1)}, bf16[64,4096]{1,0:T(8,128)(2,1)S(1)}, u32[]{:S(2)}, u32[]{:S(2)}) collective-permute-start(bf16[64,4096]{1,0:T(8,128)(2,1)S(1)} %get-tuple-element.1158), channel_id=1, source_target_pairs={{112,0},{0,16},{16,32},{32,48},{48,64},{64,80},{80,96},{96,112},{1... | collective-permute-start | bytes 1572872 | tf_op jit(solution)/shard_map/while/body/eval_jaxpr/ppermute | solution.py:141
  266.9 12.8 %collective-permute-start = (bf16[64,4096]{1,0:T(8,128)(2,1)S(1)}, bf16[64,4096]{1,0:T(8,128)(2,1)S(1)}, u32[]{:S(2)}, u32[]{:S(2)}) collective-permute-start(bf16[64,4096]{1,0:T(8,128)(2,1)S(1)} %get-tuple-element.1158), channel_id=1, source_target_pairs={{112,0},{0,16},{16,32},{32,48},{48,64},{64,80},{80,96},{96,112},{1... | collective-permute-start | bytes 1572872 | tf_op jit(solution)/shard_map/while/body/eval_jaxpr/ppermute | solution.py:141
  279.9 12.8 %collective-permute-start = (bf16[64,4096]{1,0:T(8,128)(2,1)S(1)}, bf16[64,4096]{1,0:T(8,128)(2,1)S(1)}, u32[]{:S(2)}, u32[]{:S(2)}) collective-permute-start(bf16[64,4096]{1,0:T(8,128)(2,1)S(1)} %get-tuple-element.1158), channel_id=1, source_target_pairs={{112,0},{0,16},{16,32},{32,48},{48,64},{64,80},{80,96},{96,112},{1... | collective-permute-start | bytes 1572872 | tf_op jit(solution)/shard_map/while/body/eval_jaxpr/ppermute | solution.py:141
  299.6 14.5 %collective-permute-start.1 = (bf16[64,4096]{1,0:T(8,128)(2,1)}, bf16[64,4096]{1,0:T(8,128)(2,1)}, u32[]{:S(2)}, u32[]{:S(2)}) collective-permute-start(bf16[64,4096]{1,0:T(8,128)(2,1)} %get-tuple-element.1172), channel_id=1, source_target_pairs={{16,0},{32,16},{48,32},{64,48},{80,64},{96,80},{112,96},{0,112},{1... | collective-permute-start | bytes 1572872 | tf_op jit(solution)/shard_map/while/body/eval_jaxpr/ppermute | solution.py:141
  315.0 18.3 %collective-permute-start.1 = (bf16[64,4096]{1,0:T(8,128)(2,1)}, bf16[64,4096]{1,0:T(8,128)(2,1)}, u32[]{:S(2)}, u32[]{:S(2)}) collective-permute-start(bf16[64,4096]{1,0:T(8,128)(2,1)} %get-tuple-element.1172), channel_id=1, source_target_pairs={{16,0},{32,16},{48,32},{64,48},{80,64},{96,80},{112,96},{0,112},{1... | collective-permute-start | bytes 1572872 | tf_op jit(solution)/shard_map/while/body/eval_jaxpr/ppermute | solution.py:141
  334.3 18.3 %collective-permute-start.1 = (bf16[64,4096]{1,0:T(8,128)(2,1)}, bf16[64,4096]{1,0:T(8,128)(2,1)}, u32[]{:S(2)}, u32[]{:S(2)}) collective-permute-start(bf16[64,4096]{1,0:T(8,128)(2,1)} %get-tuple-element.1172), channel_id=1, source_target_pairs={{16,0},{32,16},{48,32},{64,48},{80,64},{96,80},{112,96},{0,112},{1... | collective-permute-start | bytes 1572872 | tf_op jit(solution)/shard_map/while/body/eval_jaxpr/ppermute | solution.py:141
  353.5 18.3 %collective-permute-start.1 = (bf16[64,4096]{1,0:T(8,128)(2,1)}, bf16[64,4096]{1,0:T(8,128)(2,1)}, u32[]{:S(2)}, u32[]{:S(2)}) collective-permute-start(bf16[64,4096]{1,0:T(8,128)(2,1)} %get-tuple-element.1172), channel_id=1, source_target_pairs={{16,0},{32,16},{48,32},{64,48},{80,64},{96,80},{112,96},{0,112},{1... | collective-permute-start | bytes 1572872 | tf_op jit(solution)/shard_map/while/body/eval_jaxpr/ppermute | solution.py:141
  372.8 10.1 %collective-permute-start.1 = (bf16[64,4096]{1,0:T(8,128)(2,1)}, bf16[64,4096]{1,0:T(8,128)(2,1)}, u32[]{:S(2)}, u32[]{:S(2)}) collective-permute-start(bf16[64,4096]{1,0:T(8,128)(2,1)} %get-tuple-element.1172), channel_id=1, source_target_pairs={{16,0},{32,16},{48,32},{64,48},{80,64},{96,80},{112,96},{0,112},{1... | collective-permute-start | bytes 1572872 | tf_op jit(solution)/shard_map/while/body/eval_jaxpr/ppermute | solution.py:141
  383.8 10.1 %collective-permute-start.1 = (bf16[64,4096]{1,0:T(8,128)(2,1)}, bf16[64,4096]{1,0:T(8,128)(2,1)}, u32[]{:S(2)}, u32[]{:S(2)}) collective-permute-start(bf16[64,4096]{1,0:T(8,128)(2,1)} %get-tuple-element.1172), channel_id=1, source_target_pairs={{16,0},{32,16},{48,32},{64,48},{80,64},{96,80},{112,96},{0,112},{1... | collective-permute-start | bytes 1572872 | tf_op jit(solution)/shard_map/while/body/eval_jaxpr/ppermute | solution.py:141
  394.9 10.1 %collective-permute-start.1 = (bf16[64,4096]{1,0:T(8,128)(2,1)}, bf16[64,4096]{1,0:T(8,128)(2,1)}, u32[]{:S(2)}, u32[]{:S(2)}) collective-permute-start(bf16[64,4096]{1,0:T(8,128)(2,1)} %get-tuple-element.1172), channel_id=1, source_target_pairs={{16,0},{32,16},{48,32},{64,48},{80,64},{96,80},{112,96},{0,112},{1... | collective-permute-start | bytes 1572872 | tf_op jit(solution)/shard_map/while/body/eval_jaxpr/ppermute | solution.py:141
  430.2 10.1 %collective-permute-start.1 = (bf16[64,4096]{1,0:T(8,128)(2,1)}, bf16[64,4096]{1,0:T(8,128)(2,1)}, u32[]{:S(2)}, u32[]{:S(2)}) collective-permute-start(bf16[64,4096]{1,0:T(8,128)(2,1)} %get-tuple-element.1172), channel_id=1, source_target_pairs={{16,0},{32,16},{48,32},{64,48},{80,64},{96,80},{112,96},{0,112},{1... | collective-permute-start | bytes 1572872 | tf_op jit(solution)/shard_map/while/body/eval_jaxpr/ppermute | solution.py:141
  449.5 10.1 %collective-permute-start.1 = (bf16[64,4096]{1,0:T(8,128)(2,1)}, bf16[64,4096]{1,0:T(8,128)(2,1)}, u32[]{:S(2)}, u32[]{:S(2)}) collective-permute-start(bf16[64,4096]{1,0:T(8,128)(2,1)} %get-tuple-element.1172), channel_id=1, source_target_pairs={{16,0},{32,16},{48,32},{64,48},{80,64},{96,80},{112,96},{0,112},{1... | collective-permute-start | bytes 1572872 | tf_op jit(solution)/shard_map/while/body/eval_jaxpr/ppermute | solution.py:141
  468.7 10.1 %collective-permute-start.1 = (bf16[64,4096]{1,0:T(8,128)(2,1)}, bf16[64,4096]{1,0:T(8,128)(2,1)}, u32[]{:S(2)}, u32[]{:S(2)}) collective-permute-start(bf16[64,4096]{1,0:T(8,128)(2,1)} %get-tuple-element.1172), channel_id=1, source_target_pairs={{16,0},{32,16},{48,32},{64,48},{80,64},{96,80},{112,96},{0,112},{1... | collective-permute-start | bytes 1572872 | tf_op jit(solution)/shard_map/while/body/eval_jaxpr/ppermute | solution.py:141
  489.8 18.3 %collective-permute-start.2 = (bf16[64,4096]{1,0:T(8,128)(2,1)}, bf16[64,4096]{1,0:T(8,128)(2,1)}, u32[]{:S(2)}, u32[]{:S(2)}) collective-permute-start(bf16[64,4096]{1,0:T(8,128)(2,1)} %get-tuple-element.1189), channel_id=1, source_target_pairs={{16,0},{32,16},{48,32},{64,48},{80,64},{96,80},{112,96},{0,112},{1... | collective-permute-start | bytes 1572872 | tf_op jit(solution)/shard_map/while/body/eval_jaxpr/ppermute | solution.py:141
  509.0 10.1 %collective-permute-start.2 = (bf16[64,4096]{1,0:T(8,128)(2,1)}, bf16[64,4096]{1,0:T(8,128)(2,1)}, u32[]{:S(2)}, u32[]{:S(2)}) collective-permute-start(bf16[64,4096]{1,0:T(8,128)(2,1)} %get-tuple-element.1189), channel_id=1, source_target_pairs={{16,0},{32,16},{48,32},{64,48},{80,64},{96,80},{112,96},{0,112},{1... | collective-permute-start | bytes 1572872 | tf_op jit(solution)/shard_map/while/body/eval_jaxpr/ppermute | solution.py:141
  520.1 10.4 %collective-permute-start.2 = (bf16[64,4096]{1,0:T(8,128)(2,1)}, bf16[64,4096]{1,0:T(8,128)(2,1)}, u32[]{:S(2)}, u32[]{:S(2)}) collective-permute-start(bf16[64,4096]{1,0:T(8,128)(2,1)} %get-tuple-element.1189), channel_id=1, source_target_pairs={{16,0},{32,16},{48,32},{64,48},{80,64},{96,80},{112,96},{0,112},{1... | collective-permute-start | bytes 1572872 | tf_op jit(solution)/shard_map/while/body/eval_jaxpr/ppermute | solution.py:141
  531.4 10.4 %collective-permute-start.2 = (bf16[64,4096]{1,0:T(8,128)(2,1)}, bf16[64,4096]{1,0:T(8,128)(2,1)}, u32[]{:S(2)}, u32[]{:S(2)}) collective-permute-start(bf16[64,4096]{1,0:T(8,128)(2,1)} %get-tuple-element.1189), channel_id=1, source_target_pairs={{16,0},{32,16},{48,32},{64,48},{80,64},{96,80},{112,96},{0,112},{1... | collective-permute-start | bytes 1572872 | tf_op jit(solution)/shard_map/while/body/eval_jaxpr/ppermute | solution.py:141
  617.0 130.0 %all-to-all-start = ((bf16[16,256,1024]{2,1,0:T(8,128)(2,1)}), bf16[16,256,1024]{2,1,0:T(8,128)(2,1)}, u32[]{:S(2)}, u32[]{:S(2)}) async-start(bf16[16,256,1024]{2,1,0:T(8,128)(2,1)} %bitcast.93), calls=%async_computation | async-start | bytes 16777216 | tf_op jit(solution)/shard_map/all_to_all | solution.py:241
  (15 other events, 101.6 us)
Sparse Core Ops, SparseCore 0:
  488.9 88.5 reduce-scatter.1

commit v13 on v10

--- a/solution.py
+++ b/solution.py
@@ -7,7 +7,7 @@
 
 BLK = 64
 SPLIT = 1
-TK = 128
+TK = 256
 TKB = 512
 LANES = 128
 

time: 719 us -> 718 us (level)
  no operation moved by 1% of the time
where the time goes in v13:
time: 718 us; the launch traced here: 717 us
  waiting for transfers between devices  415 us (58%)
  Pallas kernels  151 us (21%)
  starting transfers between devices  82.9 us (12%)
  local copies, waits for them, and re-layouts  32.7 us (5%)
  between operations  14.3 us (2%)
  matrix products  13.7 us (2%)
    ppermute x38, waiting for transfers between devices, shifted(): return lax.ppermute(block, axis, route)  333 us
    ppermute x38, starting transfers between devices, shifted(): return lax.ppermute(block, axis, route)  82.7 us
    reduce_scatter x2, waiting for transfers between devices, settle(): lax.psum_scatter(joined, 'dp', scatter_dimension=0, tiled=True)  81.9 us
    pallas_call x8, Pallas kernels, bwd_call(): pl.pallas_call(_bwd_kernel, grid_spec=pltpu.PrefetchScalarGridSpec(num_sc...  72.9 us
    pallas_call x8, Pallas kernels, fwd_call(): pl.pallas_call(_fwd_kernel, grid_spec=pltpu.PrefetchScalarGridSpec(num_sc...  53.8 us
    pallas_call x2, Pallas kernels, masked(): pl.pallas_call(kernel, grid_spec=pltpu.PrefetchScalarGridSpec(num_scalar_...  24.3 us
    another operation x29, local copies, waits for them, and re-layouts  18 us
  transfers between devices with their start and end apart: 40, of which 39 were waited for; matrix products, arithmetic and copies ran while one was open for 3% of the time, Pallas kernels for 5%

profile of v13, /device:TPU:0, one launch (start us, length us, event | category | flops | bytes accessed | tf_op | source)
XLA Modules:
  0.0 717.2 jit_solution(10896694039997024493)
XLA Ops:
  8.0 14.2 %shard_map.77 = bf16[2,4096,512]{2,1,0:T(8,128)(2,1)} custom-call(s32[2,64,8]{2,1,0:T(8,128)S(1)} %bitcast.85, bf16[2,4096,512]{2,1,0:T(8,128)(2,1)} %bitcast.91), custom_call_target="tpu_custom_call" | custom-call | tf_op jit(solution)/shard_map/pallas_call | solution.py:166
  22.2 10.2 %shard_map.78 = bf16[2,512,4096]{2,1,0:T(8,128)(2,1)} custom-call(s32[2,8,64]{2,1,0:T(8,128)S(1)} %bitcast.86, bf16[2,512,4096]{2,1,0:T(8,128)(2,1)} %bitcast.92), custom_call_target="tpu_custom_call" | custom-call | tf_op jit(solution)/shard_map/pallas_call | solution.py:166
  35.0 257.5 %while.66 = (s32[]{:T(128)}, bf16[64,4096]{1,0:T(8,128)(2,1)S(1)}, bf16[2,4,64,4096]{3,2,1,0:T(8,128)(2,1)}, s32[]{:T(128)}, pred[]{:T(512)}, /*index=5*/bf16[4,...) while((s32[]{:T(128)}, bf16[64,4096]{1,0:T(8,128)(2,1)S(1)}, ...), condition=%wide.region_3.4_spmd, body=%wide.region_0.3_spmd.sunk | while | flops 31 | bytes 2621852 | solution.py:295
  41.8 9.8 %collective-permute-done = bf16[64,4096]{1,0:T(8,128)(2,1)S(1)} collective-permute-done((bf16[64,4096]{1,0:T(8,128)(2,1)S(1)}, bf16[64,4096]{1,0:T(8,128)(2,1)S(1)}, u32[]{:S(2)}, u32[]{:S(2)}) %collective-permute-start) | collective-permute-done | bytes 524320 | tf_op jit(solution)/shard_map/while/body/eval_jaxpr/ppermute | solution.py:141
  58.4 9.8 %collective-permute-done = bf16[64,4096]{1,0:T(8,128)(2,1)S(1)} collective-permute-done((bf16[64,4096]{1,0:T(8,128)(2,1)S(1)}, bf16[64,4096]{1,0:T(8,128)(2,1)S(1)}, u32[]{:S(2)}, u32[]{:S(2)}) %collective-permute-start) | collective-permute-done | bytes 524320 | tf_op jit(solution)/shard_map/while/body/eval_jaxpr/ppermute | solution.py:141
  75.0 9.8 %collective-permute-done = bf16[64,4096]{1,0:T(8,128)(2,1)S(1)} collective-permute-done((bf16[64,4096]{1,0:T(8,128)(2,1)S(1)}, bf16[64,4096]{1,0:T(8,128)(2,1)S(1)}, u32[]{:S(2)}, u32[]{:S(2)}) %collective-permute-start) | collective-permute-done | bytes 524320 | tf_op jit(solution)/shard_map/while/body/eval_jaxpr/ppermute | solution.py:141
  91.7 9.8 %collective-permute-done = bf16[64,4096]{1,0:T(8,128)(2,1)S(1)} collective-permute-done((bf16[64,4096]{1,0:T(8,128)(2,1)S(1)}, bf16[64,4096]{1,0:T(8,128)(2,1)S(1)}, u32[]{:S(2)}, u32[]{:S(2)}) %collective-permute-start) | collective-permute-done | bytes 524320 | tf_op jit(solution)/shard_map/while/body/eval_jaxpr/ppermute | solution.py:141
  101.7 9.8 %collective-permute-done = bf16[64,4096]{1,0:T(8,128)(2,1)S(1)} collective-permute-done((bf16[64,4096]{1,0:T(8,128)(2,1)S(1)}, bf16[64,4096]{1,0:T(8,128)(2,1)S(1)}, u32[]{:S(2)}, u32[]{:S(2)}) %collective-permute-start) | collective-permute-done | bytes 524320 | tf_op jit(solution)/shard_map/while/body/eval_jaxpr/ppermute | solution.py:141
  111.6 9.8 %collective-permute-done = bf16[64,4096]{1,0:T(8,128)(2,1)S(1)} collective-permute-done((bf16[64,4096]{1,0:T(8,128)(2,1)S(1)}, bf16[64,4096]{1,0:T(8,128)(2,1)S(1)}, u32[]{:S(2)}, u32[]{:S(2)}) %collective-permute-start) | collective-permute-done | bytes 524320 | tf_op jit(solution)/shard_map/while/body/eval_jaxpr/ppermute | solution.py:141
  122.1 9.3 %collective-permute-done = bf16[64,4096]{1,0:T(8,128)(2,1)S(1)} collective-permute-done((bf16[64,4096]{1,0:T(8,128)(2,1)S(1)}, bf16[64,4096]{1,0:T(8,128)(2,1)S(1)}, u32[]{:S(2)}, u32[]{:S(2)}) %collective-permute-start) | collective-permute-done | bytes 524320 | tf_op jit(solution)/shard_map/while/body/eval_jaxpr/ppermute | solution.py:141
  131.5 12.8 %collective-permute-done = bf16[64,4096]{1,0:T(8,128)(2,1)S(1)} collective-permute-done((bf16[64,4096]{1,0:T(8,128)(2,1)S(1)}, bf16[64,4096]{1,0:T(8,128)(2,1)S(1)}, u32[]{:S(2)}, u32[]{:S(2)}) %collective-permute-start) | collective-permute-done | bytes 524320 | tf_op jit(solution)/shard_map/while/body/eval_jaxpr/ppermute | solution.py:141
  151.1 9.8 %collective-permute-done = bf16[64,4096]{1,0:T(8,128)(2,1)S(1)} collective-permute-done((bf16[64,4096]{1,0:T(8,128)(2,1)S(1)}, bf16[64,4096]{1,0:T(8,128)(2,1)S(1)}, u32[]{:S(2)}, u32[]{:S(2)}) %collective-permute-start) | collective-permute-done | bytes 524320 | tf_op jit(solution)/shard_map/while/body/eval_jaxpr/ppermute | solution.py:141
  167.7 9.8 %collective-permute-done = bf16[64,4096]{1,0:T(8,128)(2,1)S(1)} collective-permute-done((bf16[64,4096]{1,0:T(8,128)(2,1)S(1)}, bf16[64,4096]{1,0:T(8,128)(2,1)S(1)}, u32[]{:S(2)}, u32[]{:S(2)}) %collective-permute-start) | collective-permute-done | bytes 524320 | tf_op jit(solution)/shard_map/while/body/eval_jaxpr/ppermute | solution.py:141
  184.4 9.8 %collective-permute-done = bf16[64,4096]{1,0:T(8,128)(2,1)S(1)} collective-permute-done((bf16[64,4096]{1,0:T(8,128)(2,1)S(1)}, bf16[64,4096]{1,0:T(8,128)(2,1)S(1)}, u32[]{:S(2)}, u32[]{:S(2)}) %collective-permute-start) | collective-permute-done | bytes 524320 | tf_op jit(solution)/shard_map/while/body/eval_jaxpr/ppermute | solution.py:141
  201.0 9.8 %collective-permute-done = bf16[64,4096]{1,0:T(8,128)(2,1)S(1)} collective-permute-done((bf16[64,4096]{1,0:T(8,128)(2,1)S(1)}, bf16[64,4096]{1,0:T(8,128)(2,1)S(1)}, u32[]{:S(2)}, u32[]{:S(2)}) %collective-permute-start) | collective-permute-done | bytes 524320 | tf_op jit(solution)/shard_map/while/body/eval_jaxpr/ppermute | solution.py:141
  211.0 9.8 %collective-permute-done = bf16[64,4096]{1,0:T(8,128)(2,1)S(1)} collective-permute-done((bf16[64,4096]{1,0:T(8,128)(2,1)S(1)}, bf16[64,4096]{1,0:T(8,128)(2,1)S(1)}, u32[]{:S(2)}, u32[]{:S(2)}) %collective-permute-start) | collective-permute-done | bytes 524320 | tf_op jit(solution)/shard_map/while/body/eval_jaxpr/ppermute | solution.py:141
  220.9 9.8 %collective-permute-done = bf16[64,4096]{1,0:T(8,128)(2,1)S(1)} collective-permute-done((bf16[64,4096]{1,0:T(8,128)(2,1)S(1)}, bf16[64,4096]{1,0:T(8,128)(2,1)S(1)}, u32[]{:S(2)}, u32[]{:S(2)}) %collective-permute-start) | collective-permute-done | bytes 524320 | tf_op jit(solution)/shard_map/while/body/eval_jaxpr/ppermute | solution.py:141
  231.4 9.3 %collective-permute-done = bf16[64,4096]{1,0:T(8,128)(2,1)S(1)} collective-permute-done((bf16[64,4096]{1,0:T(8,128)(2,1)S(1)}, bf16[64,4096]{1,0:T(8,128)(2,1)S(1)}, u32[]{:S(2)}, u32[]{:S(2)}) %collective-permute-start) | collective-permute-done | bytes 524320 | tf_op jit(solution)/shard_map/while/body/eval_jaxpr/ppermute | solution.py:141
  240.9 12.8 %collective-permute-done = bf16[64,4096]{1,0:T(8,128)(2,1)S(1)} collective-permute-done((bf16[64,4096]{1,0:T(8,128)(2,1)S(1)}, bf16[64,4096]{1,0:T(8,128)(2,1)S(1)}, u32[]{:S(2)}, u32[]{:S(2)}) %collective-permute-start) | collective-permute-done | bytes 524320 | tf_op jit(solution)/shard_map/while/body/eval_jaxpr/ppermute | solution.py:141
  253.8 12.8 %collective-permute-done = bf16[64,4096]{1,0:T(8,128)(2,1)S(1)} collective-permute-done((bf16[64,4096]{1,0:T(8,128)(2,1)S(1)}, bf16[64,4096]{1,0:T(8,128)(2,1)S(1)}, u32[]{:S(2)}, u32[]{:S(2)}) %collective-permute-start) | collective-permute-done | bytes 524320 | tf_op jit(solution)/shard_map/while/body/eval_jaxpr/ppermute | solution.py:141
  266.7 12.8 %collective-permute-done = bf16[64,4096]{1,0:T(8,128)(2,1)S(1)} collective-permute-done((bf16[64,4096]{1,0:T(8,128)(2,1)S(1)}, bf16[64,4096]{1,0:T(8,128)(2,1)S(1)}, u32[]{:S(2)}, u32[]{:S(2)}) %collective-permute-start) | collective-permute-done | bytes 524320 | tf_op jit(solution)/shard_map/while/body/eval_jaxpr/ppermute | solution.py:141
  279.7 12.8 %collective-permute-done = bf16[64,4096]{1,0:T(8,128)(2,1)S(1)} collective-permute-done((bf16[64,4096]{1,0:T(8,128)(2,1)S(1)}, bf16[64,4096]{1,0:T(8,128)(2,1)S(1)}, u32[]{:S(2)}, u32[]{:S(2)}) %collective-permute-start) | collective-permute-done | bytes 524320 | tf_op jit(solution)/shard_map/while/body/eval_jaxpr/ppermute | solution.py:141
  298.4 180.2 %while.67 = (s32[]{:T(128)}, bf16[64,4096]{1,0:T(8,128)(2,1)}, bf16[2,4,64,4096]{3,2,1,0:T(8,128)(2,1)}, bf16[2,4,64,4096]{3,2,1,0:T(8,128)(2,1)}, bf16[2,4,64,5...) while((s32[]{:T(128)}, bf16[64,4096]{1,0:T(8,128)(2,1)}, ...), condition=%wide.region_7.8_spmd, body=%wide.region_4.7_spmd.sunk | while | flops 31 | bytes 2621980 | solution.py:343
  314.7 11.3 %collective-permute-start.1 = (bf16[64,4096]{1,0:T(8,128)(2,1)}, bf16[64,4096]{1,0:T(8,128)(2,1)}, u32[]{:S(2)}, u32[]{:S(2)}) collective-permute-start(bf16[64,4096]{1,0:T(8,128)(2,1)} %get-tuple-element.1172), channel_id=1, source_target_pairs={{16,0},{32,16},{48,32},{64,48},{80,64},{96,80},{112,96},{0,112},{1... | collective-permute-start | bytes 1572872 | tf_op jit(solution)/shard_map/while/body/eval_jaxpr/ppermute | solution.py:141
  334.0 11.3 %collective-permute-start.1 = (bf16[64,4096]{1,0:T(8,128)(2,1)}, bf16[64,4096]{1,0:T(8,128)(2,1)}, u32[]{:S(2)}, u32[]{:S(2)}) collective-permute-start(bf16[64,4096]{1,0:T(8,128)(2,1)} %get-tuple-element.1172), channel_id=1, source_target_pairs={{16,0},{32,16},{48,32},{64,48},{80,64},{96,80},{112,96},{0,112},{1... | collective-permute-start | bytes 1572872 | tf_op jit(solution)/shard_map/while/body/eval_jaxpr/ppermute | solution.py:141
  353.2 11.3 %collective-permute-start.1 = (bf16[64,4096]{1,0:T(8,128)(2,1)}, bf16[64,4096]{1,0:T(8,128)(2,1)}, u32[]{:S(2)}, u32[]{:S(2)}) collective-permute-start(bf16[64,4096]{1,0:T(8,128)(2,1)} %get-tuple-element.1172), channel_id=1, source_target_pairs={{16,0},{32,16},{48,32},{64,48},{80,64},{96,80},{112,96},{0,112},{1... | collective-permute-start | bytes 1572872 | tf_op jit(solution)/shard_map/while/body/eval_jaxpr/ppermute | solution.py:141
  488.8 118.2 %while.68 = (s32[]{:T(128)}, bf16[64,4096]{1,0:T(8,128)(2,1)}, bf16[2,4,64,4096]{3,2,1,0:T(8,128)(2,1)}, bf16[2,4,64,4096]{3,2,1,0:T(8,128)(2,1)}, bf16[2,4,64,5...) while((s32[]{:T(128)}, bf16[64,4096]{1,0:T(8,128)(2,1)}, ...), condition=%wide.region_11.12_spmd, body=%wide.region_8.11_spmd.sunk | while | flops 32 | bytes 2622000 | solution.py:345
  489.7 11.3 %collective-permute-start.2 = (bf16[64,4096]{1,0:T(8,128)(2,1)}, bf16[64,4096]{1,0:T(8,128)(2,1)}, u32[]{:S(2)}, u32[]{:S(2)}) collective-permute-start(bf16[64,4096]{1,0:T(8,128)(2,1)} %get-tuple-element.1189), channel_id=1, source_target_pairs={{16,0},{32,16},{48,32},{64,48},{80,64},{96,80},{112,96},{0,112},{1... | collective-permute-start | bytes 1572872 | tf_op jit(solution)/shard_map/while/body/eval_jaxpr/ppermute | solution.py:141
  558.0 9.4 %conditional.8 = ((bf16[64,4096]{1,0:T(8,128)(2,1)}, bf16[2,4,64,4096]{3,2,1,0:T(8,128)(2,1)}, bf16[2,4,64,4096]{3,2,1,0:T(8,128)(2,1)}, bf16[2,4,64,512]{3,2,1,0:T(8,128)(2,1)S(1)}, bf16[2,4,64,512]{3,2,1,0:T(8,128)(2,1)S(1)})) conditional(s32[]{:T(128)} %convert_element_type.165, (bf16[2,4,64,4096]{3,2,1,0:T(8,128)(2,1)}, ...), branch_computations={%region_9.9_spmd, %region_10.10_spmd} | conditional | bytes 524338 | solution.py:327
  558.1 9.4 %branch_1_fun.5 = (bf16[64,4096]{1,0:T(8,128)(2,1)}, bf16[2,4,64,4096]{3,2,1,0:T(8,128)(2,1)}, bf16[2,4,64,4096]{3,2,1,0:T(8,128)(2,1)}, bf16[2,4,64,512]{3,2,1,0:T(8,128)(2,1)S(1)}, bf16[2,4,64,512]{3,2,1,0:T(8,128)(2,1)S(1)}) custom-call(s32[4]{0:T(128)S(1)} %get-tuple-element.853.sc_ref, ...), custom_call_target="tpu_custom_call", output_to_operand_aliasing={{1}: (6, {}), {2}: (7, {}), {3}: (8, {}), {4}: (9, {})} | custom-call | tf_op jit(solution)/shard_map/while/body/eval_jaxpr/cond/branch_1_fun/pallas_call | solution.py:110
  574.6 9.2 %conditional.8 = ((bf16[64,4096]{1,0:T(8,128)(2,1)}, bf16[2,4,64,4096]{3,2,1,0:T(8,128)(2,1)}, bf16[2,4,64,4096]{3,2,1,0:T(8,128)(2,1)}, bf16[2,4,64,512]{3,2,1,0:T(8,128)(2,1)S(1)}, bf16[2,4,64,512]{3,2,1,0:T(8,128)(2,1)S(1)})) conditional(s32[]{:T(128)} %convert_element_type.165, (bf16[2,4,64,4096]{3,2,1,0:T(8,128)(2,1)}, ...), branch_computations={%region_9.9_spmd, %region_10.10_spmd} | conditional | bytes 524338 | solution.py:327
  623.7 81.9 %reduce-scatter.3.cloned.1.call-done = bf16[256,1024]{1,0:T(8,128)(2,1)} async-done(((bf16[4096,1024]{1,0:T(8,128)(2,1)}), bf16[256,1024]{1,0:T(8,128)(2,1)}) %reduce-scatter.3.cloned.1.call-update) | async-done | bytes 524304 | tf_op jit(solution)/shard_map/reduce_scatter | solution.py:239
  (230 shorter events, 459.1 us)
Async XLA Ops:
  7.2 614.1 %reduce-scatter.5.cloned.1.call-start = ((), (), s32[]{:S(2)}) async-start(), calls=%async_computation.3 | async-start | bytes 8912896 | tf_op jit(solution)/shard_map/reduce_scatter | solution.py:239
  41.8 9.8 %collective-permute-start = (bf16[64,4096]{1,0:T(8,128)(2,1)S(1)}, bf16[64,4096]{1,0:T(8,128)(2,1)S(1)}, u32[]{:S(2)}, u32[]{:S(2)}) collective-permute-start(bf16[64,4096]{1,0:T(8,128)(2,1)S(1)} %get-tuple-element.1158), channel_id=1, source_target_pairs={{112,0},{0,16},{16,32},{32,48},{48,64},{64,80},{80,96},{96,112},{1... | collective-permute-start | bytes 1572872 | tf_op jit(solution)/shard_map/while/body/eval_jaxpr/ppermute | solution.py:141
  58.4 9.8 %collective-permute-start = (bf16[64,4096]{1,0:T(8,128)(2,1)S(1)}, bf16[64,4096]{1,0:T(8,128)(2,1)S(1)}, u32[]{:S(2)}, u32[]{:S(2)}) collective-permute-start(bf16[64,4096]{1,0:T(8,128)(2,1)S(1)} %get-tuple-element.1158), channel_id=1, source_target_pairs={{112,0},{0,16},{16,32},{32,48},{48,64},{64,80},{80,96},{96,112},{1... | collective-permute-start | bytes 1572872 | tf_op jit(solution)/shard_map/while/body/eval_jaxpr/ppermute | solution.py:141
  75.0 9.8 %collective-permute-start = (bf16[64,4096]{1,0:T(8,128)(2,1)S(1)}, bf16[64,4096]{1,0:T(8,128)(2,1)S(1)}, u32[]{:S(2)}, u32[]{:S(2)}) collective-permute-start(bf16[64,4096]{1,0:T(8,128)(2,1)S(1)} %get-tuple-element.1158), channel_id=1, source_target_pairs={{112,0},{0,16},{16,32},{32,48},{48,64},{64,80},{80,96},{96,112},{1... | collective-permute-start | bytes 1572872 | tf_op jit(solution)/shard_map/while/body/eval_jaxpr/ppermute | solution.py:141
  91.7 9.8 %collective-permute-start = (bf16[64,4096]{1,0:T(8,128)(2,1)S(1)}, bf16[64,4096]{1,0:T(8,128)(2,1)S(1)}, u32[]{:S(2)}, u32[]{:S(2)}) collective-permute-start(bf16[64,4096]{1,0:T(8,128)(2,1)S(1)} %get-tuple-element.1158), channel_id=1, source_target_pairs={{112,0},{0,16},{16,32},{32,48},{48,64},{64,80},{80,96},{96,112},{1... | collective-permute-start | bytes 1572872 | tf_op jit(solution)/shard_map/while/body/eval_jaxpr/ppermute | solution.py:141
  101.6 9.8 %collective-permute-start = (bf16[64,4096]{1,0:T(8,128)(2,1)S(1)}, bf16[64,4096]{1,0:T(8,128)(2,1)S(1)}, u32[]{:S(2)}, u32[]{:S(2)}) collective-permute-start(bf16[64,4096]{1,0:T(8,128)(2,1)S(1)} %get-tuple-element.1158), channel_id=1, source_target_pairs={{112,0},{0,16},{16,32},{32,48},{48,64},{64,80},{80,96},{96,112},{1... | collective-permute-start | bytes 1572872 | tf_op jit(solution)/shard_map/while/body/eval_jaxpr/ppermute | solution.py:141
  111.6 9.8 %collective-permute-start = (bf16[64,4096]{1,0:T(8,128)(2,1)S(1)}, bf16[64,4096]{1,0:T(8,128)(2,1)S(1)}, u32[]{:S(2)}, u32[]{:S(2)}) collective-permute-start(bf16[64,4096]{1,0:T(8,128)(2,1)S(1)} %get-tuple-element.1158), channel_id=1, source_target_pairs={{112,0},{0,16},{16,32},{32,48},{48,64},{64,80},{80,96},{96,112},{1... | collective-permute-start | bytes 1572872 | tf_op jit(solution)/shard_map/while/body/eval_jaxpr/ppermute | solution.py:141
  121.6 9.8 %collective-permute-start = (bf16[64,4096]{1,0:T(8,128)(2,1)S(1)}, bf16[64,4096]{1,0:T(8,128)(2,1)S(1)}, u32[]{:S(2)}, u32[]{:S(2)}) collective-permute-start(bf16[64,4096]{1,0:T(8,128)(2,1)S(1)} %get-tuple-element.1158), channel_id=1, source_target_pairs={{112,0},{0,16},{16,32},{32,48},{48,64},{64,80},{80,96},{96,112},{1... | collective-permute-start | bytes 1572872 | tf_op jit(solution)/shard_map/while/body/eval_jaxpr/ppermute | solution.py:141
  131.5 12.8 %collective-permute-start = (bf16[64,4096]{1,0:T(8,128)(2,1)S(1)}, bf16[64,4096]{1,0:T(8,128)(2,1)S(1)}, u32[]{:S(2)}, u32[]{:S(2)}) collective-permute-start(bf16[64,4096]{1,0:T(8,128)(2,1)S(1)} %get-tuple-element.1158), channel_id=1, source_target_pairs={{112,0},{0,16},{16,32},{32,48},{48,64},{64,80},{80,96},{96,112},{1... | collective-permute-start | bytes 1572872 | tf_op jit(solution)/shard_map/while/body/eval_jaxpr/ppermute | solution.py:141
  151.1 9.8 %collective-permute-start = (bf16[64,4096]{1,0:T(8,128)(2,1)S(1)}, bf16[64,4096]{1,0:T(8,128)(2,1)S(1)}, u32[]{:S(2)}, u32[]{:S(2)}) collective-permute-start(bf16[64,4096]{1,0:T(8,128)(2,1)S(1)} %get-tuple-element.1158), channel_id=1, source_target_pairs={{112,0},{0,16},{16,32},{32,48},{48,64},{64,80},{80,96},{96,112},{1... | collective-permute-start | bytes 1572872 | tf_op jit(solution)/shard_map/while/body/eval_jaxpr/ppermute | solution.py:141
  210.9 9.8 %collective-permute-start = (bf16[64,4096]{1,0:T(8,128)(2,1)S(1)}, bf16[64,4096]{1,0:T(8,128)(2,1)S(1)}, u32[]{:S(2)}, u32[]{:S(2)}) collective-permute-start(bf16[64,4096]{1,0:T(8,128)(2,1)S(1)} %get-tuple-element.1158), channel_id=1, source_target_pairs={{112,0},{0,16},{16,32},{32,48},{48,64},{64,80},{80,96},{96,112},{1... | collective-permute-start | bytes 1572872 | tf_op jit(solution)/shard_map/while/body/eval_jaxpr/ppermute | solution.py:141
  220.9 9.8 %collective-permute-start = (bf16[64,4096]{1,0:T(8,128)(2,1)S(1)}, bf16[64,4096]{1,0:T(8,128)(2,1)S(1)}, u32[]{:S(2)}, u32[]{:S(2)}) collective-permute-start(bf16[64,4096]{1,0:T(8,128)(2,1)S(1)} %get-tuple-element.1158), channel_id=1, source_target_pairs={{112,0},{0,16},{16,32},{32,48},{48,64},{64,80},{80,96},{96,112},{1... | collective-permute-start | bytes 1572872 | tf_op jit(solution)/shard_map/while/body/eval_jaxpr/ppermute | solution.py:141
  230.9 9.8 %collective-permute-start = (bf16[64,4096]{1,0:T(8,128)(2,1)S(1)}, bf16[64,4096]{1,0:T(8,128)(2,1)S(1)}, u32[]{:S(2)}, u32[]{:S(2)}) collective-permute-start(bf16[64,4096]{1,0:T(8,128)(2,1)S(1)} %get-tuple-element.1158), channel_id=1, source_target_pairs={{112,0},{0,16},{16,32},{32,48},{48,64},{64,80},{80,96},{96,112},{1... | collective-permute-start | bytes 1572872 | tf_op jit(solution)/shard_map/while/body/eval_jaxpr/ppermute | solution.py:141
  240.8 12.8 %collective-permute-start = (bf16[64,4096]{1,0:T(8,128)(2,1)S(1)}, bf16[64,4096]{1,0:T(8,128)(2,1)S(1)}, u32[]{:S(2)}, u32[]{:S(2)}) collective-permute-start(bf16[64,4096]{1,0:T(8,128)(2,1)S(1)} %get-tuple-element.1158), channel_id=1, source_target_pairs={{112,0},{0,16},{16,32},{32,48},{48,64},{64,80},{80,96},{96,112},{1... | collective-permute-start | bytes 1572872 | tf_op jit(solution)/shard_map/while/body/eval_jaxpr/ppermute | solution.py:141
  253.8 12.8 %collective-permute-start = (bf16[64,4096]{1,0:T(8,128)(2,1)S(1)}, bf16[64,4096]{1,0:T(8,128)(2,1)S(1)}, u32[]{:S(2)}, u32[]{:S(2)}) collective-permute-start(bf16[64,4096]{1,0:T(8,128)(2,1)S(1)} %get-tuple-element.1158), channel_id=1, source_target_pairs={{112,0},{0,16},{16,32},{32,48},{48,64},{64,80},{80,96},{96,112},{1... | collective-permute-start | bytes 1572872 | tf_op jit(solution)/shard_map/while/body/eval_jaxpr/ppermute | solution.py:141
  266.7 12.8 %collective-permute-start = (bf16[64,4096]{1,0:T(8,128)(2,1)S(1)}, bf16[64,4096]{1,0:T(8,128)(2,1)S(1)}, u32[]{:S(2)}, u32[]{:S(2)}) collective-permute-start(bf16[64,4096]{1,0:T(8,128)(2,1)S(1)} %get-tuple-element.1158), channel_id=1, source_target_pairs={{112,0},{0,16},{16,32},{32,48},{48,64},{64,80},{80,96},{96,112},{1... | collective-permute-start | bytes 1572872 | tf_op jit(solution)/shard_map/while/body/eval_jaxpr/ppermute | solution.py:141
  279.7 12.8 %collective-permute-start = (bf16[64,4096]{1,0:T(8,128)(2,1)S(1)}, bf16[64,4096]{1,0:T(8,128)(2,1)S(1)}, u32[]{:S(2)}, u32[]{:S(2)}) collective-permute-start(bf16[64,4096]{1,0:T(8,128)(2,1)S(1)} %get-tuple-element.1158), channel_id=1, source_target_pairs={{112,0},{0,16},{16,32},{32,48},{48,64},{64,80},{80,96},{96,112},{1... | collective-permute-start | bytes 1572872 | tf_op jit(solution)/shard_map/while/body/eval_jaxpr/ppermute | solution.py:141
  299.3 14.5 %collective-permute-start.1 = (bf16[64,4096]{1,0:T(8,128)(2,1)}, bf16[64,4096]{1,0:T(8,128)(2,1)}, u32[]{:S(2)}, u32[]{:S(2)}) collective-permute-start(bf16[64,4096]{1,0:T(8,128)(2,1)} %get-tuple-element.1172), channel_id=1, source_target_pairs={{16,0},{32,16},{48,32},{64,48},{80,64},{96,80},{112,96},{0,112},{1... | collective-permute-start | bytes 1572872 | tf_op jit(solution)/shard_map/while/body/eval_jaxpr/ppermute | solution.py:141
  314.7 18.3 %collective-permute-start.1 = (bf16[64,4096]{1,0:T(8,128)(2,1)}, bf16[64,4096]{1,0:T(8,128)(2,1)}, u32[]{:S(2)}, u32[]{:S(2)}) collective-permute-start(bf16[64,4096]{1,0:T(8,128)(2,1)} %get-tuple-element.1172), channel_id=1, source_target_pairs={{16,0},{32,16},{48,32},{64,48},{80,64},{96,80},{112,96},{0,112},{1... | collective-permute-start | bytes 1572872 | tf_op jit(solution)/shard_map/while/body/eval_jaxpr/ppermute | solution.py:141
  334.0 18.3 %collective-permute-start.1 = (bf16[64,4096]{1,0:T(8,128)(2,1)}, bf16[64,4096]{1,0:T(8,128)(2,1)}, u32[]{:S(2)}, u32[]{:S(2)}) collective-permute-start(bf16[64,4096]{1,0:T(8,128)(2,1)} %get-tuple-element.1172), channel_id=1, source_target_pairs={{16,0},{32,16},{48,32},{64,48},{80,64},{96,80},{112,96},{0,112},{1... | collective-permute-start | bytes 1572872 | tf_op jit(solution)/shard_map/while/body/eval_jaxpr/ppermute | solution.py:141
  353.2 18.3 %collective-permute-start.1 = (bf16[64,4096]{1,0:T(8,128)(2,1)}, bf16[64,4096]{1,0:T(8,128)(2,1)}, u32[]{:S(2)}, u32[]{:S(2)}) collective-permute-start(bf16[64,4096]{1,0:T(8,128)(2,1)} %get-tuple-element.1172), channel_id=1, source_target_pairs={{16,0},{32,16},{48,32},{64,48},{80,64},{96,80},{112,96},{0,112},{1... | collective-permute-start | bytes 1572872 | tf_op jit(solution)/shard_map/while/body/eval_jaxpr/ppermute | solution.py:141
  372.5 10.1 %collective-permute-start.1 = (bf16[64,4096]{1,0:T(8,128)(2,1)}, bf16[64,4096]{1,0:T(8,128)(2,1)}, u32[]{:S(2)}, u32[]{:S(2)}) collective-permute-start(bf16[64,4096]{1,0:T(8,128)(2,1)} %get-tuple-element.1172), channel_id=1, source_target_pairs={{16,0},{32,16},{48,32},{64,48},{80,64},{96,80},{112,96},{0,112},{1... | collective-permute-start | bytes 1572872 | tf_op jit(solution)/shard_map/while/body/eval_jaxpr/ppermute | solution.py:141
  383.5 10.1 %collective-permute-start.1 = (bf16[64,4096]{1,0:T(8,128)(2,1)}, bf16[64,4096]{1,0:T(8,128)(2,1)}, u32[]{:S(2)}, u32[]{:S(2)}) collective-permute-start(bf16[64,4096]{1,0:T(8,128)(2,1)} %get-tuple-element.1172), channel_id=1, source_target_pairs={{16,0},{32,16},{48,32},{64,48},{80,64},{96,80},{112,96},{0,112},{1... | collective-permute-start | bytes 1572872 | tf_op jit(solution)/shard_map/while/body/eval_jaxpr/ppermute | solution.py:141
  394.6 10.1 %collective-permute-start.1 = (bf16[64,4096]{1,0:T(8,128)(2,1)}, bf16[64,4096]{1,0:T(8,128)(2,1)}, u32[]{:S(2)}, u32[]{:S(2)}) collective-permute-start(bf16[64,4096]{1,0:T(8,128)(2,1)} %get-tuple-element.1172), channel_id=1, source_target_pairs={{16,0},{32,16},{48,32},{64,48},{80,64},{96,80},{112,96},{0,112},{1... | collective-permute-start | bytes 1572872 | tf_op jit(solution)/shard_map/while/body/eval_jaxpr/ppermute | solution.py:141
  429.9 10.1 %collective-permute-start.1 = (bf16[64,4096]{1,0:T(8,128)(2,1)}, bf16[64,4096]{1,0:T(8,128)(2,1)}, u32[]{:S(2)}, u32[]{:S(2)}) collective-permute-start(bf16[64,4096]{1,0:T(8,128)(2,1)} %get-tuple-element.1172), channel_id=1, source_target_pairs={{16,0},{32,16},{48,32},{64,48},{80,64},{96,80},{112,96},{0,112},{1... | collective-permute-start | bytes 1572872 | tf_op jit(solution)/shard_map/while/body/eval_jaxpr/ppermute | solution.py:141
  449.2 10.1 %collective-permute-start.1 = (bf16[64,4096]{1,0:T(8,128)(2,1)}, bf16[64,4096]{1,0:T(8,128)(2,1)}, u32[]{:S(2)}, u32[]{:S(2)}) collective-permute-start(bf16[64,4096]{1,0:T(8,128)(2,1)} %get-tuple-element.1172), channel_id=1, source_target_pairs={{16,0},{32,16},{48,32},{64,48},{80,64},{96,80},{112,96},{0,112},{1... | collective-permute-start | bytes 1572872 | tf_op jit(solution)/shard_map/while/body/eval_jaxpr/ppermute | solution.py:141
  468.4 10.1 %collective-permute-start.1 = (bf16[64,4096]{1,0:T(8,128)(2,1)}, bf16[64,4096]{1,0:T(8,128)(2,1)}, u32[]{:S(2)}, u32[]{:S(2)}) collective-permute-start(bf16[64,4096]{1,0:T(8,128)(2,1)} %get-tuple-element.1172), channel_id=1, source_target_pairs={{16,0},{32,16},{48,32},{64,48},{80,64},{96,80},{112,96},{0,112},{1... | collective-permute-start | bytes 1572872 | tf_op jit(solution)/shard_map/while/body/eval_jaxpr/ppermute | solution.py:141
  488.5 217.0 %reduce-scatter.3.cloned.1.call-start = ((), (), s32[]{:S(2)}) async-start(), calls=%async_computation.2 | async-start | bytes 8912896 | tf_op jit(solution)/shard_map/reduce_scatter | solution.py:239
  489.7 18.3 %collective-permute-start.2 = (bf16[64,4096]{1,0:T(8,128)(2,1)}, bf16[64,4096]{1,0:T(8,128)(2,1)}, u32[]{:S(2)}, u32[]{:S(2)}) collective-permute-start(bf16[64,4096]{1,0:T(8,128)(2,1)} %get-tuple-element.1189), channel_id=1, source_target_pairs={{16,0},{32,16},{48,32},{64,48},{80,64},{96,80},{112,96},{0,112},{1... | collective-permute-start | bytes 1572872 | tf_op jit(solution)/shard_map/while/body/eval_jaxpr/ppermute | solution.py:141
  509.0 10.1 %collective-permute-start.2 = (bf16[64,4096]{1,0:T(8,128)(2,1)}, bf16[64,4096]{1,0:T(8,128)(2,1)}, u32[]{:S(2)}, u32[]{:S(2)}) collective-permute-start(bf16[64,4096]{1,0:T(8,128)(2,1)} %get-tuple-element.1189), channel_id=1, source_target_pairs={{16,0},{32,16},{48,32},{64,48},{80,64},{96,80},{112,96},{0,112},{1... | collective-permute-start | bytes 1572872 | tf_op jit(solution)/shard_map/while/body/eval_jaxpr/ppermute | solution.py:141
  520.0 10.4 %collective-permute-start.2 = (bf16[64,4096]{1,0:T(8,128)(2,1)}, bf16[64,4096]{1,0:T(8,128)(2,1)}, u32[]{:S(2)}, u32[]{:S(2)}) collective-permute-start(bf16[64,4096]{1,0:T(8,128)(2,1)} %get-tuple-element.1189), channel_id=1, source_target_pairs={{16,0},{32,16},{48,32},{64,48},{80,64},{96,80},{112,96},{0,112},{1... | collective-permute-start | bytes 1572872 | tf_op jit(solution)/shard_map/while/body/eval_jaxpr/ppermute | solution.py:141
  531.3 10.4 %collective-permute-start.2 = (bf16[64,4096]{1,0:T(8,128)(2,1)}, bf16[64,4096]{1,0:T(8,128)(2,1)}, u32[]{:S(2)}, u32[]{:S(2)}) collective-permute-start(bf16[64,4096]{1,0:T(8,128)(2,1)} %get-tuple-element.1189), channel_id=1, source_target_pairs={{16,0},{32,16},{48,32},{64,48},{80,64},{96,80},{112,96},{0,112},{1... | collective-permute-start | bytes 1572872 | tf_op jit(solution)/shard_map/while/body/eval_jaxpr/ppermute | solution.py:141
  (15 other events, 94.0 us)
Sparse Core Ops, SparseCore 0:
  488.7 88.4 reduce-scatter.4
  617.0 88.5 reduce-scatter.2

commit v14 on v13

--- a/solution.py
+++ b/solution.py
@@ -7,7 +7,7 @@
 
 BLK = 64
 SPLIT = 1
-TK = 256
+TK = 512
 TKB = 512
 LANES = 128
 

time: 718 us -> 707 us (0.985)
  no operation moved by 1% of the time
where the time goes in v14:
time: 707 us; the launch traced here: 706 us
  waiting for transfers between devices  412 us (58%)
  Pallas kernels  144 us (20%)
  starting transfers between devices  81.9 us (12%)
  local copies, waits for them, and re-layouts  32.7 us (5%)
  between operations  14.3 us (2%)
  matrix products  13.7 us (2%)
    ppermute x38, waiting for transfers between devices, shifted(): return lax.ppermute(block, axis, route)  330 us
    reduce_scatter x2, waiting for transfers between devices, settle(): lax.psum_scatter(joined, 'dp', scatter_dimension=0, tiled=True)  82.1 us
    ppermute x38, starting transfers between devices, shifted(): return lax.ppermute(block, axis, route)  81.6 us
    pallas_call x8, Pallas kernels, bwd_call(): pl.pallas_call(_bwd_kernel, grid_spec=pltpu.PrefetchScalarGridSpec(num_sc...  72.9 us
    pallas_call x8, Pallas kernels, fwd_call(): pl.pallas_call(_fwd_kernel, grid_spec=pltpu.PrefetchScalarGridSpec(num_sc...  46.7 us
    pallas_call x2, Pallas kernels, masked(): pl.pallas_call(kernel, grid_spec=pltpu.PrefetchScalarGridSpec(num_scalar_...  24.3 us
    another operation x29, local copies, waits for them, and re-layouts  18 us
  transfers between devices with their start and end apart: 40, of which 39 were waited for; matrix products, arithmetic and copies ran while one was open for 3% of the time, Pallas kernels for 5%

profile of v14, /device:TPU:0, one launch (start us, length us, event | category | flops | bytes accessed | tf_op | source)
XLA Modules:
  0.0 706.2 jit_solution(11994347829980820199)
XLA Ops:
  8.0 14.2 %shard_map.77 = bf16[2,4096,512]{2,1,0:T(8,128)(2,1)} custom-call(s32[2,64,8]{2,1,0:T(8,128)S(1)} %bitcast.85, bf16[2,4096,512]{2,1,0:T(8,128)(2,1)} %bitcast.91), custom_call_target="tpu_custom_call" | custom-call | tf_op jit(solution)/shard_map/pallas_call | solution.py:166
  22.2 10.2 %shard_map.78 = bf16[2,512,4096]{2,1,0:T(8,128)(2,1)} custom-call(s32[2,8,64]{2,1,0:T(8,128)S(1)} %bitcast.86, bf16[2,512,4096]{2,1,0:T(8,128)(2,1)} %bitcast.92), custom_call_target="tpu_custom_call" | custom-call | tf_op jit(solution)/shard_map/pallas_call | solution.py:166
  35.0 246.3 %while.66 = (s32[]{:T(128)}, bf16[64,4096]{1,0:T(8,128)(2,1)S(1)}, bf16[2,4,64,4096]{3,2,1,0:T(8,128)(2,1)}, s32[]{:T(128)}, pred[]{:T(512)}, /*index=5*/bf16[4,...) while((s32[]{:T(128)}, bf16[64,4096]{1,0:T(8,128)(2,1)S(1)}, ...), condition=%wide.region_3.4_spmd, body=%wide.region_0.3_spmd.sunk | while | flops 31 | bytes 2621852 | solution.py:295
  41.0 9.8 %collective-permute-done = bf16[64,4096]{1,0:T(8,128)(2,1)S(1)} collective-permute-done((bf16[64,4096]{1,0:T(8,128)(2,1)S(1)}, bf16[64,4096]{1,0:T(8,128)(2,1)S(1)}, u32[]{:S(2)}, u32[]{:S(2)}) %collective-permute-start) | collective-permute-done | bytes 524320 | tf_op jit(solution)/shard_map/while/body/eval_jaxpr/ppermute | solution.py:141
  56.7 9.8 %collective-permute-done = bf16[64,4096]{1,0:T(8,128)(2,1)S(1)} collective-permute-done((bf16[64,4096]{1,0:T(8,128)(2,1)S(1)}, bf16[64,4096]{1,0:T(8,128)(2,1)S(1)}, u32[]{:S(2)}, u32[]{:S(2)}) %collective-permute-start) | collective-permute-done | bytes 524320 | tf_op jit(solution)/shard_map/while/body/eval_jaxpr/ppermute | solution.py:141
  72.5 9.8 %collective-permute-done = bf16[64,4096]{1,0:T(8,128)(2,1)S(1)} collective-permute-done((bf16[64,4096]{1,0:T(8,128)(2,1)S(1)}, bf16[64,4096]{1,0:T(8,128)(2,1)S(1)}, u32[]{:S(2)}, u32[]{:S(2)}) %collective-permute-start) | collective-permute-done | bytes 524320 | tf_op jit(solution)/shard_map/while/body/eval_jaxpr/ppermute | solution.py:141
  88.2 9.8 %collective-permute-done = bf16[64,4096]{1,0:T(8,128)(2,1)S(1)} collective-permute-done((bf16[64,4096]{1,0:T(8,128)(2,1)S(1)}, bf16[64,4096]{1,0:T(8,128)(2,1)S(1)}, u32[]{:S(2)}, u32[]{:S(2)}) %collective-permute-start) | collective-permute-done | bytes 524320 | tf_op jit(solution)/shard_map/while/body/eval_jaxpr/ppermute | solution.py:141
  98.2 9.8 %collective-permute-done = bf16[64,4096]{1,0:T(8,128)(2,1)S(1)} collective-permute-done((bf16[64,4096]{1,0:T(8,128)(2,1)S(1)}, bf16[64,4096]{1,0:T(8,128)(2,1)S(1)}, u32[]{:S(2)}, u32[]{:S(2)}) %collective-permute-start) | collective-permute-done | bytes 524320 | tf_op jit(solution)/shard_map/while/body/eval_jaxpr/ppermute | solution.py:141
  108.2 9.8 %collective-permute-done = bf16[64,4096]{1,0:T(8,128)(2,1)S(1)} collective-permute-done((bf16[64,4096]{1,0:T(8,128)(2,1)S(1)}, bf16[64,4096]{1,0:T(8,128)(2,1)S(1)}, u32[]{:S(2)}, u32[]{:S(2)}) %collective-permute-start) | collective-permute-done | bytes 524320 | tf_op jit(solution)/shard_map/while/body/eval_jaxpr/ppermute | solution.py:141
  118.1 9.8 %collective-permute-done = bf16[64,4096]{1,0:T(8,128)(2,1)S(1)} collective-permute-done((bf16[64,4096]{1,0:T(8,128)(2,1)S(1)}, bf16[64,4096]{1,0:T(8,128)(2,1)S(1)}, u32[]{:S(2)}, u32[]{:S(2)}) %collective-permute-start) | collective-permute-done | bytes 524320 | tf_op jit(solution)/shard_map/while/body/eval_jaxpr/ppermute | solution.py:141
  128.1 11.9 %collective-permute-done = bf16[64,4096]{1,0:T(8,128)(2,1)S(1)} collective-permute-done((bf16[64,4096]{1,0:T(8,128)(2,1)S(1)}, bf16[64,4096]{1,0:T(8,128)(2,1)S(1)}, u32[]{:S(2)}, u32[]{:S(2)}) %collective-permute-start) | collective-permute-done | bytes 524320 | tf_op jit(solution)/shard_map/while/body/eval_jaxpr/ppermute | solution.py:141
  146.0 9.8 %collective-permute-done = bf16[64,4096]{1,0:T(8,128)(2,1)S(1)} collective-permute-done((bf16[64,4096]{1,0:T(8,128)(2,1)S(1)}, bf16[64,4096]{1,0:T(8,128)(2,1)S(1)}, u32[]{:S(2)}, u32[]{:S(2)}) %collective-permute-start) | collective-permute-done | bytes 524320 | tf_op jit(solution)/shard_map/while/body/eval_jaxpr/ppermute | solution.py:141
  161.7 9.8 %collective-permute-done = bf16[64,4096]{1,0:T(8,128)(2,1)S(1)} collective-permute-done((bf16[64,4096]{1,0:T(8,128)(2,1)S(1)}, bf16[64,4096]{1,0:T(8,128)(2,1)S(1)}, u32[]{:S(2)}, u32[]{:S(2)}) %collective-permute-start) | collective-permute-done | bytes 524320 | tf_op jit(solution)/shard_map/while/body/eval_jaxpr/ppermute | solution.py:141
  177.5 9.8 %collective-permute-done = bf16[64,4096]{1,0:T(8,128)(2,1)S(1)} collective-permute-done((bf16[64,4096]{1,0:T(8,128)(2,1)S(1)}, bf16[64,4096]{1,0:T(8,128)(2,1)S(1)}, u32[]{:S(2)}, u32[]{:S(2)}) %collective-permute-start) | collective-permute-done | bytes 524320 | tf_op jit(solution)/shard_map/while/body/eval_jaxpr/ppermute | solution.py:141
  193.3 9.8 %collective-permute-done = bf16[64,4096]{1,0:T(8,128)(2,1)S(1)} collective-permute-done((bf16[64,4096]{1,0:T(8,128)(2,1)S(1)}, bf16[64,4096]{1,0:T(8,128)(2,1)S(1)}, u32[]{:S(2)}, u32[]{:S(2)}) %collective-permute-start) | collective-permute-done | bytes 524320 | tf_op jit(solution)/shard_map/while/body/eval_jaxpr/ppermute | solution.py:141
  203.2 9.8 %collective-permute-done = bf16[64,4096]{1,0:T(8,128)(2,1)S(1)} collective-permute-done((bf16[64,4096]{1,0:T(8,128)(2,1)S(1)}, bf16[64,4096]{1,0:T(8,128)(2,1)S(1)}, u32[]{:S(2)}, u32[]{:S(2)}) %collective-permute-start) | collective-permute-done | bytes 524320 | tf_op jit(solution)/shard_map/while/body/eval_jaxpr/ppermute | solution.py:141
  213.2 9.8 %collective-permute-done = bf16[64,4096]{1,0:T(8,128)(2,1)S(1)} collective-permute-done((bf16[64,4096]{1,0:T(8,128)(2,1)S(1)}, bf16[64,4096]{1,0:T(8,128)(2,1)S(1)}, u32[]{:S(2)}, u32[]{:S(2)}) %collective-permute-start) | collective-permute-done | bytes 524320 | tf_op jit(solution)/shard_map/while/body/eval_jaxpr/ppermute | solution.py:141
  223.1 9.8 %collective-permute-done = bf16[64,4096]{1,0:T(8,128)(2,1)S(1)} collective-permute-done((bf16[64,4096]{1,0:T(8,128)(2,1)S(1)}, bf16[64,4096]{1,0:T(8,128)(2,1)S(1)}, u32[]{:S(2)}, u32[]{:S(2)}) %collective-permute-start) | collective-permute-done | bytes 524320 | tf_op jit(solution)/shard_map/while/body/eval_jaxpr/ppermute | solution.py:141
  233.1 11.9 %collective-permute-done = bf16[64,4096]{1,0:T(8,128)(2,1)S(1)} collective-permute-done((bf16[64,4096]{1,0:T(8,128)(2,1)S(1)}, bf16[64,4096]{1,0:T(8,128)(2,1)S(1)}, u32[]{:S(2)}, u32[]{:S(2)}) %collective-permute-start) | collective-permute-done | bytes 524320 | tf_op jit(solution)/shard_map/while/body/eval_jaxpr/ppermute | solution.py:141
  245.2 11.9 %collective-permute-done = bf16[64,4096]{1,0:T(8,128)(2,1)S(1)} collective-permute-done((bf16[64,4096]{1,0:T(8,128)(2,1)S(1)}, bf16[64,4096]{1,0:T(8,128)(2,1)S(1)}, u32[]{:S(2)}, u32[]{:S(2)}) %collective-permute-start) | collective-permute-done | bytes 524320 | tf_op jit(solution)/shard_map/while/body/eval_jaxpr/ppermute | solution.py:141
  257.3 11.9 %collective-permute-done = bf16[64,4096]{1,0:T(8,128)(2,1)S(1)} collective-permute-done((bf16[64,4096]{1,0:T(8,128)(2,1)S(1)}, bf16[64,4096]{1,0:T(8,128)(2,1)S(1)}, u32[]{:S(2)}, u32[]{:S(2)}) %collective-permute-start) | collective-permute-done | bytes 524320 | tf_op jit(solution)/shard_map/while/body/eval_jaxpr/ppermute | solution.py:141
  269.3 11.9 %collective-permute-done = bf16[64,4096]{1,0:T(8,128)(2,1)S(1)} collective-permute-done((bf16[64,4096]{1,0:T(8,128)(2,1)S(1)}, bf16[64,4096]{1,0:T(8,128)(2,1)S(1)}, u32[]{:S(2)}, u32[]{:S(2)}) %collective-permute-start) | collective-permute-done | bytes 524320 | tf_op jit(solution)/shard_map/while/body/eval_jaxpr/ppermute | solution.py:141
  287.2 180.2 %while.67 = (s32[]{:T(128)}, bf16[64,4096]{1,0:T(8,128)(2,1)}, bf16[2,4,64,4096]{3,2,1,0:T(8,128)(2,1)}, bf16[2,4,64,4096]{3,2,1,0:T(8,128)(2,1)}, bf16[2,4,64,5...) while((s32[]{:T(128)}, bf16[64,4096]{1,0:T(8,128)(2,1)}, ...), condition=%wide.region_7.8_spmd, body=%wide.region_4.7_spmd.sunk | while | flops 31 | bytes 2621980 | solution.py:343
  303.5 11.3 %collective-permute-start.1 = (bf16[64,4096]{1,0:T(8,128)(2,1)}, bf16[64,4096]{1,0:T(8,128)(2,1)}, u32[]{:S(2)}, u32[]{:S(2)}) collective-permute-start(bf16[64,4096]{1,0:T(8,128)(2,1)} %get-tuple-element.1172), channel_id=1, source_target_pairs={{16,0},{32,16},{48,32},{64,48},{80,64},{96,80},{112,96},{0,112},{1... | collective-permute-start | bytes 1572872 | tf_op jit(solution)/shard_map/while/body/eval_jaxpr/ppermute | solution.py:141
  322.8 11.3 %collective-permute-start.1 = (bf16[64,4096]{1,0:T(8,128)(2,1)}, bf16[64,4096]{1,0:T(8,128)(2,1)}, u32[]{:S(2)}, u32[]{:S(2)}) collective-permute-start(bf16[64,4096]{1,0:T(8,128)(2,1)} %get-tuple-element.1172), channel_id=1, source_target_pairs={{16,0},{32,16},{48,32},{64,48},{80,64},{96,80},{112,96},{0,112},{1... | collective-permute-start | bytes 1572872 | tf_op jit(solution)/shard_map/while/body/eval_jaxpr/ppermute | solution.py:141
  342.0 11.3 %collective-permute-start.1 = (bf16[64,4096]{1,0:T(8,128)(2,1)}, bf16[64,4096]{1,0:T(8,128)(2,1)}, u32[]{:S(2)}, u32[]{:S(2)}) collective-permute-start(bf16[64,4096]{1,0:T(8,128)(2,1)} %get-tuple-element.1172), channel_id=1, source_target_pairs={{16,0},{32,16},{48,32},{64,48},{80,64},{96,80},{112,96},{0,112},{1... | collective-permute-start | bytes 1572872 | tf_op jit(solution)/shard_map/while/body/eval_jaxpr/ppermute | solution.py:141
  477.6 118.0 %while.68 = (s32[]{:T(128)}, bf16[64,4096]{1,0:T(8,128)(2,1)}, bf16[2,4,64,4096]{3,2,1,0:T(8,128)(2,1)}, bf16[2,4,64,4096]{3,2,1,0:T(8,128)(2,1)}, bf16[2,4,64,5...) while((s32[]{:T(128)}, bf16[64,4096]{1,0:T(8,128)(2,1)}, ...), condition=%wide.region_11.12_spmd, body=%wide.region_8.11_spmd.sunk | while | flops 32 | bytes 2622000 | solution.py:345
  478.5 11.3 %collective-permute-start.2 = (bf16[64,4096]{1,0:T(8,128)(2,1)}, bf16[64,4096]{1,0:T(8,128)(2,1)}, u32[]{:S(2)}, u32[]{:S(2)}) collective-permute-start(bf16[64,4096]{1,0:T(8,128)(2,1)} %get-tuple-element.1189), channel_id=1, source_target_pairs={{16,0},{32,16},{48,32},{64,48},{80,64},{96,80},{112,96},{0,112},{1... | collective-permute-start | bytes 1572872 | tf_op jit(solution)/shard_map/while/body/eval_jaxpr/ppermute | solution.py:141
  546.7 9.4 %conditional.8 = ((bf16[64,4096]{1,0:T(8,128)(2,1)}, bf16[2,4,64,4096]{3,2,1,0:T(8,128)(2,1)}, bf16[2,4,64,4096]{3,2,1,0:T(8,128)(2,1)}, bf16[2,4,64,512]{3,2,1,0:T(8,128)(2,1)S(1)}, bf16[2,4,64,512]{3,2,1,0:T(8,128)(2,1)S(1)})) conditional(s32[]{:T(128)} %convert_element_type.165, (bf16[2,4,64,4096]{3,2,1,0:T(8,128)(2,1)}, ...), branch_computations={%region_9.9_spmd, %region_10.10_spmd} | conditional | bytes 524338 | solution.py:327
  546.7 9.4 %branch_1_fun.5 = (bf16[64,4096]{1,0:T(8,128)(2,1)}, bf16[2,4,64,4096]{3,2,1,0:T(8,128)(2,1)}, bf16[2,4,64,4096]{3,2,1,0:T(8,128)(2,1)}, bf16[2,4,64,512]{3,2,1,0:T(8,128)(2,1)S(1)}, bf16[2,4,64,512]{3,2,1,0:T(8,128)(2,1)S(1)}) custom-call(s32[4]{0:T(128)S(1)} %get-tuple-element.853.sc_ref, ...), custom_call_target="tpu_custom_call", output_to_operand_aliasing={{1}: (6, {}), {2}: (7, {}), {3}: (8, {}), {4}: (9, {})} | custom-call | tf_op jit(solution)/shard_map/while/body/eval_jaxpr/cond/branch_1_fun/pallas_call | solution.py:110
  563.2 9.2 %conditional.8 = ((bf16[64,4096]{1,0:T(8,128)(2,1)}, bf16[2,4,64,4096]{3,2,1,0:T(8,128)(2,1)}, bf16[2,4,64,4096]{3,2,1,0:T(8,128)(2,1)}, bf16[2,4,64,512]{3,2,1,0:T(8,128)(2,1)S(1)}, bf16[2,4,64,512]{3,2,1,0:T(8,128)(2,1)S(1)})) conditional(s32[]{:T(128)} %convert_element_type.165, (bf16[2,4,64,4096]{3,2,1,0:T(8,128)(2,1)}, ...), branch_computations={%region_9.9_spmd, %region_10.10_spmd} | conditional | bytes 524338 | solution.py:327
  612.4 82.1 %reduce-scatter.3.cloned.1.call-done = bf16[256,1024]{1,0:T(8,128)(2,1)} async-done(((bf16[4096,1024]{1,0:T(8,128)(2,1)}), bf16[256,1024]{1,0:T(8,128)(2,1)}) %reduce-scatter.3.cloned.1.call-update) | async-done | bytes 524304 | tf_op jit(solution)/shard_map/reduce_scatter | solution.py:239
  (230 shorter events, 444.0 us)
Async XLA Ops:
  7.2 602.8 %reduce-scatter.5.cloned.1.call-start = ((), (), s32[]{:S(2)}) async-start(), calls=%async_computation.3 | async-start | bytes 8912896 | tf_op jit(solution)/shard_map/reduce_scatter | solution.py:239
  40.9 9.8 %collective-permute-start = (bf16[64,4096]{1,0:T(8,128)(2,1)S(1)}, bf16[64,4096]{1,0:T(8,128)(2,1)S(1)}, u32[]{:S(2)}, u32[]{:S(2)}) collective-permute-start(bf16[64,4096]{1,0:T(8,128)(2,1)S(1)} %get-tuple-element.1158), channel_id=1, source_target_pairs={{112,0},{0,16},{16,32},{32,48},{48,64},{64,80},{80,96},{96,112},{1... | collective-permute-start | bytes 1572872 | tf_op jit(solution)/shard_map/while/body/eval_jaxpr/ppermute | solution.py:141
  56.7 9.8 %collective-permute-start = (bf16[64,4096]{1,0:T(8,128)(2,1)S(1)}, bf16[64,4096]{1,0:T(8,128)(2,1)S(1)}, u32[]{:S(2)}, u32[]{:S(2)}) collective-permute-start(bf16[64,4096]{1,0:T(8,128)(2,1)S(1)} %get-tuple-element.1158), channel_id=1, source_target_pairs={{112,0},{0,16},{16,32},{32,48},{48,64},{64,80},{80,96},{96,112},{1... | collective-permute-start | bytes 1572872 | tf_op jit(solution)/shard_map/while/body/eval_jaxpr/ppermute | solution.py:141
  72.5 9.8 %collective-permute-start = (bf16[64,4096]{1,0:T(8,128)(2,1)S(1)}, bf16[64,4096]{1,0:T(8,128)(2,1)S(1)}, u32[]{:S(2)}, u32[]{:S(2)}) collective-permute-start(bf16[64,4096]{1,0:T(8,128)(2,1)S(1)} %get-tuple-element.1158), channel_id=1, source_target_pairs={{112,0},{0,16},{16,32},{32,48},{48,64},{64,80},{80,96},{96,112},{1... | collective-permute-start | bytes 1572872 | tf_op jit(solution)/shard_map/while/body/eval_jaxpr/ppermute | solution.py:141
  88.2 9.8 %collective-permute-start = (bf16[64,4096]{1,0:T(8,128)(2,1)S(1)}, bf16[64,4096]{1,0:T(8,128)(2,1)S(1)}, u32[]{:S(2)}, u32[]{:S(2)}) collective-permute-start(bf16[64,4096]{1,0:T(8,128)(2,1)S(1)} %get-tuple-element.1158), channel_id=1, source_target_pairs={{112,0},{0,16},{16,32},{32,48},{48,64},{64,80},{80,96},{96,112},{1... | collective-permute-start | bytes 1572872 | tf_op jit(solution)/shard_map/while/body/eval_jaxpr/ppermute | solution.py:141
  98.2 9.8 %collective-permute-start = (bf16[64,4096]{1,0:T(8,128)(2,1)S(1)}, bf16[64,4096]{1,0:T(8,128)(2,1)S(1)}, u32[]{:S(2)}, u32[]{:S(2)}) collective-permute-start(bf16[64,4096]{1,0:T(8,128)(2,1)S(1)} %get-tuple-element.1158), channel_id=1, source_target_pairs={{112,0},{0,16},{16,32},{32,48},{48,64},{64,80},{80,96},{96,112},{1... | collective-permute-start | bytes 1572872 | tf_op jit(solution)/shard_map/while/body/eval_jaxpr/ppermute | solution.py:141
  108.1 9.8 %collective-permute-start = (bf16[64,4096]{1,0:T(8,128)(2,1)S(1)}, bf16[64,4096]{1,0:T(8,128)(2,1)S(1)}, u32[]{:S(2)}, u32[]{:S(2)}) collective-permute-start(bf16[64,4096]{1,0:T(8,128)(2,1)S(1)} %get-tuple-element.1158), channel_id=1, source_target_pairs={{112,0},{0,16},{16,32},{32,48},{48,64},{64,80},{80,96},{96,112},{1... | collective-permute-start | bytes 1572872 | tf_op jit(solution)/shard_map/while/body/eval_jaxpr/ppermute | solution.py:141
  118.1 9.8 %collective-permute-start = (bf16[64,4096]{1,0:T(8,128)(2,1)S(1)}, bf16[64,4096]{1,0:T(8,128)(2,1)S(1)}, u32[]{:S(2)}, u32[]{:S(2)}) collective-permute-start(bf16[64,4096]{1,0:T(8,128)(2,1)S(1)} %get-tuple-element.1158), channel_id=1, source_target_pairs={{112,0},{0,16},{16,32},{32,48},{48,64},{64,80},{80,96},{96,112},{1... | collective-permute-start | bytes 1572872 | tf_op jit(solution)/shard_map/while/body/eval_jaxpr/ppermute | solution.py:141
  128.1 11.9 %collective-permute-start = (bf16[64,4096]{1,0:T(8,128)(2,1)S(1)}, bf16[64,4096]{1,0:T(8,128)(2,1)S(1)}, u32[]{:S(2)}, u32[]{:S(2)}) collective-permute-start(bf16[64,4096]{1,0:T(8,128)(2,1)S(1)} %get-tuple-element.1158), channel_id=1, source_target_pairs={{112,0},{0,16},{16,32},{32,48},{48,64},{64,80},{80,96},{96,112},{1... | collective-permute-start | bytes 1572872 | tf_op jit(solution)/shard_map/while/body/eval_jaxpr/ppermute | solution.py:141
  145.9 9.8 %collective-permute-start = (bf16[64,4096]{1,0:T(8,128)(2,1)S(1)}, bf16[64,4096]{1,0:T(8,128)(2,1)S(1)}, u32[]{:S(2)}, u32[]{:S(2)}) collective-permute-start(bf16[64,4096]{1,0:T(8,128)(2,1)S(1)} %get-tuple-element.1158), channel_id=1, source_target_pairs={{112,0},{0,16},{16,32},{32,48},{48,64},{64,80},{80,96},{96,112},{1... | collective-permute-start | bytes 1572872 | tf_op jit(solution)/shard_map/while/body/eval_jaxpr/ppermute | solution.py:141
  161.7 9.8 %collective-permute-start = (bf16[64,4096]{1,0:T(8,128)(2,1)S(1)}, bf16[64,4096]{1,0:T(8,128)(2,1)S(1)}, u32[]{:S(2)}, u32[]{:S(2)}) collective-permute-start(bf16[64,4096]{1,0:T(8,128)(2,1)S(1)} %get-tuple-element.1158), channel_id=1, source_target_pairs={{112,0},{0,16},{16,32},{32,48},{48,64},{64,80},{80,96},{96,112},{1... | collective-permute-start | bytes 1572872 | tf_op jit(solution)/shard_map/while/body/eval_jaxpr/ppermute | solution.py:141
  177.5 9.8 %collective-permute-start = (bf16[64,4096]{1,0:T(8,128)(2,1)S(1)}, bf16[64,4096]{1,0:T(8,128)(2,1)S(1)}, u32[]{:S(2)}, u32[]{:S(2)}) collective-permute-start(bf16[64,4096]{1,0:T(8,128)(2,1)S(1)} %get-tuple-element.1158), channel_id=1, source_target_pairs={{112,0},{0,16},{16,32},{32,48},{48,64},{64,80},{80,96},{96,112},{1... | collective-permute-start | bytes 1572872 | tf_op jit(solution)/shard_map/while/body/eval_jaxpr/ppermute | solution.py:141
  193.2 9.8 %collective-permute-start = (bf16[64,4096]{1,0:T(8,128)(2,1)S(1)}, bf16[64,4096]{1,0:T(8,128)(2,1)S(1)}, u32[]{:S(2)}, u32[]{:S(2)}) collective-permute-start(bf16[64,4096]{1,0:T(8,128)(2,1)S(1)} %get-tuple-element.1158), channel_id=1, source_target_pairs={{112,0},{0,16},{16,32},{32,48},{48,64},{64,80},{80,96},{96,112},{1... | collective-permute-start | bytes 1572872 | tf_op jit(solution)/shard_map/while/body/eval_jaxpr/ppermute | solution.py:141
  233.1 11.9 %collective-permute-start = (bf16[64,4096]{1,0:T(8,128)(2,1)S(1)}, bf16[64,4096]{1,0:T(8,128)(2,1)S(1)}, u32[]{:S(2)}, u32[]{:S(2)}) collective-permute-start(bf16[64,4096]{1,0:T(8,128)(2,1)S(1)} %get-tuple-element.1158), channel_id=1, source_target_pairs={{112,0},{0,16},{16,32},{32,48},{48,64},{64,80},{80,96},{96,112},{1... | collective-permute-start | bytes 1572872 | tf_op jit(solution)/shard_map/while/body/eval_jaxpr/ppermute | solution.py:141
  245.2 11.9 %collective-permute-start = (bf16[64,4096]{1,0:T(8,128)(2,1)S(1)}, bf16[64,4096]{1,0:T(8,128)(2,1)S(1)}, u32[]{:S(2)}, u32[]{:S(2)}) collective-permute-start(bf16[64,4096]{1,0:T(8,128)(2,1)S(1)} %get-tuple-element.1158), channel_id=1, source_target_pairs={{112,0},{0,16},{16,32},{32,48},{48,64},{64,80},{80,96},{96,112},{1... | collective-permute-start | bytes 1572872 | tf_op jit(solution)/shard_map/while/body/eval_jaxpr/ppermute | solution.py:141
  257.2 11.9 %collective-permute-start = (bf16[64,4096]{1,0:T(8,128)(2,1)S(1)}, bf16[64,4096]{1,0:T(8,128)(2,1)S(1)}, u32[]{:S(2)}, u32[]{:S(2)}) collective-permute-start(bf16[64,4096]{1,0:T(8,128)(2,1)S(1)} %get-tuple-element.1158), channel_id=1, source_target_pairs={{112,0},{0,16},{16,32},{32,48},{48,64},{64,80},{80,96},{96,112},{1... | collective-permute-start | bytes 1572872 | tf_op jit(solution)/shard_map/while/body/eval_jaxpr/ppermute | solution.py:141
  269.3 11.9 %collective-permute-start = (bf16[64,4096]{1,0:T(8,128)(2,1)S(1)}, bf16[64,4096]{1,0:T(8,128)(2,1)S(1)}, u32[]{:S(2)}, u32[]{:S(2)}) collective-permute-start(bf16[64,4096]{1,0:T(8,128)(2,1)S(1)} %get-tuple-element.1158), channel_id=1, source_target_pairs={{112,0},{0,16},{16,32},{32,48},{48,64},{64,80},{80,96},{96,112},{1... | collective-permute-start | bytes 1572872 | tf_op jit(solution)/shard_map/while/body/eval_jaxpr/ppermute | solution.py:141
  288.1 14.5 %collective-permute-start.1 = (bf16[64,4096]{1,0:T(8,128)(2,1)}, bf16[64,4096]{1,0:T(8,128)(2,1)}, u32[]{:S(2)}, u32[]{:S(2)}) collective-permute-start(bf16[64,4096]{1,0:T(8,128)(2,1)} %get-tuple-element.1172), channel_id=1, source_target_pairs={{16,0},{32,16},{48,32},{64,48},{80,64},{96,80},{112,96},{0,112},{1... | collective-permute-start | bytes 1572872 | tf_op jit(solution)/shard_map/while/body/eval_jaxpr/ppermute | solution.py:141
  303.5 18.3 %collective-permute-start.1 = (bf16[64,4096]{1,0:T(8,128)(2,1)}, bf16[64,4096]{1,0:T(8,128)(2,1)}, u32[]{:S(2)}, u32[]{:S(2)}) collective-permute-start(bf16[64,4096]{1,0:T(8,128)(2,1)} %get-tuple-element.1172), channel_id=1, source_target_pairs={{16,0},{32,16},{48,32},{64,48},{80,64},{96,80},{112,96},{0,112},{1... | collective-permute-start | bytes 1572872 | tf_op jit(solution)/shard_map/while/body/eval_jaxpr/ppermute | solution.py:141
  322.8 18.3 %collective-permute-start.1 = (bf16[64,4096]{1,0:T(8,128)(2,1)}, bf16[64,4096]{1,0:T(8,128)(2,1)}, u32[]{:S(2)}, u32[]{:S(2)}) collective-permute-start(bf16[64,4096]{1,0:T(8,128)(2,1)} %get-tuple-element.1172), channel_id=1, source_target_pairs={{16,0},{32,16},{48,32},{64,48},{80,64},{96,80},{112,96},{0,112},{1... | collective-permute-start | bytes 1572872 | tf_op jit(solution)/shard_map/while/body/eval_jaxpr/ppermute | solution.py:141
  342.0 18.3 %collective-permute-start.1 = (bf16[64,4096]{1,0:T(8,128)(2,1)}, bf16[64,4096]{1,0:T(8,128)(2,1)}, u32[]{:S(2)}, u32[]{:S(2)}) collective-permute-start(bf16[64,4096]{1,0:T(8,128)(2,1)} %get-tuple-element.1172), channel_id=1, source_target_pairs={{16,0},{32,16},{48,32},{64,48},{80,64},{96,80},{112,96},{0,112},{1... | collective-permute-start | bytes 1572872 | tf_op jit(solution)/shard_map/while/body/eval_jaxpr/ppermute | solution.py:141
  361.3 10.1 %collective-permute-start.1 = (bf16[64,4096]{1,0:T(8,128)(2,1)}, bf16[64,4096]{1,0:T(8,128)(2,1)}, u32[]{:S(2)}, u32[]{:S(2)}) collective-permute-start(bf16[64,4096]{1,0:T(8,128)(2,1)} %get-tuple-element.1172), channel_id=1, source_target_pairs={{16,0},{32,16},{48,32},{64,48},{80,64},{96,80},{112,96},{0,112},{1... | collective-permute-start | bytes 1572872 | tf_op jit(solution)/shard_map/while/body/eval_jaxpr/ppermute | solution.py:141
  372.3 10.1 %collective-permute-start.1 = (bf16[64,4096]{1,0:T(8,128)(2,1)}, bf16[64,4096]{1,0:T(8,128)(2,1)}, u32[]{:S(2)}, u32[]{:S(2)}) collective-permute-start(bf16[64,4096]{1,0:T(8,128)(2,1)} %get-tuple-element.1172), channel_id=1, source_target_pairs={{16,0},{32,16},{48,32},{64,48},{80,64},{96,80},{112,96},{0,112},{1... | collective-permute-start | bytes 1572872 | tf_op jit(solution)/shard_map/while/body/eval_jaxpr/ppermute | solution.py:141
  383.3 10.1 %collective-permute-start.1 = (bf16[64,4096]{1,0:T(8,128)(2,1)}, bf16[64,4096]{1,0:T(8,128)(2,1)}, u32[]{:S(2)}, u32[]{:S(2)}) collective-permute-start(bf16[64,4096]{1,0:T(8,128)(2,1)} %get-tuple-element.1172), channel_id=1, source_target_pairs={{16,0},{32,16},{48,32},{64,48},{80,64},{96,80},{112,96},{0,112},{1... | collective-permute-start | bytes 1572872 | tf_op jit(solution)/shard_map/while/body/eval_jaxpr/ppermute | solution.py:141
  418.7 10.1 %collective-permute-start.1 = (bf16[64,4096]{1,0:T(8,128)(2,1)}, bf16[64,4096]{1,0:T(8,128)(2,1)}, u32[]{:S(2)}, u32[]{:S(2)}) collective-permute-start(bf16[64,4096]{1,0:T(8,128)(2,1)} %get-tuple-element.1172), channel_id=1, source_target_pairs={{16,0},{32,16},{48,32},{64,48},{80,64},{96,80},{112,96},{0,112},{1... | collective-permute-start | bytes 1572872 | tf_op jit(solution)/shard_map/while/body/eval_jaxpr/ppermute | solution.py:141
  438.0 10.1 %collective-permute-start.1 = (bf16[64,4096]{1,0:T(8,128)(2,1)}, bf16[64,4096]{1,0:T(8,128)(2,1)}, u32[]{:S(2)}, u32[]{:S(2)}) collective-permute-start(bf16[64,4096]{1,0:T(8,128)(2,1)} %get-tuple-element.1172), channel_id=1, source_target_pairs={{16,0},{32,16},{48,32},{64,48},{80,64},{96,80},{112,96},{0,112},{1... | collective-permute-start | bytes 1572872 | tf_op jit(solution)/shard_map/while/body/eval_jaxpr/ppermute | solution.py:141
  457.2 10.1 %collective-permute-start.1 = (bf16[64,4096]{1,0:T(8,128)(2,1)}, bf16[64,4096]{1,0:T(8,128)(2,1)}, u32[]{:S(2)}, u32[]{:S(2)}) collective-permute-start(bf16[64,4096]{1,0:T(8,128)(2,1)} %get-tuple-element.1172), channel_id=1, source_target_pairs={{16,0},{32,16},{48,32},{64,48},{80,64},{96,80},{112,96},{0,112},{1... | collective-permute-start | bytes 1572872 | tf_op jit(solution)/shard_map/while/body/eval_jaxpr/ppermute | solution.py:141
  477.3 217.2 %reduce-scatter.3.cloned.1.call-start = ((), (), s32[]{:S(2)}) async-start(), calls=%async_computation.2 | async-start | bytes 8912896 | tf_op jit(solution)/shard_map/reduce_scatter | solution.py:239
  478.5 18.3 %collective-permute-start.2 = (bf16[64,4096]{1,0:T(8,128)(2,1)}, bf16[64,4096]{1,0:T(8,128)(2,1)}, u32[]{:S(2)}, u32[]{:S(2)}) collective-permute-start(bf16[64,4096]{1,0:T(8,128)(2,1)} %get-tuple-element.1189), channel_id=1, source_target_pairs={{16,0},{32,16},{48,32},{64,48},{80,64},{96,80},{112,96},{0,112},{1... | collective-permute-start | bytes 1572872 | tf_op jit(solution)/shard_map/while/body/eval_jaxpr/ppermute | solution.py:141
  497.8 10.1 %collective-permute-start.2 = (bf16[64,4096]{1,0:T(8,128)(2,1)}, bf16[64,4096]{1,0:T(8,128)(2,1)}, u32[]{:S(2)}, u32[]{:S(2)}) collective-permute-start(bf16[64,4096]{1,0:T(8,128)(2,1)} %get-tuple-element.1189), channel_id=1, source_target_pairs={{16,0},{32,16},{48,32},{64,48},{80,64},{96,80},{112,96},{0,112},{1... | collective-permute-start | bytes 1572872 | tf_op jit(solution)/shard_map/while/body/eval_jaxpr/ppermute | solution.py:141
  508.8 10.4 %collective-permute-start.2 = (bf16[64,4096]{1,0:T(8,128)(2,1)}, bf16[64,4096]{1,0:T(8,128)(2,1)}, u32[]{:S(2)}, u32[]{:S(2)}) collective-permute-start(bf16[64,4096]{1,0:T(8,128)(2,1)} %get-tuple-element.1189), channel_id=1, source_target_pairs={{16,0},{32,16},{48,32},{64,48},{80,64},{96,80},{112,96},{0,112},{1... | collective-permute-start | bytes 1572872 | tf_op jit(solution)/shard_map/while/body/eval_jaxpr/ppermute | solution.py:141
  520.1 10.3 %collective-permute-start.2 = (bf16[64,4096]{1,0:T(8,128)(2,1)}, bf16[64,4096]{1,0:T(8,128)(2,1)}, u32[]{:S(2)}, u32[]{:S(2)}) collective-permute-start(bf16[64,4096]{1,0:T(8,128)(2,1)} %get-tuple-element.1189), channel_id=1, source_target_pairs={{16,0},{32,16},{48,32},{64,48},{80,64},{96,80},{112,96},{0,112},{1... | collective-permute-start | bytes 1572872 | tf_op jit(solution)/shard_map/while/body/eval_jaxpr/ppermute | solution.py:141
  (15 other events, 94.1 us)
Sparse Core Ops, SparseCore 0:
  477.4 88.5 reduce-scatter.4
  605.7 88.7 reduce-scatter.2
